TPU v7x, 32 devices: a whole 2x2x4 slice. The times are simulated.
32 devices in a mesh: dp: 4 (over z), pipe: 2 (over core), expert: 4 (over y, x).
Axes of the slice: x: 2, y: 2, z: 4, core: 2. Of those that a mesh axis runs over, the one named last changes fastest.
Arguments:
- tokens: bfloat16 [2, 96, 3072], P(None, 'expert'), may hold values from -6 to 6
- expert_ids: int32 [2, 2, 96, 2], P('pipe', None, 'expert'), may hold values from 0 to 3, all different within a row; in each aligned block of 24 rows (0 to 23, 24 to 47, ..., all dimensions but the last counted through in order) at most 16 rows name the same one
- gates: float32 [2, 2, 96, 2], P('pipe', None, 'expert'), may hold values from 0.1 to 1
- w_gate: bfloat16 [2, 4, 3072, 704], P('pipe', 'expert', None, 'dp'), may hold values from -0.109375 to 0.109375
- w_up: bfloat16 [2, 4, 3072, 704], P('pipe', 'expert', None, 'dp'), may hold values from -0.109375 to 0.109375
- w_down: bfloat16 [2, 4, 704, 3072], P('pipe', 'expert', 'dp'), may hold values from -0.3125 to 0.3125
Outputs:
- layer_out: bfloat16 [2, 2, 96, 3072], P('pipe', None, 'expert', 'dp')
Inputs may be any that keep to these rules, and one draw needn't show every extreme that they name: `expert_ids`: each token names 2 different experts in each layer. Among the tokens of one index of expert in one layer and micro-batch (aligned blocks of 24 tokens) no expert is named by more than 16 tokens, and in some block an expert is named by exactly 16.
All inputs are finite; a program needn't handle non-finite values.
Results may differ from a plain program's by a relative error of at most 0.0052.
Values may be sent and summed in bfloat16 or wider, within the bound.
No kernel may reach another device: no remote copies, remote signals or barrier semaphores. Data moves between devices by JAX's collectives and lax.ppermute only.
A program may use at most 64 MiB of HBM per device.

v0:
```python
import jax
import jax.numpy as jnp
from jax import lax
from jax.sharding import PartitionSpec as P

TOP = 2
CAP = 16


def passed_along(value, axis, by):
    length = lax.axis_size(axis)
    pairs = [(i, i + by) for i in range(length) if 0 <= i + by < length]
    return lax.ppermute(value, axis, pairs)


def build_maps(route_ids, route_gates, experts, rows_all):
    flat_ids = route_ids.reshape(-1)
    onehot = (flat_ids[:, None] == jnp.arange(experts, dtype=jnp.int32)[None, :]).astype(jnp.int32)
    before = jnp.cumsum(onehot, axis=0) - onehot
    placed = flat_ids * CAP + jnp.sum(before * onehot, axis=1)
    matches = jnp.arange(rows_all, dtype=jnp.int32)[:, None] == placed[None, :]
    dispatch_map = jnp.sum(matches.astype(jnp.float32).reshape(rows_all, -1, TOP), axis=2).astype(
        jnp.bfloat16
    )
    combine_map = jnp.sum(
        jnp.where(matches, route_gates.reshape(-1)[None, :], 0.0).reshape(rows_all, -1, TOP), axis=2
    )
    return (dispatch_map, combine_map)


def per_device(tokens, expert_ids, gates, w_gate, w_up, w_down):
    experts = lax.axis_size("expert")
    dp_size = lax.axis_size("dp")
    sections = lax.axis_size("pipe")
    micro_count = tokens.shape[0]
    tok_rows = tokens.shape[1]
    model_width = tokens.shape[2]
    unit_count = w_gate.shape[3]
    columns = model_width // dp_size
    rows_all = experts * CAP
    gate_local = w_gate[0, 0]
    up_local = w_up[0, 0]
    down_local = w_down[0, 0]
    section = lax.axis_index("pipe")
    is_first = section == 0
    column_start = lax.axis_index("dp") * columns
    outputs = jnp.zeros((1, micro_count, tok_rows, columns), jnp.bfloat16)
    carried = jnp.zeros((tok_rows, model_width), jnp.bfloat16)
    turns = micro_count + sections - 1
    for moment in range(turns):
        offset_micro = moment - section
        in_window = (offset_micro >= 0) & (offset_micro < micro_count)
        micro_index = jnp.clip(offset_micro, 0, micro_count - 1)
        own_rows = tokens[min(moment, micro_count - 1)]
        route_ids = lax.dynamic_index_in_dim(expert_ids[0], micro_index, 0, keepdims=False)
        route_gates = lax.dynamic_index_in_dim(gates[0], micro_index, 0, keepdims=False)
        dispatch_map, combine_map = build_maps(route_ids, route_gates, experts, rows_all)
        current = jnp.where(is_first, own_rows, carried)
        current_cols = lax.dynamic_slice_in_dim(current, column_start, columns, 1)
        outgoing = jnp.dot(dispatch_map, current, preferred_element_type=jnp.float32)
        outgoing = outgoing.astype(jnp.bfloat16).reshape(experts, CAP, model_width)
        arrived = lax.all_to_all(outgoing, "expert", split_axis=0, concat_axis=0, tiled=True)
        flat_rows = arrived.reshape(-1, model_width)
        squares = jnp.mean(jnp.square(flat_rows.astype(jnp.float32)), axis=1, keepdims=True)
        inv_rms = lax.rsqrt(squares + 1e-05)
        gate_act = jnp.dot(flat_rows, gate_local, preferred_element_type=jnp.float32) * inv_rms
        up_act = jnp.dot(flat_rows, up_local, preferred_element_type=jnp.float32) * inv_rms
        hidden_rows = (jax.nn.silu(gate_act) * up_act).astype(jnp.bfloat16)
        hidden = hidden_rows.reshape(arrived.shape[0], arrived.shape[1], unit_count)
        hidden = hidden.reshape(rows_all, unit_count)
        summed = lax.psum_scatter(
            lax.dot_general(
                down_local, hidden, (((0,), (1,)), ((), ())), preferred_element_type=jnp.float32
            ),
            "dp",
            scatter_dimension=0,
            tiled=True,
        )
        shares = summed.astype(jnp.bfloat16).reshape(columns, experts, CAP)
        returned = lax.all_to_all(
            shares, "expert", split_axis=1, concat_axis=1, tiled=True
        ).reshape(columns, rows_all)
        mixed = lax.dot_general(
            combine_map,
            returned.astype(jnp.float32),
            (((0,), (1,)), ((), ())),
            precision=lax.Precision.HIGHEST,
            preferred_element_type=jnp.float32,
        )
        new_cols = (current_cols.astype(jnp.float32) + mixed).astype(jnp.bfloat16)
        updated = lax.dynamic_update_slice_in_dim(outputs, new_cols[None, None], micro_index, 1)
        outputs = jnp.where(in_window, updated, outputs)
        if moment + 1 < turns:
            full_rows = lax.all_gather(new_cols, "dp", axis=1, tiled=True)
            carried = passed_along(full_rows, "pipe", 1)
    return outputs


def solution(mesh):
    return jax.shard_map(
        per_device,
        mesh=mesh,
        in_specs=(
            P(None, "expert", None),
            P("pipe", None, "expert", None),
            P("pipe", None, "expert", None),
            P("pipe", "expert", None, "dp"),
            P("pipe", "expert", None, "dp"),
            P("pipe", "expert", "dp", None),
        ),
        out_specs=P("pipe", None, "expert", "dp"),
        check_vma=False,
    )
```

profile of v0, /device:TPU:0, one launch (start us, length us, event | category | flops | bytes accessed | tf_op | source)
XLA Modules:
  0.0 198.9 jit_solution(14078611586446322383)
XLA Ops:
  10.1 12.1 %all_to_all.30 = bf16[4,16,3072]{2,1,0:T(8,128)(2,1)S(1)} all-to-all(bf16[4,16,3072]{2,1,0:T(8,128)(2,1)S(1)} %bitcast.104), channel_id=1, replica_groups=mesh['dp'=4,'pipe'=2,'expert'=4] {'expert'}, dimensions={0} | all-to-all | bytes 786432 | tf_op jit(solution)/shard_map/all_to_all | solution.py:62
  23.2 1.5 convolution_multiply_fusion.5
  24.8 2.8 %convolution_bitcast_fusion.2 = f32[3072,64]{0,1:T(8,128)} fusion(bf16[64,3072]{1,0:T(8,128)(2,1)} %bitcast.99, bf16[1,1,176,3072]{3,2,1,0:T(8,128)(2,1)S(1)} %copy-done, bf16[1,1,3072,176]{2,3,1,0:T(8,128)(2,1)S(1)} %copy-done.2, f32[64,176]{1,0:T(8,128)S(1)} %convolution_multiply_fusion.5, f32[64]{0:T(128)S(1)} %rsqrt.34), kind=kOutput, calls=%fused_computation.2 | convolution fusion | flops 138490880 | bytes 3387648 | tf_op jit(solution)/shard_map/dot_general | solution.py:72
  28.7 22.1 %reduce-scatter.4.cloned.1.call-done = f32[768,64]{0,1:T(8,128)} async-done(((f32[3072,64]{0,1:T(8,128)}), f32[768,64]{0,1:T(8,128)}) %reduce-scatter.4.cloned.1.call-update) | async-done | bytes 196624 | tf_op jit(solution)/shard_map/reduce_scatter | solution.py:71
  50.8 1.6 convert_element_type.101
  52.4 3.6 %all-to-all-start.1 = ((bf16[768,4,16]{0,2,1:T(8,128)(2,1)}), bf16[768,4,16]{0,2,1:T(8,128)(2,1)S(1)}, u32[]{:S(2)}, u32[]{:S(2)}) async-start(bf16[768,4,16]{0,2,1:T(8,128)(2,1)} %bitcast.110), calls=%async_computation.2 | async-start | bytes 196608 | tf_op jit(solution)/shard_map/all_to_all | solution.py:80
  56.4 4.6 %all-to-all-done.1 = bf16[768,4,16]{0,2,1:T(8,128)(2,1)S(1)} async-done(((bf16[768,4,16]{0,2,1:T(8,128)(2,1)}), bf16[768,4,16]{0,2,1:T(8,128)(2,1)S(1)}, u32[]{:S(2)}, u32[]{:S(2)}) %all-to-all-start.1) | async-done | bytes 98336 | tf_op jit(solution)/shard_map/all_to_all | solution.py:80
  61.2 13.5 %all_gather.6 = bf16[24,3072]{1,0:T(8,128)(2,1)S(1)} all-gather(bf16[24,768]{1,0:T(8,128)(2,1)S(1)} %get-tuple-element.20), channel_id=1, replica_groups=mesh['dp'=4,'pipe'=2,'expert'=4] {'dp'}, dimensions={1}, use_global_device_ids=true | all-gather | bytes 184320 | tf_op jit(solution)/shard_map/all_gather | solution.py:94
  78.1 10.3 %all_to_all.31 = bf16[4,16,3072]{2,1,0:T(8,128)(2,1)S(1)} all-to-all(bf16[4,16,3072]{2,1,0:T(8,128)(2,1)S(1)} %bitcast.105), channel_id=1, replica_groups=mesh['dp'=4,'pipe'=2,'expert'=4] {'expert'}, dimensions={0} | all-to-all | bytes 786432 | tf_op jit(solution)/shard_map/all_to_all | solution.py:62
  90.9 2.8 %convolution_bitcast_fusion.1 = f32[3072,64]{0,1:T(8,128)} fusion(bf16[64,3072]{1,0:T(8,128)(2,1)} %bitcast.101, bf16[1,1,176,3072]{3,2,1,0:T(8,128)(2,1)S(1)} %copy-done, bf16[1,1,3072,176]{2,3,1,0:T(8,128)(2,1)S(1)} %copy-done.2, f32[64,176]{1,0:T(8,128)S(1)} %convolution_multiply_fusion.3, f32[64]{0:T(128)S(1)} %rsqrt.36), kind=kOutput, calls=%fused_computation.1 | convolution fusion | flops 138490880 | bytes 3387648 | tf_op jit(solution)/shard_map/dot_general | solution.py:72
  93.8 21.2 %reduce-scatter.6.cloned.1.call-done = f32[768,64]{0,1:T(8,128)} async-done(((f32[3072,64]{0,1:T(8,128)}), f32[768,64]{0,1:T(8,128)}) %reduce-scatter.6.cloned.1.call-update) | async-done | bytes 196624 | tf_op jit(solution)/shard_map/reduce_scatter | solution.py:71
  115.1 1.6 convert_element_type.110
  116.6 3.7 %all-to-all-start.3 = ((bf16[768,4,16]{0,2,1:T(8,128)(2,1)}), bf16[768,4,16]{0,2,1:T(8,128)(2,1)S(1)}, u32[]{:S(2)}, u32[]{:S(2)}) async-start(bf16[768,4,16]{0,2,1:T(8,128)(2,1)} %bitcast.111), calls=%async_computation.5 | async-start | bytes 196608 | tf_op jit(solution)/shard_map/all_to_all | solution.py:80
  120.3 4.9 %all-to-all-done.3 = bf16[768,4,16]{0,2,1:T(8,128)(2,1)S(1)} async-done(((bf16[768,4,16]{0,2,1:T(8,128)(2,1)}), bf16[768,4,16]{0,2,1:T(8,128)(2,1)S(1)}, u32[]{:S(2)}, u32[]{:S(2)}) %all-to-all-start.3) | async-done | bytes 98336 | tf_op jit(solution)/shard_map/all_to_all | solution.py:80
  125.2 1.6 fusion.38
  126.8 13.4 %all_gather.7 = bf16[24,3072]{1,0:T(8,128)(2,1)S(1)} all-gather(bf16[24,768]{1,0:T(8,128)(2,1)S(1)} %get-tuple-element.12), channel_id=1, replica_groups=mesh['dp'=4,'pipe'=2,'expert'=4] {'dp'}, dimensions={1}, use_global_device_ids=true | all-gather | bytes 184320 | tf_op jit(solution)/shard_map/all_gather | solution.py:94
  143.7 10.3 %all_to_all.32 = bf16[4,16,3072]{2,1,0:T(8,128)(2,1)S(1)} all-to-all(bf16[4,16,3072]{2,1,0:T(8,128)(2,1)S(1)} %bitcast.106), channel_id=1, replica_groups=mesh['dp'=4,'pipe'=2,'expert'=4] {'expert'}, dimensions={0} | all-to-all | bytes 786432 | tf_op jit(solution)/shard_map/all_to_all | solution.py:62
  155.0 1.5 convolution_multiply_fusion.1
  156.5 2.9 %convolution_bitcast_fusion = f32[3072,64]{0,1:T(8,128)} fusion(bf16[64,3072]{1,0:T(8,128)(2,1)} %bitcast.103, bf16[1,1,176,3072]{3,2,1,0:T(8,128)(2,1)S(1)} %copy-done, bf16[1,1,3072,176]{2,3,1,0:T(8,128)(2,1)S(1)} %copy-done.2, f32[64,176]{1,0:T(8,128)S(1)} %convolution_multiply_fusion.1, f32[64]{0:T(128)S(1)} %rsqrt.38), kind=kOutput, calls=%fused_computation | convolution fusion | flops 138490880 | bytes 3387648 | tf_op jit(solution)/shard_map/dot_general | solution.py:72
  159.3 21.3 %reduce-scatter.8.cloned.1.call-done = f32[768,64]{0,1:T(8,128)} async-done(((f32[3072,64]{0,1:T(8,128)}), f32[768,64]{0,1:T(8,128)}) %reduce-scatter.8.cloned.1.call-update) | async-done | bytes 196624 | tf_op jit(solution)/shard_map/reduce_scatter | solution.py:71
  180.7 1.6 convert_element_type.119
  182.2 3.7 %all-to-all-start.5 = ((bf16[768,4,16]{0,2,1:T(8,128)(2,1)}), bf16[768,4,16]{0,2,1:T(8,128)(2,1)S(1)}, u32[]{:S(2)}, u32[]{:S(2)}) async-start(bf16[768,4,16]{0,2,1:T(8,128)(2,1)} %bitcast.27), calls=%async_computation.8 | async-start | bytes 196608 | tf_op jit(solution)/shard_map/all_to_all | solution.py:80
  185.9 4.9 %all-to-all-done.5 = bf16[768,4,16]{0,2,1:T(8,128)(2,1)S(1)} async-done(((bf16[768,4,16]{0,2,1:T(8,128)(2,1)}), bf16[768,4,16]{0,2,1:T(8,128)(2,1)S(1)}, u32[]{:S(2)}, u32[]{:S(2)}) %all-to-all-start.5) | async-done | bytes 98336 | tf_op jit(solution)/shard_map/all_to_all | solution.py:80
  190.8 1.6 fusion.37
  (70 shorter events, 16.6 us)
Async XLA Ops:
  6.5 18.2 %copy-start = (bf16[1,1,176,3072]{3,2,1,0:T(8,128)(2,1)S(1)}, bf16[1,1,176,3072]{3,2,1,0:T(8,128)(2,1)}, u32[]{:S(2)}) copy-start(bf16[1,1,176,3072]{3,2,1,0:T(8,128)(2,1)} %param.11) | copy-start | bytes 3244036
  6.5 44.3 %reduce-scatter.4.cloned.1.call-start = ((), (), s32[]{:S(2)}) async-start(), calls=%async_computation.9 | async-start | bytes 983040 | tf_op jit(solution)/shard_map/reduce_scatter | solution.py:71
  7.6 15.6 %copy-start.1 = (bf16[1,1,3072,176]{2,3,1,0:T(8,128)(2,1)S(1)}, bf16[1,1,3072,176]{2,3,1,0:T(8,128)(2,1)}, u32[]{:S(2)}) copy-start(bf16[1,1,3072,176]{2,3,1,0:T(8,128)(2,1)} %param.9) | copy-start | bytes 3244036
  22.2 0.7 copy-start.3
  23.0 1.8 copy-start.2
  52.4 8.6 %all-to-all-start.1 = ((bf16[768,4,16]{0,2,1:T(8,128)(2,1)}), bf16[768,4,16]{0,2,1:T(8,128)(2,1)S(1)}, u32[]{:S(2)}, u32[]{:S(2)}) async-start(bf16[768,4,16]{0,2,1:T(8,128)(2,1)} %bitcast.110), calls=%async_computation.2 | async-start | bytes 196608 | tf_op jit(solution)/shard_map/all_to_all | solution.py:80
  56.0 59.0 %reduce-scatter.6.cloned.1.call-start = ((), (), s32[]{:S(2)}) async-start(), calls=%async_computation.10 | async-start | bytes 983040 | tf_op jit(solution)/shard_map/reduce_scatter | solution.py:71
  61.2 16.7 %copy-start.6 = (bf16[1,2,24,768]{3,2,1,0:T(8,128)(2,1)}, bf16[1,2,24,768]{3,2,1,0:T(8,128)(2,1)S(1)}, u32[]{:S(2)}) copy-start(bf16[1,2,24,768]{3,2,1,0:T(8,128)(2,1)S(1)} %get-tuple-element.19) | copy-start | bytes 221188
  74.6 2.3 %collective-permute-start = (bf16[24,3072]{1,0:T(8,128)(2,1)S(1)}, bf16[24,3072]{1,0:T(8,128)(2,1)S(1)}, u32[]{:S(2)}, u32[]{:S(2)}) collective-permute-start(bf16[24,3072]{1,0:T(8,128)(2,1)S(1)} %all_gather.6), channel_id=1, source_target_pairs={{0,4},{1,5},{2,6},{3,7},{8,12},{9,13},{10,14},{11,15},{16,20},{17,... | collective-permute-start | bytes 442376 | tf_op jit(solution)/shard_map/ppermute | solution.py:13
  88.5 0.7 copy-start.4
  116.6 8.6 %all-to-all-start.3 = ((bf16[768,4,16]{0,2,1:T(8,128)(2,1)}), bf16[768,4,16]{0,2,1:T(8,128)(2,1)S(1)}, u32[]{:S(2)}, u32[]{:S(2)}) async-start(bf16[768,4,16]{0,2,1:T(8,128)(2,1)} %bitcast.111), calls=%async_computation.5 | async-start | bytes 196608 | tf_op jit(solution)/shard_map/all_to_all | solution.py:80
  120.3 60.4 %reduce-scatter.8.cloned.1.call-start = ((), (), s32[]{:S(2)}) async-start(), calls=%async_computation.11 | async-start | bytes 983040 | tf_op jit(solution)/shard_map/reduce_scatter | solution.py:71
  140.2 2.3 %collective-permute-start.1 = (bf16[24,3072]{1,0:T(8,128)(2,1)S(1)}, bf16[24,3072]{1,0:T(8,128)(2,1)S(1)}, u32[]{:S(2)}, u32[]{:S(2)}) collective-permute-start(bf16[24,3072]{1,0:T(8,128)(2,1)S(1)} %all_gather.7), channel_id=1, source_target_pairs={{0,4},{1,5},{2,6},{3,7},{8,12},{9,13},{10,14},{11,15},{16,20},{17,... | collective-permute-start | bytes 442376 | tf_op jit(solution)/shard_map/ppermute | solution.py:13
  154.0 0.7 copy-start.5
  182.2 8.6 %all-to-all-start.5 = ((bf16[768,4,16]{0,2,1:T(8,128)(2,1)}), bf16[768,4,16]{0,2,1:T(8,128)(2,1)S(1)}, u32[]{:S(2)}, u32[]{:S(2)}) async-start(bf16[768,4,16]{0,2,1:T(8,128)(2,1)} %bitcast.27), calls=%async_computation.8 | async-start | bytes 196608 | tf_op jit(solution)/shard_map/all_to_all | solution.py:80
Sparse Core Ops, SparseCore 0:
  27.8 23.0 reduce-scatter.3
  93.9 21.0 reduce-scatter.5
  159.5 21.1 reduce-scatter.7
where the time goes:
time: 200 us; the launch traced here: 199 us
  waiting for transfers between devices  81 us (40%)
  blocking collectives  59.6 us (30%)
  matrix products  17.2 us (9%)
  starting transfers between devices  13.5 us (7%)
  between operations  13.3 us (7%)
  other arithmetic  9.16 us (5%)
  local copies, waits for them, and re-layouts  5.17 us (3%)
    reduce_scatter x3, waiting for transfers between devices, per_device(): lax.psum_scatter(lax.dot_general(down_local, hidden, (((0,), (1,)), ((),...  64.7 us
    all_to_all x3, blocking collectives, per_device(): lax.all_to_all(outgoing, 'expert', split_axis=0, concat_axis=0, tiled=True)  32.7 us
    all_gather x2, blocking collectives, per_device(): full_rows = lax.all_gather(new_cols, 'dp', axis=1, tiled=True)  26.9 us
    all_to_all x3, waiting for transfers between devices, per_device(): lax.all_to_all(shares, 'expert', split_axis=1, concat_axis=1, tiled=True)  14.4 us
    all_to_all x3, starting transfers between devices, per_device(): lax.all_to_all(shares, 'expert', split_axis=1, concat_axis=1, tiled=True)  11 us
    dot_general x3, matrix products, per_device(): lax.dot_general(down_local, hidden, (((0,), (1,)), ((), ())), preferred_e...  8.54 us
    convert_element_type x3, other arithmetic, per_device(): shares = summed.astype(jnp.bfloat16).reshape(columns, experts, CAP)  4.68 us
    dot_general x3, matrix products, per_device(): jnp.dot(flat_rows, gate_local, preferred_element_type=jnp.float32) * inv_rms  4.54 us
  transfers between devices with their start and end apart: 8, of which 8 were waited for; matrix products, arithmetic and copies ran while one was open for 1% of the time, Pallas kernels for 0%

commit v1 on v0

v1 whole, which is shorter than its diff:
```python
import jax
import jax.numpy as jnp
from jax import lax
from jax.sharding import PartitionSpec as P

TOP = 2
CAP = 16
AXES = ("dp", "pipe", "expert")
SMALL_GROUP = 8


class Ring:
    def __init__(self, n):
        self.n = n
        self.xor = n & (n - 1) == 0

    def ahead(self, me, s):
        return me ^ s if self.xor else (me + s) % self.n

    def behind(self, me, s):
        return me ^ s if self.xor else (me - s) % self.n

    def place(self, target, me):
        return target ^ me if self.xor else (target - me) % self.n


def build_maps(route_ids, route_gates, ring, me, rows_all):
    experts = ring.n
    flat_ids = route_ids.reshape(-1)
    onehot = (flat_ids[:, None] == jnp.arange(experts, dtype=jnp.int32)[None, :]).astype(jnp.int32)
    before = jnp.cumsum(onehot, axis=0) - onehot
    slot = jnp.sum(before * onehot, axis=1)
    placed = ring.place(flat_ids, me) * CAP + slot
    matches = jnp.arange(rows_all, dtype=jnp.int32)[:, None] == placed[None, :]
    dispatch_map = jnp.sum(matches.astype(jnp.float32).reshape(rows_all, -1, TOP), axis=2).astype(jnp.bfloat16)
    combine_map = jnp.sum(
        jnp.where(matches, route_gates.reshape(-1)[None, :], 0.0).reshape(rows_all, -1, TOP), axis=2
    )
    return dispatch_map, combine_map


def per_device(tokens, expert_ids, gates, w_gate, w_up, w_down):
    n_dp = lax.axis_size("dp")
    n_pipe = lax.axis_size("pipe")
    n_exp = lax.axis_size("expert")
    micro, tok_rows, width = tokens.shape
    units = w_gate.shape[3]
    columns = width // n_dp
    rows_all = n_exp * CAP
    d_me = lax.axis_index("dp")
    p_me = lax.axis_index("pipe")
    e_me = lax.axis_index("expert")
    dring = Ring(n_dp)
    ering = Ring(n_exp)
    small_dp = n_dp <= SMALL_GROUP

    def lin(d, p, e):
        return (d * n_pipe + p) * n_exp + e

    def expert_pairs(p, s, back):
        step = ering.behind if back else ering.ahead
        return [(lin(d, p, e), lin(d, p, step(e, s))) for d in range(n_dp) for e in range(n_exp)]

    def dp_pairs(p, s):
        return [(lin(d, p, e), lin(dring.ahead(d, s), p, e)) for d in range(n_dp) for e in range(n_exp)]

    gate_local = w_gate[0, 0]
    up_local = w_up[0, 0]
    down_local = w_down[0, 0]

    if small_dp:
        down_parts = []
        for s in range(n_dp):
            piece = lax.dynamic_slice_in_dim(down_local, dring.ahead(d_me, s) * columns, columns, 1)
            if s:
                piece = lax.ppermute(piece, "dp", [(i, dring.ahead(i, s)) for i in range(n_dp)])
            down_parts.append(piece)
        down_full = jnp.concatenate(down_parts, axis=0)
    else:
        down_full = lax.all_to_all(down_local, "dp", 1, 0, tiled=True)

    route_ids = expert_ids[0]
    route_gates = gates[0]
    maps = [build_maps(route_ids[m], route_gates[m], ering, e_me, rows_all) for m in range(micro)]
    dispatch_map = jnp.stack([mp[0] for mp in maps])
    combine_map = jnp.stack([mp[1] for mp in maps])

    def layer(current, p):
        outgoing = jnp.einsum("mrt,mtd->mrd", dispatch_map, current, preferred_element_type=jnp.float32)
        outgoing = outgoing.astype(jnp.bfloat16).reshape(micro, n_exp, CAP, width)
        arrived = [outgoing[:, 0]]
        for s in range(1, n_exp):
            arrived.append(lax.ppermute(outgoing[:, s], AXES, expert_pairs(p, s, False)))
        flat_rows = jnp.stack(arrived, axis=1).reshape(-1, width)
        squares = jnp.mean(jnp.square(flat_rows.astype(jnp.float32)), axis=1, keepdims=True)
        inv_rms = lax.rsqrt(squares + 1e-05)
        gate_act = jnp.dot(flat_rows, gate_local, preferred_element_type=jnp.float32) * inv_rms
        up_act = jnp.dot(flat_rows, up_local, preferred_element_type=jnp.float32) * inv_rms
        hidden = (jax.nn.silu(gate_act) * up_act).astype(jnp.bfloat16)
        if small_dp:
            parts = [hidden]
            for s in range(1, n_dp):
                parts.append(lax.ppermute(hidden, AXES, dp_pairs(p, s)))
            hidden_full = jnp.concatenate(parts, axis=1)
        else:
            hidden_full = lax.all_gather(hidden, "dp", axis=1, tiled=True)
        expert_out = jnp.dot(hidden_full, down_full, preferred_element_type=jnp.float32).astype(jnp.bfloat16)
        expert_out = expert_out.reshape(micro, n_exp, CAP, columns)
        returned = [expert_out[:, 0]]
        for s in range(1, n_exp):
            returned.append(lax.ppermute(expert_out[:, s], AXES, expert_pairs(p, s, True)))
        returned = jnp.stack(returned, axis=1).reshape(micro, rows_all, columns)
        mixed = jnp.einsum(
            "mrt,mrc->mtc",
            combine_map,
            returned.astype(jnp.float32),
            precision=lax.Precision.HIGHEST,
            preferred_element_type=jnp.float32,
        )
        current_cols = lax.dynamic_slice_in_dim(current, d_me * columns, columns, 2)
        return (current_cols.astype(jnp.float32) + mixed).astype(jnp.bfloat16)

    current = tokens
    result = None
    for p in range(n_pipe):
        cols = layer(current, p)
        result = cols if result is None else jnp.where(p_me == p, cols, result)
        if p + 1 < n_pipe:
            if small_dp:
                parts = []
                for s in range(n_dp):
                    pairs = [
                        (lin(d, p, e), lin(dring.ahead(d, s), p + 1, e)) for d in range(n_dp) for e in range(n_exp)
                    ]
                    parts.append(lax.ppermute(cols, AXES, pairs))
                stacked = jnp.stack(parts)
                order = jnp.stack([dring.place(d_me, k) for k in range(n_dp)])
                stacked = jnp.take(stacked, order, axis=0)
                current = jnp.transpose(stacked, (1, 2, 0, 3)).reshape(micro, tok_rows, width)
            else:
                full = lax.all_gather(cols, "dp", axis=2, tiled=True)
                current = lax.ppermute(full, "pipe", [(p, p + 1)])
    return result[None]


def solution(mesh):
    return jax.shard_map(
        per_device,
        mesh=mesh,
        in_specs=(
            P(None, "expert", None),
            P("pipe", None, "expert", None),
            P("pipe", None, "expert", None),
            P("pipe", "expert", None, "dp"),
            P("pipe", "expert", None, "dp"),
            P("pipe", "expert", "dp", None),
        ),
        out_specs=P("pipe", None, "expert", "dp"),
        check_vma=False,
    )
```

time: 200 us -> 109 us (0.55)
  the two profiles are of different devices: /device:TPU:0 before, /device:TPU:1 now
where the time goes in v1:
time: 109 us; the launch traced here: 108 us
  waiting for transfers between devices  48 us (44%)
  starting transfers between devices  42.3 us (39%)
  matrix products  8.48 us (8%)
  local copies, waits for them, and re-layouts  5.55 us (5%)
  other arithmetic  3.25 us (3%)
    ppermute x4, waiting for transfers between devices, per_device(): parts.append(lax.ppermute(cols, AXES, pairs))  22.8 us
    ppermute x3, waiting for transfers between devices, per_device(): lax.ppermute(piece, 'dp', [(i, dring.ahead(i, s)) for i in range(n_dp)])  17 us
    ppermute x6, starting transfers between devices, layer(): parts.append(lax.ppermute(hidden, AXES, dp_pairs(p, s)))  11.3 us
    ppermute x6, starting transfers between devices, layer(): lax.ppermute(outgoing[:, s], AXES, expert_pairs(p, s, False))  11.1 us
    ppermute x6, starting transfers between devices, layer(): lax.ppermute(expert_out[:, s], AXES, expert_pairs(p, s, True))  10.4 us
    ppermute x4, starting transfers between devices, per_device(): parts.append(lax.ppermute(cols, AXES, pairs))  5.17 us
    ppermute x3, starting transfers between devices, per_device(): lax.ppermute(piece, 'dp', [(i, dring.ahead(i, s)) for i in range(n_dp)])  4.44 us
    ppermute x6, waiting for transfers between devices, layer(): lax.ppermute(outgoing[:, s], AXES, expert_pairs(p, s, False))  4.19 us
  transfers between devices with their start and end apart: 25, of which 9 were waited for; matrix products, arithmetic and copies ran while one was open for 3% of the time, Pallas kernels for 0%

profile of v1, /device:TPU:1, one launch (start us, length us, event | category | flops | bytes accessed | tf_op | source)
XLA Modules:
  0.0 108.1 jit_solution(7862783934682264632)
XLA Ops:
  3.7 1.4 %convolution_convert_fusion.1 = bf16[2,64,3072]{2,1,0:T(8,128)(2,1)S(1)} fusion(bf16[2,24,3072]{2,1,0:T(8,128)(2,1)} %param.6, bf16[1,64,24]{1,2,0:T(8,128)(2,1)S(1)} %bitcast.159, bf16[1,64,24]{1,2,0:T(8,128)(2,1)S(1)} %bitcast.161), kind=kOutput, calls=%fused_computation.2 | convolution fusion | flops 19270656 | bytes 1087488 | tf_op jit(solution)/shard_map/mrt,mtd->mrd/dot_general | solution.py:89
  7.3 1.4 %collective-permute-start.2 = (bf16[2,16,3072]{2,1,0:T(8,128)(2,1)S(1)}, bf16[2,16,3072]{2,1,0:T(8,128)(2,1)}, u32[]{:S(2)}, u32[]{:S(2)}) collective-permute-start(bf16[2,16,3072]{2,1,0:T(8,128)(2,1)S(1)} %get-tuple-element.24), channel_id=1, source_target_pairs={{0,3},{1,2},{2,1},{3,0},{8,11},{9,10},{10,9},{11,8},{16,19},{17,18... | collective-permute-start | bytes 589832 | tf_op jit(solution)/shard_map/ppermute | solution.py:93
  9.6 2.1 %collective-permute-start.6 = (bf16[176,768]{1,0:T(8,128)(2,1)}, bf16[176,768]{1,0:T(8,128)(2,1)}, u32[]{:S(2)}, u32[]{:S(2)}) collective-permute-start(bf16[176,768]{1,0:T(8,128)(2,1)} %get-tuple-element.14), channel_id=1, source_target_pairs={{0,8},{8,0},{16,24},{24,16},{1,9},{9,1},{17,25},{25,17},{2,10},{10... | collective-permute-start | bytes 811016 | tf_op jit(solution)/shard_map/ppermute | solution.py:76
  11.7 2.2 %collective-permute-start.8 = (bf16[176,768]{1,0:T(8,128)(2,1)}, bf16[176,768]{1,0:T(8,128)(2,1)}, u32[]{:S(2)}, u32[]{:S(2)}) collective-permute-start(bf16[176,768]{1,0:T(8,128)(2,1)} %get-tuple-element.15), channel_id=1, source_target_pairs={{0,24},{8,16},{16,8},{24,0},{1,25},{9,17},{17,9},{25,1},{2,26},{10... | collective-permute-start | bytes 811016 | tf_op jit(solution)/shard_map/ppermute | solution.py:76
  19.0 2.1 %collective-permute-done.8 = bf16[176,768]{1,0:T(8,128)(2,1)} collective-permute-done((bf16[176,768]{1,0:T(8,128)(2,1)}, bf16[176,768]{1,0:T(8,128)(2,1)}, u32[]{:S(2)}, u32[]{:S(2)}) %collective-permute-start.8) | collective-permute-done | bytes 270368 | tf_op jit(solution)/shard_map/ppermute | solution.py:76
  21.1 14.9 %collective-permute-done.7 = bf16[176,768]{1,0:T(8,128)(2,1)} collective-permute-done((bf16[176,768]{1,0:T(8,128)(2,1)S(1)}, bf16[176,768]{1,0:T(8,128)(2,1)}, u32[]{:S(2)}, u32[]{:S(2)}) %collective-permute-start.7) | collective-permute-done | bytes 270368 | tf_op jit(solution)/shard_map/ppermute | solution.py:76
  36.0 1.5 %convolution_convert_fusion.3 = bf16[128,768]{1,0:T(8,128)(2,1)S(1)} fusion(bf16[176,768]{1,0:T(8,128)(2,1)} %collective-permute-done.8, bf16[176,768]{1,0:T(8,128)(2,1)} %collective-permute-done.7, bf16[176,768]{1,0:T(8,128)(2,1)} %collective-permute-done.6, bf16[176,768]{1,0:T(8,128)(2,1)S(1)} %get-tuple-element.13, ...), kind=kOutput, calls=%fused_computation.6 | convolution fusion | flops 143556608 | bytes 1458176 | tf_op jit(solution)/shard_map/dot_general | solution.py:107
  40.7 1.3 %collective-permute-start.15 = (bf16[2,24,768]{2,1,0:T(8,128)(2,1)S(1)}, bf16[2,24,768]{2,1,0:T(8,128)(2,1)S(1)}, u32[]{:S(2)}, u32[]{:S(2)}) collective-permute-start(bf16[2,24,768]{2,1,0:T(8,128)(2,1)S(1)} %fusion), channel_id=1, source_target_pairs={{0,28},{1,29},{2,30},{3,31},{8,20},{9,21},{10,22},{11,23},{16,12},... | collective-permute-start | bytes 221192 | tf_op jit(solution)/shard_map/ppermute | solution.py:135
  42.0 1.3 %collective-permute-start.14 = (bf16[2,24,768]{2,1,0:T(8,128)(2,1)S(1)}, bf16[2,24,768]{2,1,0:T(8,128)(2,1)S(1)}, u32[]{:S(2)}, u32[]{:S(2)}) collective-permute-start(bf16[2,24,768]{2,1,0:T(8,128)(2,1)S(1)} %fusion), channel_id=1, source_target_pairs={{0,20},{1,21},{2,22},{3,23},{8,28},{9,29},{10,30},{11,31},{16,4},{... | collective-permute-start | bytes 221192 | tf_op jit(solution)/shard_map/ppermute | solution.py:135
  46.0 20.0 %collective-permute-done.15 = bf16[2,24,768]{2,1,0:T(8,128)(2,1)S(1)} collective-permute-done((bf16[2,24,768]{2,1,0:T(8,128)(2,1)S(1)}, bf16[2,24,768]{2,1,0:T(8,128)(2,1)S(1)}, u32[]{:S(2)}, u32[]{:S(2)}) %collective-permute-start.15) | collective-permute-done | bytes 73760 | tf_op jit(solution)/shard_map/ppermute | solution.py:135
  66.0 2.5 %collective-permute-done.14 = bf16[2,24,768]{2,1,0:T(8,128)(2,1)S(1)} collective-permute-done((bf16[2,24,768]{2,1,0:T(8,128)(2,1)S(1)}, bf16[2,24,768]{2,1,0:T(8,128)(2,1)S(1)}, u32[]{:S(2)}, u32[]{:S(2)}) %collective-permute-start.14) | collective-permute-done | bytes 73760 | tf_op jit(solution)/shard_map/ppermute | solution.py:135
  70.0 2.1 %collective-permute-start.17 = (bf16[2,16,3072]{2,1,0:T(8,128)(2,1)S(1)}, bf16[2,16,3072]{2,1,0:T(8,128)(2,1)S(1)}, u32[]{:S(2)}, u32[]{:S(2)}) collective-permute-start(bf16[2,16,3072]{2,1,0:T(8,128)(2,1)S(1)} %get-tuple-element.18), channel_id=1, source_target_pairs={{4,6},{5,7},{6,4},{7,5},{12,14},{13,15},{14,12},{15,13},{20,22},{2... | collective-permute-start | bytes 589832 | tf_op jit(solution)/shard_map/ppermute | solution.py:93
  72.2 3.1 %collective-permute-start.16 = (bf16[2,16,3072]{2,1,0:T(8,128)(2,1)S(1)}, bf16[2,16,3072]{2,1,0:T(8,128)(2,1)S(1)}, u32[]{:S(2)}, u32[]{:S(2)}) collective-permute-start(bf16[2,16,3072]{2,1,0:T(8,128)(2,1)S(1)} %get-tuple-element.19), channel_id=1, source_target_pairs={{4,5},{5,4},{6,7},{7,6},{12,13},{13,12},{14,15},{15,14},{20,21},{2... | collective-permute-start | bytes 589832 | tf_op jit(solution)/shard_map/ppermute | solution.py:93
  75.3 3.1 %collective-permute-start.18 = (bf16[2,16,3072]{2,1,0:T(8,128)(2,1)S(1)}, bf16[2,16,3072]{2,1,0:T(8,128)(2,1)S(1)}, u32[]{:S(2)}, u32[]{:S(2)}) collective-permute-start(bf16[2,16,3072]{2,1,0:T(8,128)(2,1)S(1)} %get-tuple-element.20), channel_id=1, source_target_pairs={{4,7},{5,6},{6,5},{7,4},{12,15},{13,14},{14,13},{15,12},{20,23},{2... | collective-permute-start | bytes 589832 | tf_op jit(solution)/shard_map/ppermute | solution.py:93
  78.6 4.0 %collective-permute-done.18 = bf16[2,16,3072]{2,1,0:T(8,128)(2,1)S(1)} collective-permute-done((bf16[2,16,3072]{2,1,0:T(8,128)(2,1)S(1)}, bf16[2,16,3072]{2,1,0:T(8,128)(2,1)S(1)}, u32[]{:S(2)}, u32[]{:S(2)}) %collective-permute-start.18) | collective-permute-done | bytes 196640 | tf_op jit(solution)/shard_map/ppermute | solution.py:93
  83.9 3.5 %collective-permute-start.21 = (bf16[128,176]{0,1:T(8,128)(2,1)S(1)}, bf16[128,176]{0,1:T(8,128)(2,1)S(1)}, u32[]{:S(2)}, u32[]{:S(2)}) collective-permute-start(bf16[128,176]{0,1:T(8,128)(2,1)S(1)} %fusion.7), channel_id=1, source_target_pairs={{4,28},{5,29},{6,30},{7,31},{12,20},{13,21},{14,22},{15,23},{20,12... | collective-permute-start | bytes 135176 | tf_op jit(solution)/shard_map/ppermute | solution.py:103
  87.4 1.9 %collective-permute-start.20 = (bf16[128,176]{0,1:T(8,128)(2,1)S(1)}, bf16[128,176]{0,1:T(8,128)(2,1)S(1)}, u32[]{:S(2)}, u32[]{:S(2)}) collective-permute-start(bf16[128,176]{0,1:T(8,128)(2,1)S(1)} %fusion.7), channel_id=1, source_target_pairs={{4,20},{5,21},{6,22},{7,23},{12,28},{13,29},{14,30},{15,31},{20,4}... | collective-permute-start | bytes 135176 | tf_op jit(solution)/shard_map/ppermute | solution.py:103
  89.3 3.9 %collective-permute-start.19 = (bf16[128,176]{0,1:T(8,128)(2,1)S(1)}, bf16[128,176]{0,1:T(8,128)(2,1)S(1)}, u32[]{:S(2)}, u32[]{:S(2)}) collective-permute-start(bf16[128,176]{0,1:T(8,128)(2,1)S(1)} %fusion.7), channel_id=1, source_target_pairs={{4,12},{5,13},{6,14},{7,15},{12,4},{13,5},{14,6},{15,7},{20,28},{2... | collective-permute-start | bytes 135176 | tf_op jit(solution)/shard_map/ppermute | solution.py:103
  93.2 1.4 %collective-permute-done.19 = bf16[128,176]{0,1:T(8,128)(2,1)S(1)} collective-permute-done((bf16[128,176]{0,1:T(8,128)(2,1)S(1)}, bf16[128,176]{0,1:T(8,128)(2,1)S(1)}, u32[]{:S(2)}, u32[]{:S(2)}) %collective-permute-start.19) | collective-permute-done | bytes 45088 | tf_op jit(solution)/shard_map/ppermute | solution.py:103
  94.6 1.5 %convolution_convert_fusion.2 = bf16[128,768]{1,0:T(8,128)(2,1)S(1)} fusion(bf16[176,768]{1,0:T(8,128)(2,1)} %collective-permute-done.8, bf16[176,768]{1,0:T(8,128)(2,1)} %collective-permute-done.7, bf16[176,768]{1,0:T(8,128)(2,1)} %collective-permute-done.6, bf16[176,768]{1,0:T(8,128)(2,1)S(1)} %copy-done.4, ...), kind=kOutput, calls=%fused_computation.5 | convolution fusion | flops 143556608 | bytes 1458176 | tf_op jit(solution)/shard_map/dot_general | solution.py:107
  96.1 2.2 %collective-permute-start.22 = (bf16[2,16,768]{2,1,0:T(8,128)(2,1)S(1)}, bf16[2,16,768]{2,1,0:T(8,128)(2,1)S(1)}, u32[]{:S(2)}, u32[]{:S(2)}) collective-permute-start(bf16[2,16,768]{2,1,0:T(8,128)(2,1)S(1)} %get-tuple-element.26), channel_id=1, source_target_pairs={{4,5},{5,4},{6,7},{7,6},{12,13},{13,12},{14,15},{15,14},{20,21},{2... | collective-permute-start | bytes 147464 | tf_op jit(solution)/shard_map/ppermute | solution.py:111
  98.3 4.1 %collective-permute-start.24 = (bf16[2,16,768]{2,1,0:T(8,128)(2,1)S(1)}, bf16[2,16,768]{2,1,0:T(8,128)(2,1)S(1)}, u32[]{:S(2)}, u32[]{:S(2)}) collective-permute-start(bf16[2,16,768]{2,1,0:T(8,128)(2,1)S(1)} %get-tuple-element.27), channel_id=1, source_target_pairs={{4,7},{5,6},{6,5},{7,4},{12,15},{13,14},{14,13},{15,12},{20,23},{2... | collective-permute-start | bytes 147464 | tf_op jit(solution)/shard_map/ppermute | solution.py:111
  102.3 2.1 %collective-permute-start.23 = (bf16[2,16,768]{2,1,0:T(8,128)(2,1)S(1)}, bf16[2,16,768]{2,1,0:T(8,128)(2,1)S(1)}, u32[]{:S(2)}, u32[]{:S(2)}) collective-permute-start(bf16[2,16,768]{2,1,0:T(8,128)(2,1)S(1)} %get-tuple-element.28), channel_id=1, source_target_pairs={{4,6},{5,7},{6,4},{7,5},{12,14},{13,15},{14,12},{15,13},{20,22},{2... | collective-permute-start | bytes 147464 | tf_op jit(solution)/shard_map/ppermute | solution.py:111
  104.5 2.7 %collective-permute-done.23 = bf16[2,16,768]{2,1,0:T(8,128)(2,1)S(1)} collective-permute-done((bf16[2,16,768]{2,1,0:T(8,128)(2,1)S(1)}, bf16[2,16,768]{2,1,0:T(8,128)(2,1)S(1)}, u32[]{:S(2)}, u32[]{:S(2)}) %collective-permute-start.23) | collective-permute-done | bytes 49184 | tf_op jit(solution)/shard_map/ppermute | solution.py:111
  (86 shorter events, 21.5 us)
Async XLA Ops:
  5.9 8.0 %collective-permute-start.1 = (bf16[2,16,3072]{2,1,0:T(8,128)(2,1)}, bf16[2,16,3072]{2,1,0:T(8,128)(2,1)S(1)}, u32[]{:S(2)}, u32[]{:S(2)}) collective-permute-start(bf16[2,16,3072]{2,1,0:T(8,128)(2,1)} %get-tuple-element.22), channel_id=1, source_target_pairs={{0,2},{1,3},{2,0},{3,1},{8,10},{9,11},{10,8},{11,9},{16,18},{17,19... | collective-permute-start | bytes 589832 | tf_op jit(solution)/shard_map/ppermute | solution.py:93
  6.6 7.4 %collective-permute-start = (bf16[2,16,3072]{2,1,0:T(8,128)(2,1)}, bf16[2,16,3072]{2,1,0:T(8,128)(2,1)S(1)}, u32[]{:S(2)}, u32[]{:S(2)}) collective-permute-start(bf16[2,16,3072]{2,1,0:T(8,128)(2,1)} %get-tuple-element.23), channel_id=1, source_target_pairs={{0,1},{1,0},{2,3},{3,2},{8,9},{9,8},{10,11},{11,10},{16,17},{17,16... | collective-permute-start | bytes 589832 | tf_op jit(solution)/shard_map/ppermute | solution.py:93
  7.3 6.7 %collective-permute-start.2 = (bf16[2,16,3072]{2,1,0:T(8,128)(2,1)S(1)}, bf16[2,16,3072]{2,1,0:T(8,128)(2,1)}, u32[]{:S(2)}, u32[]{:S(2)}) collective-permute-start(bf16[2,16,3072]{2,1,0:T(8,128)(2,1)S(1)} %get-tuple-element.24), channel_id=1, source_target_pairs={{0,3},{1,2},{2,1},{3,0},{8,11},{9,10},{10,9},{11,8},{16,19},{17,18... | collective-permute-start | bytes 589832 | tf_op jit(solution)/shard_map/ppermute | solution.py:93
  9.6 9.4 %collective-permute-start.6 = (bf16[176,768]{1,0:T(8,128)(2,1)}, bf16[176,768]{1,0:T(8,128)(2,1)}, u32[]{:S(2)}, u32[]{:S(2)}) collective-permute-start(bf16[176,768]{1,0:T(8,128)(2,1)} %get-tuple-element.14), channel_id=1, source_target_pairs={{0,8},{8,0},{16,24},{24,16},{1,9},{9,1},{17,25},{25,17},{2,10},{10... | collective-permute-start | bytes 811016 | tf_op jit(solution)/shard_map/ppermute | solution.py:76
  11.7 9.4 %collective-permute-start.8 = (bf16[176,768]{1,0:T(8,128)(2,1)}, bf16[176,768]{1,0:T(8,128)(2,1)}, u32[]{:S(2)}, u32[]{:S(2)}) collective-permute-start(bf16[176,768]{1,0:T(8,128)(2,1)} %get-tuple-element.15), channel_id=1, source_target_pairs={{0,24},{8,16},{16,8},{24,0},{1,25},{9,17},{17,9},{25,1},{2,26},{10... | collective-permute-start | bytes 811016 | tf_op jit(solution)/shard_map/ppermute | solution.py:76
  13.9 22.1 %collective-permute-start.7 = (bf16[176,768]{1,0:T(8,128)(2,1)S(1)}, bf16[176,768]{1,0:T(8,128)(2,1)}, u32[]{:S(2)}, u32[]{:S(2)}) collective-permute-start(bf16[176,768]{1,0:T(8,128)(2,1)S(1)} %get-tuple-element.16), channel_id=1, source_target_pairs={{0,16},{8,24},{16,0},{24,8},{1,17},{9,25},{17,1},{25,9},{2,18},{10... | collective-permute-start | bytes 811016 | tf_op jit(solution)/shard_map/ppermute | solution.py:76
  16.9 1.3 %collective-permute-start.5 = (bf16[128,176]{0,1:T(8,128)(2,1)S(1)}, bf16[128,176]{0,1:T(8,128)(2,1)S(1)}, u32[]{:S(2)}, u32[]{:S(2)}) collective-permute-start(bf16[128,176]{0,1:T(8,128)(2,1)S(1)} %fusion.6), channel_id=1, source_target_pairs={{0,24},{1,25},{2,26},{3,27},{8,16},{9,17},{10,18},{11,19},{16,8},{... | collective-permute-start | bytes 135176 | tf_op jit(solution)/shard_map/ppermute | solution.py:103
  17.6 1.4 %collective-permute-start.4 = (bf16[128,176]{0,1:T(8,128)(2,1)S(1)}, bf16[128,176]{0,1:T(8,128)(2,1)S(1)}, u32[]{:S(2)}, u32[]{:S(2)}) collective-permute-start(bf16[128,176]{0,1:T(8,128)(2,1)S(1)} %fusion.6), channel_id=1, source_target_pairs={{0,16},{1,17},{2,18},{3,19},{8,24},{9,25},{10,26},{11,27},{16,0},{... | collective-permute-start | bytes 135176 | tf_op jit(solution)/shard_map/ppermute | solution.py:103
  18.3 0.8 collective-permute-start.3
  37.5 2.0 %collective-permute-start.9 = (bf16[2,16,768]{2,1,0:T(8,128)(2,1)S(1)}, bf16[2,16,768]{2,1,0:T(8,128)(2,1)S(1)}, u32[]{:S(2)}, u32[]{:S(2)}) collective-permute-start(bf16[2,16,768]{2,1,0:T(8,128)(2,1)S(1)} %get-tuple-element.30), channel_id=1, source_target_pairs={{0,1},{1,0},{2,3},{3,2},{8,9},{9,8},{10,11},{11,10},{16,17},{17,16... | collective-permute-start | bytes 147464 | tf_op jit(solution)/shard_map/ppermute | solution.py:111
  38.2 1.4 %collective-permute-start.11 = (bf16[2,16,768]{2,1,0:T(8,128)(2,1)S(1)}, bf16[2,16,768]{2,1,0:T(8,128)(2,1)S(1)}, u32[]{:S(2)}, u32[]{:S(2)}) collective-permute-start(bf16[2,16,768]{2,1,0:T(8,128)(2,1)S(1)} %get-tuple-element.31), channel_id=1, source_target_pairs={{0,3},{1,2},{2,1},{3,0},{8,11},{9,10},{10,9},{11,8},{16,19},{17,18... | collective-permute-start | bytes 147464 | tf_op jit(solution)/shard_map/ppermute | solution.py:111
  40.7 25.3 %collective-permute-start.15 = (bf16[2,24,768]{2,1,0:T(8,128)(2,1)S(1)}, bf16[2,24,768]{2,1,0:T(8,128)(2,1)S(1)}, u32[]{:S(2)}, u32[]{:S(2)}) collective-permute-start(bf16[2,24,768]{2,1,0:T(8,128)(2,1)S(1)} %fusion), channel_id=1, source_target_pairs={{0,28},{1,29},{2,30},{3,31},{8,20},{9,21},{10,22},{11,23},{16,12},... | collective-permute-start | bytes 221192 | tf_op jit(solution)/shard_map/ppermute | solution.py:135
  42.0 26.5 %collective-permute-start.14 = (bf16[2,24,768]{2,1,0:T(8,128)(2,1)S(1)}, bf16[2,24,768]{2,1,0:T(8,128)(2,1)S(1)}, u32[]{:S(2)}, u32[]{:S(2)}) collective-permute-start(bf16[2,24,768]{2,1,0:T(8,128)(2,1)S(1)} %fusion), channel_id=1, source_target_pairs={{0,20},{1,21},{2,22},{3,23},{8,28},{9,29},{10,30},{11,31},{16,4},{... | collective-permute-start | bytes 221192 | tf_op jit(solution)/shard_map/ppermute | solution.py:135
  43.3 25.4 %collective-permute-start.13 = (bf16[2,24,768]{2,1,0:T(8,128)(2,1)S(1)}, bf16[2,24,768]{2,1,0:T(8,128)(2,1)S(1)}, u32[]{:S(2)}, u32[]{:S(2)}) collective-permute-start(bf16[2,24,768]{2,1,0:T(8,128)(2,1)S(1)} %fusion), channel_id=1, source_target_pairs={{0,12},{1,13},{2,14},{3,15},{8,4},{9,5},{10,6},{11,7},{16,28},{17,... | collective-permute-start | bytes 221192 | tf_op jit(solution)/shard_map/ppermute | solution.py:135
  44.6 24.1 %collective-permute-start.12 = (bf16[2,24,768]{2,1,0:T(8,128)(2,1)S(1)}, bf16[2,24,768]{2,1,0:T(8,128)(2,1)S(1)}, u32[]{:S(2)}, u32[]{:S(2)}) collective-permute-start(bf16[2,24,768]{2,1,0:T(8,128)(2,1)S(1)} %fusion), channel_id=1, source_target_pairs={{0,4},{1,5},{2,6},{3,7},{8,12},{9,13},{10,14},{11,15},{16,20},{17,... | collective-permute-start | bytes 221192 | tf_op jit(solution)/shard_map/ppermute | solution.py:135
  70.0 8.4 %collective-permute-start.17 = (bf16[2,16,3072]{2,1,0:T(8,128)(2,1)S(1)}, bf16[2,16,3072]{2,1,0:T(8,128)(2,1)S(1)}, u32[]{:S(2)}, u32[]{:S(2)}) collective-permute-start(bf16[2,16,3072]{2,1,0:T(8,128)(2,1)S(1)} %get-tuple-element.18), channel_id=1, source_target_pairs={{4,6},{5,7},{6,4},{7,5},{12,14},{13,15},{14,12},{15,13},{20,22},{2... | collective-permute-start | bytes 589832 | tf_op jit(solution)/shard_map/ppermute | solution.py:93
  72.2 6.4 %collective-permute-start.16 = (bf16[2,16,3072]{2,1,0:T(8,128)(2,1)S(1)}, bf16[2,16,3072]{2,1,0:T(8,128)(2,1)S(1)}, u32[]{:S(2)}, u32[]{:S(2)}) collective-permute-start(bf16[2,16,3072]{2,1,0:T(8,128)(2,1)S(1)} %get-tuple-element.19), channel_id=1, source_target_pairs={{4,5},{5,4},{6,7},{7,6},{12,13},{13,12},{14,15},{15,14},{20,21},{2... | collective-permute-start | bytes 589832 | tf_op jit(solution)/shard_map/ppermute | solution.py:93
  75.3 7.3 %collective-permute-start.18 = (bf16[2,16,3072]{2,1,0:T(8,128)(2,1)S(1)}, bf16[2,16,3072]{2,1,0:T(8,128)(2,1)S(1)}, u32[]{:S(2)}, u32[]{:S(2)}) collective-permute-start(bf16[2,16,3072]{2,1,0:T(8,128)(2,1)S(1)} %get-tuple-element.20), channel_id=1, source_target_pairs={{4,7},{5,6},{6,5},{7,4},{12,15},{13,14},{14,13},{15,12},{20,23},{2... | collective-permute-start | bytes 589832 | tf_op jit(solution)/shard_map/ppermute | solution.py:93
  83.9 9.3 %collective-permute-start.21 = (bf16[128,176]{0,1:T(8,128)(2,1)S(1)}, bf16[128,176]{0,1:T(8,128)(2,1)S(1)}, u32[]{:S(2)}, u32[]{:S(2)}) collective-permute-start(bf16[128,176]{0,1:T(8,128)(2,1)S(1)} %fusion.7), channel_id=1, source_target_pairs={{4,28},{5,29},{6,30},{7,31},{12,20},{13,21},{14,22},{15,23},{20,12... | collective-permute-start | bytes 135176 | tf_op jit(solution)/shard_map/ppermute | solution.py:103
  87.4 5.8 %collective-permute-start.20 = (bf16[128,176]{0,1:T(8,128)(2,1)S(1)}, bf16[128,176]{0,1:T(8,128)(2,1)S(1)}, u32[]{:S(2)}, u32[]{:S(2)}) collective-permute-start(bf16[128,176]{0,1:T(8,128)(2,1)S(1)} %fusion.7), channel_id=1, source_target_pairs={{4,20},{5,21},{6,22},{7,23},{12,28},{13,29},{14,30},{15,31},{20,4}... | collective-permute-start | bytes 135176 | tf_op jit(solution)/shard_map/ppermute | solution.py:103
  89.3 5.3 %collective-permute-start.19 = (bf16[128,176]{0,1:T(8,128)(2,1)S(1)}, bf16[128,176]{0,1:T(8,128)(2,1)S(1)}, u32[]{:S(2)}, u32[]{:S(2)}) collective-permute-start(bf16[128,176]{0,1:T(8,128)(2,1)S(1)} %fusion.7), channel_id=1, source_target_pairs={{4,12},{5,13},{6,14},{7,15},{12,4},{13,5},{14,6},{15,7},{20,28},{2... | collective-permute-start | bytes 135176 | tf_op jit(solution)/shard_map/ppermute | solution.py:103
  96.1 8.4 %collective-permute-start.22 = (bf16[2,16,768]{2,1,0:T(8,128)(2,1)S(1)}, bf16[2,16,768]{2,1,0:T(8,128)(2,1)S(1)}, u32[]{:S(2)}, u32[]{:S(2)}) collective-permute-start(bf16[2,16,768]{2,1,0:T(8,128)(2,1)S(1)} %get-tuple-element.26), channel_id=1, source_target_pairs={{4,5},{5,4},{6,7},{7,6},{12,13},{13,12},{14,15},{15,14},{20,21},{2... | collective-permute-start | bytes 147464 | tf_op jit(solution)/shard_map/ppermute | solution.py:111
  98.3 6.2 %collective-permute-start.24 = (bf16[2,16,768]{2,1,0:T(8,128)(2,1)S(1)}, bf16[2,16,768]{2,1,0:T(8,128)(2,1)S(1)}, u32[]{:S(2)}, u32[]{:S(2)}) collective-permute-start(bf16[2,16,768]{2,1,0:T(8,128)(2,1)S(1)} %get-tuple-element.27), channel_id=1, source_target_pairs={{4,7},{5,6},{6,5},{7,4},{12,15},{13,14},{14,13},{15,12},{20,23},{2... | collective-permute-start | bytes 147464 | tf_op jit(solution)/shard_map/ppermute | solution.py:111
  102.3 4.8 %collective-permute-start.23 = (bf16[2,16,768]{2,1,0:T(8,128)(2,1)S(1)}, bf16[2,16,768]{2,1,0:T(8,128)(2,1)S(1)}, u32[]{:S(2)}, u32[]{:S(2)}) collective-permute-start(bf16[2,16,768]{2,1,0:T(8,128)(2,1)S(1)} %get-tuple-element.28), channel_id=1, source_target_pairs={{4,6},{5,7},{6,4},{7,5},{12,14},{13,15},{14,12},{15,13},{20,22},{2... | collective-permute-start | bytes 147464 | tf_op jit(solution)/shard_map/ppermute | solution.py:111
  (6 other events, 58.4 us)

commit v2 on v1

--- a/solution.py
+++ b/solution.py
@@ -68,16 +68,18 @@
     up_local = w_up[0, 0]
     down_local = w_down[0, 0]
 
-    if small_dp:
-        down_parts = []
+    def resplit_down(p, anchor):
+        if not small_dp:
+            return lax.all_to_all(down_local, "dp", 1, 0, tiled=True), anchor
+        parts = []
         for s in range(n_dp):
             piece = lax.dynamic_slice_in_dim(down_local, dring.ahead(d_me, s) * columns, columns, 1)
             if s:
-                piece = lax.ppermute(piece, "dp", [(i, dring.ahead(i, s)) for i in range(n_dp)])
-            down_parts.append(piece)
-        down_full = jnp.concatenate(down_parts, axis=0)
-    else:
-        down_full = lax.all_to_all(down_local, "dp", 1, 0, tiled=True)
+                if anchor is not None:
+                    piece, anchor = lax.optimization_barrier((piece, anchor))
+                piece = lax.ppermute(piece, AXES, dp_pairs(p, s))
+            parts.append(piece)
+        return jnp.concatenate(parts, axis=0), anchor
 
     route_ids = expert_ids[0]
     route_gates = gates[0]
@@ -85,7 +87,7 @@
     dispatch_map = jnp.stack([mp[0] for mp in maps])
     combine_map = jnp.stack([mp[1] for mp in maps])
 
-    def layer(current, p):
+    def layer(current, p, down_full):
         outgoing = jnp.einsum("mrt,mtd->mrd", dispatch_map, current, preferred_element_type=jnp.float32)
         outgoing = outgoing.astype(jnp.bfloat16).reshape(micro, n_exp, CAP, width)
         arrived = [outgoing[:, 0]]
@@ -123,7 +125,9 @@
     current = tokens
     result = None
     for p in range(n_pipe):
-        cols = layer(current, p)
+        down_full, anchor = resplit_down(p, current if p else None)
+        current = current if anchor is None else anchor
+        cols = layer(current, p, down_full)
         result = cols if result is None else jnp.where(p_me == p, cols, result)
         if p + 1 < n_pipe:
             if small_dp:

time: 109 us -> 113 us (1.037)
  starting transfers between devices: 42.3 us -> 49.9 us
  waiting for transfers between devices: 48 us -> 44.9 us
    ppermute x4, waiting for transfers between devices: 22.8 us -> 39.8 us  [per_device(): parts.append(lax.ppermute(cols, AXES, pairs))]
    ppermute x3 -> x6, waiting for transfers between devices: 17 us -> 0.02 us  [resplit_down(): piece = lax.ppermute(piece, AXES, dp_pairs(p, s))]
    ppermute x3 -> x6, starting transfers between devices: 4.44 us -> 13.4 us  [resplit_down(): piece = lax.ppermute(piece, AXES, dp_pairs(p, s))]
    ppermute x6, waiting for transfers between devices: 4.19 us -> 0.02 us  [layer(): lax.ppermute(outgoing[:, s], AXES, expert_pairs(p, s, False))]
    ppermute x6, waiting for transfers between devices: 1.41 us -> 3.4 us  [layer(): parts.append(lax.ppermute(hidden, AXES, dp_pairs(p, s)))]
    ppermute x6, starting transfers between devices: 11.3 us -> 9.94 us  [layer(): parts.append(lax.ppermute(hidden, AXES, dp_pairs(p, s)))]
  transfers between devices with their start and end apart: 25 -> 28, of which waited for: 9 -> 6; matrix products, arithmetic and copies ran while one was open for 3% -> 4% of each run, Pallas kernels for 0% -> 0%
where the time goes in v2:
time: 113 us
  starting transfers between devices  49.9 us (44%)
  waiting for transfers between devices  44.9 us (40%)
  matrix products  8.48 us (8%)
  local copies, waits for them, and re-layouts  5.42 us (5%)
  other arithmetic  3.25 us (3%)
    ppermute x4, waiting for transfers between devices, per_device(): parts.append(lax.ppermute(cols, AXES, pairs))  39.8 us
    ppermute x6, starting transfers between devices, resplit_down(): piece = lax.ppermute(piece, AXES, dp_pairs(p, s))  13.4 us
    ppermute x6, starting transfers between devices, layer(): lax.ppermute(outgoing[:, s], AXES, expert_pairs(p, s, False))  11.1 us
    ppermute x6, starting transfers between devices, layer(): lax.ppermute(expert_out[:, s], AXES, expert_pairs(p, s, True))  10.4 us
    ppermute x6, starting transfers between devices, layer(): parts.append(lax.ppermute(hidden, AXES, dp_pairs(p, s)))  9.94 us
    ppermute x4, starting transfers between devices, per_device(): parts.append(lax.ppermute(cols, AXES, pairs))  5.17 us
    ppermute x6, waiting for transfers between devices, layer(): parts.append(lax.ppermute(hidden, AXES, dp_pairs(p, s)))  3.4 us
    dot_general x2, matrix products, layer(): jnp.dot(hidden_full, down_full, preferred_element_type=jnp.float32)  2.94 us
  transfers between devices with their start and end apart: 28, of which 6 were waited for; matrix products, arithmetic and copies ran while one was open for 4% of the time, Pallas kernels for 0%

profile of v2, /device:TPU:1, one launch (start us, length us, event | category | flops | bytes accessed | tf_op | source)
XLA Modules:
  0.0 112.5 jit_solution(11175598271959236486)
XLA Ops:
  3.7 1.4 %convolution_convert_fusion.1 = bf16[2,64,3072]{2,1,0:T(8,128)(2,1)S(1)} fusion(bf16[2,24,3072]{2,1,0:T(8,128)(2,1)} %param.6, bf16[1,64,24]{1,2,0:T(8,128)(2,1)S(1)} %bitcast.159, bf16[1,64,24]{1,2,0:T(8,128)(2,1)S(1)} %bitcast.161), kind=kOutput, calls=%fused_computation.2 | convolution fusion | flops 19270656 | bytes 1087488 | tf_op jit(solution)/shard_map/mrt,mtd->mrd/dot_general | solution.py:91
  7.2 1.4 %collective-permute-start.2 = (bf16[2,16,3072]{2,1,0:T(8,128)(2,1)S(1)}, bf16[2,16,3072]{2,1,0:T(8,128)(2,1)}, u32[]{:S(2)}, u32[]{:S(2)}) collective-permute-start(bf16[2,16,3072]{2,1,0:T(8,128)(2,1)S(1)} %get-tuple-element.36), channel_id=1, source_target_pairs={{0,3},{1,2},{2,1},{3,0},{8,11},{9,10},{10,9},{11,8},{16,19},{17,18... | collective-permute-start | bytes 589832 | tf_op jit(solution)/shard_map/ppermute | solution.py:95
  9.5 1.4 %collective-permute-start.6 = (bf16[176,768]{1,0:T(8,128)(2,1)}, bf16[176,768]{1,0:T(8,128)(2,1)}, u32[]{:S(2)}, u32[]{:S(2)}) collective-permute-start(bf16[176,768]{1,0:T(8,128)(2,1)} %get-tuple-element.14), channel_id=1, source_target_pairs={{0,8},{1,9},{2,10},{3,11},{8,0},{9,1},{10,2},{11,3},{16,24},{17,25... | collective-permute-start | bytes 811016 | tf_op jit(solution)/shard_map/ppermute | solution.py:80
  10.8 1.4 %collective-permute-start.7 = (bf16[176,768]{1,0:T(8,128)(2,1)}, bf16[176,768]{1,0:T(8,128)(2,1)}, u32[]{:S(2)}, u32[]{:S(2)}) collective-permute-start(bf16[176,768]{1,0:T(8,128)(2,1)} %get-tuple-element.15), channel_id=1, source_target_pairs={{0,16},{1,17},{2,18},{3,19},{8,24},{9,25},{10,26},{11,27},{16,0},{... | collective-permute-start | bytes 811016 | tf_op jit(solution)/shard_map/ppermute | solution.py:80
  12.2 1.4 %collective-permute-start.8 = (bf16[176,768]{1,0:T(8,128)(2,1)}, bf16[176,768]{1,0:T(8,128)(2,1)}, u32[]{:S(2)}, u32[]{:S(2)}) collective-permute-start(bf16[176,768]{1,0:T(8,128)(2,1)} %get-tuple-element.16), channel_id=1, source_target_pairs={{0,24},{1,25},{2,26},{3,27},{8,16},{9,17},{10,18},{11,19},{16,8},{... | collective-permute-start | bytes 811016 | tf_op jit(solution)/shard_map/ppermute | solution.py:80
  18.6 1.5 %convolution_convert_fusion.3 = bf16[128,768]{1,0:T(8,128)(2,1)S(1)} fusion(bf16[176,768]{1,0:T(8,128)(2,1)S(1)} %get-tuple-element.28, bf16[176,768]{1,0:T(8,128)(2,1)} %collective-permute-done.8, bf16[176,768]{1,0:T(8,128)(2,1)} %collective-permute-done.7, bf16[176,768]{1,0:T(8,128)(2,1)} %collective-permute-done.6, ...), kind=kOutput, calls=%fused_computation.8 | convolution fusion | flops 143556608 | bytes 1458176 | tf_op jit(solution)/shard_map/dot_general | solution.py:109
  23.3 1.3 %collective-permute-start.15 = (bf16[2,24,768]{2,1,0:T(8,128)(2,1)S(1)}, bf16[2,24,768]{2,1,0:T(8,128)(2,1)S(1)}, u32[]{:S(2)}, u32[]{:S(2)}) collective-permute-start(bf16[2,24,768]{2,1,0:T(8,128)(2,1)S(1)} %fusion), channel_id=1, source_target_pairs={{0,28},{1,29},{2,30},{3,31},{8,20},{9,21},{10,22},{11,23},{16,12},... | collective-permute-start | bytes 221192 | tf_op jit(solution)/shard_map/ppermute | solution.py:139
  28.6 37.8 %collective-permute-done.15 = bf16[2,24,768]{2,1,0:T(8,128)(2,1)S(1)} collective-permute-done((bf16[2,24,768]{2,1,0:T(8,128)(2,1)S(1)}, bf16[2,24,768]{2,1,0:T(8,128)(2,1)S(1)}, u32[]{:S(2)}, u32[]{:S(2)}) %collective-permute-start.15) | collective-permute-done | bytes 73760 | tf_op jit(solution)/shard_map/ppermute | solution.py:139
  66.4 2.0 %collective-permute-done.14 = bf16[2,24,768]{2,1,0:T(8,128)(2,1)S(1)} collective-permute-done((bf16[2,24,768]{2,1,0:T(8,128)(2,1)S(1)}, bf16[2,24,768]{2,1,0:T(8,128)(2,1)S(1)}, u32[]{:S(2)}, u32[]{:S(2)}) %collective-permute-start.14) | collective-permute-done | bytes 73760 | tf_op jit(solution)/shard_map/ppermute | solution.py:139
  69.6 2.1 %collective-permute-start.17 = (bf16[2,16,3072]{2,1,0:T(8,128)(2,1)S(1)}, bf16[2,16,3072]{2,1,0:T(8,128)(2,1)S(1)}, u32[]{:S(2)}, u32[]{:S(2)}) collective-permute-start(bf16[2,16,3072]{2,1,0:T(8,128)(2,1)S(1)} %get-tuple-element.30), channel_id=1, source_target_pairs={{4,6},{5,7},{6,4},{7,5},{12,14},{13,15},{14,12},{15,13},{20,22},{2... | collective-permute-start | bytes 589832 | tf_op jit(solution)/shard_map/ppermute | solution.py:95
  71.8 3.1 %collective-permute-start.16 = (bf16[2,16,3072]{2,1,0:T(8,128)(2,1)S(1)}, bf16[2,16,3072]{2,1,0:T(8,128)(2,1)S(1)}, u32[]{:S(2)}, u32[]{:S(2)}) collective-permute-start(bf16[2,16,3072]{2,1,0:T(8,128)(2,1)S(1)} %get-tuple-element.31), channel_id=1, source_target_pairs={{4,5},{5,4},{6,7},{7,6},{12,13},{13,12},{14,15},{15,14},{20,21},{2... | collective-permute-start | bytes 589832 | tf_op jit(solution)/shard_map/ppermute | solution.py:95
  74.9 3.1 %collective-permute-start.18 = (bf16[2,16,3072]{2,1,0:T(8,128)(2,1)S(1)}, bf16[2,16,3072]{2,1,0:T(8,128)(2,1)S(1)}, u32[]{:S(2)}, u32[]{:S(2)}) collective-permute-start(bf16[2,16,3072]{2,1,0:T(8,128)(2,1)S(1)} %get-tuple-element.32), channel_id=1, source_target_pairs={{4,7},{5,6},{6,5},{7,4},{12,15},{13,14},{14,13},{15,12},{20,23},{2... | collective-permute-start | bytes 589832 | tf_op jit(solution)/shard_map/ppermute | solution.py:95
  78.0 3.3 %collective-permute-start.24 = (bf16[176,768]{1,0:T(8,128)(2,1)}, bf16[176,768]{1,0:T(8,128)(2,1)}, u32[]{:S(2)}, u32[]{:S(2)}) collective-permute-start(bf16[176,768]{1,0:T(8,128)(2,1)} %get-tuple-element.16), channel_id=1, source_target_pairs={{4,28},{5,29},{6,30},{7,31},{12,20},{13,21},{14,22},{15,23},{20,12... | collective-permute-start | bytes 811016 | tf_op jit(solution)/shard_map/ppermute | solution.py:80
  81.4 1.9 %collective-permute-start.23 = (bf16[176,768]{1,0:T(8,128)(2,1)}, bf16[176,768]{1,0:T(8,128)(2,1)}, u32[]{:S(2)}, u32[]{:S(2)}) collective-permute-start(bf16[176,768]{1,0:T(8,128)(2,1)} %get-tuple-element.15), channel_id=1, source_target_pairs={{4,20},{5,21},{6,22},{7,23},{12,28},{13,29},{14,30},{15,31},{20,4}... | collective-permute-start | bytes 811016 | tf_op jit(solution)/shard_map/ppermute | solution.py:80
  83.3 4.0 %collective-permute-start.22 = (bf16[176,768]{1,0:T(8,128)(2,1)}, bf16[176,768]{1,0:T(8,128)(2,1)}, u32[]{:S(2)}, u32[]{:S(2)}) collective-permute-start(bf16[176,768]{1,0:T(8,128)(2,1)} %get-tuple-element.14), channel_id=1, source_target_pairs={{4,12},{5,13},{6,14},{7,15},{12,4},{13,5},{14,6},{15,7},{20,28},{2... | collective-permute-start | bytes 811016 | tf_op jit(solution)/shard_map/ppermute | solution.py:80
  88.6 3.3 %collective-permute-start.21 = (bf16[128,176]{0,1:T(8,128)(2,1)S(1)}, bf16[128,176]{0,1:T(8,128)(2,1)S(1)}, u32[]{:S(2)}, u32[]{:S(2)}) collective-permute-start(bf16[128,176]{0,1:T(8,128)(2,1)S(1)} %fusion.7), channel_id=1, source_target_pairs={{4,28},{5,29},{6,30},{7,31},{12,20},{13,21},{14,22},{15,23},{20,12... | collective-permute-start | bytes 135176 | tf_op jit(solution)/shard_map/ppermute | solution.py:105
  92.0 1.9 %collective-permute-start.20 = (bf16[128,176]{0,1:T(8,128)(2,1)S(1)}, bf16[128,176]{0,1:T(8,128)(2,1)S(1)}, u32[]{:S(2)}, u32[]{:S(2)}) collective-permute-start(bf16[128,176]{0,1:T(8,128)(2,1)S(1)} %fusion.7), channel_id=1, source_target_pairs={{4,20},{5,21},{6,22},{7,23},{12,28},{13,29},{14,30},{15,31},{20,4}... | collective-permute-start | bytes 135176 | tf_op jit(solution)/shard_map/ppermute | solution.py:105
  93.9 1.3 %collective-permute-done.21 = bf16[128,176]{0,1:T(8,128)(2,1)S(1)} collective-permute-done((bf16[128,176]{0,1:T(8,128)(2,1)S(1)}, bf16[128,176]{0,1:T(8,128)(2,1)S(1)}, u32[]{:S(2)}, u32[]{:S(2)}) %collective-permute-start.21) | collective-permute-done | bytes 45088 | tf_op jit(solution)/shard_map/ppermute | solution.py:105
  95.2 2.7 %collective-permute-start.19 = (bf16[128,176]{0,1:T(8,128)(2,1)S(1)}, bf16[128,176]{0,1:T(8,128)(2,1)S(1)}, u32[]{:S(2)}, u32[]{:S(2)}) collective-permute-start(bf16[128,176]{0,1:T(8,128)(2,1)S(1)} %fusion.7), channel_id=1, source_target_pairs={{4,12},{5,13},{6,14},{7,15},{12,4},{13,5},{14,6},{15,7},{20,28},{2... | collective-permute-start | bytes 135176 | tf_op jit(solution)/shard_map/ppermute | solution.py:105
  98.0 2.1 %collective-permute-done.19 = bf16[128,176]{0,1:T(8,128)(2,1)S(1)} collective-permute-done((bf16[128,176]{0,1:T(8,128)(2,1)S(1)}, bf16[128,176]{0,1:T(8,128)(2,1)S(1)}, u32[]{:S(2)}, u32[]{:S(2)}) %collective-permute-start.19) | collective-permute-done | bytes 45088 | tf_op jit(solution)/shard_map/ppermute | solution.py:105
  100.0 1.5 %convolution_convert_fusion.2 = bf16[128,768]{1,0:T(8,128)(2,1)S(1)} fusion(bf16[176,768]{1,0:T(8,128)(2,1)S(1)} %copy-done.4, bf16[176,768]{1,0:T(8,128)(2,1)} %collective-permute-done.24, bf16[176,768]{1,0:T(8,128)(2,1)} %collective-permute-done.23, bf16[176,768]{1,0:T(8,128)(2,1)} %collective-permute-done.22, ...), kind=kOutput, calls=%fused_computation.7 | convolution fusion | flops 143556608 | bytes 1458176 | tf_op jit(solution)/shard_map/dot_general | solution.py:109
  101.5 3.1 %collective-permute-start.25 = (bf16[2,16,768]{2,1,0:T(8,128)(2,1)S(1)}, bf16[2,16,768]{2,1,0:T(8,128)(2,1)S(1)}, u32[]{:S(2)}, u32[]{:S(2)}) collective-permute-start(bf16[2,16,768]{2,1,0:T(8,128)(2,1)S(1)} %get-tuple-element.38), channel_id=1, source_target_pairs={{4,5},{5,4},{6,7},{7,6},{12,13},{13,12},{14,15},{15,14},{20,21},{2... | collective-permute-start | bytes 147464 | tf_op jit(solution)/shard_map/ppermute | solution.py:113
  104.7 2.1 %collective-permute-start.27 = (bf16[2,16,768]{2,1,0:T(8,128)(2,1)S(1)}, bf16[2,16,768]{2,1,0:T(8,128)(2,1)S(1)}, u32[]{:S(2)}, u32[]{:S(2)}) collective-permute-start(bf16[2,16,768]{2,1,0:T(8,128)(2,1)S(1)} %get-tuple-element.39), channel_id=1, source_target_pairs={{4,7},{5,6},{6,5},{7,4},{12,15},{13,14},{14,13},{15,12},{20,23},{2... | collective-permute-start | bytes 147464 | tf_op jit(solution)/shard_map/ppermute | solution.py:113
  106.8 3.1 %collective-permute-start.26 = (bf16[2,16,768]{2,1,0:T(8,128)(2,1)S(1)}, bf16[2,16,768]{2,1,0:T(8,128)(2,1)S(1)}, u32[]{:S(2)}, u32[]{:S(2)}) collective-permute-start(bf16[2,16,768]{2,1,0:T(8,128)(2,1)S(1)} %get-tuple-element.40), channel_id=1, source_target_pairs={{4,6},{5,7},{6,4},{7,5},{12,14},{13,15},{14,12},{15,13},{20,22},{2... | collective-permute-start | bytes 147464 | tf_op jit(solution)/shard_map/ppermute | solution.py:113
  (92 shorter events, 23.8 us)
Async XLA Ops:
  5.8 6.4 %collective-permute-start.1 = (bf16[2,16,3072]{2,1,0:T(8,128)(2,1)}, bf16[2,16,3072]{2,1,0:T(8,128)(2,1)S(1)}, u32[]{:S(2)}, u32[]{:S(2)}) collective-permute-start(bf16[2,16,3072]{2,1,0:T(8,128)(2,1)} %get-tuple-element.34), channel_id=1, source_target_pairs={{0,2},{1,3},{2,0},{3,1},{8,10},{9,11},{10,8},{11,9},{16,18},{17,19... | collective-permute-start | bytes 589832 | tf_op jit(solution)/shard_map/ppermute | solution.py:95
  6.5 7.1 %collective-permute-start = (bf16[2,16,3072]{2,1,0:T(8,128)(2,1)S(1)}, bf16[2,16,3072]{2,1,0:T(8,128)(2,1)S(1)}, u32[]{:S(2)}, u32[]{:S(2)}) collective-permute-start(bf16[2,16,3072]{2,1,0:T(8,128)(2,1)S(1)} %get-tuple-element.35), channel_id=1, source_target_pairs={{0,1},{1,0},{2,3},{3,2},{8,9},{9,8},{10,11},{11,10},{16,17},{17,16... | collective-permute-start | bytes 589832 | tf_op jit(solution)/shard_map/ppermute | solution.py:95
  7.2 6.4 %collective-permute-start.2 = (bf16[2,16,3072]{2,1,0:T(8,128)(2,1)S(1)}, bf16[2,16,3072]{2,1,0:T(8,128)(2,1)}, u32[]{:S(2)}, u32[]{:S(2)}) collective-permute-start(bf16[2,16,3072]{2,1,0:T(8,128)(2,1)S(1)} %get-tuple-element.36), channel_id=1, source_target_pairs={{0,3},{1,2},{2,1},{3,0},{8,11},{9,10},{10,9},{11,8},{16,19},{17,18... | collective-permute-start | bytes 589832 | tf_op jit(solution)/shard_map/ppermute | solution.py:95
  9.5 9.1 %collective-permute-start.6 = (bf16[176,768]{1,0:T(8,128)(2,1)}, bf16[176,768]{1,0:T(8,128)(2,1)}, u32[]{:S(2)}, u32[]{:S(2)}) collective-permute-start(bf16[176,768]{1,0:T(8,128)(2,1)} %get-tuple-element.14), channel_id=1, source_target_pairs={{0,8},{1,9},{2,10},{3,11},{8,0},{9,1},{10,2},{11,3},{16,24},{17,25... | collective-permute-start | bytes 811016 | tf_op jit(solution)/shard_map/ppermute | solution.py:80
  10.8 7.7 %collective-permute-start.7 = (bf16[176,768]{1,0:T(8,128)(2,1)}, bf16[176,768]{1,0:T(8,128)(2,1)}, u32[]{:S(2)}, u32[]{:S(2)}) collective-permute-start(bf16[176,768]{1,0:T(8,128)(2,1)} %get-tuple-element.15), channel_id=1, source_target_pairs={{0,16},{1,17},{2,18},{3,19},{8,24},{9,25},{10,26},{11,27},{16,0},{... | collective-permute-start | bytes 811016 | tf_op jit(solution)/shard_map/ppermute | solution.py:80
  12.2 6.4 %collective-permute-start.8 = (bf16[176,768]{1,0:T(8,128)(2,1)}, bf16[176,768]{1,0:T(8,128)(2,1)}, u32[]{:S(2)}, u32[]{:S(2)}) collective-permute-start(bf16[176,768]{1,0:T(8,128)(2,1)} %get-tuple-element.16), channel_id=1, source_target_pairs={{0,24},{1,25},{2,26},{3,27},{8,16},{9,17},{10,18},{11,19},{16,8},{... | collective-permute-start | bytes 811016 | tf_op jit(solution)/shard_map/ppermute | solution.py:80
  17.1 1.4 %collective-permute-start.4 = (bf16[128,176]{0,1:T(8,128)(2,1)S(1)}, bf16[128,176]{0,1:T(8,128)(2,1)S(1)}, u32[]{:S(2)}, u32[]{:S(2)}) collective-permute-start(bf16[128,176]{0,1:T(8,128)(2,1)S(1)} %fusion.6), channel_id=1, source_target_pairs={{0,16},{1,17},{2,18},{3,19},{8,24},{9,25},{10,26},{11,27},{16,0},{... | collective-permute-start | bytes 135176 | tf_op jit(solution)/shard_map/ppermute | solution.py:105
  20.1 2.0 %collective-permute-start.9 = (bf16[2,16,768]{2,1,0:T(8,128)(2,1)S(1)}, bf16[2,16,768]{2,1,0:T(8,128)(2,1)S(1)}, u32[]{:S(2)}, u32[]{:S(2)}) collective-permute-start(bf16[2,16,768]{2,1,0:T(8,128)(2,1)S(1)} %get-tuple-element.42), channel_id=1, source_target_pairs={{0,1},{1,0},{2,3},{3,2},{8,9},{9,8},{10,11},{11,10},{16,17},{17,16... | collective-permute-start | bytes 147464 | tf_op jit(solution)/shard_map/ppermute | solution.py:113
  23.3 43.1 %collective-permute-start.15 = (bf16[2,24,768]{2,1,0:T(8,128)(2,1)S(1)}, bf16[2,24,768]{2,1,0:T(8,128)(2,1)S(1)}, u32[]{:S(2)}, u32[]{:S(2)}) collective-permute-start(bf16[2,24,768]{2,1,0:T(8,128)(2,1)S(1)} %fusion), channel_id=1, source_target_pairs={{0,28},{1,29},{2,30},{3,31},{8,20},{9,21},{10,22},{11,23},{16,12},... | collective-permute-start | bytes 221192 | tf_op jit(solution)/shard_map/ppermute | solution.py:139
  24.6 43.8 %collective-permute-start.14 = (bf16[2,24,768]{2,1,0:T(8,128)(2,1)S(1)}, bf16[2,24,768]{2,1,0:T(8,128)(2,1)S(1)}, u32[]{:S(2)}, u32[]{:S(2)}) collective-permute-start(bf16[2,24,768]{2,1,0:T(8,128)(2,1)S(1)} %fusion), channel_id=1, source_target_pairs={{0,20},{1,21},{2,22},{3,23},{8,28},{9,29},{10,30},{11,31},{16,4},{... | collective-permute-start | bytes 221192 | tf_op jit(solution)/shard_map/ppermute | solution.py:139
  25.9 42.5 %collective-permute-start.13 = (bf16[2,24,768]{2,1,0:T(8,128)(2,1)S(1)}, bf16[2,24,768]{2,1,0:T(8,128)(2,1)S(1)}, u32[]{:S(2)}, u32[]{:S(2)}) collective-permute-start(bf16[2,24,768]{2,1,0:T(8,128)(2,1)S(1)} %fusion), channel_id=1, source_target_pairs={{0,12},{1,13},{2,14},{3,15},{8,4},{9,5},{10,6},{11,7},{16,28},{17,... | collective-permute-start | bytes 221192 | tf_op jit(solution)/shard_map/ppermute | solution.py:139
  27.2 41.2 %collective-permute-start.12 = (bf16[2,24,768]{2,1,0:T(8,128)(2,1)S(1)}, bf16[2,24,768]{2,1,0:T(8,128)(2,1)S(1)}, u32[]{:S(2)}, u32[]{:S(2)}) collective-permute-start(bf16[2,24,768]{2,1,0:T(8,128)(2,1)S(1)} %fusion), channel_id=1, source_target_pairs={{0,4},{1,5},{2,6},{3,7},{8,12},{9,13},{10,14},{11,15},{16,20},{17,... | collective-permute-start | bytes 221192 | tf_op jit(solution)/shard_map/ppermute | solution.py:139
  69.6 13.7 %collective-permute-start.17 = (bf16[2,16,3072]{2,1,0:T(8,128)(2,1)S(1)}, bf16[2,16,3072]{2,1,0:T(8,128)(2,1)S(1)}, u32[]{:S(2)}, u32[]{:S(2)}) collective-permute-start(bf16[2,16,3072]{2,1,0:T(8,128)(2,1)S(1)} %get-tuple-element.30), channel_id=1, source_target_pairs={{4,6},{5,7},{6,4},{7,5},{12,14},{13,15},{14,12},{15,13},{20,22},{2... | collective-permute-start | bytes 589832 | tf_op jit(solution)/shard_map/ppermute | solution.py:95
  71.8 15.6 %collective-permute-start.16 = (bf16[2,16,3072]{2,1,0:T(8,128)(2,1)S(1)}, bf16[2,16,3072]{2,1,0:T(8,128)(2,1)S(1)}, u32[]{:S(2)}, u32[]{:S(2)}) collective-permute-start(bf16[2,16,3072]{2,1,0:T(8,128)(2,1)S(1)} %get-tuple-element.31), channel_id=1, source_target_pairs={{4,5},{5,4},{6,7},{7,6},{12,13},{13,12},{14,15},{15,14},{20,21},{2... | collective-permute-start | bytes 589832 | tf_op jit(solution)/shard_map/ppermute | solution.py:95
  74.9 12.4 %collective-permute-start.18 = (bf16[2,16,3072]{2,1,0:T(8,128)(2,1)S(1)}, bf16[2,16,3072]{2,1,0:T(8,128)(2,1)S(1)}, u32[]{:S(2)}, u32[]{:S(2)}) collective-permute-start(bf16[2,16,3072]{2,1,0:T(8,128)(2,1)S(1)} %get-tuple-element.32), channel_id=1, source_target_pairs={{4,7},{5,6},{6,5},{7,4},{12,15},{13,14},{14,13},{15,12},{20,23},{2... | collective-permute-start | bytes 589832 | tf_op jit(solution)/shard_map/ppermute | solution.py:95
  78.0 22.0 %collective-permute-start.24 = (bf16[176,768]{1,0:T(8,128)(2,1)}, bf16[176,768]{1,0:T(8,128)(2,1)}, u32[]{:S(2)}, u32[]{:S(2)}) collective-permute-start(bf16[176,768]{1,0:T(8,128)(2,1)} %get-tuple-element.16), channel_id=1, source_target_pairs={{4,28},{5,29},{6,30},{7,31},{12,20},{13,21},{14,22},{15,23},{20,12... | collective-permute-start | bytes 811016 | tf_op jit(solution)/shard_map/ppermute | solution.py:80
  81.4 18.6 %collective-permute-start.23 = (bf16[176,768]{1,0:T(8,128)(2,1)}, bf16[176,768]{1,0:T(8,128)(2,1)}, u32[]{:S(2)}, u32[]{:S(2)}) collective-permute-start(bf16[176,768]{1,0:T(8,128)(2,1)} %get-tuple-element.15), channel_id=1, source_target_pairs={{4,20},{5,21},{6,22},{7,23},{12,28},{13,29},{14,30},{15,31},{20,4}... | collective-permute-start | bytes 811016 | tf_op jit(solution)/shard_map/ppermute | solution.py:80
  83.3 16.7 %collective-permute-start.22 = (bf16[176,768]{1,0:T(8,128)(2,1)}, bf16[176,768]{1,0:T(8,128)(2,1)}, u32[]{:S(2)}, u32[]{:S(2)}) collective-permute-start(bf16[176,768]{1,0:T(8,128)(2,1)} %get-tuple-element.14), channel_id=1, source_target_pairs={{4,12},{5,13},{6,14},{7,15},{12,4},{13,5},{14,6},{15,7},{20,28},{2... | collective-permute-start | bytes 811016 | tf_op jit(solution)/shard_map/ppermute | solution.py:80
  88.6 6.6 %collective-permute-start.21 = (bf16[128,176]{0,1:T(8,128)(2,1)S(1)}, bf16[128,176]{0,1:T(8,128)(2,1)S(1)}, u32[]{:S(2)}, u32[]{:S(2)}) collective-permute-start(bf16[128,176]{0,1:T(8,128)(2,1)S(1)} %fusion.7), channel_id=1, source_target_pairs={{4,28},{5,29},{6,30},{7,31},{12,20},{13,21},{14,22},{15,23},{20,12... | collective-permute-start | bytes 135176 | tf_op jit(solution)/shard_map/ppermute | solution.py:105
  92.0 6.0 %collective-permute-start.20 = (bf16[128,176]{0,1:T(8,128)(2,1)S(1)}, bf16[128,176]{0,1:T(8,128)(2,1)S(1)}, u32[]{:S(2)}, u32[]{:S(2)}) collective-permute-start(bf16[128,176]{0,1:T(8,128)(2,1)S(1)} %fusion.7), channel_id=1, source_target_pairs={{4,20},{5,21},{6,22},{7,23},{12,28},{13,29},{14,30},{15,31},{20,4}... | collective-permute-start | bytes 135176 | tf_op jit(solution)/shard_map/ppermute | solution.py:105
  95.2 4.8 %collective-permute-start.19 = (bf16[128,176]{0,1:T(8,128)(2,1)S(1)}, bf16[128,176]{0,1:T(8,128)(2,1)S(1)}, u32[]{:S(2)}, u32[]{:S(2)}) collective-permute-start(bf16[128,176]{0,1:T(8,128)(2,1)S(1)} %fusion.7), channel_id=1, source_target_pairs={{4,12},{5,13},{6,14},{7,15},{12,4},{13,5},{14,6},{15,7},{20,28},{2... | collective-permute-start | bytes 135176 | tf_op jit(solution)/shard_map/ppermute | solution.py:105
  101.5 8.4 %collective-permute-start.25 = (bf16[2,16,768]{2,1,0:T(8,128)(2,1)S(1)}, bf16[2,16,768]{2,1,0:T(8,128)(2,1)S(1)}, u32[]{:S(2)}, u32[]{:S(2)}) collective-permute-start(bf16[2,16,768]{2,1,0:T(8,128)(2,1)S(1)} %get-tuple-element.38), channel_id=1, source_target_pairs={{4,5},{5,4},{6,7},{7,6},{12,13},{13,12},{14,15},{15,14},{20,21},{2... | collective-permute-start | bytes 147464 | tf_op jit(solution)/shard_map/ppermute | solution.py:113
  104.7 5.7 %collective-permute-start.27 = (bf16[2,16,768]{2,1,0:T(8,128)(2,1)S(1)}, bf16[2,16,768]{2,1,0:T(8,128)(2,1)S(1)}, u32[]{:S(2)}, u32[]{:S(2)}) collective-permute-start(bf16[2,16,768]{2,1,0:T(8,128)(2,1)S(1)} %get-tuple-element.39), channel_id=1, source_target_pairs={{4,7},{5,6},{6,5},{7,4},{12,15},{13,14},{14,13},{15,12},{20,23},{2... | collective-permute-start | bytes 147464 | tf_op jit(solution)/shard_map/ppermute | solution.py:113
  106.8 4.8 %collective-permute-start.26 = (bf16[2,16,768]{2,1,0:T(8,128)(2,1)S(1)}, bf16[2,16,768]{2,1,0:T(8,128)(2,1)S(1)}, u32[]{:S(2)}, u32[]{:S(2)}) collective-permute-start(bf16[2,16,768]{2,1,0:T(8,128)(2,1)S(1)} %get-tuple-element.40), channel_id=1, source_target_pairs={{4,6},{5,7},{6,4},{7,5},{12,14},{13,15},{14,12},{15,13},{20,22},{2... | collective-permute-start | bytes 147464 | tf_op jit(solution)/shard_map/ppermute | solution.py:113
  (9 other events, 44.7 us)

commit v3 on v1

--- a/solution.py
+++ b/solution.py
@@ -68,17 +68,6 @@
     up_local = w_up[0, 0]
     down_local = w_down[0, 0]
 
-    if small_dp:
-        down_parts = []
-        for s in range(n_dp):
-            piece = lax.dynamic_slice_in_dim(down_local, dring.ahead(d_me, s) * columns, columns, 1)
-            if s:
-                piece = lax.ppermute(piece, "dp", [(i, dring.ahead(i, s)) for i in range(n_dp)])
-            down_parts.append(piece)
-        down_full = jnp.concatenate(down_parts, axis=0)
-    else:
-        down_full = lax.all_to_all(down_local, "dp", 1, 0, tiled=True)
-
     route_ids = expert_ids[0]
     route_gates = gates[0]
     maps = [build_maps(route_ids[m], route_gates[m], ering, e_me, rows_all) for m in range(micro)]
@@ -98,13 +87,24 @@
         up_act = jnp.dot(flat_rows, up_local, preferred_element_type=jnp.float32) * inv_rms
         hidden = (jax.nn.silu(gate_act) * up_act).astype(jnp.bfloat16)
         if small_dp:
-            parts = [hidden]
+            hidden_t = hidden.T
+            hidden_parts = [hidden_t]
+            down_parts = [lax.dynamic_slice_in_dim(down_local, d_me * columns, columns, 1)]
             for s in range(1, n_dp):
-                parts.append(lax.ppermute(hidden, AXES, dp_pairs(p, s)))
-            hidden_full = jnp.concatenate(parts, axis=1)
+                piece = lax.dynamic_slice_in_dim(down_local, dring.ahead(d_me, s) * columns, columns, 1)
+                packet = lax.ppermute(jnp.concatenate([hidden_t, piece], axis=1), AXES, dp_pairs(p, s))
+                hidden_parts.append(packet[:, : hidden_t.shape[1]])
+                down_parts.append(packet[:, hidden_t.shape[1] :])
+            expert_out = lax.dot_general(
+                jnp.concatenate(hidden_parts, axis=0),
+                jnp.concatenate(down_parts, axis=0),
+                (((0,), (0,)), ((), ())),
+                preferred_element_type=jnp.float32,
+            ).astype(jnp.bfloat16)
         else:
             hidden_full = lax.all_gather(hidden, "dp", axis=1, tiled=True)
-        expert_out = jnp.dot(hidden_full, down_full, preferred_element_type=jnp.float32).astype(jnp.bfloat16)
+            down_full = lax.all_to_all(down_local, "dp", 1, 0, tiled=True)
+            expert_out = jnp.dot(hidden_full, down_full, preferred_element_type=jnp.float32).astype(jnp.bfloat16)
         expert_out = expert_out.reshape(micro, n_exp, CAP, columns)
         returned = [expert_out[:, 0]]
         for s in range(1, n_exp):

time: 109 us -> 118 us (1.083)
  waiting for transfers between devices: 48 us -> 59.4 us
  starting transfers between devices: 42.3 us -> 38.2 us
  local copies, waits for them, and re-layouts: 5.55 us -> 7.33 us
  matrix products: 8.48 us -> 7.15 us
    ppermute x4, waiting for transfers between devices: 22.8 us -> 45.5 us  [per_device(): parts.append(lax.ppermute(cols, AXES, pairs))]
    ppermute x9 -> x6, waiting for transfers between devices: 18.4 us -> 7.99 us  [layer(): lax.ppermute(jnp.concatenate([hidden_t, piece], axis=1), AXES, dp_pairs(p...]
    ppermute x9 -> x6, starting transfers between devices: 15.7 us -> 11.6 us  [layer(): lax.ppermute(jnp.concatenate([hidden_t, piece], axis=1), AXES, dp_pairs(p...]
    dot_general x2, matrix products: 2.93 us -> 0.71 us  [layer(): lax.dot_general(jnp.concatenate(hidden_parts, axis=0), jnp.concatenate(do...]
    unnamed x12 -> x22, local copies, waits for them, and re-layouts: 0.73 us -> 2.44 us
  transfers between devices with their start and end apart: 25 -> 22, of which waited for: 9 -> 8; matrix products, arithmetic and copies ran while one was open for 3% -> 1% of each run, Pallas kernels for 0% -> 0%
where the time goes in v3:
time: 118 us; the launch traced here: 116 us
  waiting for transfers between devices  59.4 us (50%)
  starting transfers between devices  38.2 us (32%)
  local copies, waits for them, and re-layouts  7.33 us (6%)
  matrix products  7.15 us (6%)
  other arithmetic  3.42 us (3%)
    ppermute x4, waiting for transfers between devices, per_device(): parts.append(lax.ppermute(cols, AXES, pairs))  45.5 us
    ppermute x6, starting transfers between devices, layer(): lax.ppermute(jnp.concatenate([hidden_t, piece], axis=1), AXES, dp_pairs(p...  11.6 us
    ppermute x6, starting transfers between devices, layer(): lax.ppermute(outgoing[:, s], AXES, expert_pairs(p, s, False))  11 us
    ppermute x6, starting transfers between devices, layer(): lax.ppermute(expert_out[:, s], AXES, expert_pairs(p, s, True))  10.4 us
    ppermute x6, waiting for transfers between devices, layer(): lax.ppermute(jnp.concatenate([hidden_t, piece], axis=1), AXES, dp_pairs(p...  7.99 us
    ppermute x4, starting transfers between devices, per_device(): parts.append(lax.ppermute(cols, AXES, pairs))  5.17 us
    ppermute x6, waiting for transfers between devices, layer(): lax.ppermute(outgoing[:, s], AXES, expert_pairs(p, s, False))  4.23 us
    dot_general x2, matrix products, layer(): jnp.einsum('mrt,mrc->mtc', combine_map, returned.astype(jnp.float32), pre...  2.84 us
  transfers between devices with their start and end apart: 22, of which 8 were waited for; matrix products, arithmetic and copies ran while one was open for 1% of the time, Pallas kernels for 0%

profile of v3, /device:TPU:1, one launch (start us, length us, event | category | flops | bytes accessed | tf_op | source)
XLA Modules:
  0.0 116.0 jit_solution(3708120548785853063)
XLA Ops:
  3.7 1.4 %convolution_convert_fusion.1 = bf16[2,64,3072]{2,1,0:T(8,128)(2,1)S(1)} fusion(bf16[2,24,3072]{2,1,0:T(8,128)(2,1)} %param.6, bf16[1,64,24]{1,2,0:T(8,128)(2,1)S(1)} %bitcast.175, bf16[1,64,24]{1,2,0:T(8,128)(2,1)S(1)} %bitcast.177), kind=kOutput, calls=%fused_computation.2 | convolution fusion | flops 19270656 | bytes 1087488 | tf_op jit(solution)/shard_map/mrt,mtd->mrd/dot_general | solution.py:78
  7.3 1.3 %collective-permute-start.2 = (bf16[2,16,3072]{2,1,0:T(8,128)(2,1)S(1)}, bf16[2,16,3072]{2,1,0:T(8,128)(2,1)}, u32[]{:S(2)}, u32[]{:S(2)}) collective-permute-start(bf16[2,16,3072]{2,1,0:T(8,128)(2,1)S(1)} %get-tuple-element.24), channel_id=1, source_target_pairs={{0,3},{1,2},{2,1},{3,0},{8,11},{9,10},{10,9},{11,8},{16,19},{17,18... | collective-permute-start | bytes 589832 | tf_op jit(solution)/shard_map/ppermute | solution.py:82
  9.5 1.2 multiply_reduce_fusion.1
  17.9 1.1 fusion
  19.0 1.3 %collective-permute-start.12 = (bf16[2,24,768]{2,1,0:T(8,128)(2,1)S(1)}, bf16[2,24,768]{2,1,0:T(8,128)(2,1)S(1)}, u32[]{:S(2)}, u32[]{:S(2)}) collective-permute-start(bf16[2,24,768]{2,1,0:T(8,128)(2,1)S(1)} %fusion), channel_id=1, source_target_pairs={{0,28},{1,29},{2,30},{3,31},{8,20},{9,21},{10,22},{11,23},{16,12},... | collective-permute-start | bytes 221192 | tf_op jit(solution)/shard_map/ppermute | solution.py:135
  20.3 1.3 %collective-permute-start.11 = (bf16[2,24,768]{2,1,0:T(8,128)(2,1)S(1)}, bf16[2,24,768]{2,1,0:T(8,128)(2,1)S(1)}, u32[]{:S(2)}, u32[]{:S(2)}) collective-permute-start(bf16[2,24,768]{2,1,0:T(8,128)(2,1)S(1)} %fusion), channel_id=1, source_target_pairs={{0,20},{1,21},{2,22},{3,23},{8,28},{9,29},{10,30},{11,31},{16,4},{... | collective-permute-start | bytes 221192 | tf_op jit(solution)/shard_map/ppermute | solution.py:135
  21.6 1.3 %collective-permute-start.10 = (bf16[2,24,768]{2,1,0:T(8,128)(2,1)S(1)}, bf16[2,24,768]{2,1,0:T(8,128)(2,1)S(1)}, u32[]{:S(2)}, u32[]{:S(2)}) collective-permute-start(bf16[2,24,768]{2,1,0:T(8,128)(2,1)S(1)} %fusion), channel_id=1, source_target_pairs={{0,12},{1,13},{2,14},{3,15},{8,4},{9,5},{10,6},{11,7},{16,28},{17,... | collective-permute-start | bytes 221192 | tf_op jit(solution)/shard_map/ppermute | solution.py:135
  22.9 1.3 %collective-permute-start.9 = (bf16[2,24,768]{2,1,0:T(8,128)(2,1)S(1)}, bf16[2,24,768]{2,1,0:T(8,128)(2,1)S(1)}, u32[]{:S(2)}, u32[]{:S(2)}) collective-permute-start(bf16[2,24,768]{2,1,0:T(8,128)(2,1)S(1)} %fusion), channel_id=1, source_target_pairs={{0,4},{1,5},{2,6},{3,7},{8,12},{9,13},{10,14},{11,15},{16,20},{17,... | collective-permute-start | bytes 221192 | tf_op jit(solution)/shard_map/ppermute | solution.py:135
  24.3 40.9 %collective-permute-done.12 = bf16[2,24,768]{2,1,0:T(8,128)(2,1)S(1)} collective-permute-done((bf16[2,24,768]{2,1,0:T(8,128)(2,1)S(1)}, bf16[2,24,768]{2,1,0:T(8,128)(2,1)S(1)}, u32[]{:S(2)}, u32[]{:S(2)}) %collective-permute-start.12) | collective-permute-done | bytes 73760 | tf_op jit(solution)/shard_map/ppermute | solution.py:135
  65.3 3.8 %collective-permute-done.11 = bf16[2,24,768]{2,1,0:T(8,128)(2,1)S(1)} collective-permute-done((bf16[2,24,768]{2,1,0:T(8,128)(2,1)S(1)}, bf16[2,24,768]{2,1,0:T(8,128)(2,1)S(1)}, u32[]{:S(2)}, u32[]{:S(2)}) %collective-permute-start.11) | collective-permute-done | bytes 73760 | tf_op jit(solution)/shard_map/ppermute | solution.py:135
  71.7 3.1 %collective-permute-start.14 = (bf16[2,16,3072]{2,1,0:T(8,128)(2,1)S(1)}, bf16[2,16,3072]{2,1,0:T(8,128)(2,1)S(1)}, u32[]{:S(2)}, u32[]{:S(2)}) collective-permute-start(bf16[2,16,3072]{2,1,0:T(8,128)(2,1)S(1)} %get-tuple-element.18), channel_id=1, source_target_pairs={{4,6},{5,7},{6,4},{7,5},{12,14},{13,15},{14,12},{15,13},{20,22},{2... | collective-permute-start | bytes 589832 | tf_op jit(solution)/shard_map/ppermute | solution.py:82
  74.9 2.2 %collective-permute-start.13 = (bf16[2,16,3072]{2,1,0:T(8,128)(2,1)S(1)}, bf16[2,16,3072]{2,1,0:T(8,128)(2,1)S(1)}, u32[]{:S(2)}, u32[]{:S(2)}) collective-permute-start(bf16[2,16,3072]{2,1,0:T(8,128)(2,1)S(1)} %get-tuple-element.19), channel_id=1, source_target_pairs={{4,5},{5,4},{6,7},{7,6},{12,13},{13,12},{14,15},{15,14},{20,21},{2... | collective-permute-start | bytes 589832 | tf_op jit(solution)/shard_map/ppermute | solution.py:82
  77.1 3.1 %collective-permute-start.15 = (bf16[2,16,3072]{2,1,0:T(8,128)(2,1)S(1)}, bf16[2,16,3072]{2,1,0:T(8,128)(2,1)S(1)}, u32[]{:S(2)}, u32[]{:S(2)}) collective-permute-start(bf16[2,16,3072]{2,1,0:T(8,128)(2,1)S(1)} %get-tuple-element.20), channel_id=1, source_target_pairs={{4,7},{5,6},{6,5},{7,4},{12,15},{13,14},{14,13},{15,12},{20,23},{2... | collective-permute-start | bytes 589832 | tf_op jit(solution)/shard_map/ppermute | solution.py:82
  80.1 1.2 %collective-permute-done.13 = bf16[2,16,3072]{2,1,0:T(8,128)(2,1)S(1)} collective-permute-done((bf16[2,16,3072]{2,1,0:T(8,128)(2,1)S(1)}, bf16[2,16,3072]{2,1,0:T(8,128)(2,1)S(1)}, u32[]{:S(2)}, u32[]{:S(2)}) %collective-permute-start.13) | collective-permute-done | bytes 196640 | tf_op jit(solution)/shard_map/ppermute | solution.py:82
  81.3 3.1 %collective-permute-done.15 = bf16[2,16,3072]{2,1,0:T(8,128)(2,1)S(1)} collective-permute-done((bf16[2,16,3072]{2,1,0:T(8,128)(2,1)S(1)}, bf16[2,16,3072]{2,1,0:T(8,128)(2,1)S(1)}, u32[]{:S(2)}, u32[]{:S(2)}) %collective-permute-start.15) | collective-permute-done | bytes 196640 | tf_op jit(solution)/shard_map/ppermute | solution.py:82
  86.2 2.1 %collective-permute-start.16 = (bf16[176,896]{1,0:T(8,128)(2,1)S(1)}, bf16[176,896]{1,0:T(8,128)(2,1)S(1)}, u32[]{:S(2)}, u32[]{:S(2)}) collective-permute-start(bf16[176,896]{1,0:T(8,128)(2,1)S(1)} %get-tuple-element.33), channel_id=1, source_target_pairs={{4,12},{5,13},{6,14},{7,15},{12,4},{13,5},{14,6},{15,7},{20,28},{2... | collective-permute-start | bytes 946184 | tf_op jit(solution)/shard_map/ppermute | solution.py:95
  88.3 3.9 %collective-permute-start.17 = (bf16[176,896]{1,0:T(8,128)(2,1)S(1)}, bf16[176,896]{1,0:T(8,128)(2,1)S(1)}, u32[]{:S(2)}, u32[]{:S(2)}) collective-permute-start(bf16[176,896]{1,0:T(8,128)(2,1)S(1)} %get-tuple-element.34), channel_id=1, source_target_pairs={{4,20},{5,21},{6,22},{7,23},{12,28},{13,29},{14,30},{15,31},{20,4}... | collective-permute-start | bytes 946184 | tf_op jit(solution)/shard_map/ppermute | solution.py:95
  92.2 3.5 %collective-permute-start.18 = (bf16[176,896]{1,0:T(8,128)(2,1)S(1)}, bf16[176,896]{1,0:T(8,128)(2,1)S(1)}, u32[]{:S(2)}, u32[]{:S(2)}) collective-permute-start(bf16[176,896]{1,0:T(8,128)(2,1)S(1)} %get-tuple-element.35), channel_id=1, source_target_pairs={{4,28},{5,29},{6,30},{7,31},{12,20},{13,21},{14,22},{15,23},{20,12... | collective-permute-start | bytes 946184 | tf_op jit(solution)/shard_map/ppermute | solution.py:95
  95.7 8.0 %collective-permute-done.17 = bf16[176,896]{1,0:T(8,128)(2,1)S(1)} collective-permute-done((bf16[176,896]{1,0:T(8,128)(2,1)S(1)}, bf16[176,896]{1,0:T(8,128)(2,1)S(1)}, u32[]{:S(2)}, u32[]{:S(2)}) %collective-permute-start.17) | collective-permute-done | bytes 315424 | tf_op jit(solution)/shard_map/ppermute | solution.py:95
  104.2 3.1 %collective-permute-start.19 = (bf16[2,16,768]{2,1,0:T(8,128)(2,1)S(1)}, bf16[2,16,768]{2,1,0:T(8,128)(2,1)S(1)}, u32[]{:S(2)}, u32[]{:S(2)}) collective-permute-start(bf16[2,16,768]{2,1,0:T(8,128)(2,1)S(1)} %get-tuple-element.26), channel_id=1, source_target_pairs={{4,5},{5,4},{6,7},{7,6},{12,13},{13,12},{14,15},{15,14},{20,21},{2... | collective-permute-start | bytes 147464 | tf_op jit(solution)/shard_map/ppermute | solution.py:111
  107.3 2.1 %collective-permute-start.21 = (bf16[2,16,768]{2,1,0:T(8,128)(2,1)S(1)}, bf16[2,16,768]{2,1,0:T(8,128)(2,1)S(1)}, u32[]{:S(2)}, u32[]{:S(2)}) collective-permute-start(bf16[2,16,768]{2,1,0:T(8,128)(2,1)S(1)} %get-tuple-element.27), channel_id=1, source_target_pairs={{4,7},{5,6},{6,5},{7,4},{12,15},{13,14},{14,13},{15,12},{20,23},{2... | collective-permute-start | bytes 147464 | tf_op jit(solution)/shard_map/ppermute | solution.py:111
  109.4 3.1 %collective-permute-start.20 = (bf16[2,16,768]{2,1,0:T(8,128)(2,1)S(1)}, bf16[2,16,768]{2,1,0:T(8,128)(2,1)S(1)}, u32[]{:S(2)}, u32[]{:S(2)}) collective-permute-start(bf16[2,16,768]{2,1,0:T(8,128)(2,1)S(1)} %get-tuple-element.28), channel_id=1, source_target_pairs={{4,6},{5,7},{6,4},{7,5},{12,14},{13,15},{14,12},{15,13},{20,22},{2... | collective-permute-start | bytes 147464 | tf_op jit(solution)/shard_map/ppermute | solution.py:111
  113.0 1.2 %collective-permute-done.20 = bf16[2,16,768]{2,1,0:T(8,128)(2,1)S(1)} collective-permute-done((bf16[2,16,768]{2,1,0:T(8,128)(2,1)S(1)}, bf16[2,16,768]{2,1,0:T(8,128)(2,1)S(1)}, u32[]{:S(2)}, u32[]{:S(2)}) %collective-permute-start.20) | collective-permute-done | bytes 49184 | tf_op jit(solution)/shard_map/ppermute | solution.py:111
  114.3 1.7 %fusion.9 = bf16[1,2,24,768]{3,2,1,0:T(8,128)(2,1)} fusion(bf16[2,24,768]{2,1,0:T(8,128)(2,1)S(1)} %copy-done.7, bf16[2,64,768]{2,1,0:T(8,128)(2,1)S(1)} %bitcast.158, bf16[2,24,3072]{2,1,0:T(8,128)(2,1)} %bitcast.157, s32[]{:T(128)S(6)} %select_n.61, pred[]{:T(512)S(6)} %eq.63, f32[1,64,24]{1,2,0:T(8,128)S(1)} %bitcast.168, f32[1,64,24]{1,2,0:T(8,128)S(1)} %bitcast.170), kind=kOutput, calls=%fused_computation.24 | convolution fusion | flops 28462080 | bytes 430085 | tf_op jit(solution)/shard_map/mrt,mrc->mtc/dot_general | solution.py:113
  (104 shorter events, 19.3 us)
Async XLA Ops:
  5.9 3.6 %collective-permute-start.1 = (bf16[2,16,3072]{2,1,0:T(8,128)(2,1)}, bf16[2,16,3072]{2,1,0:T(8,128)(2,1)S(1)}, u32[]{:S(2)}, u32[]{:S(2)}) collective-permute-start(bf16[2,16,3072]{2,1,0:T(8,128)(2,1)} %get-tuple-element.22), channel_id=1, source_target_pairs={{0,2},{1,3},{2,0},{3,1},{8,10},{9,11},{10,8},{11,9},{16,18},{17,19... | collective-permute-start | bytes 589832 | tf_op jit(solution)/shard_map/ppermute | solution.py:82
  6.6 2.9 %collective-permute-start = (bf16[2,16,3072]{2,1,0:T(8,128)(2,1)}, bf16[2,16,3072]{2,1,0:T(8,128)(2,1)S(1)}, u32[]{:S(2)}, u32[]{:S(2)}) collective-permute-start(bf16[2,16,3072]{2,1,0:T(8,128)(2,1)} %get-tuple-element.23), channel_id=1, source_target_pairs={{0,1},{1,0},{2,3},{3,2},{8,9},{9,8},{10,11},{11,10},{16,17},{17,16... | collective-permute-start | bytes 589832 | tf_op jit(solution)/shard_map/ppermute | solution.py:82
  7.3 2.2 %collective-permute-start.2 = (bf16[2,16,3072]{2,1,0:T(8,128)(2,1)S(1)}, bf16[2,16,3072]{2,1,0:T(8,128)(2,1)}, u32[]{:S(2)}, u32[]{:S(2)}) collective-permute-start(bf16[2,16,3072]{2,1,0:T(8,128)(2,1)S(1)} %get-tuple-element.24), channel_id=1, source_target_pairs={{0,3},{1,2},{2,1},{3,0},{8,11},{9,10},{10,9},{11,8},{16,19},{17,18... | collective-permute-start | bytes 589832 | tf_op jit(solution)/shard_map/ppermute | solution.py:82
  13.0 2.3 %collective-permute-start.3 = (bf16[176,896]{1,0:T(8,128)(2,1)S(1)}, bf16[176,896]{1,0:T(8,128)(2,1)S(1)}, u32[]{:S(2)}, u32[]{:S(2)}) collective-permute-start(bf16[176,896]{1,0:T(8,128)(2,1)S(1)} %get-tuple-element.36), channel_id=1, source_target_pairs={{0,8},{1,9},{2,10},{3,11},{8,0},{9,1},{10,2},{11,3},{16,24},{17,25... | collective-permute-start | bytes 946184 | tf_op jit(solution)/shard_map/ppermute | solution.py:95
  13.8 1.5 %collective-permute-start.4 = (bf16[176,896]{1,0:T(8,128)(2,1)S(1)}, bf16[176,896]{1,0:T(8,128)(2,1)S(1)}, u32[]{:S(2)}, u32[]{:S(2)}) collective-permute-start(bf16[176,896]{1,0:T(8,128)(2,1)S(1)} %get-tuple-element.37), channel_id=1, source_target_pairs={{0,16},{1,17},{2,18},{3,19},{8,24},{9,25},{10,26},{11,27},{16,0},{... | collective-permute-start | bytes 946184 | tf_op jit(solution)/shard_map/ppermute | solution.py:95
  14.5 0.9 collective-permute-start.5
  15.8 2.0 %collective-permute-start.6 = (bf16[2,16,768]{2,1,0:T(8,128)(2,1)S(1)}, bf16[2,16,768]{2,1,0:T(8,128)(2,1)S(1)}, u32[]{:S(2)}, u32[]{:S(2)}) collective-permute-start(bf16[2,16,768]{2,1,0:T(8,128)(2,1)S(1)} %get-tuple-element.30), channel_id=1, source_target_pairs={{0,1},{1,0},{2,3},{3,2},{8,9},{9,8},{10,11},{11,10},{16,17},{17,16... | collective-permute-start | bytes 147464 | tf_op jit(solution)/shard_map/ppermute | solution.py:111
  16.5 1.4 %collective-permute-start.8 = (bf16[2,16,768]{2,1,0:T(8,128)(2,1)S(1)}, bf16[2,16,768]{2,1,0:T(8,128)(2,1)S(1)}, u32[]{:S(2)}, u32[]{:S(2)}) collective-permute-start(bf16[2,16,768]{2,1,0:T(8,128)(2,1)S(1)} %get-tuple-element.31), channel_id=1, source_target_pairs={{0,3},{1,2},{2,1},{3,0},{8,11},{9,10},{10,9},{11,8},{16,19},{17,18... | collective-permute-start | bytes 147464 | tf_op jit(solution)/shard_map/ppermute | solution.py:111
  17.1 0.7 collective-permute-start.7
  19.0 50.8 %copy-start.6 = (bf16[2,24,768]{2,1,0:T(8,128)(2,1)}, bf16[2,24,768]{2,1,0:T(8,128)(2,1)S(1)}, u32[]{:S(2)}) copy-start(bf16[2,24,768]{2,1,0:T(8,128)(2,1)S(1)} %fusion) | copy-start | bytes 221188
  19.0 46.2 %collective-permute-start.12 = (bf16[2,24,768]{2,1,0:T(8,128)(2,1)S(1)}, bf16[2,24,768]{2,1,0:T(8,128)(2,1)S(1)}, u32[]{:S(2)}, u32[]{:S(2)}) collective-permute-start(bf16[2,24,768]{2,1,0:T(8,128)(2,1)S(1)} %fusion), channel_id=1, source_target_pairs={{0,28},{1,29},{2,30},{3,31},{8,20},{9,21},{10,22},{11,23},{16,12},... | collective-permute-start | bytes 221192 | tf_op jit(solution)/shard_map/ppermute | solution.py:135
  20.3 48.7 %collective-permute-start.11 = (bf16[2,24,768]{2,1,0:T(8,128)(2,1)S(1)}, bf16[2,24,768]{2,1,0:T(8,128)(2,1)S(1)}, u32[]{:S(2)}, u32[]{:S(2)}) collective-permute-start(bf16[2,24,768]{2,1,0:T(8,128)(2,1)S(1)} %fusion), channel_id=1, source_target_pairs={{0,20},{1,21},{2,22},{3,23},{8,28},{9,29},{10,30},{11,31},{16,4},{... | collective-permute-start | bytes 221192 | tf_op jit(solution)/shard_map/ppermute | solution.py:135
  21.6 48.2 %collective-permute-start.10 = (bf16[2,24,768]{2,1,0:T(8,128)(2,1)S(1)}, bf16[2,24,768]{2,1,0:T(8,128)(2,1)S(1)}, u32[]{:S(2)}, u32[]{:S(2)}) collective-permute-start(bf16[2,24,768]{2,1,0:T(8,128)(2,1)S(1)} %fusion), channel_id=1, source_target_pairs={{0,12},{1,13},{2,14},{3,15},{8,4},{9,5},{10,6},{11,7},{16,28},{17,... | collective-permute-start | bytes 221192 | tf_op jit(solution)/shard_map/ppermute | solution.py:135
  22.9 46.9 %collective-permute-start.9 = (bf16[2,24,768]{2,1,0:T(8,128)(2,1)S(1)}, bf16[2,24,768]{2,1,0:T(8,128)(2,1)S(1)}, u32[]{:S(2)}, u32[]{:S(2)}) collective-permute-start(bf16[2,24,768]{2,1,0:T(8,128)(2,1)S(1)} %fusion), channel_id=1, source_target_pairs={{0,4},{1,5},{2,6},{3,7},{8,12},{9,13},{10,14},{11,15},{16,20},{17,... | collective-permute-start | bytes 221192 | tf_op jit(solution)/shard_map/ppermute | solution.py:135
  71.7 8.4 %collective-permute-start.14 = (bf16[2,16,3072]{2,1,0:T(8,128)(2,1)S(1)}, bf16[2,16,3072]{2,1,0:T(8,128)(2,1)S(1)}, u32[]{:S(2)}, u32[]{:S(2)}) collective-permute-start(bf16[2,16,3072]{2,1,0:T(8,128)(2,1)S(1)} %get-tuple-element.18), channel_id=1, source_target_pairs={{4,6},{5,7},{6,4},{7,5},{12,14},{13,15},{14,12},{15,13},{20,22},{2... | collective-permute-start | bytes 589832 | tf_op jit(solution)/shard_map/ppermute | solution.py:82
  74.9 6.4 %collective-permute-start.13 = (bf16[2,16,3072]{2,1,0:T(8,128)(2,1)S(1)}, bf16[2,16,3072]{2,1,0:T(8,128)(2,1)S(1)}, u32[]{:S(2)}, u32[]{:S(2)}) collective-permute-start(bf16[2,16,3072]{2,1,0:T(8,128)(2,1)S(1)} %get-tuple-element.19), channel_id=1, source_target_pairs={{4,5},{5,4},{6,7},{7,6},{12,13},{13,12},{14,15},{15,14},{20,21},{2... | collective-permute-start | bytes 589832 | tf_op jit(solution)/shard_map/ppermute | solution.py:82
  77.1 7.3 %collective-permute-start.15 = (bf16[2,16,3072]{2,1,0:T(8,128)(2,1)S(1)}, bf16[2,16,3072]{2,1,0:T(8,128)(2,1)S(1)}, u32[]{:S(2)}, u32[]{:S(2)}) collective-permute-start(bf16[2,16,3072]{2,1,0:T(8,128)(2,1)S(1)} %get-tuple-element.20), channel_id=1, source_target_pairs={{4,7},{5,6},{6,5},{7,4},{12,15},{13,14},{14,13},{15,12},{20,23},{2... | collective-permute-start | bytes 589832 | tf_op jit(solution)/shard_map/ppermute | solution.py:82
  86.2 17.5 %copy-start.9 = (bf16[176,768]{1,0:T(8,128)(2,1)S(1)}, bf16[176,768]{1,0:T(8,128)(2,1)}, u32[]{:S(2)}) copy-start(bf16[176,768]{1,0:T(8,128)(2,1)} %get-tuple-element.15) | copy-start | bytes 811012
  86.2 9.4 %collective-permute-start.16 = (bf16[176,896]{1,0:T(8,128)(2,1)S(1)}, bf16[176,896]{1,0:T(8,128)(2,1)S(1)}, u32[]{:S(2)}, u32[]{:S(2)}) collective-permute-start(bf16[176,896]{1,0:T(8,128)(2,1)S(1)} %get-tuple-element.33), channel_id=1, source_target_pairs={{4,12},{5,13},{6,14},{7,15},{12,4},{13,5},{14,6},{15,7},{20,28},{2... | collective-permute-start | bytes 946184 | tf_op jit(solution)/shard_map/ppermute | solution.py:95
  88.3 15.4 %collective-permute-start.17 = (bf16[176,896]{1,0:T(8,128)(2,1)S(1)}, bf16[176,896]{1,0:T(8,128)(2,1)S(1)}, u32[]{:S(2)}, u32[]{:S(2)}) collective-permute-start(bf16[176,896]{1,0:T(8,128)(2,1)S(1)} %get-tuple-element.34), channel_id=1, source_target_pairs={{4,20},{5,21},{6,22},{7,23},{12,28},{13,29},{14,30},{15,31},{20,4}... | collective-permute-start | bytes 946184 | tf_op jit(solution)/shard_map/ppermute | solution.py:95
  92.2 11.5 %collective-permute-start.18 = (bf16[176,896]{1,0:T(8,128)(2,1)S(1)}, bf16[176,896]{1,0:T(8,128)(2,1)S(1)}, u32[]{:S(2)}, u32[]{:S(2)}) collective-permute-start(bf16[176,896]{1,0:T(8,128)(2,1)S(1)} %get-tuple-element.35), channel_id=1, source_target_pairs={{4,28},{5,29},{6,30},{7,31},{12,20},{13,21},{14,22},{15,23},{20,12... | collective-permute-start | bytes 946184 | tf_op jit(solution)/shard_map/ppermute | solution.py:95
  104.2 8.4 %collective-permute-start.19 = (bf16[2,16,768]{2,1,0:T(8,128)(2,1)S(1)}, bf16[2,16,768]{2,1,0:T(8,128)(2,1)S(1)}, u32[]{:S(2)}, u32[]{:S(2)}) collective-permute-start(bf16[2,16,768]{2,1,0:T(8,128)(2,1)S(1)} %get-tuple-element.26), channel_id=1, source_target_pairs={{4,5},{5,4},{6,7},{7,6},{12,13},{13,12},{14,15},{15,14},{20,21},{2... | collective-permute-start | bytes 147464 | tf_op jit(solution)/shard_map/ppermute | solution.py:111
  107.3 5.7 %collective-permute-start.21 = (bf16[2,16,768]{2,1,0:T(8,128)(2,1)S(1)}, bf16[2,16,768]{2,1,0:T(8,128)(2,1)S(1)}, u32[]{:S(2)}, u32[]{:S(2)}) collective-permute-start(bf16[2,16,768]{2,1,0:T(8,128)(2,1)S(1)} %get-tuple-element.27), channel_id=1, source_target_pairs={{4,7},{5,6},{6,5},{7,4},{12,15},{13,14},{14,13},{15,12},{20,23},{2... | collective-permute-start | bytes 147464 | tf_op jit(solution)/shard_map/ppermute | solution.py:111
  109.4 4.8 %collective-permute-start.20 = (bf16[2,16,768]{2,1,0:T(8,128)(2,1)S(1)}, bf16[2,16,768]{2,1,0:T(8,128)(2,1)S(1)}, u32[]{:S(2)}, u32[]{:S(2)}) collective-permute-start(bf16[2,16,768]{2,1,0:T(8,128)(2,1)S(1)} %get-tuple-element.28), channel_id=1, source_target_pairs={{4,6},{5,7},{6,4},{7,5},{12,14},{13,15},{14,12},{15,13},{20,22},{2... | collective-permute-start | bytes 147464 | tf_op jit(solution)/shard_map/ppermute | solution.py:111
  (8 other events, 30.8 us)

commit v4 on v1

--- a/solution.py
+++ b/solution.py
@@ -68,16 +68,16 @@
     up_local = w_up[0, 0]
     down_local = w_down[0, 0]
 
-    if small_dp:
-        down_parts = []
-        for s in range(n_dp):
-            piece = lax.dynamic_slice_in_dim(down_local, dring.ahead(d_me, s) * columns, columns, 1)
-            if s:
-                piece = lax.ppermute(piece, "dp", [(i, dring.ahead(i, s)) for i in range(n_dp)])
-            down_parts.append(piece)
-        down_full = jnp.concatenate(down_parts, axis=0)
-    else:
-        down_full = lax.all_to_all(down_local, "dp", 1, 0, tiled=True)
+    down_full = {}
+    for p in range(1, n_pipe):
+        if small_dp:
+            parts = [lax.dynamic_slice_in_dim(down_local, d_me * columns, columns, 1)]
+            for s in range(1, n_dp):
+                piece = lax.dynamic_slice_in_dim(down_local, dring.ahead(d_me, s) * columns, columns, 1)
+                parts.append(lax.ppermute(piece, AXES, dp_pairs(p, s)))
+            down_full[p] = jnp.concatenate(parts, axis=0)
+        else:
+            down_full[p] = lax.all_to_all(down_local, "dp", 1, 0, tiled=True)
 
     route_ids = expert_ids[0]
     route_gates = gates[0]
@@ -97,14 +97,26 @@
         gate_act = jnp.dot(flat_rows, gate_local, preferred_element_type=jnp.float32) * inv_rms
         up_act = jnp.dot(flat_rows, up_local, preferred_element_type=jnp.float32) * inv_rms
         hidden = (jax.nn.silu(gate_act) * up_act).astype(jnp.bfloat16)
-        if small_dp:
-            parts = [hidden]
+        if p == 0 and small_dp:
+            partial = jnp.dot(hidden, down_local, preferred_element_type=jnp.float32)
+            total = lax.dynamic_slice_in_dim(partial, d_me * columns, columns, 1)
             for s in range(1, n_dp):
-                parts.append(lax.ppermute(hidden, AXES, dp_pairs(p, s)))
-            hidden_full = jnp.concatenate(parts, axis=1)
+                chunk = lax.dynamic_slice_in_dim(partial, dring.ahead(d_me, s) * columns, columns, 1)
+                total = total + lax.ppermute(chunk.astype(jnp.bfloat16), AXES, dp_pairs(p, s)).astype(jnp.float32)
+            expert_out = total.astype(jnp.bfloat16)
         else:
-            hidden_full = lax.all_gather(hidden, "dp", axis=1, tiled=True)
-        expert_out = jnp.dot(hidden_full, down_full, preferred_element_type=jnp.float32).astype(jnp.bfloat16)
+            if p == 0:
+                down_p = lax.all_to_all(down_local, "dp", 1, 0, tiled=True)
+            else:
+                down_p = down_full[p]
+            if small_dp:
+                parts = [hidden]
+                for s in range(1, n_dp):
+                    parts.append(lax.ppermute(hidden, AXES, dp_pairs(p, s)))
+                hidden_full = jnp.concatenate(parts, axis=1)
+            else:
+                hidden_full = lax.all_gather(hidden, "dp", axis=1, tiled=True)
+            expert_out = jnp.dot(hidden_full, down_p, preferred_element_type=jnp.float32).astype(jnp.bfloat16)
         expert_out = expert_out.reshape(micro, n_exp, CAP, columns)
         returned = [expert_out[:, 0]]
         for s in range(1, n_exp):
@@ -121,6 +133,8 @@
         return (current_cols.astype(jnp.float32) + mixed).astype(jnp.bfloat16)
 
     current = tokens
+    if down_full:
+        down_full, current = lax.optimization_barrier((down_full, current))
     result = None
     for p in range(n_pipe):
         cols = layer(current, p)

time: 109 us -> 109 us (level)
  starting transfers between devices: 42.3 us -> 47.5 us
  waiting for transfers between devices: 48 us -> 45 us
  matrix products: 8.48 us -> 7.3 us
  local copies, waits for them, and re-layouts: 5.55 us -> 4.37 us
    ppermute x3 -> x6, waiting for transfers between devices: 17 us -> 6.18 us  [the longest x3 6.17 us: per_device(): parts.append(lax.ppermute(piece, AXES, dp_pairs(p, s)))]
    ppermute x3 -> x6, starting transfers between devices: 4.44 us -> 12.2 us  [the longest x3 10.2 us: per_device(): parts.append(lax.ppermute(piece, AXES, dp_pairs(p, s)))]
    ppermute x4, waiting for transfers between devices: 22.8 us -> 28.9 us  [per_device(): parts.append(lax.ppermute(cols, AXES, pairs))]
    ppermute x6 -> x3, starting transfers between devices: 11.3 us -> 9.27 us  [layer(): parts.append(lax.ppermute(hidden, AXES, dp_pairs(p, s)))]
    ppermute x6 -> x3, waiting for transfers between devices: 1.41 us -> 3.14 us  [layer(): parts.append(lax.ppermute(hidden, AXES, dp_pairs(p, s)))]
    dot_general x2, matrix products: 0.91 us -> 2.22 us  [layer(): jnp.dot(flat_rows, gate_local, preferred_element_type=jnp.float32) * inv_rms]
    convert_element_type x0 -> x1, local copies, waits for them, and re-layouts: none -> 1.29 us  [layer(): chunk.astype(jnp.bfloat16)]
    convert_element_type x0 -> x1, other arithmetic: none -> 1.1 us  [layer(): expert_out = total.astype(jnp.bfloat16)]
  transfers between devices with their start and end apart: 25 -> 25, of which waited for: 9 -> 8; matrix products, arithmetic and copies ran while one was open for 3% -> 2% of each run, Pallas kernels for 0% -> 0%
where the time goes in v4:
time: 109 us
  starting transfers between devices  47.5 us (44%)
  waiting for transfers between devices  45 us (41%)
  matrix products  7.3 us (7%)
  local copies, waits for them, and re-layouts  4.37 us (4%)
  other arithmetic  3.8 us (3%)
    ppermute x4, waiting for transfers between devices, per_device(): parts.append(lax.ppermute(cols, AXES, pairs))  28.9 us
    ppermute x6, starting transfers between devices, layer(): lax.ppermute(outgoing[:, s], AXES, expert_pairs(p, s, False))  10.5 us
    ppermute x6, starting transfers between devices, layer(): lax.ppermute(expert_out[:, s], AXES, expert_pairs(p, s, True))  10.4 us
    ppermute x3, starting transfers between devices, per_device(): parts.append(lax.ppermute(piece, AXES, dp_pairs(p, s)))  10.2 us
    ppermute x3, starting transfers between devices, layer(): parts.append(lax.ppermute(hidden, AXES, dp_pairs(p, s)))  9.27 us
    ppermute x3, waiting for transfers between devices, per_device(): parts.append(lax.ppermute(piece, AXES, dp_pairs(p, s)))  6.17 us
    ppermute x6, waiting for transfers between devices, layer(): lax.ppermute(outgoing[:, s], AXES, expert_pairs(p, s, False))  5.2 us
    ppermute x4, starting transfers between devices, per_device(): parts.append(lax.ppermute(cols, AXES, pairs))  5.17 us
  transfers between devices with their start and end apart: 25, of which 8 were waited for; matrix products, arithmetic and copies ran while one was open for 2% of the time, Pallas kernels for 0%

profile of v4, /device:TPU:1, one launch (start us, length us, event | category | flops | bytes accessed | tf_op | source)
XLA Modules:
  0.0 108.6 jit_solution(5721352229448413829)
XLA Ops:
  0.0 1.4 %dynamic-slice_bitcast_fusion.3 = (bf16[176,768]{1,0:T(8,128)(2,1)S(1)}, bf16[176,768]{1,0:T(8,128)(2,1)S(1)}, bf16[176,768]{1,0:T(8,128)(2,1)S(1)}, bf16[176,768]{1,0:T(8,128)(2,1)S(1)}) fusion(bf16[1,1,176,3072]{3,2,1,0:T(8,128)(2,1)} %param.11, s32[]{:T(128)S(6)} %select_n.61, s32[]{:T(128)S(6)} %select_n.63, s32[]{:T(128)S(6)} %select_n.62, s32[]{:T(128)S(6)} %select_n.64), kind=kLoop, calls=%fused_computation.38 | loop fusion | bytes 2162704 | tf_op jit(solution)/shard_map/dynamic_slice | solution.py:74
  1.4 4.0 %collective-permute-start = (bf16[176,768]{1,0:T(8,128)(2,1)S(1)}, bf16[176,768]{1,0:T(8,128)(2,1)S(1)}, u32[]{:S(2)}, u32[]{:S(2)}) collective-permute-start(bf16[176,768]{1,0:T(8,128)(2,1)S(1)} %get-tuple-element.22), channel_id=1, source_target_pairs={{4,12},{5,13},{6,14},{7,15},{12,4},{13,5},{14,6},{15,7},{20,28},{2... | collective-permute-start | bytes 811016 | tf_op jit(solution)/shard_map/ppermute | solution.py:77
  5.4 4.2 %collective-permute-start.1 = (bf16[176,768]{1,0:T(8,128)(2,1)S(1)}, bf16[176,768]{1,0:T(8,128)(2,1)S(1)}, u32[]{:S(2)}, u32[]{:S(2)}) collective-permute-start(bf16[176,768]{1,0:T(8,128)(2,1)S(1)} %get-tuple-element.21), channel_id=1, source_target_pairs={{4,20},{5,21},{6,22},{7,23},{12,28},{13,29},{14,30},{15,31},{20,4}... | collective-permute-start | bytes 811016 | tf_op jit(solution)/shard_map/ppermute | solution.py:77
  9.7 1.9 %collective-permute-start.2 = (bf16[176,768]{1,0:T(8,128)(2,1)S(1)}, bf16[176,768]{1,0:T(8,128)(2,1)S(1)}, u32[]{:S(2)}, u32[]{:S(2)}) collective-permute-start(bf16[176,768]{1,0:T(8,128)(2,1)S(1)} %get-tuple-element.23), channel_id=1, source_target_pairs={{4,28},{5,29},{6,30},{7,31},{12,20},{13,21},{14,22},{15,23},{20,12... | collective-permute-start | bytes 811016 | tf_op jit(solution)/shard_map/ppermute | solution.py:77
  13.2 6.2 %collective-permute-done.1 = bf16[176,768]{1,0:T(8,128)(2,1)S(1)} collective-permute-done((bf16[176,768]{1,0:T(8,128)(2,1)S(1)}, bf16[176,768]{1,0:T(8,128)(2,1)S(1)}, u32[]{:S(2)}, u32[]{:S(2)}) %collective-permute-start.1) | collective-permute-done | bytes 270368 | tf_op jit(solution)/shard_map/ppermute | solution.py:77
  23.3 1.8 %convolution_multiply_fusion.3 = f32[128,176]{0,1:T(8,128)S(1)} fusion(bf16[128,3072]{1,0:T(8,128)(2,1)S(1)} %bitcast.139, bf16[1,1,3072,176]{2,3,1,0:T(8,128)(2,1)} %param.9, f32[128]{0:T(128)S(1)} %rsqrt.23), kind=kOutput, calls=%fused_computation.15 | convolution fusion | flops 138434560 | bytes 1958400 | tf_op jit(solution)/shard_map/dot_general | solution.py:97
  25.1 2.4 %fusion.8 = f32[128,3072]{1,0:T(8,128)} fusion(bf16[128,3072]{1,0:T(8,128)(2,1)S(1)} %bitcast.140, bf16[1,1,176,3072]{3,2,1,0:T(8,128)(2,1)S(1)} %copy-done.1, bf16[1,1,3072,176]{2,3,1,0:T(8,128)(2,1)S(1)} %copy-done, f32[128,176]{0,1:T(8,128)S(1)} %convolution_multiply_fusion.3, f32[128]{0:T(128)S(1)} %rsqrt.23), kind=kOutput, calls=%fused_computation.20 | convolution fusion | flops 276981760 | bytes 4612608 | tf_op jit(solution)/shard_map/dot_general | solution.py:101
  27.5 1.3 %dynamic-slice_convert_fusion.2 = (bf16[128,768]{1,0:T(8,128)(2,1)S(1)}, bf16[128,768]{1,0:T(8,128)(2,1)S(1)}, bf16[128,768]{1,0:T(8,128)(2,1)S(1)}) fusion(f32[128,3072]{1,0:T(8,128)} %fusion.8, s32[]{:T(128)S(6)} %select_n.62, s32[]{:T(128)S(6)} %select_n.64, s32[]{:T(128)S(6)} %select_n.63), kind=kLoop, calls=%fused_computation.32 | loop fusion | bytes 1179660 | tf_op jit(solution)/shard_map/convert_element_type | solution.py:105
  34.4 1.3 %collective-permute-start.12 = (bf16[2,24,768]{2,1,0:T(8,128)(2,1)S(1)}, bf16[2,24,768]{2,1,0:T(8,128)(2,1)S(1)}, u32[]{:S(2)}, u32[]{:S(2)}) collective-permute-start(bf16[2,24,768]{2,1,0:T(8,128)(2,1)S(1)} %fusion), channel_id=1, source_target_pairs={{0,4},{1,5},{2,6},{3,7},{8,12},{9,13},{10,14},{11,15},{16,20},{17,... | collective-permute-start | bytes 221192 | tf_op jit(solution)/shard_map/ppermute | solution.py:149
  39.7 22.2 %collective-permute-done.12 = bf16[2,24,768]{2,1,0:T(8,128)(2,1)S(1)} collective-permute-done((bf16[2,24,768]{2,1,0:T(8,128)(2,1)S(1)}, bf16[2,24,768]{2,1,0:T(8,128)(2,1)S(1)}, u32[]{:S(2)}, u32[]{:S(2)}) %collective-permute-start.12) | collective-permute-done | bytes 73760 | tf_op jit(solution)/shard_map/ppermute | solution.py:149
  61.9 3.3 %collective-permute-done.13 = bf16[2,24,768]{2,1,0:T(8,128)(2,1)S(1)} collective-permute-done((bf16[2,24,768]{2,1,0:T(8,128)(2,1)S(1)}, bf16[2,24,768]{2,1,0:T(8,128)(2,1)S(1)}, u32[]{:S(2)}, u32[]{:S(2)}) %collective-permute-start.13) | collective-permute-done | bytes 73760 | tf_op jit(solution)/shard_map/ppermute | solution.py:149
  65.2 3.4 %collective-permute-done.14 = bf16[2,24,768]{2,1,0:T(8,128)(2,1)S(1)} collective-permute-done((bf16[2,24,768]{2,1,0:T(8,128)(2,1)S(1)}, bf16[2,24,768]{2,1,0:T(8,128)(2,1)S(1)}, u32[]{:S(2)}, u32[]{:S(2)}) %collective-permute-start.14) | collective-permute-done | bytes 73760 | tf_op jit(solution)/shard_map/ppermute | solution.py:149
  69.8 3.3 %collective-permute-start.16 = (bf16[2,16,3072]{2,1,0:T(8,128)(2,1)S(1)}, bf16[2,16,3072]{2,1,0:T(8,128)(2,1)S(1)}, u32[]{:S(2)}, u32[]{:S(2)}) collective-permute-start(bf16[2,16,3072]{2,1,0:T(8,128)(2,1)S(1)} %get-tuple-element.26), channel_id=1, source_target_pairs={{4,5},{5,4},{6,7},{7,6},{12,13},{13,12},{14,15},{15,14},{20,21},{2... | collective-permute-start | bytes 589832 | tf_op jit(solution)/shard_map/ppermute | solution.py:93
  73.1 3.1 %collective-permute-start.17 = (bf16[2,16,3072]{2,1,0:T(8,128)(2,1)S(1)}, bf16[2,16,3072]{2,1,0:T(8,128)(2,1)S(1)}, u32[]{:S(2)}, u32[]{:S(2)}) collective-permute-start(bf16[2,16,3072]{2,1,0:T(8,128)(2,1)S(1)} %get-tuple-element.25), channel_id=1, source_target_pairs={{4,6},{5,7},{6,4},{7,5},{12,14},{13,15},{14,12},{15,13},{20,22},{2... | collective-permute-start | bytes 589832 | tf_op jit(solution)/shard_map/ppermute | solution.py:93
  76.2 2.1 %collective-permute-start.18 = (bf16[2,16,3072]{2,1,0:T(8,128)(2,1)S(1)}, bf16[2,16,3072]{2,1,0:T(8,128)(2,1)S(1)}, u32[]{:S(2)}, u32[]{:S(2)}) collective-permute-start(bf16[2,16,3072]{2,1,0:T(8,128)(2,1)S(1)} %get-tuple-element.27), channel_id=1, source_target_pairs={{4,7},{5,6},{6,5},{7,4},{12,15},{13,14},{14,13},{15,12},{20,23},{2... | collective-permute-start | bytes 589832 | tf_op jit(solution)/shard_map/ppermute | solution.py:93
  79.5 4.0 %collective-permute-done.18 = bf16[2,16,3072]{2,1,0:T(8,128)(2,1)S(1)} collective-permute-done((bf16[2,16,3072]{2,1,0:T(8,128)(2,1)S(1)}, bf16[2,16,3072]{2,1,0:T(8,128)(2,1)S(1)}, u32[]{:S(2)}, u32[]{:S(2)}) %collective-permute-start.18) | collective-permute-done | bytes 196640 | tf_op jit(solution)/shard_map/ppermute | solution.py:93
  84.8 3.0 %collective-permute-start.19 = (bf16[128,176]{0,1:T(8,128)(2,1)S(1)}, bf16[128,176]{0,1:T(8,128)(2,1)S(1)}, u32[]{:S(2)}, u32[]{:S(2)}) collective-permute-start(bf16[128,176]{0,1:T(8,128)(2,1)S(1)} %fusion.7), channel_id=1, source_target_pairs={{4,12},{5,13},{6,14},{7,15},{12,4},{13,5},{14,6},{15,7},{20,28},{2... | collective-permute-start | bytes 135176 | tf_op jit(solution)/shard_map/ppermute | solution.py:115
  87.8 2.9 %collective-permute-start.20 = (bf16[128,176]{0,1:T(8,128)(2,1)S(1)}, bf16[128,176]{0,1:T(8,128)(2,1)S(1)}, u32[]{:S(2)}, u32[]{:S(2)}) collective-permute-start(bf16[128,176]{0,1:T(8,128)(2,1)S(1)} %fusion.7), channel_id=1, source_target_pairs={{4,20},{5,21},{6,22},{7,23},{12,28},{13,29},{14,30},{15,31},{20,4}... | collective-permute-start | bytes 135176 | tf_op jit(solution)/shard_map/ppermute | solution.py:115
  90.7 3.4 %collective-permute-start.21 = (bf16[128,176]{0,1:T(8,128)(2,1)S(1)}, bf16[128,176]{0,1:T(8,128)(2,1)S(1)}, u32[]{:S(2)}, u32[]{:S(2)}) collective-permute-start(bf16[128,176]{0,1:T(8,128)(2,1)S(1)} %fusion.7), channel_id=1, source_target_pairs={{4,28},{5,29},{6,30},{7,31},{12,20},{13,21},{14,22},{15,23},{20,12... | collective-permute-start | bytes 135176 | tf_op jit(solution)/shard_map/ppermute | solution.py:115
  94.1 3.1 %collective-permute-done.21 = bf16[128,176]{0,1:T(8,128)(2,1)S(1)} collective-permute-done((bf16[128,176]{0,1:T(8,128)(2,1)S(1)}, bf16[128,176]{0,1:T(8,128)(2,1)S(1)}, u32[]{:S(2)}, u32[]{:S(2)}) %collective-permute-start.21) | collective-permute-done | bytes 45088 | tf_op jit(solution)/shard_map/ppermute | solution.py:115
  97.6 2.2 %collective-permute-start.22 = (bf16[2,16,768]{2,1,0:T(8,128)(2,1)S(1)}, bf16[2,16,768]{2,1,0:T(8,128)(2,1)S(1)}, u32[]{:S(2)}, u32[]{:S(2)}) collective-permute-start(bf16[2,16,768]{2,1,0:T(8,128)(2,1)S(1)} %get-tuple-element.33), channel_id=1, source_target_pairs={{4,5},{5,4},{6,7},{7,6},{12,13},{13,12},{14,15},{15,14},{20,21},{2... | collective-permute-start | bytes 147464 | tf_op jit(solution)/shard_map/ppermute | solution.py:123
  99.8 2.1 %collective-permute-start.23 = (bf16[2,16,768]{2,1,0:T(8,128)(2,1)S(1)}, bf16[2,16,768]{2,1,0:T(8,128)(2,1)S(1)}, u32[]{:S(2)}, u32[]{:S(2)}) collective-permute-start(bf16[2,16,768]{2,1,0:T(8,128)(2,1)S(1)} %get-tuple-element.35), channel_id=1, source_target_pairs={{4,6},{5,7},{6,4},{7,5},{12,14},{13,15},{14,12},{15,13},{20,22},{2... | collective-permute-start | bytes 147464 | tf_op jit(solution)/shard_map/ppermute | solution.py:123
  101.9 4.1 %collective-permute-start.24 = (bf16[2,16,768]{2,1,0:T(8,128)(2,1)S(1)}, bf16[2,16,768]{2,1,0:T(8,128)(2,1)S(1)}, u32[]{:S(2)}, u32[]{:S(2)}) collective-permute-start(bf16[2,16,768]{2,1,0:T(8,128)(2,1)S(1)} %get-tuple-element.34), channel_id=1, source_target_pairs={{4,7},{5,6},{6,5},{7,4},{12,15},{13,14},{14,13},{15,12},{20,23},{2... | collective-permute-start | bytes 147464 | tf_op jit(solution)/shard_map/ppermute | solution.py:123
  106.1 1.6 %collective-permute-done.24 = bf16[2,16,768]{2,1,0:T(8,128)(2,1)S(1)} collective-permute-done((bf16[2,16,768]{2,1,0:T(8,128)(2,1)S(1)}, bf16[2,16,768]{2,1,0:T(8,128)(2,1)S(1)}, u32[]{:S(2)}, u32[]{:S(2)}) %collective-permute-start.24) | collective-permute-done | bytes 49184 | tf_op jit(solution)/shard_map/ppermute | solution.py:123
  (92 shorter events, 19.7 us)
Async XLA Ops:
  1.4 11.8 %collective-permute-start = (bf16[176,768]{1,0:T(8,128)(2,1)S(1)}, bf16[176,768]{1,0:T(8,128)(2,1)S(1)}, u32[]{:S(2)}, u32[]{:S(2)}) collective-permute-start(bf16[176,768]{1,0:T(8,128)(2,1)S(1)} %get-tuple-element.22), channel_id=1, source_target_pairs={{4,12},{5,13},{6,14},{7,15},{12,4},{13,5},{14,6},{15,7},{20,28},{2... | collective-permute-start | bytes 811016 | tf_op jit(solution)/shard_map/ppermute | solution.py:77
  5.4 13.9 %collective-permute-start.1 = (bf16[176,768]{1,0:T(8,128)(2,1)S(1)}, bf16[176,768]{1,0:T(8,128)(2,1)S(1)}, u32[]{:S(2)}, u32[]{:S(2)}) collective-permute-start(bf16[176,768]{1,0:T(8,128)(2,1)S(1)} %get-tuple-element.21), channel_id=1, source_target_pairs={{4,20},{5,21},{6,22},{7,23},{12,28},{13,29},{14,30},{15,31},{20,4}... | collective-permute-start | bytes 811016 | tf_op jit(solution)/shard_map/ppermute | solution.py:77
  9.7 9.7 %collective-permute-start.2 = (bf16[176,768]{1,0:T(8,128)(2,1)S(1)}, bf16[176,768]{1,0:T(8,128)(2,1)S(1)}, u32[]{:S(2)}, u32[]{:S(2)}) collective-permute-start(bf16[176,768]{1,0:T(8,128)(2,1)S(1)} %get-tuple-element.23), channel_id=1, source_target_pairs={{4,28},{5,29},{6,30},{7,31},{12,20},{13,21},{14,22},{15,23},{20,12... | collective-permute-start | bytes 811016 | tf_op jit(solution)/shard_map/ppermute | solution.py:77
  20.9 2.0 %collective-permute-start.3 = (bf16[2,16,3072]{2,1,0:T(8,128)(2,1)S(1)}, bf16[2,16,3072]{2,1,0:T(8,128)(2,1)S(1)}, u32[]{:S(2)}, u32[]{:S(2)}) collective-permute-start(bf16[2,16,3072]{2,1,0:T(8,128)(2,1)S(1)} %get-tuple-element.30), channel_id=1, source_target_pairs={{0,1},{1,0},{2,3},{3,2},{8,9},{9,8},{10,11},{11,10},{16,17},{17,16... | collective-permute-start | bytes 589832 | tf_op jit(solution)/shard_map/ppermute | solution.py:93
  21.6 1.4 %collective-permute-start.4 = (bf16[2,16,3072]{2,1,0:T(8,128)(2,1)S(1)}, bf16[2,16,3072]{2,1,0:T(8,128)(2,1)S(1)}, u32[]{:S(2)}, u32[]{:S(2)}) collective-permute-start(bf16[2,16,3072]{2,1,0:T(8,128)(2,1)S(1)} %get-tuple-element.29), channel_id=1, source_target_pairs={{0,2},{1,3},{2,0},{3,1},{8,10},{9,11},{10,8},{11,9},{16,18},{17,19... | collective-permute-start | bytes 589832 | tf_op jit(solution)/shard_map/ppermute | solution.py:93
  28.8 2.1 %collective-permute-start.6 = (bf16[128,768]{1,0:T(8,128)(2,1)S(1)}, bf16[128,768]{1,0:T(8,128)(2,1)S(1)}, u32[]{:S(2)}, u32[]{:S(2)}) collective-permute-start(bf16[128,768]{1,0:T(8,128)(2,1)S(1)} %get-tuple-element.17), channel_id=1, source_target_pairs={{0,8},{1,9},{2,10},{3,11},{8,0},{9,1},{10,2},{11,3},{16,24},{17,25... | collective-permute-start | bytes 589832 | tf_op jit(solution)/shard_map/ppermute | solution.py:105
  29.5 1.4 %collective-permute-start.7 = (bf16[128,768]{1,0:T(8,128)(2,1)S(1)}, bf16[128,768]{1,0:T(8,128)(2,1)S(1)}, u32[]{:S(2)}, u32[]{:S(2)}) collective-permute-start(bf16[128,768]{1,0:T(8,128)(2,1)S(1)} %get-tuple-element.19), channel_id=1, source_target_pairs={{0,16},{1,17},{2,18},{3,19},{8,24},{9,25},{10,26},{11,27},{16,0},{... | collective-permute-start | bytes 589832 | tf_op jit(solution)/shard_map/ppermute | solution.py:105
  30.1 0.8 collective-permute-start.8
  32.1 2.0 %collective-permute-start.9 = (bf16[2,16,768]{2,1,0:T(8,128)(2,1)S(1)}, bf16[2,16,768]{2,1,0:T(8,128)(2,1)S(1)}, u32[]{:S(2)}, u32[]{:S(2)}) collective-permute-start(bf16[2,16,768]{2,1,0:T(8,128)(2,1)S(1)} %get-tuple-element.37), channel_id=1, source_target_pairs={{0,1},{1,0},{2,3},{3,2},{8,9},{9,8},{10,11},{11,10},{16,17},{17,16... | collective-permute-start | bytes 147464 | tf_op jit(solution)/shard_map/ppermute | solution.py:123
  32.7 1.4 %collective-permute-start.10 = (bf16[2,16,768]{2,1,0:T(8,128)(2,1)S(1)}, bf16[2,16,768]{2,1,0:T(8,128)(2,1)S(1)}, u32[]{:S(2)}, u32[]{:S(2)}) collective-permute-start(bf16[2,16,768]{2,1,0:T(8,128)(2,1)S(1)} %get-tuple-element.39), channel_id=1, source_target_pairs={{0,2},{1,3},{2,0},{3,1},{8,10},{9,11},{10,8},{11,9},{16,18},{17,19... | collective-permute-start | bytes 147464 | tf_op jit(solution)/shard_map/ppermute | solution.py:123
  33.4 0.7 collective-permute-start.11
  34.4 27.5 %collective-permute-start.12 = (bf16[2,24,768]{2,1,0:T(8,128)(2,1)S(1)}, bf16[2,24,768]{2,1,0:T(8,128)(2,1)S(1)}, u32[]{:S(2)}, u32[]{:S(2)}) collective-permute-start(bf16[2,24,768]{2,1,0:T(8,128)(2,1)S(1)} %fusion), channel_id=1, source_target_pairs={{0,4},{1,5},{2,6},{3,7},{8,12},{9,13},{10,14},{11,15},{16,20},{17,... | collective-permute-start | bytes 221192 | tf_op jit(solution)/shard_map/ppermute | solution.py:149
  35.7 29.5 %collective-permute-start.13 = (bf16[2,24,768]{2,1,0:T(8,128)(2,1)S(1)}, bf16[2,24,768]{2,1,0:T(8,128)(2,1)S(1)}, u32[]{:S(2)}, u32[]{:S(2)}) collective-permute-start(bf16[2,24,768]{2,1,0:T(8,128)(2,1)S(1)} %fusion), channel_id=1, source_target_pairs={{0,12},{1,13},{2,14},{3,15},{8,4},{9,5},{10,6},{11,7},{16,28},{17,... | collective-permute-start | bytes 221192 | tf_op jit(solution)/shard_map/ppermute | solution.py:149
  37.0 31.6 %collective-permute-start.14 = (bf16[2,24,768]{2,1,0:T(8,128)(2,1)S(1)}, bf16[2,24,768]{2,1,0:T(8,128)(2,1)S(1)}, u32[]{:S(2)}, u32[]{:S(2)}) collective-permute-start(bf16[2,24,768]{2,1,0:T(8,128)(2,1)S(1)} %fusion), channel_id=1, source_target_pairs={{0,20},{1,21},{2,22},{3,23},{8,28},{9,29},{10,30},{11,31},{16,4},{... | collective-permute-start | bytes 221192 | tf_op jit(solution)/shard_map/ppermute | solution.py:149
  38.3 30.3 %collective-permute-start.15 = (bf16[2,24,768]{2,1,0:T(8,128)(2,1)S(1)}, bf16[2,24,768]{2,1,0:T(8,128)(2,1)S(1)}, u32[]{:S(2)}, u32[]{:S(2)}) collective-permute-start(bf16[2,24,768]{2,1,0:T(8,128)(2,1)S(1)} %fusion), channel_id=1, source_target_pairs={{0,28},{1,29},{2,30},{3,31},{8,20},{9,21},{10,22},{11,23},{16,12},... | collective-permute-start | bytes 221192 | tf_op jit(solution)/shard_map/ppermute | solution.py:149
  69.8 8.5 %collective-permute-start.16 = (bf16[2,16,3072]{2,1,0:T(8,128)(2,1)S(1)}, bf16[2,16,3072]{2,1,0:T(8,128)(2,1)S(1)}, u32[]{:S(2)}, u32[]{:S(2)}) collective-permute-start(bf16[2,16,3072]{2,1,0:T(8,128)(2,1)S(1)} %get-tuple-element.26), channel_id=1, source_target_pairs={{4,5},{5,4},{6,7},{7,6},{12,13},{13,12},{14,15},{15,14},{20,21},{2... | collective-permute-start | bytes 589832 | tf_op jit(solution)/shard_map/ppermute | solution.py:93
  73.1 6.4 %collective-permute-start.17 = (bf16[2,16,3072]{2,1,0:T(8,128)(2,1)S(1)}, bf16[2,16,3072]{2,1,0:T(8,128)(2,1)S(1)}, u32[]{:S(2)}, u32[]{:S(2)}) collective-permute-start(bf16[2,16,3072]{2,1,0:T(8,128)(2,1)S(1)} %get-tuple-element.25), channel_id=1, source_target_pairs={{4,6},{5,7},{6,4},{7,5},{12,14},{13,15},{14,12},{15,13},{20,22},{2... | collective-permute-start | bytes 589832 | tf_op jit(solution)/shard_map/ppermute | solution.py:93
  76.2 7.3 %collective-permute-start.18 = (bf16[2,16,3072]{2,1,0:T(8,128)(2,1)S(1)}, bf16[2,16,3072]{2,1,0:T(8,128)(2,1)S(1)}, u32[]{:S(2)}, u32[]{:S(2)}) collective-permute-start(bf16[2,16,3072]{2,1,0:T(8,128)(2,1)S(1)} %get-tuple-element.27), channel_id=1, source_target_pairs={{4,7},{5,6},{6,5},{7,4},{12,15},{13,14},{14,13},{15,12},{20,23},{2... | collective-permute-start | bytes 589832 | tf_op jit(solution)/shard_map/ppermute | solution.py:93
  84.8 9.3 %collective-permute-start.19 = (bf16[128,176]{0,1:T(8,128)(2,1)S(1)}, bf16[128,176]{0,1:T(8,128)(2,1)S(1)}, u32[]{:S(2)}, u32[]{:S(2)}) collective-permute-start(bf16[128,176]{0,1:T(8,128)(2,1)S(1)} %fusion.7), channel_id=1, source_target_pairs={{4,12},{5,13},{6,14},{7,15},{12,4},{13,5},{14,6},{15,7},{20,28},{2... | collective-permute-start | bytes 135176 | tf_op jit(solution)/shard_map/ppermute | solution.py:115
  87.8 6.3 %collective-permute-start.20 = (bf16[128,176]{0,1:T(8,128)(2,1)S(1)}, bf16[128,176]{0,1:T(8,128)(2,1)S(1)}, u32[]{:S(2)}, u32[]{:S(2)}) collective-permute-start(bf16[128,176]{0,1:T(8,128)(2,1)S(1)} %fusion.7), channel_id=1, source_target_pairs={{4,20},{5,21},{6,22},{7,23},{12,28},{13,29},{14,30},{15,31},{20,4}... | collective-permute-start | bytes 135176 | tf_op jit(solution)/shard_map/ppermute | solution.py:115
  90.7 6.6 %collective-permute-start.21 = (bf16[128,176]{0,1:T(8,128)(2,1)S(1)}, bf16[128,176]{0,1:T(8,128)(2,1)S(1)}, u32[]{:S(2)}, u32[]{:S(2)}) collective-permute-start(bf16[128,176]{0,1:T(8,128)(2,1)S(1)} %fusion.7), channel_id=1, source_target_pairs={{4,28},{5,29},{6,30},{7,31},{12,20},{13,21},{14,22},{15,23},{20,12... | collective-permute-start | bytes 135176 | tf_op jit(solution)/shard_map/ppermute | solution.py:115
  97.6 8.4 %collective-permute-start.22 = (bf16[2,16,768]{2,1,0:T(8,128)(2,1)S(1)}, bf16[2,16,768]{2,1,0:T(8,128)(2,1)S(1)}, u32[]{:S(2)}, u32[]{:S(2)}) collective-permute-start(bf16[2,16,768]{2,1,0:T(8,128)(2,1)S(1)} %get-tuple-element.33), channel_id=1, source_target_pairs={{4,5},{5,4},{6,7},{7,6},{12,13},{13,12},{14,15},{15,14},{20,21},{2... | collective-permute-start | bytes 147464 | tf_op jit(solution)/shard_map/ppermute | solution.py:123
  99.8 6.2 %collective-permute-start.23 = (bf16[2,16,768]{2,1,0:T(8,128)(2,1)S(1)}, bf16[2,16,768]{2,1,0:T(8,128)(2,1)S(1)}, u32[]{:S(2)}, u32[]{:S(2)}) collective-permute-start(bf16[2,16,768]{2,1,0:T(8,128)(2,1)S(1)} %get-tuple-element.35), channel_id=1, source_target_pairs={{4,6},{5,7},{6,4},{7,5},{12,14},{13,15},{14,12},{15,13},{20,22},{2... | collective-permute-start | bytes 147464 | tf_op jit(solution)/shard_map/ppermute | solution.py:123
  101.9 5.7 %collective-permute-start.24 = (bf16[2,16,768]{2,1,0:T(8,128)(2,1)S(1)}, bf16[2,16,768]{2,1,0:T(8,128)(2,1)S(1)}, u32[]{:S(2)}, u32[]{:S(2)}) collective-permute-start(bf16[2,16,768]{2,1,0:T(8,128)(2,1)S(1)} %get-tuple-element.34), channel_id=1, source_target_pairs={{4,7},{5,6},{6,5},{7,4},{12,15},{13,14},{14,13},{15,12},{20,23},{2... | collective-permute-start | bytes 147464 | tf_op jit(solution)/shard_map/ppermute | solution.py:123
  (8 other events, 80.4 us)

commit v5 on v1

--- a/solution.py
+++ b/solution.py
@@ -22,6 +22,34 @@
 
     def place(self, target, me):
         return target ^ me if self.xor else (target - me) % self.n
+
+
+def hyper_all_to_all(chunks, pairs_for):
+    held = [(k, 0, chunk) for k, chunk in enumerate(chunks)]
+    bit = 1
+    while bit < len(chunks):
+        send = [h for h in held if h[0] & bit]
+        keep = [h for h in held if not h[0] & bit]
+        got = lax.ppermute(jnp.stack([h[2] for h in send]), AXES, pairs_for(bit))
+        held = keep + [(k ^ bit, j ^ bit, got[i]) for i, (k, j, _) in enumerate(send)]
+        bit *= 2
+    arrived = [None] * len(chunks)
+    for k, j, chunk in held:
+        arrived[j] = chunk
+    return arrived
+
+
+def hyper_all_gather(value, n, pairs_for):
+    held = [(0, value)]
+    bit = 1
+    while bit < n:
+        got = lax.ppermute(jnp.stack([h[1] for h in held]), AXES, pairs_for(bit))
+        held = held + [(j ^ bit, got[i]) for i, (j, _) in enumerate(held)]
+        bit *= 2
+    arrived = [None] * n
+    for j, chunk in held:
+        arrived[j] = chunk
+    return arrived
 
 
 def build_maps(route_ids, route_gates, ring, me, rows_all):
@@ -64,11 +92,19 @@
     def dp_pairs(p, s):
         return [(lin(d, p, e), lin(dring.ahead(d, s), p, e)) for d in range(n_dp) for e in range(n_exp)]
 
+    def dp_all(bit):
+        return [(lin(d, p, e), lin(d ^ bit, p, e)) for d in range(n_dp) for p in range(n_pipe) for e in range(n_exp)]
+
     gate_local = w_gate[0, 0]
     up_local = w_up[0, 0]
     down_local = w_down[0, 0]
 
-    if small_dp:
+    if small_dp and dring.xor:
+        chunks = [lax.dynamic_slice_in_dim(down_local, (d_me ^ k) * columns, columns, 1) for k in range(n_dp)]
+        down_full = jnp.concatenate(
+            hyper_all_to_all(chunks, dp_all), axis=0
+        )
+    elif small_dp:
         down_parts = []
         for s in range(n_dp):
             piece = lax.dynamic_slice_in_dim(down_local, dring.ahead(d_me, s) * columns, columns, 1)
@@ -88,16 +124,21 @@
     def layer(current, p):
         outgoing = jnp.einsum("mrt,mtd->mrd", dispatch_map, current, preferred_element_type=jnp.float32)
         outgoing = outgoing.astype(jnp.bfloat16).reshape(micro, n_exp, CAP, width)
-        arrived = [outgoing[:, 0]]
-        for s in range(1, n_exp):
-            arrived.append(lax.ppermute(outgoing[:, s], AXES, expert_pairs(p, s, False)))
+        if ering.xor:
+            arrived = hyper_all_to_all([outgoing[:, s] for s in range(n_exp)], lambda bit: expert_pairs(p, bit, False))
+        else:
+            arrived = [outgoing[:, 0]]
+            for s in range(1, n_exp):
+                arrived.append(lax.ppermute(outgoing[:, s], AXES, expert_pairs(p, s, False)))
         flat_rows = jnp.stack(arrived, axis=1).reshape(-1, width)
         squares = jnp.mean(jnp.square(flat_rows.astype(jnp.float32)), axis=1, keepdims=True)
         inv_rms = lax.rsqrt(squares + 1e-05)
         gate_act = jnp.dot(flat_rows, gate_local, preferred_element_type=jnp.float32) * inv_rms
         up_act = jnp.dot(flat_rows, up_local, preferred_element_type=jnp.float32) * inv_rms
         hidden = (jax.nn.silu(gate_act) * up_act).astype(jnp.bfloat16)
-        if small_dp:
+        if small_dp and dring.xor:
+            hidden_full = jnp.concatenate(hyper_all_gather(hidden, n_dp, lambda bit: dp_pairs(p, bit)), axis=1)
+        elif small_dp:
             parts = [hidden]
             for s in range(1, n_dp):
                 parts.append(lax.ppermute(hidden, AXES, dp_pairs(p, s)))
@@ -106,9 +147,12 @@
             hidden_full = lax.all_gather(hidden, "dp", axis=1, tiled=True)
         expert_out = jnp.dot(hidden_full, down_full, preferred_element_type=jnp.float32).astype(jnp.bfloat16)
         expert_out = expert_out.reshape(micro, n_exp, CAP, columns)
-        returned = [expert_out[:, 0]]
-        for s in range(1, n_exp):
-            returned.append(lax.ppermute(expert_out[:, s], AXES, expert_pairs(p, s, True)))
+        if ering.xor:
+            returned = hyper_all_to_all([expert_out[:, s] for s in range(n_exp)], lambda bit: expert_pairs(p, bit, True))
+        else:
+            returned = [expert_out[:, 0]]
+            for s in range(1, n_exp):
+                returned.append(lax.ppermute(expert_out[:, s], AXES, expert_pairs(p, s, True)))
         returned = jnp.stack(returned, axis=1).reshape(micro, rows_all, columns)
         mixed = jnp.einsum(
             "mrt,mrc->mtc",

time: 109 us -> 117 us (1.073)
  waiting for transfers between devices: 48 us -> 64.9 us
  starting transfers between devices: 42.3 us -> 34.7 us
  matrix products: 8.48 us -> 6.26 us
    ppermute x21 -> x14, waiting for transfers between devices: 25.3 us -> 48.5 us  [the longest x10 43.8 us: hyper_all_to_all(): got = lax.ppermute(jnp.stack([h[2] for h in send]), AXES, pairs_for(bit))]
    ppermute x21 -> x14, starting transfers between devices: 37.1 us -> 29.5 us  [the longest x10 20.9 us: hyper_all_to_all(): got = lax.ppermute(jnp.stack([h[2] for h in send]), AXES, pairs_for(bit))]
    ppermute x4, waiting for transfers between devices: 22.8 us -> 16.4 us  [per_device(): parts.append(lax.ppermute(cols, AXES, pairs))]
    dot_general x2, matrix products: 2.93 us -> 0.71 us  [layer(): jnp.dot(hidden_full, down_full, preferred_element_type=jnp.float32)]
  transfers between devices with their start and end apart: 25 -> 18, of which waited for: 9 -> 10; matrix products, arithmetic and copies ran while one was open for 3% -> 3% of each run, Pallas kernels for 0% -> 0%
where the time goes in v5:
time: 117 us; the launch traced here: 116 us
  waiting for transfers between devices  64.9 us (55%)
  starting transfers between devices  34.7 us (30%)
  matrix products  6.26 us (5%)
  local copies, waits for them, and re-layouts  6.25 us (5%)
  other arithmetic  3.48 us (3%)
    ppermute x10, waiting for transfers between devices, hyper_all_to_all(): got = lax.ppermute(jnp.stack([h[2] for h in send]), AXES, pairs_for(bit))  43.8 us
    ppermute x10, starting transfers between devices, hyper_all_to_all(): got = lax.ppermute(jnp.stack([h[2] for h in send]), AXES, pairs_for(bit))  20.9 us
    ppermute x4, waiting for transfers between devices, per_device(): parts.append(lax.ppermute(cols, AXES, pairs))  16.4 us
    ppermute x4, starting transfers between devices, hyper_all_gather(): got = lax.ppermute(jnp.stack([h[1] for h in held]), AXES, pairs_for(bit))  8.6 us
    ppermute x4, starting transfers between devices, per_device(): parts.append(lax.ppermute(cols, AXES, pairs))  5.17 us
    ppermute x4, waiting for transfers between devices, hyper_all_gather(): got = lax.ppermute(jnp.stack([h[1] for h in held]), AXES, pairs_for(bit))  4.78 us
  transfers between devices with their start and end apart: 18, of which 10 were waited for; matrix products, arithmetic and copies ran while one was open for 3% of the time, Pallas kernels for 0%

profile of v5, /device:TPU:1, one launch (start us, length us, event | category | flops | bytes accessed | tf_op | source)
XLA Modules:
  0.0 116.3 jit_solution(9846073522490023476)
XLA Ops:
  3.7 1.4 %convolution_convert_fusion.1 = bf16[2,64,3072]{2,1,0:T(8,128)(2,1)S(1)} fusion(bf16[2,24,3072]{2,1,0:T(8,128)(2,1)} %param.6, bf16[1,64,24]{1,2,0:T(8,128)(2,1)S(1)} %bitcast.196, bf16[1,64,24]{1,2,0:T(8,128)(2,1)S(1)} %bitcast.198), kind=kOutput, calls=%fused_computation.2 | convolution fusion | flops 19270656 | bytes 1087488 | tf_op jit(solution)/shard_map/mrt,mtd->mrd/dot_general | solution.py:125
  7.2 2.2 %collective-permute-start.4 = (bf16[2,176,768]{2,1,0:T(8,128)(2,1)S(1)}, bf16[2,176,768]{2,1,0:T(8,128)(2,1)S(1)}, u32[]{:S(2)}, u32[]{:S(2)}) collective-permute-start(bf16[2,176,768]{2,1,0:T(8,128)(2,1)S(1)} %pad_maximum_fusion.3), channel_id=1, source_target_pairs={{0,8},{1,9},{2,10},{3,11},{4,12},{5,13},{6,14},{7,15},{8,0},{9,1},... | collective-permute-start | bytes 1622024 | tf_op jit(solution)/shard_map/ppermute | solution.py:33
  10.2 8.2 %collective-permute-done.4 = bf16[2,176,768]{2,1,0:T(8,128)(2,1)S(1)} collective-permute-done((bf16[2,176,768]{2,1,0:T(8,128)(2,1)S(1)}, bf16[2,176,768]{2,1,0:T(8,128)(2,1)S(1)}, u32[]{:S(2)}, u32[]{:S(2)}) %collective-permute-start.4) | collective-permute-done | bytes 540704 | tf_op jit(solution)/shard_map/ppermute | solution.py:33
  19.2 0.9 pad_maximum_fusion.4
  20.0 2.6 %collective-permute-start.5 = (bf16[2,176,768]{2,1,0:T(8,128)(2,1)}, bf16[2,176,768]{2,1,0:T(8,128)(2,1)S(1)}, u32[]{:S(2)}, u32[]{:S(2)}) collective-permute-start(bf16[2,176,768]{2,1,0:T(8,128)(2,1)} %pad_maximum_fusion.4), channel_id=1, source_target_pairs={{0,16},{1,17},{2,18},{3,19},{4,20},{5,21},{6,22},{7,23},{8,24},{9,... | collective-permute-start | bytes 1622024 | tf_op jit(solution)/shard_map/ppermute | solution.py:33
  26.2 20.8 %collective-permute-done.5 = bf16[2,176,768]{2,1,0:T(8,128)(2,1)S(1)} collective-permute-done((bf16[2,176,768]{2,1,0:T(8,128)(2,1)}, bf16[2,176,768]{2,1,0:T(8,128)(2,1)S(1)}, u32[]{:S(2)}, u32[]{:S(2)}) %collective-permute-start.5) | collective-permute-done | bytes 540704 | tf_op jit(solution)/shard_map/ppermute | solution.py:33
  49.4 1.1 fusion
  50.5 1.3 %collective-permute-start.11 = (bf16[2,24,768]{2,1,0:T(8,128)(2,1)S(1)}, bf16[2,24,768]{2,1,0:T(8,128)(2,1)S(1)}, u32[]{:S(2)}, u32[]{:S(2)}) collective-permute-start(bf16[2,24,768]{2,1,0:T(8,128)(2,1)S(1)} %fusion), channel_id=1, source_target_pairs={{0,28},{1,29},{2,30},{3,31},{8,20},{9,21},{10,22},{11,23},{16,12},... | collective-permute-start | bytes 221192 | tf_op jit(solution)/shard_map/ppermute | solution.py:179
  51.8 1.3 %collective-permute-start.10 = (bf16[2,24,768]{2,1,0:T(8,128)(2,1)S(1)}, bf16[2,24,768]{2,1,0:T(8,128)(2,1)S(1)}, u32[]{:S(2)}, u32[]{:S(2)}) collective-permute-start(bf16[2,24,768]{2,1,0:T(8,128)(2,1)S(1)} %fusion), channel_id=1, source_target_pairs={{0,20},{1,21},{2,22},{3,23},{8,28},{9,29},{10,30},{11,31},{16,4},{... | collective-permute-start | bytes 221192 | tf_op jit(solution)/shard_map/ppermute | solution.py:179
  53.1 1.3 %collective-permute-start.9 = (bf16[2,24,768]{2,1,0:T(8,128)(2,1)S(1)}, bf16[2,24,768]{2,1,0:T(8,128)(2,1)S(1)}, u32[]{:S(2)}, u32[]{:S(2)}) collective-permute-start(bf16[2,24,768]{2,1,0:T(8,128)(2,1)S(1)} %fusion), channel_id=1, source_target_pairs={{0,12},{1,13},{2,14},{3,15},{8,4},{9,5},{10,6},{11,7},{16,28},{17,... | collective-permute-start | bytes 221192 | tf_op jit(solution)/shard_map/ppermute | solution.py:179
  54.4 1.3 %collective-permute-start.8 = (bf16[2,24,768]{2,1,0:T(8,128)(2,1)S(1)}, bf16[2,24,768]{2,1,0:T(8,128)(2,1)S(1)}, u32[]{:S(2)}, u32[]{:S(2)}) collective-permute-start(bf16[2,24,768]{2,1,0:T(8,128)(2,1)S(1)} %fusion), channel_id=1, source_target_pairs={{0,4},{1,5},{2,6},{3,7},{8,12},{9,13},{10,14},{11,15},{16,20},{17,... | collective-permute-start | bytes 221192 | tf_op jit(solution)/shard_map/ppermute | solution.py:179
  55.8 15.9 %collective-permute-done.11 = bf16[2,24,768]{2,1,0:T(8,128)(2,1)S(1)} collective-permute-done((bf16[2,24,768]{2,1,0:T(8,128)(2,1)S(1)}, bf16[2,24,768]{2,1,0:T(8,128)(2,1)S(1)}, u32[]{:S(2)}, u32[]{:S(2)}) %collective-permute-start.11) | collective-permute-done | bytes 73760 | tf_op jit(solution)/shard_map/ppermute | solution.py:179
  73.5 3.6 %collective-permute-start.12 = (bf16[2,2,16,3072]{3,2,1,0:T(8,128)(2,1)S(1)}, bf16[2,2,16,3072]{3,2,1,0:T(8,128)(2,1)S(1)}, u32[]{:S(2)}, u32[]{:S(2)}) collective-permute-start(bf16[2,2,16,3072]{3,2,1,0:T(8,128)(2,1)S(1)} %pad_maximum_fusion.7), channel_id=1, source_target_pairs={{4,5},{5,4},{6,7},{7,6},{12,13},{13,12},{14,15},{15,14},{20,21},{2... | collective-permute-start | bytes 1179656 | tf_op jit(solution)/shard_map/ppermute | solution.py:33
  77.1 5.2 %collective-permute-done.12 = bf16[2,2,16,3072]{3,2,1,0:T(8,128)(2,1)S(1)} collective-permute-done((bf16[2,2,16,3072]{3,2,1,0:T(8,128)(2,1)S(1)}, bf16[2,2,16,3072]{3,2,1,0:T(8,128)(2,1)S(1)}, u32[]{:S(2)}, u32[]{:S(2)}) %collective-permute-start.12) | collective-permute-done | bytes 393248 | tf_op jit(solution)/shard_map/ppermute | solution.py:33
  82.4 3.1 %collective-permute-start.13 = (bf16[2,2,16,3072]{3,2,1,0:T(8,128)(2,1)S(1)}, bf16[2,2,16,3072]{3,2,1,0:T(8,128)(2,1)S(1)}, u32[]{:S(2)}, u32[]{:S(2)}) collective-permute-start(bf16[2,2,16,3072]{3,2,1,0:T(8,128)(2,1)S(1)} %pad_maximum_fusion.8), channel_id=1, source_target_pairs={{4,6},{5,7},{6,4},{7,5},{12,14},{13,15},{14,12},{15,13},{20,22},{2... | collective-permute-start | bytes 1179656 | tf_op jit(solution)/shard_map/ppermute | solution.py:33
  85.5 5.4 %collective-permute-done.13 = bf16[2,2,16,3072]{3,2,1,0:T(8,128)(2,1)S(1)} collective-permute-done((bf16[2,2,16,3072]{3,2,1,0:T(8,128)(2,1)S(1)}, bf16[2,2,16,3072]{3,2,1,0:T(8,128)(2,1)S(1)}, u32[]{:S(2)}, u32[]{:S(2)}) %collective-permute-start.13) | collective-permute-done | bytes 393248 | tf_op jit(solution)/shard_map/ppermute | solution.py:33
  92.2 2.9 %collective-permute-start.14 = (bf16[1,128,176]{1,2,0:T(8,128)(2,1)S(1)}, bf16[1,128,176]{1,2,0:T(8,128)(2,1)S(1)}, u32[]{:S(2)}, u32[]{:S(2)}) collective-permute-start(bf16[1,128,176]{1,2,0:T(8,128)(2,1)S(1)} %bitcast.186), channel_id=1, source_target_pairs={{4,12},{5,13},{6,14},{7,15},{12,4},{13,5},{14,6},{15,7},{20,28},{2... | collective-permute-start | bytes 135176 | tf_op jit(solution)/shard_map/ppermute | solution.py:46
  95.1 1.9 %collective-permute-done.14 = bf16[1,128,176]{1,2,0:T(8,128)(2,1)S(1)} collective-permute-done((bf16[1,128,176]{1,2,0:T(8,128)(2,1)S(1)}, bf16[1,128,176]{1,2,0:T(8,128)(2,1)S(1)}, u32[]{:S(2)}, u32[]{:S(2)}) %collective-permute-start.14) | collective-permute-done | bytes 45088 | tf_op jit(solution)/shard_map/ppermute | solution.py:46
  97.0 4.2 %collective-permute-start.15 = (bf16[2,128,176]{1,2,0:T(8,128)(2,1)S(1)}, bf16[2,128,176]{1,2,0:T(8,128)(2,1)S(1)}, u32[]{:S(2)}, u32[]{:S(2)}) collective-permute-start(bf16[2,128,176]{1,2,0:T(8,128)(2,1)S(1)} %pad_maximum_fusion.19), channel_id=1, source_target_pairs={{4,20},{5,21},{6,22},{7,23},{12,28},{13,29},{14,30},{15,31},{20,4}... | collective-permute-start | bytes 270344 | tf_op jit(solution)/shard_map/ppermute | solution.py:46
  101.2 2.9 %collective-permute-done.15 = bf16[2,128,176]{1,2,0:T(8,128)(2,1)S(1)} collective-permute-done((bf16[2,128,176]{1,2,0:T(8,128)(2,1)S(1)}, bf16[2,128,176]{1,2,0:T(8,128)(2,1)S(1)}, u32[]{:S(2)}, u32[]{:S(2)}) %collective-permute-start.15) | collective-permute-done | bytes 90144 | tf_op jit(solution)/shard_map/ppermute | solution.py:46
  104.6 3.4 %collective-permute-start.16 = (bf16[2,2,16,768]{3,2,1,0:T(8,128)(2,1)S(1)}, bf16[2,2,16,768]{3,2,1,0:T(8,128)(2,1)S(1)}, u32[]{:S(2)}, u32[]{:S(2)}) collective-permute-start(bf16[2,2,16,768]{3,2,1,0:T(8,128)(2,1)S(1)} %pad_maximum_fusion.16), channel_id=1, source_target_pairs={{4,5},{5,4},{6,7},{7,6},{12,13},{13,12},{14,15},{15,14},{20,21},{2... | collective-permute-start | bytes 294920 | tf_op jit(solution)/shard_map/ppermute | solution.py:33
  108.0 2.0 %collective-permute-done.16 = bf16[2,2,16,768]{3,2,1,0:T(8,128)(2,1)S(1)} collective-permute-done((bf16[2,2,16,768]{3,2,1,0:T(8,128)(2,1)S(1)}, bf16[2,2,16,768]{3,2,1,0:T(8,128)(2,1)S(1)}, u32[]{:S(2)}, u32[]{:S(2)}) %collective-permute-start.16) | collective-permute-done | bytes 98336 | tf_op jit(solution)/shard_map/ppermute | solution.py:33
  110.0 3.1 %collective-permute-start.17 = (bf16[2,2,16,768]{3,2,1,0:T(8,128)(2,1)S(1)}, bf16[2,2,16,768]{3,2,1,0:T(8,128)(2,1)S(1)}, u32[]{:S(2)}, u32[]{:S(2)}) collective-permute-start(bf16[2,2,16,768]{3,2,1,0:T(8,128)(2,1)S(1)} %pad_maximum_fusion.17), channel_id=1, source_target_pairs={{4,6},{5,7},{6,4},{7,5},{12,14},{13,15},{14,12},{15,13},{20,22},{2... | collective-permute-start | bytes 294920 | tf_op jit(solution)/shard_map/ppermute | solution.py:33
  113.1 2.2 %collective-permute-done.17 = bf16[2,2,16,768]{3,2,1,0:T(8,128)(2,1)S(1)} collective-permute-done((bf16[2,2,16,768]{3,2,1,0:T(8,128)(2,1)S(1)}, bf16[2,2,16,768]{3,2,1,0:T(8,128)(2,1)S(1)}, u32[]{:S(2)}, u32[]{:S(2)}) %collective-permute-start.17) | collective-permute-done | bytes 98336 | tf_op jit(solution)/shard_map/ppermute | solution.py:33
  (108 shorter events, 17.4 us)
Async XLA Ops:
  0.0 23.0 %copy-start = (bf16[1,1,3072,176]{2,3,1,0:T(8,128)(2,1)S(1)}, bf16[1,1,3072,176]{2,3,1,0:T(8,128)(2,1)}, u32[]{:S(2)}) copy-start(bf16[1,1,3072,176]{2,3,1,0:T(8,128)(2,1)} %param.9) | copy-start | bytes 3244036
  5.2 4.2 %collective-permute-start = (bf16[2,2,16,3072]{3,2,1,0:T(8,128)(2,1)S(1)}, bf16[2,2,16,3072]{3,2,1,0:T(8,128)(2,1)S(1)}, u32[]{:S(2)}, u32[]{:S(2)}) collective-permute-start(bf16[2,2,16,3072]{3,2,1,0:T(8,128)(2,1)S(1)} %pad_maximum_fusion.5), channel_id=1, source_target_pairs={{0,1},{1,0},{2,3},{3,2},{8,9},{9,8},{10,11},{11,10},{16,17},{17,16... | collective-permute-start | bytes 1179656 | tf_op jit(solution)/shard_map/ppermute | solution.py:33
  7.2 11.2 %collective-permute-start.4 = (bf16[2,176,768]{2,1,0:T(8,128)(2,1)S(1)}, bf16[2,176,768]{2,1,0:T(8,128)(2,1)S(1)}, u32[]{:S(2)}, u32[]{:S(2)}) collective-permute-start(bf16[2,176,768]{2,1,0:T(8,128)(2,1)S(1)} %pad_maximum_fusion.3), channel_id=1, source_target_pairs={{0,8},{1,9},{2,10},{3,11},{4,12},{5,13},{6,14},{7,15},{8,0},{9,1},... | collective-permute-start | bytes 1622024 | tf_op jit(solution)/shard_map/ppermute | solution.py:33
  9.5 13.1 %collective-permute-start.1 = (bf16[2,2,16,3072]{3,2,1,0:T(8,128)(2,1)S(1)}, bf16[2,2,16,3072]{3,2,1,0:T(8,128)(2,1)S(1)}, u32[]{:S(2)}, u32[]{:S(2)}) collective-permute-start(bf16[2,2,16,3072]{3,2,1,0:T(8,128)(2,1)S(1)} %pad_maximum_fusion.6), channel_id=1, source_target_pairs={{0,2},{1,3},{2,0},{3,1},{8,10},{9,11},{10,8},{11,9},{16,18},{17,19... | collective-permute-start | bytes 1179656 | tf_op jit(solution)/shard_map/ppermute | solution.py:33
  20.0 26.9 %collective-permute-start.5 = (bf16[2,176,768]{2,1,0:T(8,128)(2,1)}, bf16[2,176,768]{2,1,0:T(8,128)(2,1)S(1)}, u32[]{:S(2)}, u32[]{:S(2)}) collective-permute-start(bf16[2,176,768]{2,1,0:T(8,128)(2,1)} %pad_maximum_fusion.4), channel_id=1, source_target_pairs={{0,16},{1,17},{2,18},{3,19},{4,20},{5,21},{6,22},{7,23},{8,24},{9,... | collective-permute-start | bytes 1622024 | tf_op jit(solution)/shard_map/ppermute | solution.py:33
  24.6 22.4 %copy-start.3 = (bf16[176,768]{1,0:T(8,128)(2,1)S(1)}, bf16[176,768]{1,0:T(8,128)(2,1)}, u32[]{:S(2)}) copy-start(bf16[176,768]{1,0:T(8,128)(2,1)} %get-tuple-element.13) | copy-start | bytes 811012
  24.6 22.4 %copy-start.5 = (bf16[176,768]{1,0:T(8,128)(2,1)S(1)}, bf16[176,768]{1,0:T(8,128)(2,1)}, u32[]{:S(2)}) copy-start(bf16[176,768]{1,0:T(8,128)(2,1)} %get-tuple-element.25) | copy-start | bytes 811012
  24.6 0.8 collective-permute-start.2
  25.5 0.7 collective-permute-start.3
  47.9 0.8 collective-permute-start.6
  48.7 0.7 collective-permute-start.7
  50.5 21.2 %collective-permute-start.11 = (bf16[2,24,768]{2,1,0:T(8,128)(2,1)S(1)}, bf16[2,24,768]{2,1,0:T(8,128)(2,1)S(1)}, u32[]{:S(2)}, u32[]{:S(2)}) collective-permute-start(bf16[2,24,768]{2,1,0:T(8,128)(2,1)S(1)} %fusion), channel_id=1, source_target_pairs={{0,28},{1,29},{2,30},{3,31},{8,20},{9,21},{10,22},{11,23},{16,12},... | collective-permute-start | bytes 221192 | tf_op jit(solution)/shard_map/ppermute | solution.py:179
  51.8 19.9 %collective-permute-start.10 = (bf16[2,24,768]{2,1,0:T(8,128)(2,1)S(1)}, bf16[2,24,768]{2,1,0:T(8,128)(2,1)S(1)}, u32[]{:S(2)}, u32[]{:S(2)}) collective-permute-start(bf16[2,24,768]{2,1,0:T(8,128)(2,1)S(1)} %fusion), channel_id=1, source_target_pairs={{0,20},{1,21},{2,22},{3,23},{8,28},{9,29},{10,30},{11,31},{16,4},{... | collective-permute-start | bytes 221192 | tf_op jit(solution)/shard_map/ppermute | solution.py:179
  53.1 19.1 %collective-permute-start.9 = (bf16[2,24,768]{2,1,0:T(8,128)(2,1)S(1)}, bf16[2,24,768]{2,1,0:T(8,128)(2,1)S(1)}, u32[]{:S(2)}, u32[]{:S(2)}) collective-permute-start(bf16[2,24,768]{2,1,0:T(8,128)(2,1)S(1)} %fusion), channel_id=1, source_target_pairs={{0,12},{1,13},{2,14},{3,15},{8,4},{9,5},{10,6},{11,7},{16,28},{17,... | collective-permute-start | bytes 221192 | tf_op jit(solution)/shard_map/ppermute | solution.py:179
  54.4 17.8 %collective-permute-start.8 = (bf16[2,24,768]{2,1,0:T(8,128)(2,1)S(1)}, bf16[2,24,768]{2,1,0:T(8,128)(2,1)S(1)}, u32[]{:S(2)}, u32[]{:S(2)}) collective-permute-start(bf16[2,24,768]{2,1,0:T(8,128)(2,1)S(1)} %fusion), channel_id=1, source_target_pairs={{0,4},{1,5},{2,6},{3,7},{8,12},{9,13},{10,14},{11,15},{16,20},{17,... | collective-permute-start | bytes 221192 | tf_op jit(solution)/shard_map/ppermute | solution.py:179
  73.5 8.8 %collective-permute-start.12 = (bf16[2,2,16,3072]{3,2,1,0:T(8,128)(2,1)S(1)}, bf16[2,2,16,3072]{3,2,1,0:T(8,128)(2,1)S(1)}, u32[]{:S(2)}, u32[]{:S(2)}) collective-permute-start(bf16[2,2,16,3072]{3,2,1,0:T(8,128)(2,1)S(1)} %pad_maximum_fusion.7), channel_id=1, source_target_pairs={{4,5},{5,4},{6,7},{7,6},{12,13},{13,12},{14,15},{15,14},{20,21},{2... | collective-permute-start | bytes 1179656 | tf_op jit(solution)/shard_map/ppermute | solution.py:33
  82.4 8.5 %collective-permute-start.13 = (bf16[2,2,16,3072]{3,2,1,0:T(8,128)(2,1)S(1)}, bf16[2,2,16,3072]{3,2,1,0:T(8,128)(2,1)S(1)}, u32[]{:S(2)}, u32[]{:S(2)}) collective-permute-start(bf16[2,2,16,3072]{3,2,1,0:T(8,128)(2,1)S(1)} %pad_maximum_fusion.8), channel_id=1, source_target_pairs={{4,6},{5,7},{6,4},{7,5},{12,14},{13,15},{14,12},{15,13},{20,22},{2... | collective-permute-start | bytes 1179656 | tf_op jit(solution)/shard_map/ppermute | solution.py:33
  91.7 12.4 %copy-start.4 = (bf16[176,768]{1,0:T(8,128)(2,1)S(1)}, bf16[176,768]{1,0:T(8,128)(2,1)}, u32[]{:S(2)}) copy-start(bf16[176,768]{1,0:T(8,128)(2,1)} %get-tuple-element.13) | copy-start | bytes 811012
  91.7 12.4 %copy-start.6 = (bf16[176,768]{1,0:T(8,128)(2,1)S(1)}, bf16[176,768]{1,0:T(8,128)(2,1)}, u32[]{:S(2)}) copy-start(bf16[176,768]{1,0:T(8,128)(2,1)} %get-tuple-element.25) | copy-start | bytes 811012
  91.7 12.4 %copy-start.8 = (bf16[176,768]{1,0:T(8,128)(2,1)S(1)}, bf16[176,768]{1,0:T(8,128)(2,1)}, u32[]{:S(2)}) copy-start(bf16[176,768]{1,0:T(8,128)(2,1)} %copy-done.7) | copy-start | bytes 811012
  92.2 4.8 %collective-permute-start.14 = (bf16[1,128,176]{1,2,0:T(8,128)(2,1)S(1)}, bf16[1,128,176]{1,2,0:T(8,128)(2,1)S(1)}, u32[]{:S(2)}, u32[]{:S(2)}) collective-permute-start(bf16[1,128,176]{1,2,0:T(8,128)(2,1)S(1)} %bitcast.186), channel_id=1, source_target_pairs={{4,12},{5,13},{6,14},{7,15},{12,4},{13,5},{14,6},{15,7},{20,28},{2... | collective-permute-start | bytes 135176 | tf_op jit(solution)/shard_map/ppermute | solution.py:46
  97.0 7.1 %collective-permute-start.15 = (bf16[2,128,176]{1,2,0:T(8,128)(2,1)S(1)}, bf16[2,128,176]{1,2,0:T(8,128)(2,1)S(1)}, u32[]{:S(2)}, u32[]{:S(2)}) collective-permute-start(bf16[2,128,176]{1,2,0:T(8,128)(2,1)S(1)} %pad_maximum_fusion.19), channel_id=1, source_target_pairs={{4,20},{5,21},{6,22},{7,23},{12,28},{13,29},{14,30},{15,31},{20,4}... | collective-permute-start | bytes 270344 | tf_op jit(solution)/shard_map/ppermute | solution.py:46
  104.6 5.4 %collective-permute-start.16 = (bf16[2,2,16,768]{3,2,1,0:T(8,128)(2,1)S(1)}, bf16[2,2,16,768]{3,2,1,0:T(8,128)(2,1)S(1)}, u32[]{:S(2)}, u32[]{:S(2)}) collective-permute-start(bf16[2,2,16,768]{3,2,1,0:T(8,128)(2,1)S(1)} %pad_maximum_fusion.16), channel_id=1, source_target_pairs={{4,5},{5,4},{6,7},{7,6},{12,13},{13,12},{14,15},{15,14},{20,21},{2... | collective-permute-start | bytes 294920 | tf_op jit(solution)/shard_map/ppermute | solution.py:33
  110.0 5.4 %collective-permute-start.17 = (bf16[2,2,16,768]{3,2,1,0:T(8,128)(2,1)S(1)}, bf16[2,2,16,768]{3,2,1,0:T(8,128)(2,1)S(1)}, u32[]{:S(2)}, u32[]{:S(2)}) collective-permute-start(bf16[2,2,16,768]{3,2,1,0:T(8,128)(2,1)S(1)} %pad_maximum_fusion.17), channel_id=1, source_target_pairs={{4,6},{5,7},{6,4},{7,5},{12,14},{13,15},{14,12},{15,13},{20,22},{2... | collective-permute-start | bytes 294920 | tf_op jit(solution)/shard_map/ppermute | solution.py:33
  (5 other events, 16.4 us)

commit v6 on v1

--- a/solution.py
+++ b/solution.py
@@ -64,6 +64,19 @@
     def dp_pairs(p, s):
         return [(lin(d, p, e), lin(dring.ahead(d, s), p, e)) for d in range(n_dp) for e in range(n_exp)]
 
+    relays = n_pipe == 2
+
+    def relayed(chunks, p, target):
+        q = 1 - p
+        got = []
+        for s in range(1, len(chunks) + 1):
+            pairs = [(lin(d, p, e), lin(*target(d, e, s)[:1], q, *target(d, e, s)[1:])) for d in range(n_dp) for e in range(n_exp)]
+            got.append(lax.ppermute(chunks[s - 1], AXES, pairs))
+        handed = lax.ppermute(
+            jnp.stack(got), AXES, [(lin(d, q, e), lin(d, p, e)) for d in range(n_dp) for e in range(n_exp)]
+        )
+        return [handed[i] for i in range(len(chunks))]
+
     gate_local = w_gate[0, 0]
     up_local = w_up[0, 0]
     down_local = w_down[0, 0]
@@ -88,16 +101,24 @@
     def layer(current, p):
         outgoing = jnp.einsum("mrt,mtd->mrd", dispatch_map, current, preferred_element_type=jnp.float32)
         outgoing = outgoing.astype(jnp.bfloat16).reshape(micro, n_exp, CAP, width)
-        arrived = [outgoing[:, 0]]
-        for s in range(1, n_exp):
-            arrived.append(lax.ppermute(outgoing[:, s], AXES, expert_pairs(p, s, False)))
+        if relays and ering.xor:
+            arrived = [outgoing[:, 0]] + relayed(
+                [outgoing[:, s] for s in range(1, n_exp)], p, lambda d, e, s: (d, ering.ahead(e, s))
+            )
+        else:
+            arrived = [outgoing[:, 0]]
+            for s in range(1, n_exp):
+                arrived.append(lax.ppermute(outgoing[:, s], AXES, expert_pairs(p, s, False)))
         flat_rows = jnp.stack(arrived, axis=1).reshape(-1, width)
         squares = jnp.mean(jnp.square(flat_rows.astype(jnp.float32)), axis=1, keepdims=True)
         inv_rms = lax.rsqrt(squares + 1e-05)
         gate_act = jnp.dot(flat_rows, gate_local, preferred_element_type=jnp.float32) * inv_rms
         up_act = jnp.dot(flat_rows, up_local, preferred_element_type=jnp.float32) * inv_rms
         hidden = (jax.nn.silu(gate_act) * up_act).astype(jnp.bfloat16)
-        if small_dp:
+        if small_dp and relays and dring.xor:
+            parts = [hidden] + relayed([hidden] * (n_dp - 1), p, lambda d, e, s: (dring.ahead(d, s), e))
+            hidden_full = jnp.concatenate(parts, axis=1)
+        elif small_dp:
             parts = [hidden]
             for s in range(1, n_dp):
                 parts.append(lax.ppermute(hidden, AXES, dp_pairs(p, s)))
@@ -106,9 +127,14 @@
             hidden_full = lax.all_gather(hidden, "dp", axis=1, tiled=True)
         expert_out = jnp.dot(hidden_full, down_full, preferred_element_type=jnp.float32).astype(jnp.bfloat16)
         expert_out = expert_out.reshape(micro, n_exp, CAP, columns)
-        returned = [expert_out[:, 0]]
-        for s in range(1, n_exp):
-            returned.append(lax.ppermute(expert_out[:, s], AXES, expert_pairs(p, s, True)))
+        if relays and ering.xor:
+            returned = [expert_out[:, 0]] + relayed(
+                [expert_out[:, s] for s in range(1, n_exp)], p, lambda d, e, s: (d, ering.behind(e, s))
+            )
+        else:
+            returned = [expert_out[:, 0]]
+            for s in range(1, n_exp):
+                returned.append(lax.ppermute(expert_out[:, s], AXES, expert_pairs(p, s, True)))
         returned = jnp.stack(returned, axis=1).reshape(micro, rows_all, columns)
         mixed = jnp.einsum(
             "mrt,mrc->mtc",

time: 109 us -> 124 us (1.14)
  waiting for transfers between devices: 48 us -> 63.7 us
  starting transfers between devices: 42.3 us -> 44.8 us
  matrix products: 8.48 us -> 6.25 us
    ppermute x18 -> x24, waiting for transfers between devices: 8.28 us -> 35.6 us  [the longest x18 24.7 us: relayed(): got.append(lax.ppermute(chunks[s - 1], AXES, pairs))]
    ppermute x4, waiting for transfers between devices: 22.8 us -> 3.77 us  [per_device(): parts.append(lax.ppermute(cols, AXES, pairs))]
    ppermute x3, waiting for transfers between devices: 17 us -> 24.3 us  [per_device(): lax.ppermute(piece, 'dp', [(i, dring.ahead(i, s)) for i in range(n_dp)])]
    ppermute x18 -> x24, starting transfers between devices: 32.7 us -> 36.9 us  [the longest x18 28.7 us: relayed(): got.append(lax.ppermute(chunks[s - 1], AXES, pairs))]
    dot_general x2, matrix products: 2.93 us -> 0.71 us  [layer(): jnp.dot(hidden_full, down_full, preferred_element_type=jnp.float32)]
    ppermute x3, starting transfers between devices: 4.44 us -> 2.71 us  [per_device(): lax.ppermute(piece, 'dp', [(i, dring.ahead(i, s)) for i in range(n_dp)])]
  transfers between devices with their start and end apart: 25 -> 31, of which waited for: 9 -> 23; matrix products, arithmetic and copies ran while one was open for 3% -> 1% of each run, Pallas kernels for 0% -> 0%
where the time goes in v6:
time: 124 us; the launch traced here: 123 us
  waiting for transfers between devices  63.7 us (51%)
  starting transfers between devices  44.8 us (36%)
  matrix products  6.25 us (5%)
  local copies, waits for them, and re-layouts  5.57 us (4%)
  other arithmetic  2.53 us (2%)
    ppermute x18, starting transfers between devices, relayed(): got.append(lax.ppermute(chunks[s - 1], AXES, pairs))  28.7 us
    ppermute x18, waiting for transfers between devices, relayed(): got.append(lax.ppermute(chunks[s - 1], AXES, pairs))  24.7 us
    ppermute x3, waiting for transfers between devices, per_device(): lax.ppermute(piece, 'dp', [(i, dring.ahead(i, s)) for i in range(n_dp)])  24.3 us
    ppermute x6, waiting for transfers between devices, relayed(): lax.ppermute(jnp.stack(got), AXES, [(lin(d, q, e), lin(d, p, e)) for d in...  10.9 us
    ppermute x6, starting transfers between devices, relayed(): lax.ppermute(jnp.stack(got), AXES, [(lin(d, q, e), lin(d, p, e)) for d in...  8.23 us
    ppermute x4, starting transfers between devices, per_device(): parts.append(lax.ppermute(cols, AXES, pairs))  5.17 us
    ppermute x4, waiting for transfers between devices, per_device(): parts.append(lax.ppermute(cols, AXES, pairs))  3.77 us
    ppermute x3, starting transfers between devices, per_device(): lax.ppermute(piece, 'dp', [(i, dring.ahead(i, s)) for i in range(n_dp)])  2.71 us
  transfers between devices with their start and end apart: 31, of which 23 were waited for; matrix products, arithmetic and copies ran while one was open for 1% of the time, Pallas kernels for 0%

profile of v6, /device:TPU:1, one launch (start us, length us, event | category | flops | bytes accessed | tf_op | source)
XLA Modules:
  0.0 123.5 jit_solution(433867827403428068)
XLA Ops:
  3.7 1.4 %convolution_convert_fusion.1 = bf16[2,64,3072]{2,1,0:T(8,128)(2,1)S(1)} fusion(bf16[2,24,3072]{2,1,0:T(8,128)(2,1)} %param.6, bf16[1,64,24]{1,2,0:T(8,128)(2,1)S(1)} %bitcast.210, bf16[1,64,24]{1,2,0:T(8,128)(2,1)S(1)} %bitcast.212), kind=kOutput, calls=%fused_computation.2 | convolution fusion | flops 19270656 | bytes 1087488 | tf_op jit(solution)/shard_map/mrt,mtd->mrd/dot_general | solution.py:102
  9.1 3.4 %collective-permute-done.1 = bf16[2,16,3072]{2,1,0:T(8,128)(2,1)S(1)} collective-permute-done((bf16[2,16,3072]{2,1,0:T(8,128)(2,1)S(1)}, bf16[2,16,3072]{2,1,0:T(8,128)(2,1)S(1)}, u32[]{:S(2)}, u32[]{:S(2)}) %collective-permute-start.1) | collective-permute-done | bytes 196640 | tf_op jit(solution)/shard_map/ppermute | solution.py:74
  12.4 2.9 %collective-permute-done = bf16[2,16,3072]{2,1,0:T(8,128)(2,1)S(1)} collective-permute-done((bf16[2,16,3072]{2,1,0:T(8,128)(2,1)S(1)}, bf16[2,16,3072]{2,1,0:T(8,128)(2,1)S(1)}, u32[]{:S(2)}, u32[]{:S(2)}) %collective-permute-start) | collective-permute-done | bytes 196640 | tf_op jit(solution)/shard_map/ppermute | solution.py:74
  15.3 2.1 %collective-permute-done.2 = bf16[2,16,3072]{2,1,0:T(8,128)(2,1)S(1)} collective-permute-done((bf16[2,16,3072]{2,1,0:T(8,128)(2,1)S(1)}, bf16[2,16,3072]{2,1,0:T(8,128)(2,1)S(1)}, u32[]{:S(2)}, u32[]{:S(2)}) %collective-permute-start.2) | collective-permute-done | bytes 196640 | tf_op jit(solution)/shard_map/ppermute | solution.py:74
  17.4 1.3 %collective-permute-start.3 = (bf16[3,2,16,3072]{3,2,1,0:T(8,128)(2,1)S(1)}, bf16[3,2,16,3072]{3,2,1,0:T(8,128)(2,1)S(1)}, u32[]{:S(2)}, u32[]{:S(2)}) collective-permute-start(bf16[3,2,16,3072]{3,2,1,0:T(8,128)(2,1)S(1)} %pad_maximum_fusion.3), channel_id=1, source_target_pairs={{4,0},{5,1},{6,2},{7,3},{12,8},{13,9},{14,10},{15,11},{20,16},{21,... | collective-permute-start | bytes 1769480 | tf_op jit(solution)/shard_map/ppermute | solution.py:75
  18.8 1.6 %collective-permute-done.3 = bf16[3,2,16,3072]{3,2,1,0:T(8,128)(2,1)S(1)} collective-permute-done((bf16[3,2,16,3072]{3,2,1,0:T(8,128)(2,1)S(1)}, bf16[3,2,16,3072]{3,2,1,0:T(8,128)(2,1)S(1)}, u32[]{:S(2)}, u32[]{:S(2)}) %collective-permute-start.3) | collective-permute-done | bytes 589856 | tf_op jit(solution)/shard_map/ppermute | solution.py:75
  26.2 3.2 %collective-permute-done.6 = bf16[128,176]{0,1:T(8,128)(2,1)S(1)} collective-permute-done((bf16[128,176]{0,1:T(8,128)(2,1)S(1)}, bf16[128,176]{0,1:T(8,128)(2,1)S(1)}, u32[]{:S(2)}, u32[]{:S(2)}) %collective-permute-start.6) | collective-permute-done | bytes 45088 | tf_op jit(solution)/shard_map/ppermute | solution.py:74
  30.0 2.4 %collective-permute-done.4 = bf16[128,176]{0,1:T(8,128)(2,1)S(1)} collective-permute-done((bf16[128,176]{0,1:T(8,128)(2,1)S(1)}, bf16[128,176]{0,1:T(8,128)(2,1)S(1)}, u32[]{:S(2)}, u32[]{:S(2)}) %collective-permute-start.4) | collective-permute-done | bytes 45088 | tf_op jit(solution)/shard_map/ppermute | solution.py:74
  32.4 1.7 %collective-permute-start.7 = (bf16[3,128,176]{1,2,0:T(8,128)(2,1)S(1)}, bf16[3,128,176]{1,2,0:T(8,128)(2,1)S(1)}, u32[]{:S(2)}, u32[]{:S(2)}) collective-permute-start(bf16[3,128,176]{1,2,0:T(8,128)(2,1)S(1)} %pad_maximum_fusion.12), channel_id=1, source_target_pairs={{4,0},{5,1},{6,2},{7,3},{12,8},{13,9},{14,10},{15,11},{20,16},{21,... | collective-permute-start | bytes 405512 | tf_op jit(solution)/shard_map/ppermute | solution.py:75
  38.2 5.8 %collective-permute-done.8 = bf16[176,768]{1,0:T(8,128)(2,1)S(1)} collective-permute-done((bf16[176,768]{1,0:T(8,128)(2,1)S(1)}, bf16[176,768]{1,0:T(8,128)(2,1)S(1)}, u32[]{:S(2)}, u32[]{:S(2)}) %collective-permute-start.8) | collective-permute-done | bytes 270368 | tf_op jit(solution)/shard_map/ppermute | solution.py:89
  44.0 5.7 %collective-permute-done.10 = bf16[176,768]{1,0:T(8,128)(2,1)S(1)} collective-permute-done((bf16[176,768]{1,0:T(8,128)(2,1)S(1)}, bf16[176,768]{1,0:T(8,128)(2,1)S(1)}, u32[]{:S(2)}, u32[]{:S(2)}) %collective-permute-start.10) | collective-permute-done | bytes 270368 | tf_op jit(solution)/shard_map/ppermute | solution.py:89
  49.7 12.8 %collective-permute-done.9 = bf16[176,768]{1,0:T(8,128)(2,1)S(1)} collective-permute-done((bf16[176,768]{1,0:T(8,128)(2,1)S(1)}, bf16[176,768]{1,0:T(8,128)(2,1)S(1)}, u32[]{:S(2)}, u32[]{:S(2)}) %collective-permute-start.9) | collective-permute-done | bytes 270368 | tf_op jit(solution)/shard_map/ppermute | solution.py:89
  67.1 1.5 %collective-permute-done.11 = bf16[2,16,768]{2,1,0:T(8,128)(2,1)S(1)} collective-permute-done((bf16[2,16,768]{2,1,0:T(8,128)(2,1)S(1)}, bf16[2,16,768]{2,1,0:T(8,128)(2,1)S(1)}, u32[]{:S(2)}, u32[]{:S(2)}) %collective-permute-start.11) | collective-permute-done | bytes 49184 | tf_op jit(solution)/shard_map/ppermute | solution.py:74
  68.6 2.2 %collective-permute-done.13 = bf16[2,16,768]{2,1,0:T(8,128)(2,1)S(1)} collective-permute-done((bf16[2,16,768]{2,1,0:T(8,128)(2,1)S(1)}, bf16[2,16,768]{2,1,0:T(8,128)(2,1)S(1)}, u32[]{:S(2)}, u32[]{:S(2)}) %collective-permute-start.13) | collective-permute-done | bytes 49184 | tf_op jit(solution)/shard_map/ppermute | solution.py:74
  80.9 2.2 %collective-permute-done.18 = bf16[2,24,768]{2,1,0:T(8,128)(2,1)S(1)} collective-permute-done((bf16[2,24,768]{2,1,0:T(8,128)(2,1)S(1)}, bf16[2,24,768]{2,1,0:T(8,128)(2,1)S(1)}, u32[]{:S(2)}, u32[]{:S(2)}) %collective-permute-start.18) | collective-permute-done | bytes 73760 | tf_op jit(solution)/shard_map/ppermute | solution.py:161
  83.1 1.5 %collective-permute-done.17 = bf16[2,24,768]{2,1,0:T(8,128)(2,1)S(1)} collective-permute-done((bf16[2,24,768]{2,1,0:T(8,128)(2,1)S(1)}, bf16[2,24,768]{2,1,0:T(8,128)(2,1)S(1)}, u32[]{:S(2)}, u32[]{:S(2)}) %collective-permute-start.17) | collective-permute-done | bytes 73760 | tf_op jit(solution)/shard_map/ppermute | solution.py:161
  88.5 1.7 %collective-permute-start.21 = (bf16[2,16,3072]{2,1,0:T(8,128)(2,1)S(1)}, bf16[2,16,3072]{2,1,0:T(8,128)(2,1)S(1)}, u32[]{:S(2)}, u32[]{:S(2)}) collective-permute-start(bf16[2,16,3072]{2,1,0:T(8,128)(2,1)S(1)} %get-tuple-element.20), channel_id=1, source_target_pairs={{4,3},{5,2},{6,1},{7,0},{12,11},{13,10},{14,9},{15,8},{20,19},{21,... | collective-permute-start | bytes 589832 | tf_op jit(solution)/shard_map/ppermute | solution.py:74
  91.1 2.1 %collective-permute-done.21 = bf16[2,16,3072]{2,1,0:T(8,128)(2,1)S(1)} collective-permute-done((bf16[2,16,3072]{2,1,0:T(8,128)(2,1)S(1)}, bf16[2,16,3072]{2,1,0:T(8,128)(2,1)S(1)}, u32[]{:S(2)}, u32[]{:S(2)}) %collective-permute-start.21) | collective-permute-done | bytes 196640 | tf_op jit(solution)/shard_map/ppermute | solution.py:74
  94.6 3.8 %collective-permute-done.22 = bf16[3,2,16,3072]{3,2,1,0:T(8,128)(2,1)S(1)} collective-permute-done((bf16[3,2,16,3072]{3,2,1,0:T(8,128)(2,1)S(1)}, bf16[3,2,16,3072]{3,2,1,0:T(8,128)(2,1)S(1)}, u32[]{:S(2)}, u32[]{:S(2)}) %collective-permute-start.22) | collective-permute-done | bytes 589856 | tf_op jit(solution)/shard_map/ppermute | solution.py:75
  99.7 4.4 %collective-permute-start.25 = (bf16[128,176]{0,1:T(8,128)(2,1)S(1)}, bf16[128,176]{0,1:T(8,128)(2,1)S(1)}, u32[]{:S(2)}, u32[]{:S(2)}) collective-permute-start(bf16[128,176]{0,1:T(8,128)(2,1)S(1)} %fusion.7), channel_id=1, source_target_pairs={{4,24},{5,25},{6,26},{7,27},{12,16},{13,17},{14,18},{15,19},{20,8}... | collective-permute-start | bytes 135176 | tf_op jit(solution)/shard_map/ppermute | solution.py:74
  109.2 2.1 %collective-permute-done.26 = bf16[3,128,176]{1,2,0:T(8,128)(2,1)S(1)} collective-permute-done((bf16[3,128,176]{1,2,0:T(8,128)(2,1)S(1)}, bf16[3,128,176]{1,2,0:T(8,128)(2,1)S(1)}, u32[]{:S(2)}, u32[]{:S(2)}) %collective-permute-start.26) | collective-permute-done | bytes 135200 | tf_op jit(solution)/shard_map/ppermute | solution.py:75
  111.8 2.7 %collective-permute-start.27 = (bf16[2,16,768]{2,1,0:T(8,128)(2,1)S(1)}, bf16[2,16,768]{2,1,0:T(8,128)(2,1)S(1)}, u32[]{:S(2)}, u32[]{:S(2)}) collective-permute-start(bf16[2,16,768]{2,1,0:T(8,128)(2,1)S(1)} %get-tuple-element.32), channel_id=1, source_target_pairs={{4,1},{5,0},{6,3},{7,2},{12,9},{13,8},{14,11},{15,10},{20,17},{21,... | collective-permute-start | bytes 147464 | tf_op jit(solution)/shard_map/ppermute | solution.py:74
  114.5 1.7 %collective-permute-start.29 = (bf16[2,16,768]{2,1,0:T(8,128)(2,1)S(1)}, bf16[2,16,768]{2,1,0:T(8,128)(2,1)S(1)}, u32[]{:S(2)}, u32[]{:S(2)}) collective-permute-start(bf16[2,16,768]{2,1,0:T(8,128)(2,1)S(1)} %get-tuple-element.33), channel_id=1, source_target_pairs={{4,3},{5,2},{6,1},{7,0},{12,11},{13,10},{14,9},{15,8},{20,19},{21,... | collective-permute-start | bytes 147464 | tf_op jit(solution)/shard_map/ppermute | solution.py:74
  120.0 2.6 %collective-permute-done.30 = bf16[3,2,16,768]{3,2,1,0:T(8,128)(2,1)S(1)} collective-permute-done((bf16[3,2,16,768]{3,2,1,0:T(8,128)(2,1)S(1)}, bf16[3,2,16,768]{3,2,1,0:T(8,128)(2,1)S(1)}, u32[]{:S(2)}, u32[]{:S(2)}) %collective-permute-start.30) | collective-permute-done | bytes 147488 | tf_op jit(solution)/shard_map/ppermute | solution.py:75
  (120 shorter events, 50.0 us)
Async XLA Ops:
  5.2 7.3 %collective-permute-start.1 = (bf16[2,16,3072]{2,1,0:T(8,128)(2,1)S(1)}, bf16[2,16,3072]{2,1,0:T(8,128)(2,1)S(1)}, u32[]{:S(2)}, u32[]{:S(2)}) collective-permute-start(bf16[2,16,3072]{2,1,0:T(8,128)(2,1)S(1)} %get-tuple-element.22), channel_id=1, source_target_pairs={{0,6},{1,7},{2,4},{3,5},{8,14},{9,15},{10,12},{11,13},{16,22},{17,... | collective-permute-start | bytes 589832 | tf_op jit(solution)/shard_map/ppermute | solution.py:74
  6.5 8.8 %collective-permute-start = (bf16[2,16,3072]{2,1,0:T(8,128)(2,1)S(1)}, bf16[2,16,3072]{2,1,0:T(8,128)(2,1)S(1)}, u32[]{:S(2)}, u32[]{:S(2)}) collective-permute-start(bf16[2,16,3072]{2,1,0:T(8,128)(2,1)S(1)} %get-tuple-element.23), channel_id=1, source_target_pairs={{0,5},{1,4},{2,7},{3,6},{8,13},{9,12},{10,15},{11,14},{16,21},{17,... | collective-permute-start | bytes 589832 | tf_op jit(solution)/shard_map/ppermute | solution.py:74
  7.8 9.6 %collective-permute-start.2 = (bf16[2,16,3072]{2,1,0:T(8,128)(2,1)S(1)}, bf16[2,16,3072]{2,1,0:T(8,128)(2,1)S(1)}, u32[]{:S(2)}, u32[]{:S(2)}) collective-permute-start(bf16[2,16,3072]{2,1,0:T(8,128)(2,1)S(1)} %get-tuple-element.24), channel_id=1, source_target_pairs={{0,7},{1,6},{2,5},{3,4},{8,15},{9,14},{10,13},{11,12},{16,23},{17,... | collective-permute-start | bytes 589832 | tf_op jit(solution)/shard_map/ppermute | solution.py:74
  22.3 7.2 %collective-permute-start.6 = (bf16[128,176]{0,1:T(8,128)(2,1)S(1)}, bf16[128,176]{0,1:T(8,128)(2,1)S(1)}, u32[]{:S(2)}, u32[]{:S(2)}) collective-permute-start(bf16[128,176]{0,1:T(8,128)(2,1)S(1)} %fusion.6), channel_id=1, source_target_pairs={{0,28},{1,29},{2,30},{3,31},{8,20},{9,21},{10,22},{11,23},{16,12},... | collective-permute-start | bytes 135176 | tf_op jit(solution)/shard_map/ppermute | solution.py:74
  23.6 6.4 %collective-permute-start.5 = (bf16[128,176]{0,1:T(8,128)(2,1)S(1)}, bf16[128,176]{0,1:T(8,128)(2,1)S(1)}, u32[]{:S(2)}, u32[]{:S(2)}) collective-permute-start(bf16[128,176]{0,1:T(8,128)(2,1)S(1)} %fusion.6), channel_id=1, source_target_pairs={{0,20},{1,21},{2,22},{3,23},{8,28},{9,29},{10,30},{11,31},{16,4},{... | collective-permute-start | bytes 135176 | tf_op jit(solution)/shard_map/ppermute | solution.py:74
  24.9 7.5 %collective-permute-start.4 = (bf16[128,176]{0,1:T(8,128)(2,1)S(1)}, bf16[128,176]{0,1:T(8,128)(2,1)S(1)}, u32[]{:S(2)}, u32[]{:S(2)}) collective-permute-start(bf16[128,176]{0,1:T(8,128)(2,1)S(1)} %fusion.6), channel_id=1, source_target_pairs={{0,12},{1,13},{2,14},{3,15},{8,4},{9,5},{10,6},{11,7},{16,28},{17,... | collective-permute-start | bytes 135176 | tf_op jit(solution)/shard_map/ppermute | solution.py:74
  32.4 5.8 %collective-permute-start.7 = (bf16[3,128,176]{1,2,0:T(8,128)(2,1)S(1)}, bf16[3,128,176]{1,2,0:T(8,128)(2,1)S(1)}, u32[]{:S(2)}, u32[]{:S(2)}) collective-permute-start(bf16[3,128,176]{1,2,0:T(8,128)(2,1)S(1)} %pad_maximum_fusion.12), channel_id=1, source_target_pairs={{4,0},{5,1},{6,2},{7,3},{12,8},{13,9},{14,10},{15,11},{20,16},{21,... | collective-permute-start | bytes 405512 | tf_op jit(solution)/shard_map/ppermute | solution.py:75
  35.5 8.5 %collective-permute-start.8 = (bf16[176,768]{1,0:T(8,128)(2,1)S(1)}, bf16[176,768]{1,0:T(8,128)(2,1)S(1)}, u32[]{:S(2)}, u32[]{:S(2)}) collective-permute-start(bf16[176,768]{1,0:T(8,128)(2,1)S(1)} %get-tuple-element.14), channel_id=1, source_target_pairs={{0,8},{8,0},{16,24},{24,16},{1,9},{9,1},{17,25},{25,17},{2,10},{10... | collective-permute-start | bytes 811016 | tf_op jit(solution)/shard_map/ppermute | solution.py:89
  36.3 13.4 %collective-permute-start.10 = (bf16[176,768]{1,0:T(8,128)(2,1)S(1)}, bf16[176,768]{1,0:T(8,128)(2,1)S(1)}, u32[]{:S(2)}, u32[]{:S(2)}) collective-permute-start(bf16[176,768]{1,0:T(8,128)(2,1)S(1)} %get-tuple-element.15), channel_id=1, source_target_pairs={{0,24},{8,16},{16,8},{24,0},{1,25},{9,17},{17,9},{25,1},{2,26},{10... | collective-permute-start | bytes 811016 | tf_op jit(solution)/shard_map/ppermute | solution.py:89
  37.1 25.4 %collective-permute-start.9 = (bf16[176,768]{1,0:T(8,128)(2,1)S(1)}, bf16[176,768]{1,0:T(8,128)(2,1)S(1)}, u32[]{:S(2)}, u32[]{:S(2)}) collective-permute-start(bf16[176,768]{1,0:T(8,128)(2,1)S(1)} %get-tuple-element.16), channel_id=1, source_target_pairs={{0,16},{8,24},{16,0},{24,8},{1,17},{9,25},{17,1},{25,9},{2,18},{10... | collective-permute-start | bytes 811016 | tf_op jit(solution)/shard_map/ppermute | solution.py:89
  63.2 5.4 %collective-permute-start.11 = (bf16[2,16,768]{2,1,0:T(8,128)(2,1)S(1)}, bf16[2,16,768]{2,1,0:T(8,128)(2,1)S(1)}, u32[]{:S(2)}, u32[]{:S(2)}) collective-permute-start(bf16[2,16,768]{2,1,0:T(8,128)(2,1)S(1)} %get-tuple-element.36), channel_id=1, source_target_pairs={{0,5},{1,4},{2,7},{3,6},{8,13},{9,12},{10,15},{11,14},{16,21},{17,... | collective-permute-start | bytes 147464 | tf_op jit(solution)/shard_map/ppermute | solution.py:74
  64.5 6.3 %collective-permute-start.13 = (bf16[2,16,768]{2,1,0:T(8,128)(2,1)S(1)}, bf16[2,16,768]{2,1,0:T(8,128)(2,1)S(1)}, u32[]{:S(2)}, u32[]{:S(2)}) collective-permute-start(bf16[2,16,768]{2,1,0:T(8,128)(2,1)S(1)} %get-tuple-element.37), channel_id=1, source_target_pairs={{0,7},{1,6},{2,5},{3,4},{8,15},{9,14},{10,13},{11,12},{16,23},{17,... | collective-permute-start | bytes 147464 | tf_op jit(solution)/shard_map/ppermute | solution.py:74
  65.8 6.3 %collective-permute-start.12 = (bf16[2,16,768]{2,1,0:T(8,128)(2,1)S(1)}, bf16[2,16,768]{2,1,0:T(8,128)(2,1)S(1)}, u32[]{:S(2)}, u32[]{:S(2)}) collective-permute-start(bf16[2,16,768]{2,1,0:T(8,128)(2,1)S(1)} %get-tuple-element.38), channel_id=1, source_target_pairs={{0,6},{1,7},{2,4},{3,5},{8,14},{9,15},{10,12},{11,13},{16,22},{17,... | collective-permute-start | bytes 147464 | tf_op jit(solution)/shard_map/ppermute | solution.py:74
  75.6 7.5 %collective-permute-start.18 = (bf16[2,24,768]{2,1,0:T(8,128)(2,1)S(1)}, bf16[2,24,768]{2,1,0:T(8,128)(2,1)S(1)}, u32[]{:S(2)}, u32[]{:S(2)}) collective-permute-start(bf16[2,24,768]{2,1,0:T(8,128)(2,1)S(1)} %fusion), channel_id=1, source_target_pairs={{0,28},{1,29},{2,30},{3,31},{8,20},{9,21},{10,22},{11,23},{16,12},... | collective-permute-start | bytes 221192 | tf_op jit(solution)/shard_map/ppermute | solution.py:161
  76.9 7.8 %collective-permute-start.17 = (bf16[2,24,768]{2,1,0:T(8,128)(2,1)S(1)}, bf16[2,24,768]{2,1,0:T(8,128)(2,1)S(1)}, u32[]{:S(2)}, u32[]{:S(2)}) collective-permute-start(bf16[2,24,768]{2,1,0:T(8,128)(2,1)S(1)} %fusion), channel_id=1, source_target_pairs={{0,20},{1,21},{2,22},{3,23},{8,28},{9,29},{10,30},{11,31},{16,4},{... | collective-permute-start | bytes 221192 | tf_op jit(solution)/shard_map/ppermute | solution.py:161
  78.2 6.5 %collective-permute-start.16 = (bf16[2,24,768]{2,1,0:T(8,128)(2,1)S(1)}, bf16[2,24,768]{2,1,0:T(8,128)(2,1)S(1)}, u32[]{:S(2)}, u32[]{:S(2)}) collective-permute-start(bf16[2,24,768]{2,1,0:T(8,128)(2,1)S(1)} %fusion), channel_id=1, source_target_pairs={{0,12},{1,13},{2,14},{3,15},{8,4},{9,5},{10,6},{11,7},{16,28},{17,... | collective-permute-start | bytes 221192 | tf_op jit(solution)/shard_map/ppermute | solution.py:161
  79.5 5.2 %collective-permute-start.15 = (bf16[2,24,768]{2,1,0:T(8,128)(2,1)S(1)}, bf16[2,24,768]{2,1,0:T(8,128)(2,1)S(1)}, u32[]{:S(2)}, u32[]{:S(2)}) collective-permute-start(bf16[2,24,768]{2,1,0:T(8,128)(2,1)S(1)} %fusion), channel_id=1, source_target_pairs={{0,4},{1,5},{2,6},{3,7},{8,12},{9,13},{10,14},{11,15},{16,20},{17,... | collective-permute-start | bytes 221192 | tf_op jit(solution)/shard_map/ppermute | solution.py:161
  85.9 4.3 %collective-permute-start.20 = (bf16[2,16,3072]{2,1,0:T(8,128)(2,1)S(1)}, bf16[2,16,3072]{2,1,0:T(8,128)(2,1)S(1)}, u32[]{:S(2)}, u32[]{:S(2)}) collective-permute-start(bf16[2,16,3072]{2,1,0:T(8,128)(2,1)S(1)} %get-tuple-element.18), channel_id=1, source_target_pairs={{4,2},{5,3},{6,0},{7,1},{12,10},{13,11},{14,8},{15,9},{20,18},{21,... | collective-permute-start | bytes 589832 | tf_op jit(solution)/shard_map/ppermute | solution.py:74
  87.2 3.9 %collective-permute-start.19 = (bf16[2,16,3072]{2,1,0:T(8,128)(2,1)S(1)}, bf16[2,16,3072]{2,1,0:T(8,128)(2,1)S(1)}, u32[]{:S(2)}, u32[]{:S(2)}) collective-permute-start(bf16[2,16,3072]{2,1,0:T(8,128)(2,1)S(1)} %get-tuple-element.19), channel_id=1, source_target_pairs={{4,1},{5,0},{6,3},{7,2},{12,9},{13,8},{14,11},{15,10},{20,17},{21,... | collective-permute-start | bytes 589832 | tf_op jit(solution)/shard_map/ppermute | solution.py:74
  88.5 4.7 %collective-permute-start.21 = (bf16[2,16,3072]{2,1,0:T(8,128)(2,1)S(1)}, bf16[2,16,3072]{2,1,0:T(8,128)(2,1)S(1)}, u32[]{:S(2)}, u32[]{:S(2)}) collective-permute-start(bf16[2,16,3072]{2,1,0:T(8,128)(2,1)S(1)} %get-tuple-element.20), channel_id=1, source_target_pairs={{4,3},{5,2},{6,1},{7,0},{12,11},{13,10},{14,9},{15,8},{20,19},{21,... | collective-permute-start | bytes 589832 | tf_op jit(solution)/shard_map/ppermute | solution.py:74
  93.3 5.1 %collective-permute-start.22 = (bf16[3,2,16,3072]{3,2,1,0:T(8,128)(2,1)S(1)}, bf16[3,2,16,3072]{3,2,1,0:T(8,128)(2,1)S(1)}, u32[]{:S(2)}, u32[]{:S(2)}) collective-permute-start(bf16[3,2,16,3072]{3,2,1,0:T(8,128)(2,1)S(1)} %pad_maximum_fusion.4), channel_id=1, source_target_pairs={{0,4},{1,5},{2,6},{3,7},{8,12},{9,13},{10,14},{11,15},{16,20},{17,... | collective-permute-start | bytes 1769480 | tf_op jit(solution)/shard_map/ppermute | solution.py:75
  99.7 7.1 %collective-permute-start.25 = (bf16[128,176]{0,1:T(8,128)(2,1)S(1)}, bf16[128,176]{0,1:T(8,128)(2,1)S(1)}, u32[]{:S(2)}, u32[]{:S(2)}) collective-permute-start(bf16[128,176]{0,1:T(8,128)(2,1)S(1)} %fusion.7), channel_id=1, source_target_pairs={{4,24},{5,25},{6,26},{7,27},{12,16},{13,17},{14,18},{15,19},{20,8}... | collective-permute-start | bytes 135176 | tf_op jit(solution)/shard_map/ppermute | solution.py:74
  111.8 5.7 %collective-permute-start.27 = (bf16[2,16,768]{2,1,0:T(8,128)(2,1)S(1)}, bf16[2,16,768]{2,1,0:T(8,128)(2,1)S(1)}, u32[]{:S(2)}, u32[]{:S(2)}) collective-permute-start(bf16[2,16,768]{2,1,0:T(8,128)(2,1)S(1)} %get-tuple-element.32), channel_id=1, source_target_pairs={{4,1},{5,0},{6,3},{7,2},{12,9},{13,8},{14,11},{15,10},{20,17},{21,... | collective-permute-start | bytes 147464 | tf_op jit(solution)/shard_map/ppermute | solution.py:74
  118.7 3.9 %collective-permute-start.30 = (bf16[3,2,16,768]{3,2,1,0:T(8,128)(2,1)S(1)}, bf16[3,2,16,768]{3,2,1,0:T(8,128)(2,1)S(1)}, u32[]{:S(2)}, u32[]{:S(2)}) collective-permute-start(bf16[3,2,16,768]{3,2,1,0:T(8,128)(2,1)S(1)} %pad_maximum_fusion.11), channel_id=1, source_target_pairs={{0,4},{1,5},{2,6},{3,7},{8,12},{9,13},{10,14},{11,15},{16,20},{17,... | collective-permute-start | bytes 442376 | tf_op jit(solution)/shard_map/ppermute | solution.py:75
  (17 other events, 149.5 us)

commit v7 on v1

--- a/solution.py
+++ b/solution.py
@@ -72,9 +72,10 @@
         down_parts = []
         for s in range(n_dp):
             piece = lax.dynamic_slice_in_dim(down_local, dring.ahead(d_me, s) * columns, columns, 1)
-            if s:
-                piece = lax.ppermute(piece, "dp", [(i, dring.ahead(i, s)) for i in range(n_dp)])
             down_parts.append(piece)
+        down_parts, tokens = lax.optimization_barrier((down_parts, tokens))
+        for s in range(1, n_dp):
+            down_parts[s] = lax.ppermute(down_parts[s], "dp", [(i, dring.ahead(i, s)) for i in range(n_dp)])
         down_full = jnp.concatenate(down_parts, axis=0)
     else:
         down_full = lax.all_to_all(down_local, "dp", 1, 0, tiled=True)

time: 109 us -> 99.1 us (0.909)
  waiting for transfers between devices: 48 us -> 39.3 us
  matrix products: 8.48 us -> 5.16 us
  local copies, waits for them, and re-layouts: 5.55 us -> 8.87 us
    ppermute x3, waiting for transfers between devices: 17 us -> 2.99 us  [per_device(): lax.ppermute(down_parts[s], 'dp', [(i, dring.ahead(i, s)) for i in range(...]
    ppermute x4, waiting for transfers between devices: 22.8 us -> 28.9 us  [per_device(): parts.append(lax.ppermute(cols, AXES, pairs))]
    dot_general x2, matrix products: 2.93 us -> 0.71 us  [layer(): jnp.dot(hidden_full, down_full, preferred_element_type=jnp.float32)]
    unnamed x12 -> x21, local copies, waits for them, and re-layouts: 0.73 us -> 2.83 us
    rsqrt x2, local copies, waits for them, and re-layouts: 0.17 us -> 1.44 us  [layer(): inv_rms = lax.rsqrt(squares + 1e-05)]
    dynamic_slice x1, local copies, waits for them, and re-layouts: 0.93 us -> 2.17 us  [per_device(): lax.dynamic_slice_in_dim(down_local, dring.ahead(d_me, s) * columns, colu...]
  transfers between devices with their start and end apart: 25 -> 25, of which waited for: 9 -> 9; matrix products, arithmetic and copies ran while one was open for 3% -> 10% of each run, Pallas kernels for 0% -> 0%
where the time goes in v7:
time: 99.1 us; the launch traced here: 98.4 us
  starting transfers between devices  41.7 us (42%)
  waiting for transfers between devices  39.3 us (40%)
  local copies, waits for them, and re-layouts  8.87 us (9%)
  matrix products  5.16 us (5%)
  other arithmetic  2.77 us (3%)
    ppermute x4, waiting for transfers between devices, per_device(): parts.append(lax.ppermute(cols, AXES, pairs))  28.9 us
    ppermute x6, starting transfers between devices, layer(): parts.append(lax.ppermute(hidden, AXES, dp_pairs(p, s)))  11.3 us
    ppermute x6, starting transfers between devices, layer(): lax.ppermute(outgoing[:, s], AXES, expert_pairs(p, s, False))  10.4 us
    ppermute x6, starting transfers between devices, layer(): lax.ppermute(expert_out[:, s], AXES, expert_pairs(p, s, True))  10.4 us
    ppermute x4, starting transfers between devices, per_device(): parts.append(lax.ppermute(cols, AXES, pairs))  5.17 us
    ppermute x3, starting transfers between devices, per_device(): lax.ppermute(down_parts[s], 'dp', [(i, dring.ahead(i, s)) for i in range(...  4.51 us
    ppermute x6, waiting for transfers between devices, layer(): lax.ppermute(outgoing[:, s], AXES, expert_pairs(p, s, False))  4.24 us
    ppermute x3, waiting for transfers between devices, per_device(): lax.ppermute(down_parts[s], 'dp', [(i, dring.ahead(i, s)) for i in range(...  2.99 us
  transfers between devices with their start and end apart: 25, of which 9 were waited for; matrix products, arithmetic and copies ran while one was open for 10% of the time, Pallas kernels for 0%

profile of v7, /device:TPU:1, one launch (start us, length us, event | category | flops | bytes accessed | tf_op | source)
XLA Modules:
  0.0 98.4 jit_solution(3839529345285029059)
XLA Ops:
  0.0 2.2 %dynamic-slice_bitcast_fusion = (bf16[176,768]{1,0:T(8,128)(2,1)S(1)}, bf16[176,768]{1,0:T(8,128)(2,1)}, bf16[176,768]{1,0:T(8,128)(2,1)S(1)}, bf16[176,768]{1,0:T(8,128)(2,1)}) fusion(bf16[1,1,176,3072]{3,2,1,0:T(8,128)(2,1)} %param.11, s32[]{:T(128)S(6)} %select_n.60, s32[]{:T(128)S(6)} %select_n.58, s32[]{:T(128)S(6)} %select_n.57, s32[]{:T(128)S(6)} %select_n.59), kind=kLoop, calls=%fused_computation.29 | loop fusion | bytes 2162704 | tf_op jit(solution)/shard_map/dynamic_slice | solution.py:74
  2.2 2.1 %collective-permute-start.6 = (bf16[176,768]{1,0:T(8,128)(2,1)}, bf16[176,768]{1,0:T(8,128)(2,1)}, u32[]{:S(2)}, u32[]{:S(2)}) collective-permute-start(bf16[176,768]{1,0:T(8,128)(2,1)} %get-tuple-element.12), channel_id=1, source_target_pairs={{0,8},{8,0},{16,24},{24,16},{1,9},{9,1},{17,25},{25,17},{2,10},{10... | collective-permute-start | bytes 811016 | tf_op jit(solution)/shard_map/ppermute | solution.py:78
  4.3 2.3 %collective-permute-start.7 = (bf16[176,768]{1,0:T(8,128)(2,1)}, bf16[176,768]{1,0:T(8,128)(2,1)}, u32[]{:S(2)}, u32[]{:S(2)}) collective-permute-start(bf16[176,768]{1,0:T(8,128)(2,1)} %get-tuple-element.13), channel_id=1, source_target_pairs={{0,16},{8,24},{16,0},{24,8},{1,17},{9,25},{17,1},{25,9},{2,18},{10... | collective-permute-start | bytes 811016 | tf_op jit(solution)/shard_map/ppermute | solution.py:78
  12.3 1.3 %rsqrt.23 = f32[128]{0:T(128)} reshape(f32[2,4,16]{2,1,0:T(4,128)} %add_rsqrt_fusion.1) | data formatting | bytes 1024 | tf_op jit(solution)/shard_map/rsqrt | solution.py:97
  19.4 3.0 %collective-permute-done.8 = bf16[176,768]{1,0:T(8,128)(2,1)} collective-permute-done((bf16[176,768]{1,0:T(8,128)(2,1)S(1)}, bf16[176,768]{1,0:T(8,128)(2,1)}, u32[]{:S(2)}, u32[]{:S(2)}) %collective-permute-start.8) | collective-permute-done | bytes 270368 | tf_op jit(solution)/shard_map/ppermute | solution.py:78
  26.1 1.3 %collective-permute-start.15 = (bf16[2,24,768]{2,1,0:T(8,128)(2,1)S(1)}, bf16[2,24,768]{2,1,0:T(8,128)(2,1)S(1)}, u32[]{:S(2)}, u32[]{:S(2)}) collective-permute-start(bf16[2,24,768]{2,1,0:T(8,128)(2,1)S(1)} %fusion), channel_id=1, source_target_pairs={{0,28},{1,29},{2,30},{3,31},{8,20},{9,21},{10,22},{11,23},{16,12},... | collective-permute-start | bytes 221192 | tf_op jit(solution)/shard_map/ppermute | solution.py:136
  27.4 1.3 %collective-permute-start.14 = (bf16[2,24,768]{2,1,0:T(8,128)(2,1)S(1)}, bf16[2,24,768]{2,1,0:T(8,128)(2,1)S(1)}, u32[]{:S(2)}, u32[]{:S(2)}) collective-permute-start(bf16[2,24,768]{2,1,0:T(8,128)(2,1)S(1)} %fusion), channel_id=1, source_target_pairs={{0,20},{1,21},{2,22},{3,23},{8,28},{9,29},{10,30},{11,31},{16,4},{... | collective-permute-start | bytes 221192 | tf_op jit(solution)/shard_map/ppermute | solution.py:136
  28.7 1.3 %collective-permute-start.13 = (bf16[2,24,768]{2,1,0:T(8,128)(2,1)S(1)}, bf16[2,24,768]{2,1,0:T(8,128)(2,1)S(1)}, u32[]{:S(2)}, u32[]{:S(2)}) collective-permute-start(bf16[2,24,768]{2,1,0:T(8,128)(2,1)S(1)} %fusion), channel_id=1, source_target_pairs={{0,12},{1,13},{2,14},{3,15},{8,4},{9,5},{10,6},{11,7},{16,28},{17,... | collective-permute-start | bytes 221192 | tf_op jit(solution)/shard_map/ppermute | solution.py:136
  30.0 1.3 %collective-permute-start.12 = (bf16[2,24,768]{2,1,0:T(8,128)(2,1)S(1)}, bf16[2,24,768]{2,1,0:T(8,128)(2,1)S(1)}, u32[]{:S(2)}, u32[]{:S(2)}) collective-permute-start(bf16[2,24,768]{2,1,0:T(8,128)(2,1)S(1)} %fusion), channel_id=1, source_target_pairs={{0,4},{1,5},{2,6},{3,7},{8,12},{9,13},{10,14},{11,15},{16,20},{17,... | collective-permute-start | bytes 221192 | tf_op jit(solution)/shard_map/ppermute | solution.py:136
  31.4 25.9 %collective-permute-done.15 = bf16[2,24,768]{2,1,0:T(8,128)(2,1)S(1)} collective-permute-done((bf16[2,24,768]{2,1,0:T(8,128)(2,1)S(1)}, bf16[2,24,768]{2,1,0:T(8,128)(2,1)S(1)}, u32[]{:S(2)}, u32[]{:S(2)}) %collective-permute-start.15) | collective-permute-done | bytes 73760 | tf_op jit(solution)/shard_map/ppermute | solution.py:136
  57.3 1.8 %collective-permute-done.14 = bf16[2,24,768]{2,1,0:T(8,128)(2,1)S(1)} collective-permute-done((bf16[2,24,768]{2,1,0:T(8,128)(2,1)S(1)}, bf16[2,24,768]{2,1,0:T(8,128)(2,1)S(1)}, u32[]{:S(2)}, u32[]{:S(2)}) %collective-permute-start.14) | collective-permute-done | bytes 73760 | tf_op jit(solution)/shard_map/ppermute | solution.py:136
  59.1 1.3 %collective-permute-done.13 = bf16[2,24,768]{2,1,0:T(8,128)(2,1)S(1)} collective-permute-done((bf16[2,24,768]{2,1,0:T(8,128)(2,1)S(1)}, bf16[2,24,768]{2,1,0:T(8,128)(2,1)S(1)}, u32[]{:S(2)}, u32[]{:S(2)}) %collective-permute-start.13) | collective-permute-done | bytes 73760 | tf_op jit(solution)/shard_map/ppermute | solution.py:136
  61.6 4.1 %collective-permute-start.18 = (bf16[2,16,3072]{2,1,0:T(8,128)(2,1)S(1)}, bf16[2,16,3072]{2,1,0:T(8,128)(2,1)S(1)}, u32[]{:S(2)}, u32[]{:S(2)}) collective-permute-start(bf16[2,16,3072]{2,1,0:T(8,128)(2,1)S(1)} %get-tuple-element.30), channel_id=1, source_target_pairs={{4,7},{5,6},{6,5},{7,4},{12,15},{13,14},{14,13},{15,12},{20,23},{2... | collective-permute-start | bytes 589832 | tf_op jit(solution)/shard_map/ppermute | solution.py:94
  65.6 2.1 %collective-permute-start.17 = (bf16[2,16,3072]{2,1,0:T(8,128)(2,1)S(1)}, bf16[2,16,3072]{2,1,0:T(8,128)(2,1)S(1)}, u32[]{:S(2)}, u32[]{:S(2)}) collective-permute-start(bf16[2,16,3072]{2,1,0:T(8,128)(2,1)S(1)} %get-tuple-element.28), channel_id=1, source_target_pairs={{4,6},{5,7},{6,4},{7,5},{12,14},{13,15},{14,12},{15,13},{20,22},{2... | collective-permute-start | bytes 589832 | tf_op jit(solution)/shard_map/ppermute | solution.py:94
  67.8 2.2 %collective-permute-start.16 = (bf16[2,16,3072]{2,1,0:T(8,128)(2,1)S(1)}, bf16[2,16,3072]{2,1,0:T(8,128)(2,1)S(1)}, u32[]{:S(2)}, u32[]{:S(2)}) collective-permute-start(bf16[2,16,3072]{2,1,0:T(8,128)(2,1)S(1)} %get-tuple-element.29), channel_id=1, source_target_pairs={{4,5},{5,4},{6,7},{7,6},{12,13},{13,12},{14,15},{15,14},{20,21},{2... | collective-permute-start | bytes 589832 | tf_op jit(solution)/shard_map/ppermute | solution.py:94
  70.0 2.1 %collective-permute-done.17 = bf16[2,16,3072]{2,1,0:T(8,128)(2,1)S(1)} collective-permute-done((bf16[2,16,3072]{2,1,0:T(8,128)(2,1)S(1)}, bf16[2,16,3072]{2,1,0:T(8,128)(2,1)S(1)}, u32[]{:S(2)}, u32[]{:S(2)}) %collective-permute-start.17) | collective-permute-done | bytes 196640 | tf_op jit(solution)/shard_map/ppermute | solution.py:94
  72.0 2.1 %collective-permute-done.16 = bf16[2,16,3072]{2,1,0:T(8,128)(2,1)S(1)} collective-permute-done((bf16[2,16,3072]{2,1,0:T(8,128)(2,1)S(1)}, bf16[2,16,3072]{2,1,0:T(8,128)(2,1)S(1)}, u32[]{:S(2)}, u32[]{:S(2)}) %collective-permute-start.16) | collective-permute-done | bytes 196640 | tf_op jit(solution)/shard_map/ppermute | solution.py:94
  76.2 3.8 %collective-permute-start.21 = (bf16[128,176]{0,1:T(8,128)(2,1)S(1)}, bf16[128,176]{0,1:T(8,128)(2,1)S(1)}, u32[]{:S(2)}, u32[]{:S(2)}) collective-permute-start(bf16[128,176]{0,1:T(8,128)(2,1)S(1)} %fusion.7), channel_id=1, source_target_pairs={{4,28},{5,29},{6,30},{7,31},{12,20},{13,21},{14,22},{15,23},{20,12... | collective-permute-start | bytes 135176 | tf_op jit(solution)/shard_map/ppermute | solution.py:104
  80.0 1.9 %collective-permute-start.20 = (bf16[128,176]{0,1:T(8,128)(2,1)S(1)}, bf16[128,176]{0,1:T(8,128)(2,1)S(1)}, u32[]{:S(2)}, u32[]{:S(2)}) collective-permute-start(bf16[128,176]{0,1:T(8,128)(2,1)S(1)} %fusion.7), channel_id=1, source_target_pairs={{4,20},{5,21},{6,22},{7,23},{12,28},{13,29},{14,30},{15,31},{20,4}... | collective-permute-start | bytes 135176 | tf_op jit(solution)/shard_map/ppermute | solution.py:104
  82.0 3.6 %collective-permute-start.19 = (bf16[128,176]{0,1:T(8,128)(2,1)S(1)}, bf16[128,176]{0,1:T(8,128)(2,1)S(1)}, u32[]{:S(2)}, u32[]{:S(2)}) collective-permute-start(bf16[128,176]{0,1:T(8,128)(2,1)S(1)} %fusion.7), channel_id=1, source_target_pairs={{4,12},{5,13},{6,14},{7,15},{12,4},{13,5},{14,6},{15,7},{20,28},{2... | collective-permute-start | bytes 135176 | tf_op jit(solution)/shard_map/ppermute | solution.py:104
  87.3 3.1 %collective-permute-start.24 = (bf16[2,16,768]{2,1,0:T(8,128)(2,1)S(1)}, bf16[2,16,768]{2,1,0:T(8,128)(2,1)S(1)}, u32[]{:S(2)}, u32[]{:S(2)}) collective-permute-start(bf16[2,16,768]{2,1,0:T(8,128)(2,1)S(1)} %get-tuple-element.37), channel_id=1, source_target_pairs={{4,7},{5,6},{6,5},{7,4},{12,15},{13,14},{14,13},{15,12},{20,23},{2... | collective-permute-start | bytes 147464 | tf_op jit(solution)/shard_map/ppermute | solution.py:112
  90.5 2.1 %collective-permute-start.23 = (bf16[2,16,768]{2,1,0:T(8,128)(2,1)S(1)}, bf16[2,16,768]{2,1,0:T(8,128)(2,1)S(1)}, u32[]{:S(2)}, u32[]{:S(2)}) collective-permute-start(bf16[2,16,768]{2,1,0:T(8,128)(2,1)S(1)} %get-tuple-element.38), channel_id=1, source_target_pairs={{4,6},{5,7},{6,4},{7,5},{12,14},{13,15},{14,12},{15,13},{20,22},{2... | collective-permute-start | bytes 147464 | tf_op jit(solution)/shard_map/ppermute | solution.py:112
  92.6 3.1 %collective-permute-start.22 = (bf16[2,16,768]{2,1,0:T(8,128)(2,1)S(1)}, bf16[2,16,768]{2,1,0:T(8,128)(2,1)S(1)}, u32[]{:S(2)}, u32[]{:S(2)}) collective-permute-start(bf16[2,16,768]{2,1,0:T(8,128)(2,1)S(1)} %get-tuple-element.36), channel_id=1, source_target_pairs={{4,5},{5,4},{6,7},{7,6},{12,13},{13,12},{14,15},{15,14},{20,21},{2... | collective-permute-start | bytes 147464 | tf_op jit(solution)/shard_map/ppermute | solution.py:112
  95.8 1.7 %collective-permute-done.22 = bf16[2,16,768]{2,1,0:T(8,128)(2,1)S(1)} collective-permute-done((bf16[2,16,768]{2,1,0:T(8,128)(2,1)S(1)}, bf16[2,16,768]{2,1,0:T(8,128)(2,1)S(1)}, u32[]{:S(2)}, u32[]{:S(2)}) %collective-permute-start.22) | collective-permute-done | bytes 49184 | tf_op jit(solution)/shard_map/ppermute | solution.py:112
  (96 shorter events, 20.8 us)
Async XLA Ops:
  2.2 14.5 %collective-permute-start.6 = (bf16[176,768]{1,0:T(8,128)(2,1)}, bf16[176,768]{1,0:T(8,128)(2,1)}, u32[]{:S(2)}, u32[]{:S(2)}) collective-permute-start(bf16[176,768]{1,0:T(8,128)(2,1)} %get-tuple-element.12), channel_id=1, source_target_pairs={{0,8},{8,0},{16,24},{24,16},{1,9},{9,1},{17,25},{25,17},{2,10},{10... | collective-permute-start | bytes 811016 | tf_op jit(solution)/shard_map/ppermute | solution.py:78
  4.3 14.1 %collective-permute-start.7 = (bf16[176,768]{1,0:T(8,128)(2,1)}, bf16[176,768]{1,0:T(8,128)(2,1)}, u32[]{:S(2)}, u32[]{:S(2)}) collective-permute-start(bf16[176,768]{1,0:T(8,128)(2,1)} %get-tuple-element.13), channel_id=1, source_target_pairs={{0,16},{8,24},{16,0},{24,8},{1,17},{9,25},{17,1},{25,9},{2,18},{10... | collective-permute-start | bytes 811016 | tf_op jit(solution)/shard_map/ppermute | solution.py:78
  8.7 2.7 %collective-permute-start.2 = (bf16[2,16,3072]{2,1,0:T(8,128)(2,1)S(1)}, bf16[2,16,3072]{2,1,0:T(8,128)(2,1)S(1)}, u32[]{:S(2)}, u32[]{:S(2)}) collective-permute-start(bf16[2,16,3072]{2,1,0:T(8,128)(2,1)S(1)} %get-tuple-element.34), channel_id=1, source_target_pairs={{0,3},{1,2},{2,1},{3,0},{8,11},{9,10},{10,9},{11,8},{16,19},{17,18... | collective-permute-start | bytes 589832 | tf_op jit(solution)/shard_map/ppermute | solution.py:94
  9.4 2.1 %collective-permute-start.1 = (bf16[2,16,3072]{2,1,0:T(8,128)(2,1)S(1)}, bf16[2,16,3072]{2,1,0:T(8,128)(2,1)S(1)}, u32[]{:S(2)}, u32[]{:S(2)}) collective-permute-start(bf16[2,16,3072]{2,1,0:T(8,128)(2,1)S(1)} %get-tuple-element.32), channel_id=1, source_target_pairs={{0,2},{1,3},{2,0},{3,1},{8,10},{9,11},{10,8},{11,9},{16,18},{17,19... | collective-permute-start | bytes 589832 | tf_op jit(solution)/shard_map/ppermute | solution.py:94
  10.0 1.4 %collective-permute-start = (bf16[2,16,3072]{2,1,0:T(8,128)(2,1)S(1)}, bf16[2,16,3072]{2,1,0:T(8,128)(2,1)S(1)}, u32[]{:S(2)}, u32[]{:S(2)}) collective-permute-start(bf16[2,16,3072]{2,1,0:T(8,128)(2,1)S(1)} %get-tuple-element.33), channel_id=1, source_target_pairs={{0,1},{1,0},{2,3},{3,2},{8,9},{9,8},{10,11},{11,10},{16,17},{17,16... | collective-permute-start | bytes 589832 | tf_op jit(solution)/shard_map/ppermute | solution.py:94
  11.4 11.0 %collective-permute-start.8 = (bf16[176,768]{1,0:T(8,128)(2,1)S(1)}, bf16[176,768]{1,0:T(8,128)(2,1)}, u32[]{:S(2)}, u32[]{:S(2)}) collective-permute-start(bf16[176,768]{1,0:T(8,128)(2,1)S(1)} %get-tuple-element.14), channel_id=1, source_target_pairs={{0,24},{8,16},{16,8},{24,0},{1,25},{9,17},{17,9},{25,1},{2,26},{10... | collective-permute-start | bytes 811016 | tf_op jit(solution)/shard_map/ppermute | solution.py:78
  15.4 8.0 %collective-permute-start.5 = (bf16[128,176]{0,1:T(8,128)(2,1)S(1)}, bf16[128,176]{0,1:T(8,128)(2,1)S(1)}, u32[]{:S(2)}, u32[]{:S(2)}) collective-permute-start(bf16[128,176]{0,1:T(8,128)(2,1)S(1)} %fusion.6), channel_id=1, source_target_pairs={{0,24},{1,25},{2,26},{3,27},{8,16},{9,17},{10,18},{11,19},{16,8},{... | collective-permute-start | bytes 135176 | tf_op jit(solution)/shard_map/ppermute | solution.py:104
  16.1 7.3 %collective-permute-start.4 = (bf16[128,176]{0,1:T(8,128)(2,1)S(1)}, bf16[128,176]{0,1:T(8,128)(2,1)S(1)}, u32[]{:S(2)}, u32[]{:S(2)}) collective-permute-start(bf16[128,176]{0,1:T(8,128)(2,1)S(1)} %fusion.6), channel_id=1, source_target_pairs={{0,16},{1,17},{2,18},{3,19},{8,24},{9,25},{10,26},{11,27},{16,0},{... | collective-permute-start | bytes 135176 | tf_op jit(solution)/shard_map/ppermute | solution.py:104
  16.7 6.6 %collective-permute-start.3 = (bf16[128,176]{0,1:T(8,128)(2,1)S(1)}, bf16[128,176]{0,1:T(8,128)(2,1)S(1)}, u32[]{:S(2)}, u32[]{:S(2)}) collective-permute-start(bf16[128,176]{0,1:T(8,128)(2,1)S(1)} %fusion.6), channel_id=1, source_target_pairs={{0,8},{1,9},{2,10},{3,11},{8,0},{9,1},{10,2},{11,3},{16,24},{17,25... | collective-permute-start | bytes 135176 | tf_op jit(solution)/shard_map/ppermute | solution.py:104
  23.8 2.0 %collective-permute-start.11 = (bf16[2,16,768]{2,1,0:T(8,128)(2,1)S(1)}, bf16[2,16,768]{2,1,0:T(8,128)(2,1)S(1)}, u32[]{:S(2)}, u32[]{:S(2)}) collective-permute-start(bf16[2,16,768]{2,1,0:T(8,128)(2,1)S(1)} %get-tuple-element.41), channel_id=1, source_target_pairs={{0,3},{1,2},{2,1},{3,0},{8,11},{9,10},{10,9},{11,8},{16,19},{17,18... | collective-permute-start | bytes 147464 | tf_op jit(solution)/shard_map/ppermute | solution.py:112
  24.4 1.4 %collective-permute-start.10 = (bf16[2,16,768]{2,1,0:T(8,128)(2,1)S(1)}, bf16[2,16,768]{2,1,0:T(8,128)(2,1)S(1)}, u32[]{:S(2)}, u32[]{:S(2)}) collective-permute-start(bf16[2,16,768]{2,1,0:T(8,128)(2,1)S(1)} %get-tuple-element.42), channel_id=1, source_target_pairs={{0,2},{1,3},{2,0},{3,1},{8,10},{9,11},{10,8},{11,9},{16,18},{17,19... | collective-permute-start | bytes 147464 | tf_op jit(solution)/shard_map/ppermute | solution.py:112
  26.1 31.2 %collective-permute-start.15 = (bf16[2,24,768]{2,1,0:T(8,128)(2,1)S(1)}, bf16[2,24,768]{2,1,0:T(8,128)(2,1)S(1)}, u32[]{:S(2)}, u32[]{:S(2)}) collective-permute-start(bf16[2,24,768]{2,1,0:T(8,128)(2,1)S(1)} %fusion), channel_id=1, source_target_pairs={{0,28},{1,29},{2,30},{3,31},{8,20},{9,21},{10,22},{11,23},{16,12},... | collective-permute-start | bytes 221192 | tf_op jit(solution)/shard_map/ppermute | solution.py:136
  27.4 31.7 %collective-permute-start.14 = (bf16[2,24,768]{2,1,0:T(8,128)(2,1)S(1)}, bf16[2,24,768]{2,1,0:T(8,128)(2,1)S(1)}, u32[]{:S(2)}, u32[]{:S(2)}) collective-permute-start(bf16[2,24,768]{2,1,0:T(8,128)(2,1)S(1)} %fusion), channel_id=1, source_target_pairs={{0,20},{1,21},{2,22},{3,23},{8,28},{9,29},{10,30},{11,31},{16,4},{... | collective-permute-start | bytes 221192 | tf_op jit(solution)/shard_map/ppermute | solution.py:136
  28.7 31.6 %collective-permute-start.13 = (bf16[2,24,768]{2,1,0:T(8,128)(2,1)S(1)}, bf16[2,24,768]{2,1,0:T(8,128)(2,1)S(1)}, u32[]{:S(2)}, u32[]{:S(2)}) collective-permute-start(bf16[2,24,768]{2,1,0:T(8,128)(2,1)S(1)} %fusion), channel_id=1, source_target_pairs={{0,12},{1,13},{2,14},{3,15},{8,4},{9,5},{10,6},{11,7},{16,28},{17,... | collective-permute-start | bytes 221192 | tf_op jit(solution)/shard_map/ppermute | solution.py:136
  30.0 30.3 %collective-permute-start.12 = (bf16[2,24,768]{2,1,0:T(8,128)(2,1)S(1)}, bf16[2,24,768]{2,1,0:T(8,128)(2,1)S(1)}, u32[]{:S(2)}, u32[]{:S(2)}) collective-permute-start(bf16[2,24,768]{2,1,0:T(8,128)(2,1)S(1)} %fusion), channel_id=1, source_target_pairs={{0,4},{1,5},{2,6},{3,7},{8,12},{9,13},{10,14},{11,15},{16,20},{17,... | collective-permute-start | bytes 221192 | tf_op jit(solution)/shard_map/ppermute | solution.py:136
  61.6 8.4 %collective-permute-start.18 = (bf16[2,16,3072]{2,1,0:T(8,128)(2,1)S(1)}, bf16[2,16,3072]{2,1,0:T(8,128)(2,1)S(1)}, u32[]{:S(2)}, u32[]{:S(2)}) collective-permute-start(bf16[2,16,3072]{2,1,0:T(8,128)(2,1)S(1)} %get-tuple-element.30), channel_id=1, source_target_pairs={{4,7},{5,6},{6,5},{7,4},{12,15},{13,14},{14,13},{15,12},{20,23},{2... | collective-permute-start | bytes 589832 | tf_op jit(solution)/shard_map/ppermute | solution.py:94
  65.6 6.4 %collective-permute-start.17 = (bf16[2,16,3072]{2,1,0:T(8,128)(2,1)S(1)}, bf16[2,16,3072]{2,1,0:T(8,128)(2,1)S(1)}, u32[]{:S(2)}, u32[]{:S(2)}) collective-permute-start(bf16[2,16,3072]{2,1,0:T(8,128)(2,1)S(1)} %get-tuple-element.28), channel_id=1, source_target_pairs={{4,6},{5,7},{6,4},{7,5},{12,14},{13,15},{14,12},{15,13},{20,22},{2... | collective-permute-start | bytes 589832 | tf_op jit(solution)/shard_map/ppermute | solution.py:94
  67.8 6.4 %collective-permute-start.16 = (bf16[2,16,3072]{2,1,0:T(8,128)(2,1)S(1)}, bf16[2,16,3072]{2,1,0:T(8,128)(2,1)S(1)}, u32[]{:S(2)}, u32[]{:S(2)}) collective-permute-start(bf16[2,16,3072]{2,1,0:T(8,128)(2,1)S(1)} %get-tuple-element.29), channel_id=1, source_target_pairs={{4,5},{5,4},{6,7},{7,6},{12,13},{13,12},{14,15},{15,14},{20,21},{2... | collective-permute-start | bytes 589832 | tf_op jit(solution)/shard_map/ppermute | solution.py:94
  76.2 9.3 %collective-permute-start.21 = (bf16[128,176]{0,1:T(8,128)(2,1)S(1)}, bf16[128,176]{0,1:T(8,128)(2,1)S(1)}, u32[]{:S(2)}, u32[]{:S(2)}) collective-permute-start(bf16[128,176]{0,1:T(8,128)(2,1)S(1)} %fusion.7), channel_id=1, source_target_pairs={{4,28},{5,29},{6,30},{7,31},{12,20},{13,21},{14,22},{15,23},{20,12... | collective-permute-start | bytes 135176 | tf_op jit(solution)/shard_map/ppermute | solution.py:104
  80.0 5.7 %collective-permute-start.20 = (bf16[128,176]{0,1:T(8,128)(2,1)S(1)}, bf16[128,176]{0,1:T(8,128)(2,1)S(1)}, u32[]{:S(2)}, u32[]{:S(2)}) collective-permute-start(bf16[128,176]{0,1:T(8,128)(2,1)S(1)} %fusion.7), channel_id=1, source_target_pairs={{4,20},{5,21},{6,22},{7,23},{12,28},{13,29},{14,30},{15,31},{20,4}... | collective-permute-start | bytes 135176 | tf_op jit(solution)/shard_map/ppermute | solution.py:104
  82.0 5.0 %collective-permute-start.19 = (bf16[128,176]{0,1:T(8,128)(2,1)S(1)}, bf16[128,176]{0,1:T(8,128)(2,1)S(1)}, u32[]{:S(2)}, u32[]{:S(2)}) collective-permute-start(bf16[128,176]{0,1:T(8,128)(2,1)S(1)} %fusion.7), channel_id=1, source_target_pairs={{4,12},{5,13},{6,14},{7,15},{12,4},{13,5},{14,6},{15,7},{20,28},{2... | collective-permute-start | bytes 135176 | tf_op jit(solution)/shard_map/ppermute | solution.py:104
  87.3 8.4 %collective-permute-start.24 = (bf16[2,16,768]{2,1,0:T(8,128)(2,1)S(1)}, bf16[2,16,768]{2,1,0:T(8,128)(2,1)S(1)}, u32[]{:S(2)}, u32[]{:S(2)}) collective-permute-start(bf16[2,16,768]{2,1,0:T(8,128)(2,1)S(1)} %get-tuple-element.37), channel_id=1, source_target_pairs={{4,7},{5,6},{6,5},{7,4},{12,15},{13,14},{14,13},{15,12},{20,23},{2... | collective-permute-start | bytes 147464 | tf_op jit(solution)/shard_map/ppermute | solution.py:112
  90.5 5.3 %collective-permute-start.23 = (bf16[2,16,768]{2,1,0:T(8,128)(2,1)S(1)}, bf16[2,16,768]{2,1,0:T(8,128)(2,1)S(1)}, u32[]{:S(2)}, u32[]{:S(2)}) collective-permute-start(bf16[2,16,768]{2,1,0:T(8,128)(2,1)S(1)} %get-tuple-element.38), channel_id=1, source_target_pairs={{4,6},{5,7},{6,4},{7,5},{12,14},{13,15},{14,12},{15,13},{20,22},{2... | collective-permute-start | bytes 147464 | tf_op jit(solution)/shard_map/ppermute | solution.py:112
  92.6 4.8 %collective-permute-start.22 = (bf16[2,16,768]{2,1,0:T(8,128)(2,1)S(1)}, bf16[2,16,768]{2,1,0:T(8,128)(2,1)S(1)}, u32[]{:S(2)}, u32[]{:S(2)}) collective-permute-start(bf16[2,16,768]{2,1,0:T(8,128)(2,1)S(1)} %get-tuple-element.36), channel_id=1, source_target_pairs={{4,5},{5,4},{6,7},{7,6},{12,13},{13,12},{14,15},{15,14},{20,21},{2... | collective-permute-start | bytes 147464 | tf_op jit(solution)/shard_map/ppermute | solution.py:112
  (9 other events, 46.0 us)

commit v8 on v7

--- a/solution.py
+++ b/solution.py
@@ -76,7 +76,6 @@
         down_parts, tokens = lax.optimization_barrier((down_parts, tokens))
         for s in range(1, n_dp):
             down_parts[s] = lax.ppermute(down_parts[s], "dp", [(i, dring.ahead(i, s)) for i in range(n_dp)])
-        down_full = jnp.concatenate(down_parts, axis=0)
     else:
         down_full = lax.all_to_all(down_local, "dp", 1, 0, tiled=True)
 
@@ -102,10 +101,13 @@
             parts = [hidden]
             for s in range(1, n_dp):
                 parts.append(lax.ppermute(hidden, AXES, dp_pairs(p, s)))
-            hidden_full = jnp.concatenate(parts, axis=1)
+            expert_out = jnp.dot(parts[0], down_parts[0], preferred_element_type=jnp.float32)
+            for s in range(1, n_dp):
+                expert_out = expert_out + jnp.dot(parts[s], down_parts[s], preferred_element_type=jnp.float32)
+            expert_out = expert_out.astype(jnp.bfloat16)
         else:
             hidden_full = lax.all_gather(hidden, "dp", axis=1, tiled=True)
-        expert_out = jnp.dot(hidden_full, down_full, preferred_element_type=jnp.float32).astype(jnp.bfloat16)
+            expert_out = jnp.dot(hidden_full, down_full, preferred_element_type=jnp.float32).astype(jnp.bfloat16)
         expert_out = expert_out.reshape(micro, n_exp, CAP, columns)
         returned = [expert_out[:, 0]]
         for s in range(1, n_exp):

time: 99.1 us -> 104 us (1.049)
  matrix products: 5.16 us -> 10.2 us
  waiting for transfers between devices: 39.3 us -> 42.6 us
  local copies, waits for them, and re-layouts: 8.87 us -> 6.06 us
  other arithmetic: 2.77 us -> 1.61 us
    dot_general x2 -> x8, matrix products: 0.71 us -> 5.65 us  [the longest x6 5.19 us: layer(): jnp.dot(parts[s], down_parts[s], preferred_element_type=jnp.float32)]
    unnamed x21 -> x18, local copies, waits for them, and re-layouts: 2.83 us -> 0.74 us
    ppermute x3, waiting for transfers between devices: 2.99 us -> 4.79 us  [per_device(): lax.ppermute(down_parts[s], 'dp', [(i, dring.ahead(i, s)) for i in range(...]
    rsqrt x2, local copies, waits for them, and re-layouts: 1.44 us -> 0.17 us  [layer(): inv_rms = lax.rsqrt(squares + 1e-05)]
  transfers between devices with their start and end apart: 25 -> 25, of which waited for: 9 -> 10; matrix products, arithmetic and copies ran while one was open for 10% -> 6% of each run, Pallas kernels for 0% -> 0%
where the time goes in v8:
time: 104 us; the launch traced here: 103 us
  waiting for transfers between devices  42.6 us (41%)
  starting transfers between devices  41.7 us (40%)
  matrix products  10.2 us (10%)
  local copies, waits for them, and re-layouts  6.06 us (6%)
  other arithmetic  1.61 us (2%)
    ppermute x4, waiting for transfers between devices, per_device(): parts.append(lax.ppermute(cols, AXES, pairs))  29.7 us
    ppermute x6, starting transfers between devices, layer(): parts.append(lax.ppermute(hidden, AXES, dp_pairs(p, s)))  11.3 us
    ppermute x6, starting transfers between devices, layer(): lax.ppermute(outgoing[:, s], AXES, expert_pairs(p, s, False))  10.4 us
    ppermute x6, starting transfers between devices, layer(): lax.ppermute(expert_out[:, s], AXES, expert_pairs(p, s, True))  10.4 us
    dot_general x6, matrix products, layer(): jnp.dot(parts[s], down_parts[s], preferred_element_type=jnp.float32)  5.19 us
    ppermute x4, starting transfers between devices, per_device(): parts.append(lax.ppermute(cols, AXES, pairs))  5.17 us
    ppermute x3, waiting for transfers between devices, per_device(): lax.ppermute(down_parts[s], 'dp', [(i, dring.ahead(i, s)) for i in range(...  4.79 us
    ppermute x3, starting transfers between devices, per_device(): lax.ppermute(down_parts[s], 'dp', [(i, dring.ahead(i, s)) for i in range(...  4.51 us
  transfers between devices with their start and end apart: 25, of which 10 were waited for; matrix products, arithmetic and copies ran while one was open for 6% of the time, Pallas kernels for 0%

profile of v8, /device:TPU:1, one launch (start us, length us, event | category | flops | bytes accessed | tf_op | source)
XLA Modules:
  0.0 102.8 jit_solution(15932064326923406068)
XLA Ops:
  2.9 2.2 %dynamic-slice_bitcast_fusion = (bf16[176,768]{1,0:T(8,128)(2,1)}, bf16[176,768]{1,0:T(8,128)(2,1)}, bf16[176,768]{1,0:T(8,128)(2,1)S(1)}, bf16[176,768]{1,0:T(8,128)(2,1)}) fusion(bf16[1,1,176,3072]{3,2,1,0:T(8,128)(2,1)} %param.11, s32[]{:T(128)S(6)} %select_n.60, s32[]{:T(128)S(6)} %select_n.58, s32[]{:T(128)S(6)} %select_n.57, s32[]{:T(128)S(6)} %select_n.59), kind=kLoop, calls=%fused_computation.35 | loop fusion | bytes 2162704 | tf_op jit(solution)/shard_map/dynamic_slice | solution.py:74
  7.8 2.2 %collective-permute-start.4 = (bf16[176,768]{1,0:T(8,128)(2,1)}, bf16[176,768]{1,0:T(8,128)(2,1)}, u32[]{:S(2)}, u32[]{:S(2)}) collective-permute-start(bf16[176,768]{1,0:T(8,128)(2,1)} %get-tuple-element.12), channel_id=1, source_target_pairs={{0,8},{8,0},{16,24},{24,16},{1,9},{9,1},{17,25},{25,17},{2,10},{10... | collective-permute-start | bytes 811016 | tf_op jit(solution)/shard_map/ppermute | solution.py:78
  10.0 2.3 %collective-permute-start.6 = (bf16[176,768]{1,0:T(8,128)(2,1)}, bf16[176,768]{1,0:T(8,128)(2,1)S(1)}, u32[]{:S(2)}, u32[]{:S(2)}) collective-permute-start(bf16[176,768]{1,0:T(8,128)(2,1)} %get-tuple-element.13), channel_id=1, source_target_pairs={{0,16},{8,24},{16,0},{24,8},{1,17},{9,25},{17,1},{25,9},{2,18},{10... | collective-permute-start | bytes 811016 | tf_op jit(solution)/shard_map/ppermute | solution.py:78
  17.1 1.2 %convolution_add_fusion.3 = f32[128,768]{1,0:T(8,128)S(1)} fusion(f32[128,768]{1,0:T(8,128)S(1)} %fusion.26, bf16[128,176]{0,1:T(8,128)(2,1)S(1)} %collective-permute-done.3, bf16[176,768]{1,0:T(8,128)(2,1)} %collective-permute-done.4), kind=kOutput, calls=%fused_computation.8 | convolution fusion | flops 34701312 | bytes 1101824 | tf_op jit(solution)/shard_map/dot_general | solution.py:106
  18.3 4.3 %collective-permute-done.8 = bf16[176,768]{1,0:T(8,128)(2,1)} collective-permute-done((bf16[176,768]{1,0:T(8,128)(2,1)}, bf16[176,768]{1,0:T(8,128)(2,1)}, u32[]{:S(2)}, u32[]{:S(2)}) %collective-permute-start.8) | collective-permute-done | bytes 270368 | tf_op jit(solution)/shard_map/ppermute | solution.py:78
  27.3 1.3 %collective-permute-start.15 = (bf16[2,24,768]{2,1,0:T(8,128)(2,1)S(1)}, bf16[2,24,768]{2,1,0:T(8,128)(2,1)S(1)}, u32[]{:S(2)}, u32[]{:S(2)}) collective-permute-start(bf16[2,24,768]{2,1,0:T(8,128)(2,1)S(1)} %fusion.4), channel_id=1, source_target_pairs={{0,28},{1,29},{2,30},{3,31},{8,20},{9,21},{10,22},{11,23},{16,12},... | collective-permute-start | bytes 221192 | tf_op jit(solution)/shard_map/ppermute | solution.py:138
  28.6 1.3 %collective-permute-start.14 = (bf16[2,24,768]{2,1,0:T(8,128)(2,1)S(1)}, bf16[2,24,768]{2,1,0:T(8,128)(2,1)S(1)}, u32[]{:S(2)}, u32[]{:S(2)}) collective-permute-start(bf16[2,24,768]{2,1,0:T(8,128)(2,1)S(1)} %fusion.4), channel_id=1, source_target_pairs={{0,20},{1,21},{2,22},{3,23},{8,28},{9,29},{10,30},{11,31},{16,4},{... | collective-permute-start | bytes 221192 | tf_op jit(solution)/shard_map/ppermute | solution.py:138
  29.9 1.3 %collective-permute-start.13 = (bf16[2,24,768]{2,1,0:T(8,128)(2,1)S(1)}, bf16[2,24,768]{2,1,0:T(8,128)(2,1)S(1)}, u32[]{:S(2)}, u32[]{:S(2)}) collective-permute-start(bf16[2,24,768]{2,1,0:T(8,128)(2,1)S(1)} %fusion.4), channel_id=1, source_target_pairs={{0,12},{1,13},{2,14},{3,15},{8,4},{9,5},{10,6},{11,7},{16,28},{17,... | collective-permute-start | bytes 221192 | tf_op jit(solution)/shard_map/ppermute | solution.py:138
  31.2 1.3 %collective-permute-start.12 = (bf16[2,24,768]{2,1,0:T(8,128)(2,1)S(1)}, bf16[2,24,768]{2,1,0:T(8,128)(2,1)S(1)}, u32[]{:S(2)}, u32[]{:S(2)}) collective-permute-start(bf16[2,24,768]{2,1,0:T(8,128)(2,1)S(1)} %fusion.4), channel_id=1, source_target_pairs={{0,4},{1,5},{2,6},{3,7},{8,12},{9,13},{10,14},{11,15},{16,20},{17,... | collective-permute-start | bytes 221192 | tf_op jit(solution)/shard_map/ppermute | solution.py:138
  32.6 27.9 %collective-permute-done.15 = bf16[2,24,768]{2,1,0:T(8,128)(2,1)S(1)} collective-permute-done((bf16[2,24,768]{2,1,0:T(8,128)(2,1)S(1)}, bf16[2,24,768]{2,1,0:T(8,128)(2,1)S(1)}, u32[]{:S(2)}, u32[]{:S(2)}) %collective-permute-start.15) | collective-permute-done | bytes 73760 | tf_op jit(solution)/shard_map/ppermute | solution.py:138
  60.5 1.6 %collective-permute-done.14 = bf16[2,24,768]{2,1,0:T(8,128)(2,1)S(1)} collective-permute-done((bf16[2,24,768]{2,1,0:T(8,128)(2,1)S(1)}, bf16[2,24,768]{2,1,0:T(8,128)(2,1)S(1)}, u32[]{:S(2)}, u32[]{:S(2)}) %collective-permute-start.14) | collective-permute-done | bytes 73760 | tf_op jit(solution)/shard_map/ppermute | solution.py:138
  63.5 2.8 %collective-permute-start.17 = (bf16[2,16,3072]{2,1,0:T(8,128)(2,1)S(1)}, bf16[2,16,3072]{2,1,0:T(8,128)(2,1)S(1)}, u32[]{:S(2)}, u32[]{:S(2)}) collective-permute-start(bf16[2,16,3072]{2,1,0:T(8,128)(2,1)S(1)} %get-tuple-element.28), channel_id=1, source_target_pairs={{4,6},{5,7},{6,4},{7,5},{12,14},{13,15},{14,12},{15,13},{20,22},{2... | collective-permute-start | bytes 589832 | tf_op jit(solution)/shard_map/ppermute | solution.py:93
  66.3 2.4 %collective-permute-start.16 = (bf16[2,16,3072]{2,1,0:T(8,128)(2,1)S(1)}, bf16[2,16,3072]{2,1,0:T(8,128)(2,1)S(1)}, u32[]{:S(2)}, u32[]{:S(2)}) collective-permute-start(bf16[2,16,3072]{2,1,0:T(8,128)(2,1)S(1)} %get-tuple-element.29), channel_id=1, source_target_pairs={{4,5},{5,4},{6,7},{7,6},{12,13},{13,12},{14,15},{15,14},{20,21},{2... | collective-permute-start | bytes 589832 | tf_op jit(solution)/shard_map/ppermute | solution.py:93
  68.8 3.1 %collective-permute-start.18 = (bf16[2,16,3072]{2,1,0:T(8,128)(2,1)S(1)}, bf16[2,16,3072]{2,1,0:T(8,128)(2,1)S(1)}, u32[]{:S(2)}, u32[]{:S(2)}) collective-permute-start(bf16[2,16,3072]{2,1,0:T(8,128)(2,1)S(1)} %get-tuple-element.30), channel_id=1, source_target_pairs={{4,7},{5,6},{6,5},{7,4},{12,15},{13,14},{14,13},{15,12},{20,23},{2... | collective-permute-start | bytes 589832 | tf_op jit(solution)/shard_map/ppermute | solution.py:93
  72.7 3.4 %collective-permute-done.18 = bf16[2,16,3072]{2,1,0:T(8,128)(2,1)S(1)} collective-permute-done((bf16[2,16,3072]{2,1,0:T(8,128)(2,1)S(1)}, bf16[2,16,3072]{2,1,0:T(8,128)(2,1)S(1)}, u32[]{:S(2)}, u32[]{:S(2)}) %collective-permute-start.18) | collective-permute-done | bytes 196640 | tf_op jit(solution)/shard_map/ppermute | solution.py:93
  77.3 3.6 %collective-permute-start.21 = (bf16[128,176]{0,1:T(8,128)(2,1)S(1)}, bf16[128,176]{0,1:T(8,128)(2,1)S(1)}, u32[]{:S(2)}, u32[]{:S(2)}) collective-permute-start(bf16[128,176]{0,1:T(8,128)(2,1)S(1)} %fusion.11), channel_id=1, source_target_pairs={{4,28},{5,29},{6,30},{7,31},{12,20},{13,21},{14,22},{15,23},{20,12... | collective-permute-start | bytes 135176 | tf_op jit(solution)/shard_map/ppermute | solution.py:103
  80.9 2.8 %collective-permute-start.20 = (bf16[128,176]{0,1:T(8,128)(2,1)S(1)}, bf16[128,176]{0,1:T(8,128)(2,1)S(1)}, u32[]{:S(2)}, u32[]{:S(2)}) collective-permute-start(bf16[128,176]{0,1:T(8,128)(2,1)S(1)} %fusion.11), channel_id=1, source_target_pairs={{4,20},{5,21},{6,22},{7,23},{12,28},{13,29},{14,30},{15,31},{20,4}... | collective-permute-start | bytes 135176 | tf_op jit(solution)/shard_map/ppermute | solution.py:103
  83.7 2.9 %collective-permute-start.19 = (bf16[128,176]{0,1:T(8,128)(2,1)S(1)}, bf16[128,176]{0,1:T(8,128)(2,1)S(1)}, u32[]{:S(2)}, u32[]{:S(2)}) collective-permute-start(bf16[128,176]{0,1:T(8,128)(2,1)S(1)} %fusion.11), channel_id=1, source_target_pairs={{4,12},{5,13},{6,14},{7,15},{12,4},{13,5},{14,6},{15,7},{20,28},{2... | collective-permute-start | bytes 135176 | tf_op jit(solution)/shard_map/ppermute | solution.py:103
  86.9 1.6 %collective-permute-done.19 = bf16[128,176]{0,1:T(8,128)(2,1)S(1)} collective-permute-done((bf16[128,176]{0,1:T(8,128)(2,1)S(1)}, bf16[128,176]{0,1:T(8,128)(2,1)S(1)}, u32[]{:S(2)}, u32[]{:S(2)}) %collective-permute-start.19) | collective-permute-done | bytes 45088 | tf_op jit(solution)/shard_map/ppermute | solution.py:103
  88.5 1.2 %convolution_add_fusion.1 = f32[128,768]{1,0:T(8,128)S(1)} fusion(f32[128,768]{1,0:T(8,128)S(1)} %fusion.28, bf16[128,176]{0,1:T(8,128)(2,1)S(1)} %collective-permute-done.19, bf16[176,768]{1,0:T(8,128)(2,1)} %collective-permute-done.4), kind=kOutput, calls=%fused_computation.6 | convolution fusion | flops 34701312 | bytes 1101824 | tf_op jit(solution)/shard_map/dot_general | solution.py:106
  91.2 2.8 %collective-permute-start.22 = (bf16[2,16,768]{2,1,0:T(8,128)(2,1)S(1)}, bf16[2,16,768]{2,1,0:T(8,128)(2,1)S(1)}, u32[]{:S(2)}, u32[]{:S(2)}) collective-permute-start(bf16[2,16,768]{2,1,0:T(8,128)(2,1)S(1)} %get-tuple-element.36), channel_id=1, source_target_pairs={{4,5},{5,4},{6,7},{7,6},{12,13},{13,12},{14,15},{15,14},{20,21},{2... | collective-permute-start | bytes 147464 | tf_op jit(solution)/shard_map/ppermute | solution.py:114
  94.0 3.0 %collective-permute-start.24 = (bf16[2,16,768]{2,1,0:T(8,128)(2,1)S(1)}, bf16[2,16,768]{2,1,0:T(8,128)(2,1)S(1)}, u32[]{:S(2)}, u32[]{:S(2)}) collective-permute-start(bf16[2,16,768]{2,1,0:T(8,128)(2,1)S(1)} %get-tuple-element.37), channel_id=1, source_target_pairs={{4,7},{5,6},{6,5},{7,4},{12,15},{13,14},{14,13},{15,12},{20,23},{2... | collective-permute-start | bytes 147464 | tf_op jit(solution)/shard_map/ppermute | solution.py:114
  97.1 2.5 %collective-permute-start.23 = (bf16[2,16,768]{2,1,0:T(8,128)(2,1)S(1)}, bf16[2,16,768]{2,1,0:T(8,128)(2,1)S(1)}, u32[]{:S(2)}, u32[]{:S(2)}) collective-permute-start(bf16[2,16,768]{2,1,0:T(8,128)(2,1)S(1)} %get-tuple-element.38), channel_id=1, source_target_pairs={{4,6},{5,7},{6,4},{7,5},{12,14},{13,15},{14,12},{15,13},{20,22},{2... | collective-permute-start | bytes 147464 | tf_op jit(solution)/shard_map/ppermute | solution.py:114
  99.7 2.1 %collective-permute-done.23 = bf16[2,16,768]{2,1,0:T(8,128)(2,1)S(1)} collective-permute-done((bf16[2,16,768]{2,1,0:T(8,128)(2,1)S(1)}, bf16[2,16,768]{2,1,0:T(8,128)(2,1)S(1)}, u32[]{:S(2)}, u32[]{:S(2)}) %collective-permute-start.23) | collective-permute-done | bytes 49184 | tf_op jit(solution)/shard_map/ppermute | solution.py:114
  (98 shorter events, 21.1 us)
Async XLA Ops:
  5.7 6.6 %collective-permute-start.1 = (bf16[2,16,3072]{2,1,0:T(8,128)(2,1)S(1)}, bf16[2,16,3072]{2,1,0:T(8,128)(2,1)S(1)}, u32[]{:S(2)}, u32[]{:S(2)}) collective-permute-start(bf16[2,16,3072]{2,1,0:T(8,128)(2,1)S(1)} %get-tuple-element.32), channel_id=1, source_target_pairs={{0,2},{1,3},{2,0},{3,1},{8,10},{9,11},{10,8},{11,9},{16,18},{17,19... | collective-permute-start | bytes 589832 | tf_op jit(solution)/shard_map/ppermute | solution.py:93
  6.4 6.0 %collective-permute-start = (bf16[2,16,3072]{2,1,0:T(8,128)(2,1)S(1)}, bf16[2,16,3072]{2,1,0:T(8,128)(2,1)S(1)}, u32[]{:S(2)}, u32[]{:S(2)}) collective-permute-start(bf16[2,16,3072]{2,1,0:T(8,128)(2,1)S(1)} %get-tuple-element.33), channel_id=1, source_target_pairs={{0,1},{1,0},{2,3},{3,2},{8,9},{9,8},{10,11},{11,10},{16,17},{17,16... | collective-permute-start | bytes 589832 | tf_op jit(solution)/shard_map/ppermute | solution.py:93
  7.1 5.3 %collective-permute-start.2 = (bf16[2,16,3072]{2,1,0:T(8,128)(2,1)S(1)}, bf16[2,16,3072]{2,1,0:T(8,128)(2,1)S(1)}, u32[]{:S(2)}, u32[]{:S(2)}) collective-permute-start(bf16[2,16,3072]{2,1,0:T(8,128)(2,1)S(1)} %get-tuple-element.34), channel_id=1, source_target_pairs={{0,3},{1,2},{2,1},{3,0},{8,11},{9,10},{10,9},{11,8},{16,19},{17,18... | collective-permute-start | bytes 589832 | tf_op jit(solution)/shard_map/ppermute | solution.py:93
  7.8 9.3 %collective-permute-start.4 = (bf16[176,768]{1,0:T(8,128)(2,1)}, bf16[176,768]{1,0:T(8,128)(2,1)}, u32[]{:S(2)}, u32[]{:S(2)}) collective-permute-start(bf16[176,768]{1,0:T(8,128)(2,1)} %get-tuple-element.12), channel_id=1, source_target_pairs={{0,8},{8,0},{16,24},{24,16},{1,9},{9,1},{17,25},{25,17},{2,10},{10... | collective-permute-start | bytes 811016 | tf_op jit(solution)/shard_map/ppermute | solution.py:78
  10.0 13.8 %collective-permute-start.6 = (bf16[176,768]{1,0:T(8,128)(2,1)}, bf16[176,768]{1,0:T(8,128)(2,1)S(1)}, u32[]{:S(2)}, u32[]{:S(2)}) collective-permute-start(bf16[176,768]{1,0:T(8,128)(2,1)} %get-tuple-element.13), channel_id=1, source_target_pairs={{0,16},{8,24},{16,0},{24,8},{1,17},{9,25},{17,1},{25,9},{2,18},{10... | collective-permute-start | bytes 811016 | tf_op jit(solution)/shard_map/ppermute | solution.py:78
  12.3 10.2 %collective-permute-start.8 = (bf16[176,768]{1,0:T(8,128)(2,1)}, bf16[176,768]{1,0:T(8,128)(2,1)}, u32[]{:S(2)}, u32[]{:S(2)}) collective-permute-start(bf16[176,768]{1,0:T(8,128)(2,1)} %get-tuple-element.14), channel_id=1, source_target_pairs={{0,24},{8,16},{16,8},{24,0},{1,25},{9,17},{17,9},{25,1},{2,26},{10... | collective-permute-start | bytes 811016 | tf_op jit(solution)/shard_map/ppermute | solution.py:78
  14.3 4.0 %collective-permute-start.7 = (bf16[128,176]{0,1:T(8,128)(2,1)S(1)}, bf16[128,176]{0,1:T(8,128)(2,1)S(1)}, u32[]{:S(2)}, u32[]{:S(2)}) collective-permute-start(bf16[128,176]{0,1:T(8,128)(2,1)S(1)} %fusion.10), channel_id=1, source_target_pairs={{0,24},{1,25},{2,26},{3,27},{8,16},{9,17},{10,18},{11,19},{16,8},{... | collective-permute-start | bytes 135176 | tf_op jit(solution)/shard_map/ppermute | solution.py:103
  15.0 0.9 collective-permute-start.3
  15.9 7.8 %collective-permute-start.5 = (bf16[128,176]{0,1:T(8,128)(2,1)S(1)}, bf16[128,176]{0,1:T(8,128)(2,1)S(1)}, u32[]{:S(2)}, u32[]{:S(2)}) collective-permute-start(bf16[128,176]{0,1:T(8,128)(2,1)S(1)} %fusion.10), channel_id=1, source_target_pairs={{0,16},{1,17},{2,18},{3,19},{8,24},{9,25},{10,26},{11,27},{16,0},{... | collective-permute-start | bytes 135176 | tf_op jit(solution)/shard_map/ppermute | solution.py:103
  24.1 2.0 %collective-permute-start.9 = (bf16[2,16,768]{2,1,0:T(8,128)(2,1)S(1)}, bf16[2,16,768]{2,1,0:T(8,128)(2,1)S(1)}, u32[]{:S(2)}, u32[]{:S(2)}) collective-permute-start(bf16[2,16,768]{2,1,0:T(8,128)(2,1)S(1)} %get-tuple-element.40), channel_id=1, source_target_pairs={{0,1},{1,0},{2,3},{3,2},{8,9},{9,8},{10,11},{11,10},{16,17},{17,16... | collective-permute-start | bytes 147464 | tf_op jit(solution)/shard_map/ppermute | solution.py:114
  24.7 1.4 %collective-permute-start.11 = (bf16[2,16,768]{2,1,0:T(8,128)(2,1)S(1)}, bf16[2,16,768]{2,1,0:T(8,128)(2,1)S(1)}, u32[]{:S(2)}, u32[]{:S(2)}) collective-permute-start(bf16[2,16,768]{2,1,0:T(8,128)(2,1)S(1)} %get-tuple-element.41), channel_id=1, source_target_pairs={{0,3},{1,2},{2,1},{3,0},{8,11},{9,10},{10,9},{11,8},{16,19},{17,18... | collective-permute-start | bytes 147464 | tf_op jit(solution)/shard_map/ppermute | solution.py:114
  27.3 33.1 %collective-permute-start.15 = (bf16[2,24,768]{2,1,0:T(8,128)(2,1)S(1)}, bf16[2,24,768]{2,1,0:T(8,128)(2,1)S(1)}, u32[]{:S(2)}, u32[]{:S(2)}) collective-permute-start(bf16[2,24,768]{2,1,0:T(8,128)(2,1)S(1)} %fusion.4), channel_id=1, source_target_pairs={{0,28},{1,29},{2,30},{3,31},{8,20},{9,21},{10,22},{11,23},{16,12},... | collective-permute-start | bytes 221192 | tf_op jit(solution)/shard_map/ppermute | solution.py:138
  28.6 33.4 %collective-permute-start.14 = (bf16[2,24,768]{2,1,0:T(8,128)(2,1)S(1)}, bf16[2,24,768]{2,1,0:T(8,128)(2,1)S(1)}, u32[]{:S(2)}, u32[]{:S(2)}) collective-permute-start(bf16[2,24,768]{2,1,0:T(8,128)(2,1)S(1)} %fusion.4), channel_id=1, source_target_pairs={{0,20},{1,21},{2,22},{3,23},{8,28},{9,29},{10,30},{11,31},{16,4},{... | collective-permute-start | bytes 221192 | tf_op jit(solution)/shard_map/ppermute | solution.py:138
  29.9 32.1 %collective-permute-start.13 = (bf16[2,24,768]{2,1,0:T(8,128)(2,1)S(1)}, bf16[2,24,768]{2,1,0:T(8,128)(2,1)S(1)}, u32[]{:S(2)}, u32[]{:S(2)}) collective-permute-start(bf16[2,24,768]{2,1,0:T(8,128)(2,1)S(1)} %fusion.4), channel_id=1, source_target_pairs={{0,12},{1,13},{2,14},{3,15},{8,4},{9,5},{10,6},{11,7},{16,28},{17,... | collective-permute-start | bytes 221192 | tf_op jit(solution)/shard_map/ppermute | solution.py:138
  31.2 31.0 %collective-permute-start.12 = (bf16[2,24,768]{2,1,0:T(8,128)(2,1)S(1)}, bf16[2,24,768]{2,1,0:T(8,128)(2,1)S(1)}, u32[]{:S(2)}, u32[]{:S(2)}) collective-permute-start(bf16[2,24,768]{2,1,0:T(8,128)(2,1)S(1)} %fusion.4), channel_id=1, source_target_pairs={{0,4},{1,5},{2,6},{3,7},{8,12},{9,13},{10,14},{11,15},{16,20},{17,... | collective-permute-start | bytes 221192 | tf_op jit(solution)/shard_map/ppermute | solution.py:138
  63.5 8.4 %collective-permute-start.17 = (bf16[2,16,3072]{2,1,0:T(8,128)(2,1)S(1)}, bf16[2,16,3072]{2,1,0:T(8,128)(2,1)S(1)}, u32[]{:S(2)}, u32[]{:S(2)}) collective-permute-start(bf16[2,16,3072]{2,1,0:T(8,128)(2,1)S(1)} %get-tuple-element.28), channel_id=1, source_target_pairs={{4,6},{5,7},{6,4},{7,5},{12,14},{13,15},{14,12},{15,13},{20,22},{2... | collective-permute-start | bytes 589832 | tf_op jit(solution)/shard_map/ppermute | solution.py:93
  66.3 6.4 %collective-permute-start.16 = (bf16[2,16,3072]{2,1,0:T(8,128)(2,1)S(1)}, bf16[2,16,3072]{2,1,0:T(8,128)(2,1)S(1)}, u32[]{:S(2)}, u32[]{:S(2)}) collective-permute-start(bf16[2,16,3072]{2,1,0:T(8,128)(2,1)S(1)} %get-tuple-element.29), channel_id=1, source_target_pairs={{4,5},{5,4},{6,7},{7,6},{12,13},{13,12},{14,15},{15,14},{20,21},{2... | collective-permute-start | bytes 589832 | tf_op jit(solution)/shard_map/ppermute | solution.py:93
  68.8 7.3 %collective-permute-start.18 = (bf16[2,16,3072]{2,1,0:T(8,128)(2,1)S(1)}, bf16[2,16,3072]{2,1,0:T(8,128)(2,1)S(1)}, u32[]{:S(2)}, u32[]{:S(2)}) collective-permute-start(bf16[2,16,3072]{2,1,0:T(8,128)(2,1)S(1)} %get-tuple-element.30), channel_id=1, source_target_pairs={{4,7},{5,6},{6,5},{7,4},{12,15},{13,14},{14,13},{15,12},{20,23},{2... | collective-permute-start | bytes 589832 | tf_op jit(solution)/shard_map/ppermute | solution.py:93
  77.3 12.3 %collective-permute-start.21 = (bf16[128,176]{0,1:T(8,128)(2,1)S(1)}, bf16[128,176]{0,1:T(8,128)(2,1)S(1)}, u32[]{:S(2)}, u32[]{:S(2)}) collective-permute-start(bf16[128,176]{0,1:T(8,128)(2,1)S(1)} %fusion.11), channel_id=1, source_target_pairs={{4,28},{5,29},{6,30},{7,31},{12,20},{13,21},{14,22},{15,23},{20,12... | collective-permute-start | bytes 135176 | tf_op jit(solution)/shard_map/ppermute | solution.py:103
  80.9 10.0 %collective-permute-start.20 = (bf16[128,176]{0,1:T(8,128)(2,1)S(1)}, bf16[128,176]{0,1:T(8,128)(2,1)S(1)}, u32[]{:S(2)}, u32[]{:S(2)}) collective-permute-start(bf16[128,176]{0,1:T(8,128)(2,1)S(1)} %fusion.11), channel_id=1, source_target_pairs={{4,20},{5,21},{6,22},{7,23},{12,28},{13,29},{14,30},{15,31},{20,4}... | collective-permute-start | bytes 135176 | tf_op jit(solution)/shard_map/ppermute | solution.py:103
  83.7 4.8 %collective-permute-start.19 = (bf16[128,176]{0,1:T(8,128)(2,1)S(1)}, bf16[128,176]{0,1:T(8,128)(2,1)S(1)}, u32[]{:S(2)}, u32[]{:S(2)}) collective-permute-start(bf16[128,176]{0,1:T(8,128)(2,1)S(1)} %fusion.11), channel_id=1, source_target_pairs={{4,12},{5,13},{6,14},{7,15},{12,4},{13,5},{14,6},{15,7},{20,28},{2... | collective-permute-start | bytes 135176 | tf_op jit(solution)/shard_map/ppermute | solution.py:103
  91.2 8.4 %collective-permute-start.22 = (bf16[2,16,768]{2,1,0:T(8,128)(2,1)S(1)}, bf16[2,16,768]{2,1,0:T(8,128)(2,1)S(1)}, u32[]{:S(2)}, u32[]{:S(2)}) collective-permute-start(bf16[2,16,768]{2,1,0:T(8,128)(2,1)S(1)} %get-tuple-element.36), channel_id=1, source_target_pairs={{4,5},{5,4},{6,7},{7,6},{12,13},{13,12},{14,15},{15,14},{20,21},{2... | collective-permute-start | bytes 147464 | tf_op jit(solution)/shard_map/ppermute | solution.py:114
  94.0 5.7 %collective-permute-start.24 = (bf16[2,16,768]{2,1,0:T(8,128)(2,1)S(1)}, bf16[2,16,768]{2,1,0:T(8,128)(2,1)S(1)}, u32[]{:S(2)}, u32[]{:S(2)}) collective-permute-start(bf16[2,16,768]{2,1,0:T(8,128)(2,1)S(1)} %get-tuple-element.37), channel_id=1, source_target_pairs={{4,7},{5,6},{6,5},{7,4},{12,15},{13,14},{14,13},{15,12},{20,23},{2... | collective-permute-start | bytes 147464 | tf_op jit(solution)/shard_map/ppermute | solution.py:114
  97.1 4.8 %collective-permute-start.23 = (bf16[2,16,768]{2,1,0:T(8,128)(2,1)S(1)}, bf16[2,16,768]{2,1,0:T(8,128)(2,1)S(1)}, u32[]{:S(2)}, u32[]{:S(2)}) collective-permute-start(bf16[2,16,768]{2,1,0:T(8,128)(2,1)S(1)} %get-tuple-element.38), channel_id=1, source_target_pairs={{4,6},{5,7},{6,4},{7,5},{12,14},{13,15},{14,12},{15,13},{20,22},{2... | collective-permute-start | bytes 147464 | tf_op jit(solution)/shard_map/ppermute | solution.py:114
  (9 other events, 71.7 us)

commit v9 on v7

--- a/solution.py
+++ b/solution.py
@@ -85,6 +85,10 @@
     maps = [build_maps(route_ids[m], route_gates[m], ering, e_me, rows_all) for m in range(micro)]
     dispatch_map = jnp.stack([mp[0] for mp in maps])
     combine_map = jnp.stack([mp[1] for mp in maps])
+    if ering.xor:
+        combine_map = jnp.stack(
+            [build_maps(route_ids[m], route_gates[m], ering, 0, rows_all)[1] for m in range(micro)]
+        )
 
     def layer(current, p):
         outgoing = jnp.einsum("mrt,mtd->mrd", dispatch_map, current, preferred_element_type=jnp.float32)
@@ -107,10 +111,15 @@
             hidden_full = lax.all_gather(hidden, "dp", axis=1, tiled=True)
         expert_out = jnp.dot(hidden_full, down_full, preferred_element_type=jnp.float32).astype(jnp.bfloat16)
         expert_out = expert_out.reshape(micro, n_exp, CAP, columns)
-        returned = [expert_out[:, 0]]
-        for s in range(1, n_exp):
-            returned.append(lax.ppermute(expert_out[:, s], AXES, expert_pairs(p, s, True)))
-        returned = jnp.stack(returned, axis=1).reshape(micro, rows_all, columns)
+        if ering.xor:
+            order = jnp.stack([ering.place(j, e_me) for j in range(n_exp)])
+            by_block = jnp.take(expert_out, order, axis=1)
+            returned = lax.all_to_all(by_block, "expert", 1, 1, tiled=True).reshape(micro, rows_all, columns)
+        else:
+            returned = [expert_out[:, 0]]
+            for s in range(1, n_exp):
+                returned.append(lax.ppermute(expert_out[:, s], AXES, expert_pairs(p, s, True)))
+            returned = jnp.stack(returned, axis=1).reshape(micro, rows_all, columns)
         mixed = jnp.einsum(
             "mrt,mrc->mtc",
             combine_map,

time: 99.1 us -> 95.6 us (0.965)
  waiting for transfers between devices: 39.3 us -> 35 us
  other arithmetic: 2.77 us -> 4.39 us
  starting transfers between devices: 41.7 us -> 40.1 us
  local copies, waits for them, and re-layouts: 8.87 us -> 10.4 us
    ppermute x6 -> x0, starting transfers between devices: 10.4 us -> none  [layer(): lax.ppermute(expert_out[:, s], AXES, expert_pairs(p, s, True))]
    ppermute x4, waiting for transfers between devices: 28.9 us -> 20.3 us  [per_device(): parts.append(lax.ppermute(cols, AXES, pairs))]
    all_to_all x0 -> x2, waiting for transfers between devices: none -> 7.95 us  [layer(): lax.all_to_all(by_block, 'expert', 1, 1, tiled=True)]
    all_to_all x0 -> x2, starting transfers between devices: none -> 6.8 us  [layer(): lax.all_to_all(by_block, 'expert', 1, 1, tiled=True)]
    ppermute x6, starting transfers between devices: 10.4 us -> 12.4 us  [layer(): lax.ppermute(outgoing[:, s], AXES, expert_pairs(p, s, False))]
    ppermute x6 -> x0, waiting for transfers between devices: 1.7 us -> none  [layer(): lax.ppermute(expert_out[:, s], AXES, expert_pairs(p, s, True))]
    select_n x0 -> x2, other arithmetic: none -> 1.53 us  [layer(): by_block = jnp.take(expert_out, order, axis=1)]
    ppermute x3, waiting for transfers between devices: 2.99 us -> 1.51 us  [per_device(): lax.ppermute(down_parts[s], 'dp', [(i, dring.ahead(i, s)) for i in range(...]
  transfers between devices with their start and end apart: 25 -> 21, of which waited for: 9 -> 10; matrix products, arithmetic and copies ran while one was open for 10% -> 9% of each run, Pallas kernels for 0% -> 0%
where the time goes in v9:
time: 95.6 us; the launch traced here: 94.8 us
  starting transfers between devices  40.1 us (42%)
  waiting for transfers between devices  35 us (37%)
  local copies, waits for them, and re-layouts  10.4 us (11%)
  matrix products  4.43 us (5%)
  other arithmetic  4.39 us (5%)
    ppermute x4, waiting for transfers between devices, per_device(): parts.append(lax.ppermute(cols, AXES, pairs))  20.3 us
    ppermute x6, starting transfers between devices, layer(): lax.ppermute(outgoing[:, s], AXES, expert_pairs(p, s, False))  12.4 us
    ppermute x6, starting transfers between devices, layer(): parts.append(lax.ppermute(hidden, AXES, dp_pairs(p, s)))  11.3 us
    all_to_all x2, waiting for transfers between devices, layer(): lax.all_to_all(by_block, 'expert', 1, 1, tiled=True)  7.95 us
    all_to_all x2, starting transfers between devices, layer(): lax.all_to_all(by_block, 'expert', 1, 1, tiled=True)  6.8 us
    ppermute x4, starting transfers between devices, per_device(): parts.append(lax.ppermute(cols, AXES, pairs))  5.17 us
    ppermute x3, starting transfers between devices, per_device(): lax.ppermute(down_parts[s], 'dp', [(i, dring.ahead(i, s)) for i in range(...  4.51 us
    ppermute x6, waiting for transfers between devices, layer(): lax.ppermute(outgoing[:, s], AXES, expert_pairs(p, s, False))  3.84 us
  transfers between devices with their start and end apart: 21, of which 10 were waited for; matrix products, arithmetic and copies ran while one was open for 9% of the time, Pallas kernels for 0%

profile of v9, /device:TPU:1, one launch (start us, length us, event | category | flops | bytes accessed | tf_op | source)
XLA Modules:
  0.0 94.8 jit_solution(8418002353606631261)
XLA Ops:
  0.0 2.2 %dynamic-slice_bitcast_fusion = (bf16[176,768]{1,0:T(8,128)(2,1)}, bf16[176,768]{1,0:T(8,128)(2,1)}, bf16[176,768]{1,0:T(8,128)(2,1)S(1)}, bf16[176,768]{1,0:T(8,128)(2,1)}) fusion(bf16[1,1,176,3072]{3,2,1,0:T(8,128)(2,1)} %param.13, s32[]{:T(128)S(6)} %select_n.66, s32[]{:T(128)S(6)} %select_n.64, s32[]{:T(128)S(6)} %select_n.63, s32[]{:T(128)S(6)} %select_n.65), kind=kLoop, calls=%fused_computation.31 | loop fusion | bytes 2162704 | tf_op jit(solution)/shard_map/dynamic_slice | solution.py:74
  2.3 2.1 %collective-permute-start.6 = (bf16[176,768]{1,0:T(8,128)(2,1)}, bf16[176,768]{1,0:T(8,128)(2,1)}, u32[]{:S(2)}, u32[]{:S(2)}) collective-permute-start(bf16[176,768]{1,0:T(8,128)(2,1)} %get-tuple-element.13), channel_id=1, source_target_pairs={{0,8},{8,0},{16,24},{24,16},{1,9},{9,1},{17,25},{25,17},{2,10},{10... | collective-permute-start | bytes 811016 | tf_op jit(solution)/shard_map/ppermute | solution.py:78
  4.4 2.3 %collective-permute-start.7 = (bf16[176,768]{1,0:T(8,128)(2,1)}, bf16[176,768]{1,0:T(8,128)(2,1)}, u32[]{:S(2)}, u32[]{:S(2)}) collective-permute-start(bf16[176,768]{1,0:T(8,128)(2,1)} %get-tuple-element.14), channel_id=1, source_target_pairs={{0,16},{8,24},{16,0},{24,8},{1,17},{9,25},{17,1},{25,9},{2,18},{10... | collective-permute-start | bytes 811016 | tf_op jit(solution)/shard_map/ppermute | solution.py:78
  9.4 1.3 %collective-permute-start.2 = (bf16[2,16,3072]{2,1,0:T(8,128)(2,1)}, bf16[2,16,3072]{2,1,0:T(8,128)(2,1)}, u32[]{:S(2)}, u32[]{:S(2)}) collective-permute-start(bf16[2,16,3072]{2,1,0:T(8,128)(2,1)} %get-tuple-element.33), channel_id=1, source_target_pairs={{0,3},{1,2},{2,1},{3,0},{8,11},{9,10},{10,9},{11,8},{16,19},{17,18... | collective-permute-start | bytes 589832 | tf_op jit(solution)/shard_map/ppermute | solution.py:98
  10.8 1.3 %collective-permute-start.1 = (bf16[2,16,3072]{2,1,0:T(8,128)(2,1)S(1)}, bf16[2,16,3072]{2,1,0:T(8,128)(2,1)}, u32[]{:S(2)}, u32[]{:S(2)}) collective-permute-start(bf16[2,16,3072]{2,1,0:T(8,128)(2,1)S(1)} %get-tuple-element.31), channel_id=1, source_target_pairs={{0,2},{1,3},{2,0},{3,1},{8,10},{9,11},{10,8},{11,9},{16,18},{17,19... | collective-permute-start | bytes 589832 | tf_op jit(solution)/shard_map/ppermute | solution.py:98
  12.1 1.3 %collective-permute-start = (bf16[2,16,3072]{2,1,0:T(8,128)(2,1)S(1)}, bf16[2,16,3072]{2,1,0:T(8,128)(2,1)}, u32[]{:S(2)}, u32[]{:S(2)}) collective-permute-start(bf16[2,16,3072]{2,1,0:T(8,128)(2,1)S(1)} %get-tuple-element.32), channel_id=1, source_target_pairs={{0,1},{1,0},{2,3},{3,2},{8,9},{9,8},{10,11},{11,10},{16,17},{17,16... | collective-permute-start | bytes 589832 | tf_op jit(solution)/shard_map/ppermute | solution.py:98
  13.8 1.3 %multiply_reduce_fusion.1 = (f32[2,4,16]{2,1,0:T(4,128)S(1)}, bf16[2,4,16,3072]{3,2,1,0:T(8,128)(2,1)S(1)}) fusion(bf16[2,1,16,3072]{3,2,1,0:T(8,128)(2,1)} %bitcast.28, bf16[2,1,16,3072]{3,2,1,0:T(8,128)(2,1)} %bitcast.26, bf16[2,1,16,3072]{3,2,1,0:T(8,128)(2,1)} %bitcast.24, bf16[2,1,16,3072]{3,2,1,0:T(8,128)(2,1)S(1)} %get-tuple-element.30), kind=kLoop, calls=%fused_computation.6 | loop fusion | flops 2359168 | bytes 1573376 | tf_op jit(solution)/shard_map/reduce_sum | solution.py:100
  20.9 1.5 %collective-permute-done.8 = bf16[176,768]{1,0:T(8,128)(2,1)} collective-permute-done((bf16[176,768]{1,0:T(8,128)(2,1)}, bf16[176,768]{1,0:T(8,128)(2,1)}, u32[]{:S(2)}, u32[]{:S(2)}) %collective-permute-start.8) | collective-permute-done | bytes 270368 | tf_op jit(solution)/shard_map/ppermute | solution.py:78
  25.1 3.4 %all-to-all-start = ((bf16[2,4,16,768]{3,2,0,1:T(8,128)(2,1)}), bf16[2,4,16,768]{3,2,0,1:T(8,128)(2,1)S(1)}, u32[]{:S(2)}, u32[]{:S(2)}) async-start(bf16[2,4,16,768]{3,2,0,1:T(8,128)(2,1)} %select_bitcast_fusion.2), calls=%async_computation | async-start | bytes 393216 | tf_op jit(solution)/shard_map/all_to_all | solution.py:117
  28.7 3.9 %all-to-all-done = bf16[2,4,16,768]{3,2,0,1:T(8,128)(2,1)S(1)} async-done(((bf16[2,4,16,768]{3,2,0,1:T(8,128)(2,1)}), bf16[2,4,16,768]{3,2,0,1:T(8,128)(2,1)S(1)}, u32[]{:S(2)}, u32[]{:S(2)}) %all-to-all-start) | async-done | bytes 196640 | tf_op jit(solution)/shard_map/all_to_all | solution.py:117
  32.9 1.3 %collective-permute-start.12 = (bf16[2,24,768]{2,1,0:T(8,128)(2,1)S(1)}, bf16[2,24,768]{2,1,0:T(8,128)(2,1)S(1)}, u32[]{:S(2)}, u32[]{:S(2)}) collective-permute-start(bf16[2,24,768]{2,1,0:T(8,128)(2,1)S(1)} %fusion), channel_id=1, source_target_pairs={{0,28},{1,29},{2,30},{3,31},{8,20},{9,21},{10,22},{11,23},{16,12},... | collective-permute-start | bytes 221192 | tf_op jit(solution)/shard_map/ppermute | solution.py:145
  34.2 1.3 %collective-permute-start.11 = (bf16[2,24,768]{2,1,0:T(8,128)(2,1)S(1)}, bf16[2,24,768]{2,1,0:T(8,128)(2,1)S(1)}, u32[]{:S(2)}, u32[]{:S(2)}) collective-permute-start(bf16[2,24,768]{2,1,0:T(8,128)(2,1)S(1)} %fusion), channel_id=1, source_target_pairs={{0,20},{1,21},{2,22},{3,23},{8,28},{9,29},{10,30},{11,31},{16,4},{... | collective-permute-start | bytes 221192 | tf_op jit(solution)/shard_map/ppermute | solution.py:145
  35.5 1.3 %collective-permute-start.10 = (bf16[2,24,768]{2,1,0:T(8,128)(2,1)S(1)}, bf16[2,24,768]{2,1,0:T(8,128)(2,1)S(1)}, u32[]{:S(2)}, u32[]{:S(2)}) collective-permute-start(bf16[2,24,768]{2,1,0:T(8,128)(2,1)S(1)} %fusion), channel_id=1, source_target_pairs={{0,12},{1,13},{2,14},{3,15},{8,4},{9,5},{10,6},{11,7},{16,28},{17,... | collective-permute-start | bytes 221192 | tf_op jit(solution)/shard_map/ppermute | solution.py:145
  38.2 17.2 %collective-permute-done.12 = bf16[2,24,768]{2,1,0:T(8,128)(2,1)S(1)} collective-permute-done((bf16[2,24,768]{2,1,0:T(8,128)(2,1)S(1)}, bf16[2,24,768]{2,1,0:T(8,128)(2,1)S(1)}, u32[]{:S(2)}, u32[]{:S(2)}) %collective-permute-start.12) | collective-permute-done | bytes 73760 | tf_op jit(solution)/shard_map/ppermute | solution.py:145
  55.4 1.8 %collective-permute-done.11 = bf16[2,24,768]{2,1,0:T(8,128)(2,1)S(1)} collective-permute-done((bf16[2,24,768]{2,1,0:T(8,128)(2,1)S(1)}, bf16[2,24,768]{2,1,0:T(8,128)(2,1)S(1)}, u32[]{:S(2)}, u32[]{:S(2)}) %collective-permute-start.11) | collective-permute-done | bytes 73760 | tf_op jit(solution)/shard_map/ppermute | solution.py:145
  59.7 2.7 %collective-permute-start.15 = (bf16[2,16,3072]{2,1,0:T(8,128)(2,1)S(1)}, bf16[2,16,3072]{2,1,0:T(8,128)(2,1)S(1)}, u32[]{:S(2)}, u32[]{:S(2)}) collective-permute-start(bf16[2,16,3072]{2,1,0:T(8,128)(2,1)S(1)} %get-tuple-element.29), channel_id=1, source_target_pairs={{4,7},{5,6},{6,5},{7,4},{12,15},{13,14},{14,13},{15,12},{20,23},{2... | collective-permute-start | bytes 589832 | tf_op jit(solution)/shard_map/ppermute | solution.py:98
  62.4 3.1 %collective-permute-start.14 = (bf16[2,16,3072]{2,1,0:T(8,128)(2,1)S(1)}, bf16[2,16,3072]{2,1,0:T(8,128)(2,1)S(1)}, u32[]{:S(2)}, u32[]{:S(2)}) collective-permute-start(bf16[2,16,3072]{2,1,0:T(8,128)(2,1)S(1)} %get-tuple-element.27), channel_id=1, source_target_pairs={{4,6},{5,7},{6,4},{7,5},{12,14},{13,15},{14,12},{15,13},{20,22},{2... | collective-permute-start | bytes 589832 | tf_op jit(solution)/shard_map/ppermute | solution.py:98
  65.5 2.6 %collective-permute-start.13 = (bf16[2,16,3072]{2,1,0:T(8,128)(2,1)S(1)}, bf16[2,16,3072]{2,1,0:T(8,128)(2,1)S(1)}, u32[]{:S(2)}, u32[]{:S(2)}) collective-permute-start(bf16[2,16,3072]{2,1,0:T(8,128)(2,1)S(1)} %get-tuple-element.28), channel_id=1, source_target_pairs={{4,5},{5,4},{6,7},{7,6},{12,13},{13,12},{14,15},{15,14},{20,21},{2... | collective-permute-start | bytes 589832 | tf_op jit(solution)/shard_map/ppermute | solution.py:98
  69.1 2.8 %collective-permute-done.13 = bf16[2,16,3072]{2,1,0:T(8,128)(2,1)S(1)} collective-permute-done((bf16[2,16,3072]{2,1,0:T(8,128)(2,1)S(1)}, bf16[2,16,3072]{2,1,0:T(8,128)(2,1)S(1)}, u32[]{:S(2)}, u32[]{:S(2)}) %collective-permute-start.13) | collective-permute-done | bytes 196640 | tf_op jit(solution)/shard_map/ppermute | solution.py:98
  74.0 3.8 %collective-permute-start.18 = (bf16[128,176]{0,1:T(8,128)(2,1)S(1)}, bf16[128,176]{0,1:T(8,128)(2,1)S(1)}, u32[]{:S(2)}, u32[]{:S(2)}) collective-permute-start(bf16[128,176]{0,1:T(8,128)(2,1)S(1)} %fusion.7), channel_id=1, source_target_pairs={{4,28},{5,29},{6,30},{7,31},{12,20},{13,21},{14,22},{15,23},{20,12... | collective-permute-start | bytes 135176 | tf_op jit(solution)/shard_map/ppermute | solution.py:108
  77.8 1.9 %collective-permute-start.17 = (bf16[128,176]{0,1:T(8,128)(2,1)S(1)}, bf16[128,176]{0,1:T(8,128)(2,1)S(1)}, u32[]{:S(2)}, u32[]{:S(2)}) collective-permute-start(bf16[128,176]{0,1:T(8,128)(2,1)S(1)} %fusion.7), channel_id=1, source_target_pairs={{4,20},{5,21},{6,22},{7,23},{12,28},{13,29},{14,30},{15,31},{20,4}... | collective-permute-start | bytes 135176 | tf_op jit(solution)/shard_map/ppermute | solution.py:108
  79.7 3.6 %collective-permute-start.16 = (bf16[128,176]{0,1:T(8,128)(2,1)S(1)}, bf16[128,176]{0,1:T(8,128)(2,1)S(1)}, u32[]{:S(2)}, u32[]{:S(2)}) collective-permute-start(bf16[128,176]{0,1:T(8,128)(2,1)S(1)} %fusion.7), channel_id=1, source_target_pairs={{4,12},{5,13},{6,14},{7,15},{12,4},{13,5},{14,6},{15,7},{20,28},{2... | collective-permute-start | bytes 135176 | tf_op jit(solution)/shard_map/ppermute | solution.py:108
  86.5 3.4 %all-to-all-start.1 = ((bf16[2,4,16,768]{3,2,0,1:T(8,128)(2,1)}), bf16[2,4,16,768]{3,2,0,1:T(8,128)(2,1)S(1)}, u32[]{:S(2)}, u32[]{:S(2)}) async-start(bf16[2,4,16,768]{3,2,0,1:T(8,128)(2,1)} %select_bitcast_fusion.1), calls=%async_computation.1 | async-start | bytes 393216 | tf_op jit(solution)/shard_map/all_to_all | solution.py:117
  89.9 4.0 %all-to-all-done.1 = bf16[2,4,16,768]{3,2,0,1:T(8,128)(2,1)S(1)} async-done(((bf16[2,4,16,768]{3,2,0,1:T(8,128)(2,1)}), bf16[2,4,16,768]{3,2,0,1:T(8,128)(2,1)S(1)}, u32[]{:S(2)}, u32[]{:S(2)}) %all-to-all-start.1) | async-done | bytes 196640 | tf_op jit(solution)/shard_map/all_to_all | solution.py:117
  (93 shorter events, 22.7 us)
Async XLA Ops:
  0.0 15.2 %copy-start = (bf16[1,1,3072,176]{2,3,1,0:T(8,128)(2,1)S(1)}, bf16[1,1,3072,176]{2,3,1,0:T(8,128)(2,1)}, u32[]{:S(2)}) copy-start(bf16[1,1,3072,176]{2,3,1,0:T(8,128)(2,1)} %param.11) | copy-start | bytes 3244036
  2.3 16.0 %collective-permute-start.6 = (bf16[176,768]{1,0:T(8,128)(2,1)}, bf16[176,768]{1,0:T(8,128)(2,1)}, u32[]{:S(2)}, u32[]{:S(2)}) collective-permute-start(bf16[176,768]{1,0:T(8,128)(2,1)} %get-tuple-element.13), channel_id=1, source_target_pairs={{0,8},{8,0},{16,24},{24,16},{1,9},{9,1},{17,25},{25,17},{2,10},{10... | collective-permute-start | bytes 811016 | tf_op jit(solution)/shard_map/ppermute | solution.py:78
  4.4 15.6 %collective-permute-start.7 = (bf16[176,768]{1,0:T(8,128)(2,1)}, bf16[176,768]{1,0:T(8,128)(2,1)}, u32[]{:S(2)}, u32[]{:S(2)}) collective-permute-start(bf16[176,768]{1,0:T(8,128)(2,1)} %get-tuple-element.14), channel_id=1, source_target_pairs={{0,16},{8,24},{16,0},{24,8},{1,17},{9,25},{17,1},{25,9},{2,18},{10... | collective-permute-start | bytes 811016 | tf_op jit(solution)/shard_map/ppermute | solution.py:78
  9.4 4.2 %collective-permute-start.2 = (bf16[2,16,3072]{2,1,0:T(8,128)(2,1)}, bf16[2,16,3072]{2,1,0:T(8,128)(2,1)}, u32[]{:S(2)}, u32[]{:S(2)}) collective-permute-start(bf16[2,16,3072]{2,1,0:T(8,128)(2,1)} %get-tuple-element.33), channel_id=1, source_target_pairs={{0,3},{1,2},{2,1},{3,0},{8,11},{9,10},{10,9},{11,8},{16,19},{17,18... | collective-permute-start | bytes 589832 | tf_op jit(solution)/shard_map/ppermute | solution.py:98
  10.8 3.0 %collective-permute-start.1 = (bf16[2,16,3072]{2,1,0:T(8,128)(2,1)S(1)}, bf16[2,16,3072]{2,1,0:T(8,128)(2,1)}, u32[]{:S(2)}, u32[]{:S(2)}) collective-permute-start(bf16[2,16,3072]{2,1,0:T(8,128)(2,1)S(1)} %get-tuple-element.31), channel_id=1, source_target_pairs={{0,2},{1,3},{2,0},{3,1},{8,10},{9,11},{10,8},{11,9},{16,18},{17,19... | collective-permute-start | bytes 589832 | tf_op jit(solution)/shard_map/ppermute | solution.py:98
  12.1 1.6 %collective-permute-start = (bf16[2,16,3072]{2,1,0:T(8,128)(2,1)S(1)}, bf16[2,16,3072]{2,1,0:T(8,128)(2,1)}, u32[]{:S(2)}, u32[]{:S(2)}) collective-permute-start(bf16[2,16,3072]{2,1,0:T(8,128)(2,1)S(1)} %get-tuple-element.32), channel_id=1, source_target_pairs={{0,1},{1,0},{2,3},{3,2},{8,9},{9,8},{10,11},{11,10},{16,17},{17,16... | collective-permute-start | bytes 589832 | tf_op jit(solution)/shard_map/ppermute | solution.py:98
  13.5 10.8 %copy-start.6 = (pred[4]{0:T(512)(128)(4,1)}, pred[4]{0:T(512)(128)(4,1)S(1)}, u32[]{:S(2)}) copy-start(pred[4]{0:T(512)(128)(4,1)S(1)} %get-tuple-element.18) | copy-start | bytes 16
  13.7 8.8 %collective-permute-start.8 = (bf16[176,768]{1,0:T(8,128)(2,1)}, bf16[176,768]{1,0:T(8,128)(2,1)}, u32[]{:S(2)}, u32[]{:S(2)}) collective-permute-start(bf16[176,768]{1,0:T(8,128)(2,1)} %get-tuple-element.15), channel_id=1, source_target_pairs={{0,24},{8,16},{16,8},{24,0},{1,25},{9,17},{17,9},{25,1},{2,26},{10... | collective-permute-start | bytes 811016 | tf_op jit(solution)/shard_map/ppermute | solution.py:78
  16.9 6.5 %collective-permute-start.5 = (bf16[128,176]{0,1:T(8,128)(2,1)S(1)}, bf16[128,176]{0,1:T(8,128)(2,1)S(1)}, u32[]{:S(2)}, u32[]{:S(2)}) collective-permute-start(bf16[128,176]{0,1:T(8,128)(2,1)S(1)} %fusion.6), channel_id=1, source_target_pairs={{0,24},{1,25},{2,26},{3,27},{8,16},{9,17},{10,18},{11,19},{16,8},{... | collective-permute-start | bytes 135176 | tf_op jit(solution)/shard_map/ppermute | solution.py:108
  17.6 5.8 %collective-permute-start.4 = (bf16[128,176]{0,1:T(8,128)(2,1)S(1)}, bf16[128,176]{0,1:T(8,128)(2,1)S(1)}, u32[]{:S(2)}, u32[]{:S(2)}) collective-permute-start(bf16[128,176]{0,1:T(8,128)(2,1)S(1)} %fusion.6), channel_id=1, source_target_pairs={{0,16},{1,17},{2,18},{3,19},{8,24},{9,25},{10,26},{11,27},{16,0},{... | collective-permute-start | bytes 135176 | tf_op jit(solution)/shard_map/ppermute | solution.py:108
  18.3 5.1 %collective-permute-start.3 = (bf16[128,176]{0,1:T(8,128)(2,1)S(1)}, bf16[128,176]{0,1:T(8,128)(2,1)S(1)}, u32[]{:S(2)}, u32[]{:S(2)}) collective-permute-start(bf16[128,176]{0,1:T(8,128)(2,1)S(1)} %fusion.6), channel_id=1, source_target_pairs={{0,8},{1,9},{2,10},{3,11},{8,0},{9,1},{10,2},{11,3},{16,24},{17,25... | collective-permute-start | bytes 135176 | tf_op jit(solution)/shard_map/ppermute | solution.py:108
  25.1 7.5 %all-to-all-start = ((bf16[2,4,16,768]{3,2,0,1:T(8,128)(2,1)}), bf16[2,4,16,768]{3,2,0,1:T(8,128)(2,1)S(1)}, u32[]{:S(2)}, u32[]{:S(2)}) async-start(bf16[2,4,16,768]{3,2,0,1:T(8,128)(2,1)} %select_bitcast_fusion.2), calls=%async_computation | async-start | bytes 393216 | tf_op jit(solution)/shard_map/all_to_all | solution.py:117
  32.9 22.5 %collective-permute-start.12 = (bf16[2,24,768]{2,1,0:T(8,128)(2,1)S(1)}, bf16[2,24,768]{2,1,0:T(8,128)(2,1)S(1)}, u32[]{:S(2)}, u32[]{:S(2)}) collective-permute-start(bf16[2,24,768]{2,1,0:T(8,128)(2,1)S(1)} %fusion), channel_id=1, source_target_pairs={{0,28},{1,29},{2,30},{3,31},{8,20},{9,21},{10,22},{11,23},{16,12},... | collective-permute-start | bytes 221192 | tf_op jit(solution)/shard_map/ppermute | solution.py:145
  34.2 23.0 %collective-permute-start.11 = (bf16[2,24,768]{2,1,0:T(8,128)(2,1)S(1)}, bf16[2,24,768]{2,1,0:T(8,128)(2,1)S(1)}, u32[]{:S(2)}, u32[]{:S(2)}) collective-permute-start(bf16[2,24,768]{2,1,0:T(8,128)(2,1)S(1)} %fusion), channel_id=1, source_target_pairs={{0,20},{1,21},{2,22},{3,23},{8,28},{9,29},{10,30},{11,31},{16,4},{... | collective-permute-start | bytes 221192 | tf_op jit(solution)/shard_map/ppermute | solution.py:145
  35.5 23.0 %collective-permute-start.10 = (bf16[2,24,768]{2,1,0:T(8,128)(2,1)S(1)}, bf16[2,24,768]{2,1,0:T(8,128)(2,1)S(1)}, u32[]{:S(2)}, u32[]{:S(2)}) collective-permute-start(bf16[2,24,768]{2,1,0:T(8,128)(2,1)S(1)} %fusion), channel_id=1, source_target_pairs={{0,12},{1,13},{2,14},{3,15},{8,4},{9,5},{10,6},{11,7},{16,28},{17,... | collective-permute-start | bytes 221192 | tf_op jit(solution)/shard_map/ppermute | solution.py:145
  36.8 21.7 %collective-permute-start.9 = (bf16[2,24,768]{2,1,0:T(8,128)(2,1)S(1)}, bf16[2,24,768]{2,1,0:T(8,128)(2,1)S(1)}, u32[]{:S(2)}, u32[]{:S(2)}) collective-permute-start(bf16[2,24,768]{2,1,0:T(8,128)(2,1)S(1)} %fusion), channel_id=1, source_target_pairs={{0,4},{1,5},{2,6},{3,7},{8,12},{9,13},{10,14},{11,15},{16,20},{17,... | collective-permute-start | bytes 221192 | tf_op jit(solution)/shard_map/ppermute | solution.py:145
  59.7 8.4 %collective-permute-start.15 = (bf16[2,16,3072]{2,1,0:T(8,128)(2,1)S(1)}, bf16[2,16,3072]{2,1,0:T(8,128)(2,1)S(1)}, u32[]{:S(2)}, u32[]{:S(2)}) collective-permute-start(bf16[2,16,3072]{2,1,0:T(8,128)(2,1)S(1)} %get-tuple-element.29), channel_id=1, source_target_pairs={{4,7},{5,6},{6,5},{7,4},{12,15},{13,14},{14,13},{15,12},{20,23},{2... | collective-permute-start | bytes 589832 | tf_op jit(solution)/shard_map/ppermute | solution.py:98
  62.4 6.7 %collective-permute-start.14 = (bf16[2,16,3072]{2,1,0:T(8,128)(2,1)S(1)}, bf16[2,16,3072]{2,1,0:T(8,128)(2,1)S(1)}, u32[]{:S(2)}, u32[]{:S(2)}) collective-permute-start(bf16[2,16,3072]{2,1,0:T(8,128)(2,1)S(1)} %get-tuple-element.27), channel_id=1, source_target_pairs={{4,6},{5,7},{6,4},{7,5},{12,14},{13,15},{14,12},{15,13},{20,22},{2... | collective-permute-start | bytes 589832 | tf_op jit(solution)/shard_map/ppermute | solution.py:98
  65.5 6.4 %collective-permute-start.13 = (bf16[2,16,3072]{2,1,0:T(8,128)(2,1)S(1)}, bf16[2,16,3072]{2,1,0:T(8,128)(2,1)S(1)}, u32[]{:S(2)}, u32[]{:S(2)}) collective-permute-start(bf16[2,16,3072]{2,1,0:T(8,128)(2,1)S(1)} %get-tuple-element.28), channel_id=1, source_target_pairs={{4,5},{5,4},{6,7},{7,6},{12,13},{13,12},{14,15},{15,14},{20,21},{2... | collective-permute-start | bytes 589832 | tf_op jit(solution)/shard_map/ppermute | solution.py:98
  74.0 11.8 %copy-start.7 = (pred[4]{0:T(512)(128)(4,1)S(1)}, pred[4]{0:T(512)(128)(4,1)}, u32[]{:S(2)}) copy-start(pred[4]{0:T(512)(128)(4,1)} %copy-done.6) | copy-start | bytes 16
  74.0 9.3 %collective-permute-start.18 = (bf16[128,176]{0,1:T(8,128)(2,1)S(1)}, bf16[128,176]{0,1:T(8,128)(2,1)S(1)}, u32[]{:S(2)}, u32[]{:S(2)}) collective-permute-start(bf16[128,176]{0,1:T(8,128)(2,1)S(1)} %fusion.7), channel_id=1, source_target_pairs={{4,28},{5,29},{6,30},{7,31},{12,20},{13,21},{14,22},{15,23},{20,12... | collective-permute-start | bytes 135176 | tf_op jit(solution)/shard_map/ppermute | solution.py:108
  77.8 5.7 %collective-permute-start.17 = (bf16[128,176]{0,1:T(8,128)(2,1)S(1)}, bf16[128,176]{0,1:T(8,128)(2,1)S(1)}, u32[]{:S(2)}, u32[]{:S(2)}) collective-permute-start(bf16[128,176]{0,1:T(8,128)(2,1)S(1)} %fusion.7), channel_id=1, source_target_pairs={{4,20},{5,21},{6,22},{7,23},{12,28},{13,29},{14,30},{15,31},{20,4}... | collective-permute-start | bytes 135176 | tf_op jit(solution)/shard_map/ppermute | solution.py:108
  79.7 5.0 %collective-permute-start.16 = (bf16[128,176]{0,1:T(8,128)(2,1)S(1)}, bf16[128,176]{0,1:T(8,128)(2,1)S(1)}, u32[]{:S(2)}, u32[]{:S(2)}) collective-permute-start(bf16[128,176]{0,1:T(8,128)(2,1)S(1)} %fusion.7), channel_id=1, source_target_pairs={{4,12},{5,13},{6,14},{7,15},{12,4},{13,5},{14,6},{15,7},{20,28},{2... | collective-permute-start | bytes 135176 | tf_op jit(solution)/shard_map/ppermute | solution.py:108
  86.5 7.4 %all-to-all-start.1 = ((bf16[2,4,16,768]{3,2,0,1:T(8,128)(2,1)}), bf16[2,4,16,768]{3,2,0,1:T(8,128)(2,1)S(1)}, u32[]{:S(2)}, u32[]{:S(2)}) async-start(bf16[2,4,16,768]{3,2,0,1:T(8,128)(2,1)} %select_bitcast_fusion.1), calls=%async_computation.1 | async-start | bytes 393216 | tf_op jit(solution)/shard_map/all_to_all | solution.py:117
  (6 other events, 32.7 us)

commit v10 on v9

--- a/solution.py
+++ b/solution.py
@@ -86,17 +86,20 @@
     dispatch_map = jnp.stack([mp[0] for mp in maps])
     combine_map = jnp.stack([mp[1] for mp in maps])
     if ering.xor:
-        combine_map = jnp.stack(
-            [build_maps(route_ids[m], route_gates[m], ering, 0, rows_all)[1] for m in range(micro)]
-        )
+        maps = [build_maps(route_ids[m], route_gates[m], ering, 0, rows_all) for m in range(micro)]
+        dispatch_map = jnp.stack([mp[0] for mp in maps])
+        combine_map = jnp.stack([mp[1] for mp in maps])
 
     def layer(current, p):
         outgoing = jnp.einsum("mrt,mtd->mrd", dispatch_map, current, preferred_element_type=jnp.float32)
         outgoing = outgoing.astype(jnp.bfloat16).reshape(micro, n_exp, CAP, width)
-        arrived = [outgoing[:, 0]]
-        for s in range(1, n_exp):
-            arrived.append(lax.ppermute(outgoing[:, s], AXES, expert_pairs(p, s, False)))
-        flat_rows = jnp.stack(arrived, axis=1).reshape(-1, width)
+        if ering.xor:
+            flat_rows = lax.all_to_all(outgoing, "expert", 1, 1, tiled=True).reshape(-1, width)
+        else:
+            arrived = [outgoing[:, 0]]
+            for s in range(1, n_exp):
+                arrived.append(lax.ppermute(outgoing[:, s], AXES, expert_pairs(p, s, False)))
+            flat_rows = jnp.stack(arrived, axis=1).reshape(-1, width)
         squares = jnp.mean(jnp.square(flat_rows.astype(jnp.float32)), axis=1, keepdims=True)
         inv_rms = lax.rsqrt(squares + 1e-05)
         gate_act = jnp.dot(flat_rows, gate_local, preferred_element_type=jnp.float32) * inv_rms
@@ -112,9 +115,7 @@
         expert_out = jnp.dot(hidden_full, down_full, preferred_element_type=jnp.float32).astype(jnp.bfloat16)
         expert_out = expert_out.reshape(micro, n_exp, CAP, columns)
         if ering.xor:
-            order = jnp.stack([ering.place(j, e_me) for j in range(n_exp)])
-            by_block = jnp.take(expert_out, order, axis=1)
-            returned = lax.all_to_all(by_block, "expert", 1, 1, tiled=True).reshape(micro, rows_all, columns)
+            returned = lax.all_to_all(expert_out, "expert", 1, 1, tiled=True).reshape(micro, rows_all, columns)
         else:
             returned = [expert_out[:, 0]]
             for s in range(1, n_exp):

time: 95.6 us -> 104 us (1.088)
  blocking collectives: 0 us -> 12.3 us
  waiting for transfers between devices: 35 us -> 44.4 us
  starting transfers between devices: 40.1 us -> 31.3 us
  other arithmetic: 4.39 us -> 1.56 us
  local copies, waits for them, and re-layouts: 10.4 us -> 8.92 us
    ppermute x6 -> x0, starting transfers between devices: 12.4 us -> none  [layer(): lax.ppermute(outgoing[:, s], AXES, expert_pairs(p, s, False))]
    all_to_all x0 -> x1, blocking collectives: none -> 12.3 us  [layer(): lax.all_to_all(outgoing, 'expert', 1, 1, tiled=True).reshape(-1, width)]
    ppermute x3, waiting for transfers between devices: 1.51 us -> 13.3 us  [per_device(): lax.ppermute(down_parts[s], 'dp', [(i, dring.ahead(i, s)) for i in range(...]
    all_to_all x2 -> x3, starting transfers between devices: 6.8 us -> 11 us  [the longest x2 6.73 us: layer(): lax.all_to_all(expert_out, 'expert', 1, 1, tiled=True)]
    ppermute x6 -> x0, waiting for transfers between devices: 3.84 us -> none  [layer(): lax.ppermute(outgoing[:, s], AXES, expert_pairs(p, s, False))]
    reshape x0 -> x4, local copies, waits for them, and re-layouts: none -> 2.37 us  [the longest x2 1.36 us: layer(): expert_out = expert_out.reshape(micro, n_exp, CAP, columns)]
    unnamed x21 -> x19, local copies, waits for them, and re-layouts: 3.57 us -> 1.63 us
    select_n x2 -> x0, other arithmetic: 1.53 us -> none  [layer(): by_block = jnp.take(expert_out, order, axis=1)]
  transfers between devices with their start and end apart: 21 -> 16, of which waited for: 10 -> 10; matrix products, arithmetic and copies ran while one was open for 9% -> 2% of each run, Pallas kernels for 0% -> 0%
where the time goes in v10:
time: 104 us; the launch traced here: 103 us
  waiting for transfers between devices  44.4 us (43%)
  starting transfers between devices  31.3 us (30%)
  blocking collectives  12.3 us (12%)
  local copies, waits for them, and re-layouts  8.92 us (9%)
  matrix products  4.42 us (4%)
  other arithmetic  1.56 us (2%)
    ppermute x4, waiting for transfers between devices, per_device(): parts.append(lax.ppermute(cols, AXES, pairs))  21.7 us
    ppermute x3, waiting for transfers between devices, per_device(): lax.ppermute(down_parts[s], 'dp', [(i, dring.ahead(i, s)) for i in range(...  13.3 us
    all_to_all x1, blocking collectives, layer(): lax.all_to_all(outgoing, 'expert', 1, 1, tiled=True).reshape(-1, width)  12.3 us
    ppermute x6, starting transfers between devices, layer(): parts.append(lax.ppermute(hidden, AXES, dp_pairs(p, s)))  11.4 us
    all_to_all x2, waiting for transfers between devices, layer(): lax.all_to_all(expert_out, 'expert', 1, 1, tiled=True)  7.93 us
    all_to_all x2, starting transfers between devices, layer(): lax.all_to_all(expert_out, 'expert', 1, 1, tiled=True)  6.73 us
    ppermute x4, starting transfers between devices, per_device(): parts.append(lax.ppermute(cols, AXES, pairs))  5.17 us
    all_to_all x1, starting transfers between devices, layer(): lax.all_to_all(outgoing, 'expert', 1, 1, tiled=True).reshape(-1, width)  4.27 us
  transfers between devices with their start and end apart: 16, of which 10 were waited for; matrix products, arithmetic and copies ran while one was open for 2% of the time, Pallas kernels for 0%

profile of v10, /device:TPU:1, one launch (start us, length us, event | category | flops | bytes accessed | tf_op | source)
XLA Modules:
  0.0 103.3 jit_solution(5434581597183311634)
XLA Ops:
  0.0 2.2 %dynamic-slice_bitcast_fusion = (bf16[176,768]{1,0:T(8,128)(2,1)}, bf16[176,768]{1,0:T(8,128)(2,1)}, bf16[176,768]{1,0:T(8,128)(2,1)S(1)}, bf16[176,768]{1,0:T(8,128)(2,1)}) fusion(bf16[1,1,176,3072]{3,2,1,0:T(8,128)(2,1)} %param.11, s32[]{:T(128)S(6)} %select_n.60, s32[]{:T(128)S(6)} %select_n.58, s32[]{:T(128)S(6)} %select_n.57, s32[]{:T(128)S(6)} %select_n.59), kind=kLoop, calls=%fused_computation.27 | loop fusion | bytes 2162704 | tf_op jit(solution)/shard_map/dynamic_slice | solution.py:74
  4.3 0.9 copy.95
  5.2 4.3 %all-to-all-start = ((bf16[2,4,16,3072]{3,2,0,1:T(8,128)(2,1)}), bf16[2,4,16,3072]{3,2,0,1:T(8,128)(2,1)S(1)}, u32[]{:S(2)}, u32[]{:S(2)}) async-start(bf16[2,4,16,3072]{3,2,0,1:T(8,128)(2,1)} %copy.95), calls=%async_computation | async-start | bytes 1572864 | tf_op jit(solution)/shard_map/all_to_all | solution.py:97
  9.5 1.4 %collective-permute-start.3 = (bf16[176,768]{1,0:T(8,128)(2,1)}, bf16[176,768]{1,0:T(8,128)(2,1)S(1)}, u32[]{:S(2)}, u32[]{:S(2)}) collective-permute-start(bf16[176,768]{1,0:T(8,128)(2,1)} %get-tuple-element.12), channel_id=1, source_target_pairs={{0,8},{8,0},{16,24},{24,16},{1,9},{9,1},{17,25},{25,17},{2,10},{10... | collective-permute-start | bytes 811016 | tf_op jit(solution)/shard_map/ppermute | solution.py:78
  10.9 2.3 %collective-permute-start.4 = (bf16[176,768]{1,0:T(8,128)(2,1)}, bf16[176,768]{1,0:T(8,128)(2,1)S(1)}, u32[]{:S(2)}, u32[]{:S(2)}) collective-permute-start(bf16[176,768]{1,0:T(8,128)(2,1)} %get-tuple-element.13), channel_id=1, source_target_pairs={{0,16},{8,24},{16,0},{24,8},{1,17},{9,25},{17,1},{25,9},{2,18},{10... | collective-permute-start | bytes 811016 | tf_op jit(solution)/shard_map/ppermute | solution.py:78
  13.2 8.4 %collective-permute-done.3 = bf16[176,768]{1,0:T(8,128)(2,1)S(1)} collective-permute-done((bf16[176,768]{1,0:T(8,128)(2,1)}, bf16[176,768]{1,0:T(8,128)(2,1)S(1)}, u32[]{:S(2)}, u32[]{:S(2)}) %collective-permute-start.3) | collective-permute-done | bytes 270368 | tf_op jit(solution)/shard_map/ppermute | solution.py:78
  26.2 4.5 %collective-permute-done.5 = bf16[176,768]{1,0:T(8,128)(2,1)} collective-permute-done((bf16[176,768]{1,0:T(8,128)(2,1)}, bf16[176,768]{1,0:T(8,128)(2,1)}, u32[]{:S(2)}, u32[]{:S(2)}) %collective-permute-start.5) | collective-permute-done | bytes 270368 | tf_op jit(solution)/shard_map/ppermute | solution.py:78
  30.7 1.0 constant_dynamic-update-slice_fusion
  32.8 3.4 %all-to-all-start.1 = ((bf16[2,4,16,768]{3,2,0,1:T(8,128)(2,1)}), bf16[2,4,16,768]{3,2,0,1:T(8,128)(2,1)S(1)}, u32[]{:S(2)}, u32[]{:S(2)}) async-start(bf16[2,4,16,768]{3,2,0,1:T(8,128)(2,1)} %copy.98), calls=%async_computation.1 | async-start | bytes 393216 | tf_op jit(solution)/shard_map/all_to_all | solution.py:118
  36.3 3.9 %all-to-all-done.1 = bf16[2,4,16,768]{3,2,0,1:T(8,128)(2,1)S(1)} async-done(((bf16[2,4,16,768]{3,2,0,1:T(8,128)(2,1)}), bf16[2,4,16,768]{3,2,0,1:T(8,128)(2,1)S(1)}, u32[]{:S(2)}, u32[]{:S(2)}) %all-to-all-start.1) | async-done | bytes 196640 | tf_op jit(solution)/shard_map/all_to_all | solution.py:118
  40.4 1.3 %collective-permute-start.9 = (bf16[2,24,768]{2,1,0:T(8,128)(2,1)S(1)}, bf16[2,24,768]{2,1,0:T(8,128)(2,1)S(1)}, u32[]{:S(2)}, u32[]{:S(2)}) collective-permute-start(bf16[2,24,768]{2,1,0:T(8,128)(2,1)S(1)} %fusion), channel_id=1, source_target_pairs={{0,28},{1,29},{2,30},{3,31},{8,20},{9,21},{10,22},{11,23},{16,12},... | collective-permute-start | bytes 221192 | tf_op jit(solution)/shard_map/ppermute | solution.py:146
  41.7 1.3 %collective-permute-start.8 = (bf16[2,24,768]{2,1,0:T(8,128)(2,1)S(1)}, bf16[2,24,768]{2,1,0:T(8,128)(2,1)S(1)}, u32[]{:S(2)}, u32[]{:S(2)}) collective-permute-start(bf16[2,24,768]{2,1,0:T(8,128)(2,1)S(1)} %fusion), channel_id=1, source_target_pairs={{0,20},{1,21},{2,22},{3,23},{8,28},{9,29},{10,30},{11,31},{16,4},{... | collective-permute-start | bytes 221192 | tf_op jit(solution)/shard_map/ppermute | solution.py:146
  43.0 1.3 %collective-permute-start.7 = (bf16[2,24,768]{2,1,0:T(8,128)(2,1)S(1)}, bf16[2,24,768]{2,1,0:T(8,128)(2,1)S(1)}, u32[]{:S(2)}, u32[]{:S(2)}) collective-permute-start(bf16[2,24,768]{2,1,0:T(8,128)(2,1)S(1)} %fusion), channel_id=1, source_target_pairs={{0,12},{1,13},{2,14},{3,15},{8,4},{9,5},{10,6},{11,7},{16,28},{17,... | collective-permute-start | bytes 221192 | tf_op jit(solution)/shard_map/ppermute | solution.py:146
  44.3 1.3 %collective-permute-start.6 = (bf16[2,24,768]{2,1,0:T(8,128)(2,1)S(1)}, bf16[2,24,768]{2,1,0:T(8,128)(2,1)S(1)}, u32[]{:S(2)}, u32[]{:S(2)}) collective-permute-start(bf16[2,24,768]{2,1,0:T(8,128)(2,1)S(1)} %fusion), channel_id=1, source_target_pairs={{0,4},{1,5},{2,6},{3,7},{8,12},{9,13},{10,14},{11,15},{16,20},{17,... | collective-permute-start | bytes 221192 | tf_op jit(solution)/shard_map/ppermute | solution.py:146
  45.7 18.8 %collective-permute-done.9 = bf16[2,24,768]{2,1,0:T(8,128)(2,1)S(1)} collective-permute-done((bf16[2,24,768]{2,1,0:T(8,128)(2,1)S(1)}, bf16[2,24,768]{2,1,0:T(8,128)(2,1)S(1)}, u32[]{:S(2)}, u32[]{:S(2)}) %collective-permute-start.9) | collective-permute-done | bytes 73760 | tf_op jit(solution)/shard_map/ppermute | solution.py:146
  64.5 2.5 %collective-permute-done.8 = bf16[2,24,768]{2,1,0:T(8,128)(2,1)S(1)} collective-permute-done((bf16[2,24,768]{2,1,0:T(8,128)(2,1)S(1)}, bf16[2,24,768]{2,1,0:T(8,128)(2,1)S(1)}, u32[]{:S(2)}, u32[]{:S(2)}) %collective-permute-start.8) | collective-permute-done | bytes 73760 | tf_op jit(solution)/shard_map/ppermute | solution.py:146
  68.7 12.3 %all_to_all.20 = bf16[2,4,16,3072]{3,2,0,1:T(8,128)(2,1)S(1)} all-to-all(bf16[2,4,16,3072]{3,2,0,1:T(8,128)(2,1)S(1)} %copy.101), channel_id=1, replica_groups=mesh['dp'=4,'pipe'=2,'expert'=4] {'expert'}, dimensions={1} | all-to-all | bytes 1572864 | tf_op jit(solution)/shard_map/all_to_all | solution.py:97
  83.2 4.1 %collective-permute-start.12 = (bf16[128,176]{0,1:T(8,128)(2,1)S(1)}, bf16[128,176]{0,1:T(8,128)(2,1)S(1)}, u32[]{:S(2)}, u32[]{:S(2)}) collective-permute-start(bf16[128,176]{0,1:T(8,128)(2,1)S(1)} %fusion.7), channel_id=1, source_target_pairs={{4,28},{5,29},{6,30},{7,31},{12,20},{13,21},{14,22},{15,23},{20,12... | collective-permute-start | bytes 135176 | tf_op jit(solution)/shard_map/ppermute | solution.py:111
  87.3 1.9 %collective-permute-start.11 = (bf16[128,176]{0,1:T(8,128)(2,1)S(1)}, bf16[128,176]{0,1:T(8,128)(2,1)S(1)}, u32[]{:S(2)}, u32[]{:S(2)}) collective-permute-start(bf16[128,176]{0,1:T(8,128)(2,1)S(1)} %fusion.7), channel_id=1, source_target_pairs={{4,20},{5,21},{6,22},{7,23},{12,28},{13,29},{14,30},{15,31},{20,4}... | collective-permute-start | bytes 135176 | tf_op jit(solution)/shard_map/ppermute | solution.py:111
  89.2 3.4 %collective-permute-start.10 = (bf16[128,176]{0,1:T(8,128)(2,1)S(1)}, bf16[128,176]{0,1:T(8,128)(2,1)S(1)}, u32[]{:S(2)}, u32[]{:S(2)}) collective-permute-start(bf16[128,176]{0,1:T(8,128)(2,1)S(1)} %fusion.7), channel_id=1, source_target_pairs={{4,12},{5,13},{6,14},{7,15},{12,4},{13,5},{14,6},{15,7},{20,28},{2... | collective-permute-start | bytes 135176 | tf_op jit(solution)/shard_map/ppermute | solution.py:111
  93.2 0.9 collective-permute-done.10
  95.1 3.4 %all-to-all-start.3 = ((bf16[2,4,16,768]{3,2,0,1:T(8,128)(2,1)}), bf16[2,4,16,768]{3,2,0,1:T(8,128)(2,1)S(1)}, u32[]{:S(2)}, u32[]{:S(2)}) async-start(bf16[2,4,16,768]{3,2,0,1:T(8,128)(2,1)} %copy.104), calls=%async_computation.3 | async-start | bytes 393216 | tf_op jit(solution)/shard_map/all_to_all | solution.py:118
  98.4 4.0 %all-to-all-done.3 = bf16[2,4,16,768]{3,2,0,1:T(8,128)(2,1)S(1)} async-done(((bf16[2,4,16,768]{3,2,0,1:T(8,128)(2,1)}), bf16[2,4,16,768]{3,2,0,1:T(8,128)(2,1)S(1)}, u32[]{:S(2)}, u32[]{:S(2)}) %all-to-all-start.3) | async-done | bytes 196640 | tf_op jit(solution)/shard_map/all_to_all | solution.py:118
  102.5 0.9 fusion.5
  (79 shorter events, 13.3 us)
Async XLA Ops:
  0.0 22.5 %copy-start = (bf16[1,1,3072,176]{2,3,1,0:T(8,128)(2,1)S(1)}, bf16[1,1,3072,176]{2,3,1,0:T(8,128)(2,1)}, u32[]{:S(2)}) copy-start(bf16[1,1,3072,176]{2,3,1,0:T(8,128)(2,1)} %param.9) | copy-start | bytes 3244036
  0.0 2.3 %copy-start.7 = (f32[1,2,24,2]{2,3,1,0:T(2,128)S(1)}, f32[1,2,24,2]{2,3,1,0:T(2,128)}, u32[]{:S(2)}) copy-start(f32[1,2,24,2]{2,3,1,0:T(2,128)} %param.8) | copy-start | bytes 1156
  0.0 2.3 %copy-start.6 = (s32[1,2,24,2]{2,3,1,0:T(2,128)S(1)}, s32[1,2,24,2]{2,3,1,0:T(2,128)}, u32[]{:S(2)}) copy-start(s32[1,2,24,2]{2,3,1,0:T(2,128)} %param.7) | copy-start | bytes 1156
  0.0 3.8 %copy-start.3 = (bf16[2,24,3072]{2,1,0:T(8,128)(2,1)S(1)}, bf16[2,24,3072]{2,1,0:T(8,128)(2,1)}, u32[]{:S(2)}) copy-start(bf16[2,24,3072]{2,1,0:T(8,128)(2,1)} %param.6) | copy-start | bytes 884740
  5.2 16.8 %all-to-all-start = ((bf16[2,4,16,3072]{3,2,0,1:T(8,128)(2,1)}), bf16[2,4,16,3072]{3,2,0,1:T(8,128)(2,1)S(1)}, u32[]{:S(2)}, u32[]{:S(2)}) async-start(bf16[2,4,16,3072]{3,2,0,1:T(8,128)(2,1)} %copy.95), calls=%async_computation | async-start | bytes 1572864 | tf_op jit(solution)/shard_map/all_to_all | solution.py:97
  9.5 12.1 %collective-permute-start.3 = (bf16[176,768]{1,0:T(8,128)(2,1)}, bf16[176,768]{1,0:T(8,128)(2,1)S(1)}, u32[]{:S(2)}, u32[]{:S(2)}) collective-permute-start(bf16[176,768]{1,0:T(8,128)(2,1)} %get-tuple-element.12), channel_id=1, source_target_pairs={{0,8},{8,0},{16,24},{24,16},{1,9},{9,1},{17,25},{25,17},{2,10},{10... | collective-permute-start | bytes 811016 | tf_op jit(solution)/shard_map/ppermute | solution.py:78
  10.9 11.1 %collective-permute-start.4 = (bf16[176,768]{1,0:T(8,128)(2,1)}, bf16[176,768]{1,0:T(8,128)(2,1)S(1)}, u32[]{:S(2)}, u32[]{:S(2)}) collective-permute-start(bf16[176,768]{1,0:T(8,128)(2,1)} %get-tuple-element.13), channel_id=1, source_target_pairs={{0,16},{8,24},{16,0},{24,8},{1,17},{9,25},{17,1},{25,9},{2,18},{10... | collective-permute-start | bytes 811016 | tf_op jit(solution)/shard_map/ppermute | solution.py:78
  13.2 17.5 %collective-permute-start.5 = (bf16[176,768]{1,0:T(8,128)(2,1)}, bf16[176,768]{1,0:T(8,128)(2,1)}, u32[]{:S(2)}, u32[]{:S(2)}) collective-permute-start(bf16[176,768]{1,0:T(8,128)(2,1)} %get-tuple-element.14), channel_id=1, source_target_pairs={{0,24},{8,16},{16,8},{24,0},{1,25},{9,17},{17,9},{25,1},{2,26},{10... | collective-permute-start | bytes 811016 | tf_op jit(solution)/shard_map/ppermute | solution.py:78
  22.5 1.2 %copy-start.1 = (bf16[1,1,3072,176]{2,3,1,0:T(8,128)(2,1)S(1)}, bf16[1,1,3072,176]{2,3,1,0:T(8,128)(2,1)}, u32[]{:S(2)}) copy-start(bf16[1,1,3072,176]{2,3,1,0:T(8,128)(2,1)} %param.10) | copy-start | bytes 3244036
  24.2 7.5 %collective-permute-start.2 = (bf16[128,176]{0,1:T(8,128)(2,1)S(1)}, bf16[128,176]{0,1:T(8,128)(2,1)S(1)}, u32[]{:S(2)}, u32[]{:S(2)}) collective-permute-start(bf16[128,176]{0,1:T(8,128)(2,1)S(1)} %fusion.6), channel_id=1, source_target_pairs={{0,24},{1,25},{2,26},{3,27},{8,16},{9,17},{10,18},{11,19},{16,8},{... | collective-permute-start | bytes 135176 | tf_op jit(solution)/shard_map/ppermute | solution.py:111
  24.9 6.9 %collective-permute-start.1 = (bf16[128,176]{0,1:T(8,128)(2,1)S(1)}, bf16[128,176]{0,1:T(8,128)(2,1)S(1)}, u32[]{:S(2)}, u32[]{:S(2)}) collective-permute-start(bf16[128,176]{0,1:T(8,128)(2,1)S(1)} %fusion.6), channel_id=1, source_target_pairs={{0,16},{1,17},{2,18},{3,19},{8,24},{9,25},{10,26},{11,27},{16,0},{... | collective-permute-start | bytes 135176 | tf_op jit(solution)/shard_map/ppermute | solution.py:111
  25.5 6.2 %collective-permute-start = (bf16[128,176]{0,1:T(8,128)(2,1)S(1)}, bf16[128,176]{0,1:T(8,128)(2,1)S(1)}, u32[]{:S(2)}, u32[]{:S(2)}) collective-permute-start(bf16[128,176]{0,1:T(8,128)(2,1)S(1)} %fusion.6), channel_id=1, source_target_pairs={{0,8},{1,9},{2,10},{3,11},{8,0},{9,1},{10,2},{11,3},{16,24},{17,25... | collective-permute-start | bytes 135176 | tf_op jit(solution)/shard_map/ppermute | solution.py:111
  32.8 7.4 %all-to-all-start.1 = ((bf16[2,4,16,768]{3,2,0,1:T(8,128)(2,1)}), bf16[2,4,16,768]{3,2,0,1:T(8,128)(2,1)S(1)}, u32[]{:S(2)}, u32[]{:S(2)}) async-start(bf16[2,4,16,768]{3,2,0,1:T(8,128)(2,1)} %copy.98), calls=%async_computation.1 | async-start | bytes 393216 | tf_op jit(solution)/shard_map/all_to_all | solution.py:118
  40.4 27.0 %copy-start.4 = (bf16[2,24,768]{2,1,0:T(8,128)(2,1)}, bf16[2,24,768]{2,1,0:T(8,128)(2,1)S(1)}, u32[]{:S(2)}) copy-start(bf16[2,24,768]{2,1,0:T(8,128)(2,1)S(1)} %fusion) | copy-start | bytes 221188
  40.4 24.1 %collective-permute-start.9 = (bf16[2,24,768]{2,1,0:T(8,128)(2,1)S(1)}, bf16[2,24,768]{2,1,0:T(8,128)(2,1)S(1)}, u32[]{:S(2)}, u32[]{:S(2)}) collective-permute-start(bf16[2,24,768]{2,1,0:T(8,128)(2,1)S(1)} %fusion), channel_id=1, source_target_pairs={{0,28},{1,29},{2,30},{3,31},{8,20},{9,21},{10,22},{11,23},{16,12},... | collective-permute-start | bytes 221192 | tf_op jit(solution)/shard_map/ppermute | solution.py:146
  41.7 25.3 %collective-permute-start.8 = (bf16[2,24,768]{2,1,0:T(8,128)(2,1)S(1)}, bf16[2,24,768]{2,1,0:T(8,128)(2,1)S(1)}, u32[]{:S(2)}, u32[]{:S(2)}) collective-permute-start(bf16[2,24,768]{2,1,0:T(8,128)(2,1)S(1)} %fusion), channel_id=1, source_target_pairs={{0,20},{1,21},{2,22},{3,23},{8,28},{9,29},{10,30},{11,31},{16,4},{... | collective-permute-start | bytes 221192 | tf_op jit(solution)/shard_map/ppermute | solution.py:146
  43.0 24.4 %collective-permute-start.7 = (bf16[2,24,768]{2,1,0:T(8,128)(2,1)S(1)}, bf16[2,24,768]{2,1,0:T(8,128)(2,1)S(1)}, u32[]{:S(2)}, u32[]{:S(2)}) collective-permute-start(bf16[2,24,768]{2,1,0:T(8,128)(2,1)S(1)} %fusion), channel_id=1, source_target_pairs={{0,12},{1,13},{2,14},{3,15},{8,4},{9,5},{10,6},{11,7},{16,28},{17,... | collective-permute-start | bytes 221192 | tf_op jit(solution)/shard_map/ppermute | solution.py:146
  44.3 23.1 %collective-permute-start.6 = (bf16[2,24,768]{2,1,0:T(8,128)(2,1)S(1)}, bf16[2,24,768]{2,1,0:T(8,128)(2,1)S(1)}, u32[]{:S(2)}, u32[]{:S(2)}) collective-permute-start(bf16[2,24,768]{2,1,0:T(8,128)(2,1)S(1)} %fusion), channel_id=1, source_target_pairs={{0,4},{1,5},{2,6},{3,7},{8,12},{9,13},{10,14},{11,15},{16,20},{17,... | collective-permute-start | bytes 221192 | tf_op jit(solution)/shard_map/ppermute | solution.py:146
  81.5 1.2 %copy-start.2 = (bf16[1,1,3072,176]{2,3,1,0:T(8,128)(2,1)S(1)}, bf16[1,1,3072,176]{2,3,1,0:T(8,128)(2,1)}, u32[]{:S(2)}) copy-start(bf16[1,1,3072,176]{2,3,1,0:T(8,128)(2,1)} %param.10) | copy-start | bytes 3244036
  83.2 19.3 %copy-start.5 = (bf16[2,24,768]{2,1,0:T(8,128)(2,1)S(1)}, bf16[2,24,768]{2,1,0:T(8,128)(2,1)}, u32[]{:S(2)}) copy-start(bf16[2,24,768]{2,1,0:T(8,128)(2,1)} %copy-done.4) | copy-start | bytes 221188
  83.2 9.4 %collective-permute-start.12 = (bf16[128,176]{0,1:T(8,128)(2,1)S(1)}, bf16[128,176]{0,1:T(8,128)(2,1)S(1)}, u32[]{:S(2)}, u32[]{:S(2)}) collective-permute-start(bf16[128,176]{0,1:T(8,128)(2,1)S(1)} %fusion.7), channel_id=1, source_target_pairs={{4,28},{5,29},{6,30},{7,31},{12,20},{13,21},{14,22},{15,23},{20,12... | collective-permute-start | bytes 135176 | tf_op jit(solution)/shard_map/ppermute | solution.py:111
  87.3 5.9 %collective-permute-start.11 = (bf16[128,176]{0,1:T(8,128)(2,1)S(1)}, bf16[128,176]{0,1:T(8,128)(2,1)S(1)}, u32[]{:S(2)}, u32[]{:S(2)}) collective-permute-start(bf16[128,176]{0,1:T(8,128)(2,1)S(1)} %fusion.7), channel_id=1, source_target_pairs={{4,20},{5,21},{6,22},{7,23},{12,28},{13,29},{14,30},{15,31},{20,4}... | collective-permute-start | bytes 135176 | tf_op jit(solution)/shard_map/ppermute | solution.py:111
  89.2 4.8 %collective-permute-start.10 = (bf16[128,176]{0,1:T(8,128)(2,1)S(1)}, bf16[128,176]{0,1:T(8,128)(2,1)S(1)}, u32[]{:S(2)}, u32[]{:S(2)}) collective-permute-start(bf16[128,176]{0,1:T(8,128)(2,1)S(1)} %fusion.7), channel_id=1, source_target_pairs={{4,12},{5,13},{6,14},{7,15},{12,4},{13,5},{14,6},{15,7},{20,28},{2... | collective-permute-start | bytes 135176 | tf_op jit(solution)/shard_map/ppermute | solution.py:111
  95.1 7.4 %all-to-all-start.3 = ((bf16[2,4,16,768]{3,2,0,1:T(8,128)(2,1)}), bf16[2,4,16,768]{3,2,0,1:T(8,128)(2,1)S(1)}, u32[]{:S(2)}, u32[]{:S(2)}) async-start(bf16[2,4,16,768]{3,2,0,1:T(8,128)(2,1)} %copy.104), calls=%async_computation.3 | async-start | bytes 393216 | tf_op jit(solution)/shard_map/all_to_all | solution.py:118

commit v11 on v9

--- a/solution.py
+++ b/solution.py
@@ -97,6 +97,9 @@
         for s in range(1, n_exp):
             arrived.append(lax.ppermute(outgoing[:, s], AXES, expert_pairs(p, s, False)))
         flat_rows = jnp.stack(arrived, axis=1).reshape(-1, width)
+        down_use = down_full
+        if p == 0:
+            down_use, flat_rows = lax.optimization_barrier((down_full, flat_rows))
         squares = jnp.mean(jnp.square(flat_rows.astype(jnp.float32)), axis=1, keepdims=True)
         inv_rms = lax.rsqrt(squares + 1e-05)
         gate_act = jnp.dot(flat_rows, gate_local, preferred_element_type=jnp.float32) * inv_rms
@@ -109,7 +112,7 @@
             hidden_full = jnp.concatenate(parts, axis=1)
         else:
             hidden_full = lax.all_gather(hidden, "dp", axis=1, tiled=True)
-        expert_out = jnp.dot(hidden_full, down_full, preferred_element_type=jnp.float32).astype(jnp.bfloat16)
+        expert_out = jnp.dot(hidden_full, down_use, preferred_element_type=jnp.float32).astype(jnp.bfloat16)
         expert_out = expert_out.reshape(micro, n_exp, CAP, columns)
         if ering.xor:
             order = jnp.stack([ering.place(j, e_me) for j in range(n_exp)])

time: 95.6 us -> 99.9 us (1.045)
  waiting for transfers between devices: 35 us -> 40.5 us
  local copies, waits for them, and re-layouts: 10.4 us -> 9.13 us
    ppermute x3, waiting for transfers between devices: 1.51 us -> 5.35 us  [per_device(): lax.ppermute(down_parts[s], 'dp', [(i, dring.ahead(i, s)) for i in range(...]
    ppermute x4, waiting for transfers between devices: 20.3 us -> 21.9 us  [per_device(): parts.append(lax.ppermute(cols, AXES, pairs))]
    another operation x0 -> x1, other arithmetic: none -> 1.22 us  [layer(): flat_rows = jnp.stack(arrived, axis=1).reshape(-1, width)]
    reduce_sum x2, other arithmetic: 1.58 us -> 0.47 us  [layer(): jnp.mean(jnp.square(flat_rows.astype(jnp.float32)), axis=1, keepdims=True)]
    unnamed x21 -> x15, local copies, waits for them, and re-layouts: 3.57 us -> 3.53 us
  transfers between devices with their start and end apart: 21 -> 21, of which waited for: 10 -> 10; matrix products, arithmetic and copies ran while one was open for 9% -> 6% of each run, Pallas kernels for 0% -> 0%
where the time goes in v11:
time: 99.9 us; the launch traced here: 99.1 us
  waiting for transfers between devices  40.5 us (41%)
  starting transfers between devices  40.1 us (40%)
  local copies, waits for them, and re-layouts  9.13 us (9%)
  other arithmetic  4.48 us (4%)
  matrix products  4.44 us (4%)
    ppermute x4, waiting for transfers between devices, per_device(): parts.append(lax.ppermute(cols, AXES, pairs))  21.9 us
    ppermute x6, starting transfers between devices, layer(): lax.ppermute(outgoing[:, s], AXES, expert_pairs(p, s, False))  12.4 us
    ppermute x6, starting transfers between devices, layer(): parts.append(lax.ppermute(hidden, AXES, dp_pairs(p, s)))  11.3 us
    all_to_all x2, waiting for transfers between devices, layer(): lax.all_to_all(by_block, 'expert', 1, 1, tiled=True)  7.95 us
    all_to_all x2, starting transfers between devices, layer(): lax.all_to_all(by_block, 'expert', 1, 1, tiled=True)  6.8 us
    ppermute x3, waiting for transfers between devices, per_device(): lax.ppermute(down_parts[s], 'dp', [(i, dring.ahead(i, s)) for i in range(...  5.35 us
    ppermute x4, starting transfers between devices, per_device(): parts.append(lax.ppermute(cols, AXES, pairs))  5.17 us
    ppermute x3, starting transfers between devices, per_device(): lax.ppermute(down_parts[s], 'dp', [(i, dring.ahead(i, s)) for i in range(...  4.51 us
  transfers between devices with their start and end apart: 21, of which 10 were waited for; matrix products, arithmetic and copies ran while one was open for 6% of the time, Pallas kernels for 0%

profile of v11, /device:TPU:1, one launch (start us, length us, event | category | flops | bytes accessed | tf_op | source)
XLA Modules:
  0.0 99.1 jit_solution(4972003664022012331)
XLA Ops:
  0.0 2.1 %dynamic-slice_bitcast_fusion = (bf16[176,768]{1,0:T(8,128)(2,1)S(1)}, bf16[176,768]{1,0:T(8,128)(2,1)}, bf16[176,768]{1,0:T(8,128)(2,1)S(1)}, bf16[176,768]{1,0:T(8,128)(2,1)S(1)}) fusion(bf16[1,1,176,3072]{3,2,1,0:T(8,128)(2,1)} %param.13, s32[]{:T(128)S(6)} %select_n.66, s32[]{:T(128)S(6)} %select_n.64, s32[]{:T(128)S(6)} %select_n.63, s32[]{:T(128)S(6)} %select_n.65), kind=kLoop, calls=%fused_computation.31 | loop fusion | bytes 2162704 | tf_op jit(solution)/shard_map/dynamic_slice | solution.py:74
  2.1 2.1 %collective-permute-start = (bf16[176,768]{1,0:T(8,128)(2,1)}, bf16[176,768]{1,0:T(8,128)(2,1)}, u32[]{:S(2)}, u32[]{:S(2)}) collective-permute-start(bf16[176,768]{1,0:T(8,128)(2,1)} %get-tuple-element.15), channel_id=1, source_target_pairs={{0,8},{8,0},{16,24},{24,16},{1,9},{9,1},{17,25},{25,17},{2,10},{10... | collective-permute-start | bytes 811016 | tf_op jit(solution)/shard_map/ppermute | solution.py:78
  4.2 2.3 %collective-permute-start.1 = (bf16[176,768]{1,0:T(8,128)(2,1)S(1)}, bf16[176,768]{1,0:T(8,128)(2,1)}, u32[]{:S(2)}, u32[]{:S(2)}) collective-permute-start(bf16[176,768]{1,0:T(8,128)(2,1)S(1)} %get-tuple-element.16), channel_id=1, source_target_pairs={{0,16},{8,24},{16,0},{24,8},{1,17},{9,25},{17,1},{25,9},{2,18},{10... | collective-permute-start | bytes 811016 | tf_op jit(solution)/shard_map/ppermute | solution.py:78
  9.4 1.3 %collective-permute-start.5 = (bf16[2,16,3072]{2,1,0:T(8,128)(2,1)}, bf16[2,16,3072]{2,1,0:T(8,128)(2,1)}, u32[]{:S(2)}, u32[]{:S(2)}) collective-permute-start(bf16[2,16,3072]{2,1,0:T(8,128)(2,1)} %get-tuple-element.35), channel_id=1, source_target_pairs={{0,3},{1,2},{2,1},{3,0},{8,11},{9,10},{10,9},{11,8},{16,19},{17,18... | collective-permute-start | bytes 589832 | tf_op jit(solution)/shard_map/ppermute | solution.py:98
  10.7 1.3 %collective-permute-start.4 = (bf16[2,16,3072]{2,1,0:T(8,128)(2,1)}, bf16[2,16,3072]{2,1,0:T(8,128)(2,1)}, u32[]{:S(2)}, u32[]{:S(2)}) collective-permute-start(bf16[2,16,3072]{2,1,0:T(8,128)(2,1)} %get-tuple-element.33), channel_id=1, source_target_pairs={{0,2},{1,3},{2,0},{3,1},{8,10},{9,11},{10,8},{11,9},{16,18},{17,19... | collective-permute-start | bytes 589832 | tf_op jit(solution)/shard_map/ppermute | solution.py:98
  12.1 1.3 %collective-permute-start.3 = (bf16[2,16,3072]{2,1,0:T(8,128)(2,1)}, bf16[2,16,3072]{2,1,0:T(8,128)(2,1)}, u32[]{:S(2)}, u32[]{:S(2)}) collective-permute-start(bf16[2,16,3072]{2,1,0:T(8,128)(2,1)} %get-tuple-element.34), channel_id=1, source_target_pairs={{0,1},{1,0},{2,3},{3,2},{8,9},{9,8},{10,11},{11,10},{16,17},{17,16... | collective-permute-start | bytes 589832 | tf_op jit(solution)/shard_map/ppermute | solution.py:98
  14.9 1.7 %collective-permute-done = bf16[176,768]{1,0:T(8,128)(2,1)} collective-permute-done((bf16[176,768]{1,0:T(8,128)(2,1)}, bf16[176,768]{1,0:T(8,128)(2,1)}, u32[]{:S(2)}, u32[]{:S(2)}) %collective-permute-start) | collective-permute-done | bytes 270368 | tf_op jit(solution)/shard_map/ppermute | solution.py:78
  18.5 3.7 %collective-permute-done.2 = bf16[176,768]{1,0:T(8,128)(2,1)S(1)} collective-permute-done((bf16[176,768]{1,0:T(8,128)(2,1)S(1)}, bf16[176,768]{1,0:T(8,128)(2,1)S(1)}, u32[]{:S(2)}, u32[]{:S(2)}) %collective-permute-start.2) | collective-permute-done | bytes 270368 | tf_op jit(solution)/shard_map/ppermute | solution.py:78
  28.0 3.4 %all-to-all-start = ((bf16[2,4,16,768]{3,2,0,1:T(8,128)(2,1)}), bf16[2,4,16,768]{3,2,0,1:T(8,128)(2,1)S(1)}, u32[]{:S(2)}, u32[]{:S(2)}) async-start(bf16[2,4,16,768]{3,2,0,1:T(8,128)(2,1)} %select_bitcast_fusion.2), calls=%async_computation | async-start | bytes 393216 | tf_op jit(solution)/shard_map/all_to_all | solution.py:120
  31.5 3.9 %all-to-all-done = bf16[2,4,16,768]{3,2,0,1:T(8,128)(2,1)S(1)} async-done(((bf16[2,4,16,768]{3,2,0,1:T(8,128)(2,1)}), bf16[2,4,16,768]{3,2,0,1:T(8,128)(2,1)S(1)}, u32[]{:S(2)}, u32[]{:S(2)}) %all-to-all-start) | async-done | bytes 196640 | tf_op jit(solution)/shard_map/all_to_all | solution.py:120
  35.7 1.3 %collective-permute-start.12 = (bf16[2,24,768]{2,1,0:T(8,128)(2,1)S(1)}, bf16[2,24,768]{2,1,0:T(8,128)(2,1)S(1)}, u32[]{:S(2)}, u32[]{:S(2)}) collective-permute-start(bf16[2,24,768]{2,1,0:T(8,128)(2,1)S(1)} %fusion), channel_id=1, source_target_pairs={{0,28},{1,29},{2,30},{3,31},{8,20},{9,21},{10,22},{11,23},{16,12},... | collective-permute-start | bytes 221192 | tf_op jit(solution)/shard_map/ppermute | solution.py:148
  37.0 1.3 %collective-permute-start.11 = (bf16[2,24,768]{2,1,0:T(8,128)(2,1)S(1)}, bf16[2,24,768]{2,1,0:T(8,128)(2,1)S(1)}, u32[]{:S(2)}, u32[]{:S(2)}) collective-permute-start(bf16[2,24,768]{2,1,0:T(8,128)(2,1)S(1)} %fusion), channel_id=1, source_target_pairs={{0,20},{1,21},{2,22},{3,23},{8,28},{9,29},{10,30},{11,31},{16,4},{... | collective-permute-start | bytes 221192 | tf_op jit(solution)/shard_map/ppermute | solution.py:148
  38.3 1.3 %collective-permute-start.10 = (bf16[2,24,768]{2,1,0:T(8,128)(2,1)S(1)}, bf16[2,24,768]{2,1,0:T(8,128)(2,1)S(1)}, u32[]{:S(2)}, u32[]{:S(2)}) collective-permute-start(bf16[2,24,768]{2,1,0:T(8,128)(2,1)S(1)} %fusion), channel_id=1, source_target_pairs={{0,12},{1,13},{2,14},{3,15},{8,4},{9,5},{10,6},{11,7},{16,28},{17,... | collective-permute-start | bytes 221192 | tf_op jit(solution)/shard_map/ppermute | solution.py:148
  41.0 20.7 %collective-permute-done.12 = bf16[2,24,768]{2,1,0:T(8,128)(2,1)S(1)} collective-permute-done((bf16[2,24,768]{2,1,0:T(8,128)(2,1)S(1)}, bf16[2,24,768]{2,1,0:T(8,128)(2,1)S(1)}, u32[]{:S(2)}, u32[]{:S(2)}) %collective-permute-start.12) | collective-permute-done | bytes 73760 | tf_op jit(solution)/shard_map/ppermute | solution.py:148
  64.1 2.7 %collective-permute-start.15 = (bf16[2,16,3072]{2,1,0:T(8,128)(2,1)S(1)}, bf16[2,16,3072]{2,1,0:T(8,128)(2,1)S(1)}, u32[]{:S(2)}, u32[]{:S(2)}) collective-permute-start(bf16[2,16,3072]{2,1,0:T(8,128)(2,1)S(1)} %get-tuple-element.31), channel_id=1, source_target_pairs={{4,7},{5,6},{6,5},{7,4},{12,15},{13,14},{14,13},{15,12},{20,23},{2... | collective-permute-start | bytes 589832 | tf_op jit(solution)/shard_map/ppermute | solution.py:98
  66.8 3.1 %collective-permute-start.14 = (bf16[2,16,3072]{2,1,0:T(8,128)(2,1)S(1)}, bf16[2,16,3072]{2,1,0:T(8,128)(2,1)S(1)}, u32[]{:S(2)}, u32[]{:S(2)}) collective-permute-start(bf16[2,16,3072]{2,1,0:T(8,128)(2,1)S(1)} %get-tuple-element.29), channel_id=1, source_target_pairs={{4,6},{5,7},{6,4},{7,5},{12,14},{13,15},{14,12},{15,13},{20,22},{2... | collective-permute-start | bytes 589832 | tf_op jit(solution)/shard_map/ppermute | solution.py:98
  70.0 2.6 %collective-permute-start.13 = (bf16[2,16,3072]{2,1,0:T(8,128)(2,1)S(1)}, bf16[2,16,3072]{2,1,0:T(8,128)(2,1)S(1)}, u32[]{:S(2)}, u32[]{:S(2)}) collective-permute-start(bf16[2,16,3072]{2,1,0:T(8,128)(2,1)S(1)} %get-tuple-element.30), channel_id=1, source_target_pairs={{4,5},{5,4},{6,7},{7,6},{12,13},{13,12},{14,15},{15,14},{20,21},{2... | collective-permute-start | bytes 589832 | tf_op jit(solution)/shard_map/ppermute | solution.py:98
  73.6 2.8 %collective-permute-done.13 = bf16[2,16,3072]{2,1,0:T(8,128)(2,1)S(1)} collective-permute-done((bf16[2,16,3072]{2,1,0:T(8,128)(2,1)S(1)}, bf16[2,16,3072]{2,1,0:T(8,128)(2,1)S(1)}, u32[]{:S(2)}, u32[]{:S(2)}) %collective-permute-start.13) | collective-permute-done | bytes 196640 | tf_op jit(solution)/shard_map/ppermute | solution.py:98
  78.4 3.2 %collective-permute-start.18 = (bf16[128,176]{0,1:T(8,128)(2,1)S(1)}, bf16[128,176]{0,1:T(8,128)(2,1)S(1)}, u32[]{:S(2)}, u32[]{:S(2)}) collective-permute-start(bf16[128,176]{0,1:T(8,128)(2,1)S(1)} %fusion.7), channel_id=1, source_target_pairs={{4,28},{5,29},{6,30},{7,31},{12,20},{13,21},{14,22},{15,23},{20,12... | collective-permute-start | bytes 135176 | tf_op jit(solution)/shard_map/ppermute | solution.py:111
  81.7 2.2 %collective-permute-start.17 = (bf16[128,176]{0,1:T(8,128)(2,1)S(1)}, bf16[128,176]{0,1:T(8,128)(2,1)S(1)}, u32[]{:S(2)}, u32[]{:S(2)}) collective-permute-start(bf16[128,176]{0,1:T(8,128)(2,1)S(1)} %fusion.7), channel_id=1, source_target_pairs={{4,20},{5,21},{6,22},{7,23},{12,28},{13,29},{14,30},{15,31},{20,4}... | collective-permute-start | bytes 135176 | tf_op jit(solution)/shard_map/ppermute | solution.py:111
  83.9 3.8 %collective-permute-start.16 = (bf16[128,176]{0,1:T(8,128)(2,1)S(1)}, bf16[128,176]{0,1:T(8,128)(2,1)S(1)}, u32[]{:S(2)}, u32[]{:S(2)}) collective-permute-start(bf16[128,176]{0,1:T(8,128)(2,1)S(1)} %fusion.7), channel_id=1, source_target_pairs={{4,12},{5,13},{6,14},{7,15},{12,4},{13,5},{14,6},{15,7},{20,28},{2... | collective-permute-start | bytes 135176 | tf_op jit(solution)/shard_map/ppermute | solution.py:111
  87.8 1.3 %collective-permute-done.16 = bf16[128,176]{0,1:T(8,128)(2,1)S(1)} collective-permute-done((bf16[128,176]{0,1:T(8,128)(2,1)S(1)}, bf16[128,176]{0,1:T(8,128)(2,1)S(1)}, u32[]{:S(2)}, u32[]{:S(2)}) %collective-permute-start.16) | collective-permute-done | bytes 45088 | tf_op jit(solution)/shard_map/ppermute | solution.py:111
  90.9 3.4 %all-to-all-start.1 = ((bf16[2,4,16,768]{3,2,0,1:T(8,128)(2,1)}), bf16[2,4,16,768]{3,2,0,1:T(8,128)(2,1)S(1)}, u32[]{:S(2)}, u32[]{:S(2)}) async-start(bf16[2,4,16,768]{3,2,0,1:T(8,128)(2,1)} %select_bitcast_fusion.1), calls=%async_computation.1 | async-start | bytes 393216 | tf_op jit(solution)/shard_map/all_to_all | solution.py:120
  94.2 4.0 %all-to-all-done.1 = bf16[2,4,16,768]{3,2,0,1:T(8,128)(2,1)S(1)} async-done(((bf16[2,4,16,768]{3,2,0,1:T(8,128)(2,1)}), bf16[2,4,16,768]{3,2,0,1:T(8,128)(2,1)S(1)}, u32[]{:S(2)}, u32[]{:S(2)}) %all-to-all-start.1) | async-done | bytes 196640 | tf_op jit(solution)/shard_map/all_to_all | solution.py:120
  (87 shorter events, 21.7 us)
Async XLA Ops:
  0.0 22.5 %copy-start = (bf16[1,1,3072,176]{2,3,1,0:T(8,128)(2,1)S(1)}, bf16[1,1,3072,176]{2,3,1,0:T(8,128)(2,1)}, u32[]{:S(2)}) copy-start(bf16[1,1,3072,176]{2,3,1,0:T(8,128)(2,1)} %param.11) | copy-start | bytes 3244036
  0.0 6.5 %copy-start.4 = (s32[1,2,24,2]{2,3,1,0:T(2,128)S(1)}, s32[1,2,24,2]{2,3,1,0:T(2,128)}, u32[]{:S(2)}) copy-start(s32[1,2,24,2]{2,3,1,0:T(2,128)} %param.9) | copy-start | bytes 1156
  0.0 8.1 %copy-start.3 = (bf16[2,24,3072]{2,1,0:T(8,128)(2,1)S(1)}, bf16[2,24,3072]{2,1,0:T(8,128)(2,1)}, u32[]{:S(2)}) copy-start(bf16[2,24,3072]{2,1,0:T(8,128)(2,1)} %param.8) | copy-start | bytes 884740
  2.1 14.4 %collective-permute-start = (bf16[176,768]{1,0:T(8,128)(2,1)}, bf16[176,768]{1,0:T(8,128)(2,1)}, u32[]{:S(2)}, u32[]{:S(2)}) collective-permute-start(bf16[176,768]{1,0:T(8,128)(2,1)} %get-tuple-element.15), channel_id=1, source_target_pairs={{0,8},{8,0},{16,24},{24,16},{1,9},{9,1},{17,25},{25,17},{2,10},{10... | collective-permute-start | bytes 811016 | tf_op jit(solution)/shard_map/ppermute | solution.py:78
  4.2 13.3 %collective-permute-start.1 = (bf16[176,768]{1,0:T(8,128)(2,1)S(1)}, bf16[176,768]{1,0:T(8,128)(2,1)}, u32[]{:S(2)}, u32[]{:S(2)}) collective-permute-start(bf16[176,768]{1,0:T(8,128)(2,1)S(1)} %get-tuple-element.16), channel_id=1, source_target_pairs={{0,16},{8,24},{16,0},{24,8},{1,17},{9,25},{17,1},{25,9},{2,18},{10... | collective-permute-start | bytes 811016 | tf_op jit(solution)/shard_map/ppermute | solution.py:78
  9.4 4.1 %collective-permute-start.5 = (bf16[2,16,3072]{2,1,0:T(8,128)(2,1)}, bf16[2,16,3072]{2,1,0:T(8,128)(2,1)}, u32[]{:S(2)}, u32[]{:S(2)}) collective-permute-start(bf16[2,16,3072]{2,1,0:T(8,128)(2,1)} %get-tuple-element.35), channel_id=1, source_target_pairs={{0,3},{1,2},{2,1},{3,0},{8,11},{9,10},{10,9},{11,8},{16,19},{17,18... | collective-permute-start | bytes 589832 | tf_op jit(solution)/shard_map/ppermute | solution.py:98
  10.7 2.9 %collective-permute-start.4 = (bf16[2,16,3072]{2,1,0:T(8,128)(2,1)}, bf16[2,16,3072]{2,1,0:T(8,128)(2,1)}, u32[]{:S(2)}, u32[]{:S(2)}) collective-permute-start(bf16[2,16,3072]{2,1,0:T(8,128)(2,1)} %get-tuple-element.33), channel_id=1, source_target_pairs={{0,2},{1,3},{2,0},{3,1},{8,10},{9,11},{10,8},{11,9},{16,18},{17,19... | collective-permute-start | bytes 589832 | tf_op jit(solution)/shard_map/ppermute | solution.py:98
  12.1 1.6 %collective-permute-start.3 = (bf16[2,16,3072]{2,1,0:T(8,128)(2,1)}, bf16[2,16,3072]{2,1,0:T(8,128)(2,1)}, u32[]{:S(2)}, u32[]{:S(2)}) collective-permute-start(bf16[2,16,3072]{2,1,0:T(8,128)(2,1)} %get-tuple-element.34), channel_id=1, source_target_pairs={{0,1},{1,0},{2,3},{3,2},{8,9},{9,8},{10,11},{11,10},{16,17},{17,16... | collective-permute-start | bytes 589832 | tf_op jit(solution)/shard_map/ppermute | solution.py:98
  13.5 8.6 %collective-permute-start.2 = (bf16[176,768]{1,0:T(8,128)(2,1)S(1)}, bf16[176,768]{1,0:T(8,128)(2,1)S(1)}, u32[]{:S(2)}, u32[]{:S(2)}) collective-permute-start(bf16[176,768]{1,0:T(8,128)(2,1)S(1)} %get-tuple-element.17), channel_id=1, source_target_pairs={{0,24},{8,16},{16,8},{24,0},{1,25},{9,17},{17,9},{25,1},{2,26},{10... | collective-permute-start | bytes 811016 | tf_op jit(solution)/shard_map/ppermute | solution.py:78
  24.2 2.1 %collective-permute-start.8 = (bf16[128,176]{0,1:T(8,128)(2,1)S(1)}, bf16[128,176]{0,1:T(8,128)(2,1)S(1)}, u32[]{:S(2)}, u32[]{:S(2)}) collective-permute-start(bf16[128,176]{0,1:T(8,128)(2,1)S(1)} %fusion.6), channel_id=1, source_target_pairs={{0,24},{1,25},{2,26},{3,27},{8,16},{9,17},{10,18},{11,19},{16,8},{... | collective-permute-start | bytes 135176 | tf_op jit(solution)/shard_map/ppermute | solution.py:111
  24.8 1.4 %collective-permute-start.7 = (bf16[128,176]{0,1:T(8,128)(2,1)S(1)}, bf16[128,176]{0,1:T(8,128)(2,1)S(1)}, u32[]{:S(2)}, u32[]{:S(2)}) collective-permute-start(bf16[128,176]{0,1:T(8,128)(2,1)S(1)} %fusion.6), channel_id=1, source_target_pairs={{0,16},{1,17},{2,18},{3,19},{8,24},{9,25},{10,26},{11,27},{16,0},{... | collective-permute-start | bytes 135176 | tf_op jit(solution)/shard_map/ppermute | solution.py:111
  25.5 0.8 collective-permute-start.6
  28.0 7.5 %all-to-all-start = ((bf16[2,4,16,768]{3,2,0,1:T(8,128)(2,1)}), bf16[2,4,16,768]{3,2,0,1:T(8,128)(2,1)S(1)}, u32[]{:S(2)}, u32[]{:S(2)}) async-start(bf16[2,4,16,768]{3,2,0,1:T(8,128)(2,1)} %select_bitcast_fusion.2), calls=%async_computation | async-start | bytes 393216 | tf_op jit(solution)/shard_map/all_to_all | solution.py:120
  35.7 26.0 %collective-permute-start.12 = (bf16[2,24,768]{2,1,0:T(8,128)(2,1)S(1)}, bf16[2,24,768]{2,1,0:T(8,128)(2,1)S(1)}, u32[]{:S(2)}, u32[]{:S(2)}) collective-permute-start(bf16[2,24,768]{2,1,0:T(8,128)(2,1)S(1)} %fusion), channel_id=1, source_target_pairs={{0,28},{1,29},{2,30},{3,31},{8,20},{9,21},{10,22},{11,23},{16,12},... | collective-permute-start | bytes 221192 | tf_op jit(solution)/shard_map/ppermute | solution.py:148
  37.0 25.9 %collective-permute-start.11 = (bf16[2,24,768]{2,1,0:T(8,128)(2,1)S(1)}, bf16[2,24,768]{2,1,0:T(8,128)(2,1)S(1)}, u32[]{:S(2)}, u32[]{:S(2)}) collective-permute-start(bf16[2,24,768]{2,1,0:T(8,128)(2,1)S(1)} %fusion), channel_id=1, source_target_pairs={{0,20},{1,21},{2,22},{3,23},{8,28},{9,29},{10,30},{11,31},{16,4},{... | collective-permute-start | bytes 221192 | tf_op jit(solution)/shard_map/ppermute | solution.py:148
  38.3 24.6 %collective-permute-start.10 = (bf16[2,24,768]{2,1,0:T(8,128)(2,1)S(1)}, bf16[2,24,768]{2,1,0:T(8,128)(2,1)S(1)}, u32[]{:S(2)}, u32[]{:S(2)}) collective-permute-start(bf16[2,24,768]{2,1,0:T(8,128)(2,1)S(1)} %fusion), channel_id=1, source_target_pairs={{0,12},{1,13},{2,14},{3,15},{8,4},{9,5},{10,6},{11,7},{16,28},{17,... | collective-permute-start | bytes 221192 | tf_op jit(solution)/shard_map/ppermute | solution.py:148
  39.6 23.3 %collective-permute-start.9 = (bf16[2,24,768]{2,1,0:T(8,128)(2,1)S(1)}, bf16[2,24,768]{2,1,0:T(8,128)(2,1)S(1)}, u32[]{:S(2)}, u32[]{:S(2)}) collective-permute-start(bf16[2,24,768]{2,1,0:T(8,128)(2,1)S(1)} %fusion), channel_id=1, source_target_pairs={{0,4},{1,5},{2,6},{3,7},{8,12},{9,13},{10,14},{11,15},{16,20},{17,... | collective-permute-start | bytes 221192 | tf_op jit(solution)/shard_map/ppermute | solution.py:148
  64.1 8.4 %collective-permute-start.15 = (bf16[2,16,3072]{2,1,0:T(8,128)(2,1)S(1)}, bf16[2,16,3072]{2,1,0:T(8,128)(2,1)S(1)}, u32[]{:S(2)}, u32[]{:S(2)}) collective-permute-start(bf16[2,16,3072]{2,1,0:T(8,128)(2,1)S(1)} %get-tuple-element.31), channel_id=1, source_target_pairs={{4,7},{5,6},{6,5},{7,4},{12,15},{13,14},{14,13},{15,12},{20,23},{2... | collective-permute-start | bytes 589832 | tf_op jit(solution)/shard_map/ppermute | solution.py:98
  66.8 6.7 %collective-permute-start.14 = (bf16[2,16,3072]{2,1,0:T(8,128)(2,1)S(1)}, bf16[2,16,3072]{2,1,0:T(8,128)(2,1)S(1)}, u32[]{:S(2)}, u32[]{:S(2)}) collective-permute-start(bf16[2,16,3072]{2,1,0:T(8,128)(2,1)S(1)} %get-tuple-element.29), channel_id=1, source_target_pairs={{4,6},{5,7},{6,4},{7,5},{12,14},{13,15},{14,12},{15,13},{20,22},{2... | collective-permute-start | bytes 589832 | tf_op jit(solution)/shard_map/ppermute | solution.py:98
  70.0 6.4 %collective-permute-start.13 = (bf16[2,16,3072]{2,1,0:T(8,128)(2,1)S(1)}, bf16[2,16,3072]{2,1,0:T(8,128)(2,1)S(1)}, u32[]{:S(2)}, u32[]{:S(2)}) collective-permute-start(bf16[2,16,3072]{2,1,0:T(8,128)(2,1)S(1)} %get-tuple-element.30), channel_id=1, source_target_pairs={{4,5},{5,4},{6,7},{7,6},{12,13},{13,12},{14,15},{15,14},{20,21},{2... | collective-permute-start | bytes 589832 | tf_op jit(solution)/shard_map/ppermute | solution.py:98
  78.4 9.3 %collective-permute-start.18 = (bf16[128,176]{0,1:T(8,128)(2,1)S(1)}, bf16[128,176]{0,1:T(8,128)(2,1)S(1)}, u32[]{:S(2)}, u32[]{:S(2)}) collective-permute-start(bf16[128,176]{0,1:T(8,128)(2,1)S(1)} %fusion.7), channel_id=1, source_target_pairs={{4,28},{5,29},{6,30},{7,31},{12,20},{13,21},{14,22},{15,23},{20,12... | collective-permute-start | bytes 135176 | tf_op jit(solution)/shard_map/ppermute | solution.py:111
  81.7 6.2 %collective-permute-start.17 = (bf16[128,176]{0,1:T(8,128)(2,1)S(1)}, bf16[128,176]{0,1:T(8,128)(2,1)S(1)}, u32[]{:S(2)}, u32[]{:S(2)}) collective-permute-start(bf16[128,176]{0,1:T(8,128)(2,1)S(1)} %fusion.7), channel_id=1, source_target_pairs={{4,20},{5,21},{6,22},{7,23},{12,28},{13,29},{14,30},{15,31},{20,4}... | collective-permute-start | bytes 135176 | tf_op jit(solution)/shard_map/ppermute | solution.py:111
  83.9 5.3 %collective-permute-start.16 = (bf16[128,176]{0,1:T(8,128)(2,1)S(1)}, bf16[128,176]{0,1:T(8,128)(2,1)S(1)}, u32[]{:S(2)}, u32[]{:S(2)}) collective-permute-start(bf16[128,176]{0,1:T(8,128)(2,1)S(1)} %fusion.7), channel_id=1, source_target_pairs={{4,12},{5,13},{6,14},{7,15},{12,4},{13,5},{14,6},{15,7},{20,28},{2... | collective-permute-start | bytes 135176 | tf_op jit(solution)/shard_map/ppermute | solution.py:111
  90.9 7.4 %all-to-all-start.1 = ((bf16[2,4,16,768]{3,2,0,1:T(8,128)(2,1)}), bf16[2,4,16,768]{3,2,0,1:T(8,128)(2,1)S(1)}, u32[]{:S(2)}, u32[]{:S(2)}) async-start(bf16[2,4,16,768]{3,2,0,1:T(8,128)(2,1)} %select_bitcast_fusion.1), calls=%async_computation.1 | async-start | bytes 393216 | tf_op jit(solution)/shard_map/all_to_all | solution.py:120
  (3 other events, 7.5 us)

commit v12 on v9

--- a/solution.py
+++ b/solution.py
@@ -68,17 +68,10 @@
     up_local = w_up[0, 0]
     down_local = w_down[0, 0]
 
+    down_full = lax.all_to_all(down_local, "dp", 1, 0, tiled=True)
     if small_dp:
-        down_parts = []
-        for s in range(n_dp):
-            piece = lax.dynamic_slice_in_dim(down_local, dring.ahead(d_me, s) * columns, columns, 1)
-            down_parts.append(piece)
-        down_parts, tokens = lax.optimization_barrier((down_parts, tokens))
-        for s in range(1, n_dp):
-            down_parts[s] = lax.ppermute(down_parts[s], "dp", [(i, dring.ahead(i, s)) for i in range(n_dp)])
-        down_full = jnp.concatenate(down_parts, axis=0)
-    else:
-        down_full = lax.all_to_all(down_local, "dp", 1, 0, tiled=True)
+        order = jnp.stack([dring.behind(d_me, s) for s in range(n_dp)])
+        down_full = jnp.take(down_full.reshape(n_dp, units, columns), order, axis=0).reshape(n_dp * units, columns)
 
     route_ids = expert_ids[0]
     route_gates = gates[0]

time: 95.6 us -> 103 us (1.077)
  other arithmetic: 4.39 us -> 7.45 us
  starting transfers between devices: 40.1 us -> 41.7 us
  matrix products: 4.43 us -> 5.92 us
    all_to_all x0 -> x1, waiting for transfers between devices: none -> 8.45 us  [per_device(): down_full = lax.all_to_all(down_local, 'dp', 1, 0, tiled=True)]
    ppermute x4, waiting for transfers between devices: 20.3 us -> 13.3 us  [per_device(): parts.append(lax.ppermute(cols, AXES, pairs))]
    all_to_all x0 -> x1, starting transfers between devices: none -> 5.55 us  [per_device(): down_full = lax.all_to_all(down_local, 'dp', 1, 0, tiled=True)]
    ppermute x3 -> x0, starting transfers between devices: 4.51 us -> none  [per_device(): lax.ppermute(down_parts[s], 'dp', [(i, dring.ahead(i, s)) for i in range(...]
    all_to_all x0 -> x2, local copies, waits for them, and re-layouts: none -> 3.07 us  [per_device(): down_full = lax.all_to_all(down_local, 'dp', 1, 0, tiled=True)]
    dynamic_slice x1 -> x0, local copies, waits for them, and re-layouts: 2.25 us -> none  [per_device(): lax.dynamic_slice_in_dim(down_local, dring.ahead(d_me, s) * columns, colu...]
    ppermute x6, starting transfers between devices: 11.3 us -> 13.1 us  [layer(): parts.append(lax.ppermute(hidden, AXES, dp_pairs(p, s)))]
    ppermute x3 -> x0, waiting for transfers between devices: 1.51 us -> none  [per_device(): lax.ppermute(down_parts[s], 'dp', [(i, dring.ahead(i, s)) for i in range(...]
  transfers between devices with their start and end apart: 21 -> 19, of which waited for: 10 -> 9; matrix products, arithmetic and copies ran while one was open for 9% -> 10% of each run, Pallas kernels for 0% -> 0%
where the time goes in v12:
time: 103 us; the launch traced here: 102 us
  starting transfers between devices  41.7 us (40%)
  waiting for transfers between devices  34.9 us (34%)
  local copies, waits for them, and re-layouts  11.3 us (11%)
  other arithmetic  7.45 us (7%)
  matrix products  5.92 us (6%)
    ppermute x4, waiting for transfers between devices, per_device(): parts.append(lax.ppermute(cols, AXES, pairs))  13.3 us
    ppermute x6, starting transfers between devices, layer(): parts.append(lax.ppermute(hidden, AXES, dp_pairs(p, s)))  13.1 us
    ppermute x6, starting transfers between devices, layer(): lax.ppermute(outgoing[:, s], AXES, expert_pairs(p, s, False))  11.1 us
    all_to_all x1, waiting for transfers between devices, per_device(): down_full = lax.all_to_all(down_local, 'dp', 1, 0, tiled=True)  8.45 us
    all_to_all x2, waiting for transfers between devices, layer(): lax.all_to_all(by_block, 'expert', 1, 1, tiled=True)  7.93 us
    all_to_all x2, starting transfers between devices, layer(): lax.all_to_all(by_block, 'expert', 1, 1, tiled=True)  6.8 us
    all_to_all x1, starting transfers between devices, per_device(): down_full = lax.all_to_all(down_local, 'dp', 1, 0, tiled=True)  5.55 us
    ppermute x4, starting transfers between devices, per_device(): parts.append(lax.ppermute(cols, AXES, pairs))  5.17 us
  transfers between devices with their start and end apart: 19, of which 9 were waited for; matrix products, arithmetic and copies ran while one was open for 10% of the time, Pallas kernels for 0%

profile of v12, /device:TPU:1, one launch (start us, length us, event | category | flops | bytes accessed | tf_op | source)
XLA Modules:
  0.0 101.7 jit_solution(8005355392059099570)
XLA Ops:
  0.0 2.0 %all_to_all.18 = bf16[176,4,768]{2,1,0:T(4,128)(2,1)S(1)} reshape(bf16[1,1,176,3072]{3,2,1,0:T(8,128)(2,1)} %param.13) | data formatting | bytes 2162688 | tf_op jit(solution)/shard_map/all_to_all | solution.py:71
  3.1 5.6 %all-to-all-start = ((bf16[176,4,768]{2,0,1:T(8,128)(2,1)}), bf16[176,4,768]{2,0,1:T(8,128)(2,1)S(1)}, u32[]{:S(2)}, u32[]{:S(2)}) async-start(bf16[176,4,768]{2,0,1:T(8,128)(2,1)} %copy.92), calls=%async_computation | async-start | bytes 2162688 | tf_op jit(solution)/shard_map/all_to_all | solution.py:71
  13.3 1.4 %collective-permute-start.2 = (bf16[2,16,3072]{2,1,0:T(8,128)(2,1)S(1)}, bf16[2,16,3072]{2,1,0:T(8,128)(2,1)}, u32[]{:S(2)}, u32[]{:S(2)}) collective-permute-start(bf16[2,16,3072]{2,1,0:T(8,128)(2,1)S(1)} %get-tuple-element.19), channel_id=1, source_target_pairs={{0,3},{1,2},{2,1},{3,0},{8,11},{9,10},{10,9},{11,8},{16,19},{17,18... | collective-permute-start | bytes 589832 | tf_op jit(solution)/shard_map/ppermute | solution.py:91
  18.5 1.3 %multiply_reduce_fusion.1 = (f32[2,4,16]{2,1,0:T(4,128)S(1)}, bf16[2,4,16,3072]{3,2,1,0:T(8,128)(2,1)S(1)}) fusion(bf16[2,1,16,3072]{3,2,1,0:T(8,128)(2,1)} %bitcast.24, bf16[2,1,16,3072]{3,2,1,0:T(8,128)(2,1)} %bitcast.128, bf16[2,1,16,3072]{3,2,1,0:T(8,128)(2,1)} %bitcast.129, bf16[2,1,16,3072]{3,2,1,0:T(8,128)(2,1)S(1)} %get-tuple-element.16), kind=kLoop, calls=%fused_computation.7 | loop fusion | flops 2359168 | bytes 1573376 | tf_op jit(solution)/shard_map/reduce_sum | solution.py:93
  22.3 1.3 %collective-permute-start.5 = (bf16[128,176]{0,1:T(8,128)(2,1)}, bf16[128,176]{0,1:T(8,128)(2,1)}, u32[]{:S(2)}, u32[]{:S(2)}) collective-permute-start(bf16[128,176]{0,1:T(8,128)(2,1)} %fusion.6), channel_id=1, source_target_pairs={{0,24},{1,25},{2,26},{3,27},{8,16},{9,17},{10,18},{11,19},{16,8},{... | collective-permute-start | bytes 135176 | tf_op jit(solution)/shard_map/ppermute | solution.py:101
  24.8 1.3 %collective-permute-start.3 = (bf16[128,176]{0,1:T(8,128)(2,1)}, bf16[128,176]{0,1:T(8,128)(2,1)}, u32[]{:S(2)}, u32[]{:S(2)}) collective-permute-start(bf16[128,176]{0,1:T(8,128)(2,1)} %fusion.6), channel_id=1, source_target_pairs={{0,8},{1,9},{2,10},{3,11},{8,0},{9,1},{10,2},{11,3},{16,24},{17,25... | collective-permute-start | bytes 135176 | tf_op jit(solution)/shard_map/ppermute | solution.py:101
  26.1 8.5 %all-to-all-done = bf16[176,4,768]{2,0,1:T(8,128)(2,1)S(1)} async-done(((bf16[176,4,768]{2,0,1:T(8,128)(2,1)}), bf16[176,4,768]{2,0,1:T(8,128)(2,1)S(1)}, u32[]{:S(2)}, u32[]{:S(2)}) %all-to-all-start) | async-done | bytes 1081376 | tf_op jit(solution)/shard_map/all_to_all | solution.py:71
  38.9 3.4 %all-to-all-start.1 = ((bf16[2,4,16,768]{3,2,0,1:T(8,128)(2,1)}), bf16[2,4,16,768]{3,2,0,1:T(8,128)(2,1)S(1)}, u32[]{:S(2)}, u32[]{:S(2)}) async-start(bf16[2,4,16,768]{3,2,0,1:T(8,128)(2,1)} %select_bitcast_fusion.2), calls=%async_computation.1 | async-start | bytes 393216 | tf_op jit(solution)/shard_map/all_to_all | solution.py:110
  42.5 3.9 %all-to-all-done.1 = bf16[2,4,16,768]{3,2,0,1:T(8,128)(2,1)S(1)} async-done(((bf16[2,4,16,768]{3,2,0,1:T(8,128)(2,1)}), bf16[2,4,16,768]{3,2,0,1:T(8,128)(2,1)S(1)}, u32[]{:S(2)}, u32[]{:S(2)}) %all-to-all-start.1) | async-done | bytes 196640 | tf_op jit(solution)/shard_map/all_to_all | solution.py:110
  46.6 1.3 %collective-permute-start.9 = (bf16[2,24,768]{2,1,0:T(8,128)(2,1)S(1)}, bf16[2,24,768]{2,1,0:T(8,128)(2,1)S(1)}, u32[]{:S(2)}, u32[]{:S(2)}) collective-permute-start(bf16[2,24,768]{2,1,0:T(8,128)(2,1)S(1)} %fusion), channel_id=1, source_target_pairs={{0,28},{1,29},{2,30},{3,31},{8,20},{9,21},{10,22},{11,23},{16,12},... | collective-permute-start | bytes 221192 | tf_op jit(solution)/shard_map/ppermute | solution.py:138
  47.9 1.3 %collective-permute-start.8 = (bf16[2,24,768]{2,1,0:T(8,128)(2,1)S(1)}, bf16[2,24,768]{2,1,0:T(8,128)(2,1)S(1)}, u32[]{:S(2)}, u32[]{:S(2)}) collective-permute-start(bf16[2,24,768]{2,1,0:T(8,128)(2,1)S(1)} %fusion), channel_id=1, source_target_pairs={{0,20},{1,21},{2,22},{3,23},{8,28},{9,29},{10,30},{11,31},{16,4},{... | collective-permute-start | bytes 221192 | tf_op jit(solution)/shard_map/ppermute | solution.py:138
  49.2 1.3 %collective-permute-start.7 = (bf16[2,24,768]{2,1,0:T(8,128)(2,1)S(1)}, bf16[2,24,768]{2,1,0:T(8,128)(2,1)S(1)}, u32[]{:S(2)}, u32[]{:S(2)}) collective-permute-start(bf16[2,24,768]{2,1,0:T(8,128)(2,1)S(1)} %fusion), channel_id=1, source_target_pairs={{0,12},{1,13},{2,14},{3,15},{8,4},{9,5},{10,6},{11,7},{16,28},{17,... | collective-permute-start | bytes 221192 | tf_op jit(solution)/shard_map/ppermute | solution.py:138
  50.5 1.3 %collective-permute-start.6 = (bf16[2,24,768]{2,1,0:T(8,128)(2,1)S(1)}, bf16[2,24,768]{2,1,0:T(8,128)(2,1)S(1)}, u32[]{:S(2)}, u32[]{:S(2)}) collective-permute-start(bf16[2,24,768]{2,1,0:T(8,128)(2,1)S(1)} %fusion), channel_id=1, source_target_pairs={{0,4},{1,5},{2,6},{3,7},{8,12},{9,13},{10,14},{11,15},{16,20},{17,... | collective-permute-start | bytes 221192 | tf_op jit(solution)/shard_map/ppermute | solution.py:138
  51.8 10.9 %collective-permute-done.9 = bf16[2,24,768]{2,1,0:T(8,128)(2,1)S(1)} collective-permute-done((bf16[2,24,768]{2,1,0:T(8,128)(2,1)S(1)}, bf16[2,24,768]{2,1,0:T(8,128)(2,1)S(1)}, u32[]{:S(2)}, u32[]{:S(2)}) %collective-permute-start.9) | collective-permute-done | bytes 73760 | tf_op jit(solution)/shard_map/ppermute | solution.py:138
  62.7 2.3 %collective-permute-done.8 = bf16[2,24,768]{2,1,0:T(8,128)(2,1)S(1)} collective-permute-done((bf16[2,24,768]{2,1,0:T(8,128)(2,1)S(1)}, bf16[2,24,768]{2,1,0:T(8,128)(2,1)S(1)}, u32[]{:S(2)}, u32[]{:S(2)}) %collective-permute-start.8) | collective-permute-done | bytes 73760 | tf_op jit(solution)/shard_map/ppermute | solution.py:138
  66.5 2.7 %collective-permute-start.11 = (bf16[2,16,3072]{2,1,0:T(8,128)(2,1)S(1)}, bf16[2,16,3072]{2,1,0:T(8,128)(2,1)S(1)}, u32[]{:S(2)}, u32[]{:S(2)}) collective-permute-start(bf16[2,16,3072]{2,1,0:T(8,128)(2,1)S(1)} %get-tuple-element.13), channel_id=1, source_target_pairs={{4,6},{5,7},{6,4},{7,5},{12,14},{13,15},{14,12},{15,13},{20,22},{2... | collective-permute-start | bytes 589832 | tf_op jit(solution)/shard_map/ppermute | solution.py:91
  69.2 2.2 %collective-permute-start.10 = (bf16[2,16,3072]{2,1,0:T(8,128)(2,1)S(1)}, bf16[2,16,3072]{2,1,0:T(8,128)(2,1)S(1)}, u32[]{:S(2)}, u32[]{:S(2)}) collective-permute-start(bf16[2,16,3072]{2,1,0:T(8,128)(2,1)S(1)} %get-tuple-element.14), channel_id=1, source_target_pairs={{4,5},{5,4},{6,7},{7,6},{12,13},{13,12},{14,15},{15,14},{20,21},{2... | collective-permute-start | bytes 589832 | tf_op jit(solution)/shard_map/ppermute | solution.py:91
  71.4 3.5 %collective-permute-start.12 = (bf16[2,16,3072]{2,1,0:T(8,128)(2,1)S(1)}, bf16[2,16,3072]{2,1,0:T(8,128)(2,1)S(1)}, u32[]{:S(2)}, u32[]{:S(2)}) collective-permute-start(bf16[2,16,3072]{2,1,0:T(8,128)(2,1)S(1)} %get-tuple-element.15), channel_id=1, source_target_pairs={{4,7},{5,6},{6,5},{7,4},{12,15},{13,14},{14,13},{15,12},{20,23},{2... | collective-permute-start | bytes 589832 | tf_op jit(solution)/shard_map/ppermute | solution.py:91
  75.6 3.1 %collective-permute-done.12 = bf16[2,16,3072]{2,1,0:T(8,128)(2,1)S(1)} collective-permute-done((bf16[2,16,3072]{2,1,0:T(8,128)(2,1)S(1)}, bf16[2,16,3072]{2,1,0:T(8,128)(2,1)S(1)}, u32[]{:S(2)}, u32[]{:S(2)}) %collective-permute-start.12) | collective-permute-done | bytes 196640 | tf_op jit(solution)/shard_map/ppermute | solution.py:91
  80.7 3.8 %collective-permute-start.15 = (bf16[128,176]{0,1:T(8,128)(2,1)S(1)}, bf16[128,176]{0,1:T(8,128)(2,1)S(1)}, u32[]{:S(2)}, u32[]{:S(2)}) collective-permute-start(bf16[128,176]{0,1:T(8,128)(2,1)S(1)} %fusion.7), channel_id=1, source_target_pairs={{4,28},{5,29},{6,30},{7,31},{12,20},{13,21},{14,22},{15,23},{20,12... | collective-permute-start | bytes 135176 | tf_op jit(solution)/shard_map/ppermute | solution.py:101
  84.6 1.9 %collective-permute-start.14 = (bf16[128,176]{0,1:T(8,128)(2,1)S(1)}, bf16[128,176]{0,1:T(8,128)(2,1)S(1)}, u32[]{:S(2)}, u32[]{:S(2)}) collective-permute-start(bf16[128,176]{0,1:T(8,128)(2,1)S(1)} %fusion.7), channel_id=1, source_target_pairs={{4,20},{5,21},{6,22},{7,23},{12,28},{13,29},{14,30},{15,31},{20,4}... | collective-permute-start | bytes 135176 | tf_op jit(solution)/shard_map/ppermute | solution.py:101
  86.5 3.5 %collective-permute-start.13 = (bf16[128,176]{0,1:T(8,128)(2,1)S(1)}, bf16[128,176]{0,1:T(8,128)(2,1)S(1)}, u32[]{:S(2)}, u32[]{:S(2)}) collective-permute-start(bf16[128,176]{0,1:T(8,128)(2,1)S(1)} %fusion.7), channel_id=1, source_target_pairs={{4,12},{5,13},{6,14},{7,15},{12,4},{13,5},{14,6},{15,7},{20,28},{2... | collective-permute-start | bytes 135176 | tf_op jit(solution)/shard_map/ppermute | solution.py:101
  93.4 3.4 %all-to-all-start.2 = ((bf16[2,4,16,768]{3,2,0,1:T(8,128)(2,1)}), bf16[2,4,16,768]{3,2,0,1:T(8,128)(2,1)S(1)}, u32[]{:S(2)}, u32[]{:S(2)}) async-start(bf16[2,4,16,768]{3,2,0,1:T(8,128)(2,1)} %select_bitcast_fusion.1), calls=%async_computation.2 | async-start | bytes 393216 | tf_op jit(solution)/shard_map/all_to_all | solution.py:110
  96.8 4.0 %all-to-all-done.2 = bf16[2,4,16,768]{3,2,0,1:T(8,128)(2,1)S(1)} async-done(((bf16[2,4,16,768]{3,2,0,1:T(8,128)(2,1)}), bf16[2,4,16,768]{3,2,0,1:T(8,128)(2,1)S(1)}, u32[]{:S(2)}, u32[]{:S(2)}) %all-to-all-start.2) | async-done | bytes 196640 | tf_op jit(solution)/shard_map/all_to_all | solution.py:110
  (102 shorter events, 26.1 us)
Async XLA Ops:
  0.0 20.0 %copy-start = (bf16[1,1,3072,176]{2,3,1,0:T(8,128)(2,1)S(1)}, bf16[1,1,3072,176]{2,3,1,0:T(8,128)(2,1)}, u32[]{:S(2)}) copy-start(bf16[1,1,3072,176]{2,3,1,0:T(8,128)(2,1)} %param.11) | copy-start | bytes 3244036
  3.1 7.7 %copy-start.3 = (bf16[2,24,3072]{2,1,0:T(8,128)(2,1)S(1)}, bf16[2,24,3072]{2,1,0:T(8,128)(2,1)}, u32[]{:S(2)}) copy-start(bf16[2,24,3072]{2,1,0:T(8,128)(2,1)} %param.8) | copy-start | bytes 884740
  3.1 31.5 %all-to-all-start = ((bf16[176,4,768]{2,0,1:T(8,128)(2,1)}), bf16[176,4,768]{2,0,1:T(8,128)(2,1)S(1)}, u32[]{:S(2)}, u32[]{:S(2)}) async-start(bf16[176,4,768]{2,0,1:T(8,128)(2,1)} %copy.92), calls=%async_computation | async-start | bytes 2162688 | tf_op jit(solution)/shard_map/all_to_all | solution.py:71
  11.9 5.9 %collective-permute-start.1 = (bf16[2,16,3072]{2,1,0:T(8,128)(2,1)}, bf16[2,16,3072]{2,1,0:T(8,128)(2,1)S(1)}, u32[]{:S(2)}, u32[]{:S(2)}) collective-permute-start(bf16[2,16,3072]{2,1,0:T(8,128)(2,1)} %get-tuple-element.17), channel_id=1, source_target_pairs={{0,2},{1,3},{2,0},{3,1},{8,10},{9,11},{10,8},{11,9},{16,18},{17,19... | collective-permute-start | bytes 589832 | tf_op jit(solution)/shard_map/ppermute | solution.py:91
  12.6 5.2 %collective-permute-start = (bf16[2,16,3072]{2,1,0:T(8,128)(2,1)S(1)}, bf16[2,16,3072]{2,1,0:T(8,128)(2,1)S(1)}, u32[]{:S(2)}, u32[]{:S(2)}) collective-permute-start(bf16[2,16,3072]{2,1,0:T(8,128)(2,1)S(1)} %get-tuple-element.18), channel_id=1, source_target_pairs={{0,1},{1,0},{2,3},{3,2},{8,9},{9,8},{10,11},{11,10},{16,17},{17,16... | collective-permute-start | bytes 589832 | tf_op jit(solution)/shard_map/ppermute | solution.py:91
  13.3 4.5 %collective-permute-start.2 = (bf16[2,16,3072]{2,1,0:T(8,128)(2,1)S(1)}, bf16[2,16,3072]{2,1,0:T(8,128)(2,1)}, u32[]{:S(2)}, u32[]{:S(2)}) collective-permute-start(bf16[2,16,3072]{2,1,0:T(8,128)(2,1)S(1)} %get-tuple-element.19), channel_id=1, source_target_pairs={{0,3},{1,2},{2,1},{3,0},{8,11},{9,10},{10,9},{11,8},{16,19},{17,18... | collective-permute-start | bytes 589832 | tf_op jit(solution)/shard_map/ppermute | solution.py:91
  22.3 13.9 %collective-permute-start.5 = (bf16[128,176]{0,1:T(8,128)(2,1)}, bf16[128,176]{0,1:T(8,128)(2,1)}, u32[]{:S(2)}, u32[]{:S(2)}) collective-permute-start(bf16[128,176]{0,1:T(8,128)(2,1)} %fusion.6), channel_id=1, source_target_pairs={{0,24},{1,25},{2,26},{3,27},{8,16},{9,17},{10,18},{11,19},{16,8},{... | collective-permute-start | bytes 135176 | tf_op jit(solution)/shard_map/ppermute | solution.py:101
  23.6 12.6 %collective-permute-start.4 = (bf16[128,176]{0,1:T(8,128)(2,1)}, bf16[128,176]{0,1:T(8,128)(2,1)}, u32[]{:S(2)}, u32[]{:S(2)}) collective-permute-start(bf16[128,176]{0,1:T(8,128)(2,1)} %fusion.6), channel_id=1, source_target_pairs={{0,16},{1,17},{2,18},{3,19},{8,24},{9,25},{10,26},{11,27},{16,0},{... | collective-permute-start | bytes 135176 | tf_op jit(solution)/shard_map/ppermute | solution.py:101
  24.8 11.4 %collective-permute-start.3 = (bf16[128,176]{0,1:T(8,128)(2,1)}, bf16[128,176]{0,1:T(8,128)(2,1)}, u32[]{:S(2)}, u32[]{:S(2)}) collective-permute-start(bf16[128,176]{0,1:T(8,128)(2,1)} %fusion.6), channel_id=1, source_target_pairs={{0,8},{1,9},{2,10},{3,11},{8,0},{9,1},{10,2},{11,3},{16,24},{17,25... | collective-permute-start | bytes 135176 | tf_op jit(solution)/shard_map/ppermute | solution.py:101
  38.9 7.5 %all-to-all-start.1 = ((bf16[2,4,16,768]{3,2,0,1:T(8,128)(2,1)}), bf16[2,4,16,768]{3,2,0,1:T(8,128)(2,1)S(1)}, u32[]{:S(2)}, u32[]{:S(2)}) async-start(bf16[2,4,16,768]{3,2,0,1:T(8,128)(2,1)} %select_bitcast_fusion.2), calls=%async_computation.1 | async-start | bytes 393216 | tf_op jit(solution)/shard_map/all_to_all | solution.py:110
  42.3 23.5 %copy-start.14 = (pred[4]{0:T(512)(128)(4,1)S(1)}, pred[4]{0:T(512)(128)(4,1)}, u32[]{:S(2)}) copy-start(pred[4]{0:T(512)(128)(4,1)} %copy-done.13) | copy-start | bytes 16
  46.6 18.5 %copy-start.4 = (bf16[2,24,768]{2,1,0:T(8,128)(2,1)}, bf16[2,24,768]{2,1,0:T(8,128)(2,1)S(1)}, u32[]{:S(2)}) copy-start(bf16[2,24,768]{2,1,0:T(8,128)(2,1)S(1)} %fusion) | copy-start | bytes 221188
  46.6 16.1 %collective-permute-start.9 = (bf16[2,24,768]{2,1,0:T(8,128)(2,1)S(1)}, bf16[2,24,768]{2,1,0:T(8,128)(2,1)S(1)}, u32[]{:S(2)}, u32[]{:S(2)}) collective-permute-start(bf16[2,24,768]{2,1,0:T(8,128)(2,1)S(1)} %fusion), channel_id=1, source_target_pairs={{0,28},{1,29},{2,30},{3,31},{8,20},{9,21},{10,22},{11,23},{16,12},... | collective-permute-start | bytes 221192 | tf_op jit(solution)/shard_map/ppermute | solution.py:138
  47.9 17.2 %collective-permute-start.8 = (bf16[2,24,768]{2,1,0:T(8,128)(2,1)S(1)}, bf16[2,24,768]{2,1,0:T(8,128)(2,1)S(1)}, u32[]{:S(2)}, u32[]{:S(2)}) collective-permute-start(bf16[2,24,768]{2,1,0:T(8,128)(2,1)S(1)} %fusion), channel_id=1, source_target_pairs={{0,20},{1,21},{2,22},{3,23},{8,28},{9,29},{10,30},{11,31},{16,4},{... | collective-permute-start | bytes 221192 | tf_op jit(solution)/shard_map/ppermute | solution.py:138
  49.2 15.9 %collective-permute-start.7 = (bf16[2,24,768]{2,1,0:T(8,128)(2,1)S(1)}, bf16[2,24,768]{2,1,0:T(8,128)(2,1)S(1)}, u32[]{:S(2)}, u32[]{:S(2)}) collective-permute-start(bf16[2,24,768]{2,1,0:T(8,128)(2,1)S(1)} %fusion), channel_id=1, source_target_pairs={{0,12},{1,13},{2,14},{3,15},{8,4},{9,5},{10,6},{11,7},{16,28},{17,... | collective-permute-start | bytes 221192 | tf_op jit(solution)/shard_map/ppermute | solution.py:138
  50.5 14.6 %collective-permute-start.6 = (bf16[2,24,768]{2,1,0:T(8,128)(2,1)S(1)}, bf16[2,24,768]{2,1,0:T(8,128)(2,1)S(1)}, u32[]{:S(2)}, u32[]{:S(2)}) collective-permute-start(bf16[2,24,768]{2,1,0:T(8,128)(2,1)S(1)} %fusion), channel_id=1, source_target_pairs={{0,4},{1,5},{2,6},{3,7},{8,12},{9,13},{10,14},{11,15},{16,20},{17,... | collective-permute-start | bytes 221192 | tf_op jit(solution)/shard_map/ppermute | solution.py:138
  66.5 8.4 %collective-permute-start.11 = (bf16[2,16,3072]{2,1,0:T(8,128)(2,1)S(1)}, bf16[2,16,3072]{2,1,0:T(8,128)(2,1)S(1)}, u32[]{:S(2)}, u32[]{:S(2)}) collective-permute-start(bf16[2,16,3072]{2,1,0:T(8,128)(2,1)S(1)} %get-tuple-element.13), channel_id=1, source_target_pairs={{4,6},{5,7},{6,4},{7,5},{12,14},{13,15},{14,12},{15,13},{20,22},{2... | collective-permute-start | bytes 589832 | tf_op jit(solution)/shard_map/ppermute | solution.py:91
  69.2 6.4 %collective-permute-start.10 = (bf16[2,16,3072]{2,1,0:T(8,128)(2,1)S(1)}, bf16[2,16,3072]{2,1,0:T(8,128)(2,1)S(1)}, u32[]{:S(2)}, u32[]{:S(2)}) collective-permute-start(bf16[2,16,3072]{2,1,0:T(8,128)(2,1)S(1)} %get-tuple-element.14), channel_id=1, source_target_pairs={{4,5},{5,4},{6,7},{7,6},{12,13},{13,12},{14,15},{15,14},{20,21},{2... | collective-permute-start | bytes 589832 | tf_op jit(solution)/shard_map/ppermute | solution.py:91
  71.4 7.3 %collective-permute-start.12 = (bf16[2,16,3072]{2,1,0:T(8,128)(2,1)S(1)}, bf16[2,16,3072]{2,1,0:T(8,128)(2,1)S(1)}, u32[]{:S(2)}, u32[]{:S(2)}) collective-permute-start(bf16[2,16,3072]{2,1,0:T(8,128)(2,1)S(1)} %get-tuple-element.15), channel_id=1, source_target_pairs={{4,7},{5,6},{6,5},{7,4},{12,15},{13,14},{14,13},{15,12},{20,23},{2... | collective-permute-start | bytes 589832 | tf_op jit(solution)/shard_map/ppermute | solution.py:91
  80.7 9.3 %collective-permute-start.15 = (bf16[128,176]{0,1:T(8,128)(2,1)S(1)}, bf16[128,176]{0,1:T(8,128)(2,1)S(1)}, u32[]{:S(2)}, u32[]{:S(2)}) collective-permute-start(bf16[128,176]{0,1:T(8,128)(2,1)S(1)} %fusion.7), channel_id=1, source_target_pairs={{4,28},{5,29},{6,30},{7,31},{12,20},{13,21},{14,22},{15,23},{20,12... | collective-permute-start | bytes 135176 | tf_op jit(solution)/shard_map/ppermute | solution.py:101
  84.6 5.7 %collective-permute-start.14 = (bf16[128,176]{0,1:T(8,128)(2,1)S(1)}, bf16[128,176]{0,1:T(8,128)(2,1)S(1)}, u32[]{:S(2)}, u32[]{:S(2)}) collective-permute-start(bf16[128,176]{0,1:T(8,128)(2,1)S(1)} %fusion.7), channel_id=1, source_target_pairs={{4,20},{5,21},{6,22},{7,23},{12,28},{13,29},{14,30},{15,31},{20,4}... | collective-permute-start | bytes 135176 | tf_op jit(solution)/shard_map/ppermute | solution.py:101
  86.5 4.9 %collective-permute-start.13 = (bf16[128,176]{0,1:T(8,128)(2,1)S(1)}, bf16[128,176]{0,1:T(8,128)(2,1)S(1)}, u32[]{:S(2)}, u32[]{:S(2)}) collective-permute-start(bf16[128,176]{0,1:T(8,128)(2,1)S(1)} %fusion.7), channel_id=1, source_target_pairs={{4,12},{5,13},{6,14},{7,15},{12,4},{13,5},{14,6},{15,7},{20,28},{2... | collective-permute-start | bytes 135176 | tf_op jit(solution)/shard_map/ppermute | solution.py:101
  91.8 9.0 %copy-start.5 = (bf16[2,24,768]{2,1,0:T(8,128)(2,1)S(1)}, bf16[2,24,768]{2,1,0:T(8,128)(2,1)}, u32[]{:S(2)}) copy-start(bf16[2,24,768]{2,1,0:T(8,128)(2,1)} %copy-done.4) | copy-start | bytes 221188
  93.4 7.4 %all-to-all-start.2 = ((bf16[2,4,16,768]{3,2,0,1:T(8,128)(2,1)}), bf16[2,4,16,768]{3,2,0,1:T(8,128)(2,1)S(1)}, u32[]{:S(2)}, u32[]{:S(2)}) async-start(bf16[2,4,16,768]{3,2,0,1:T(8,128)(2,1)} %select_bitcast_fusion.1), calls=%async_computation.2 | async-start | bytes 393216 | tf_op jit(solution)/shard_map/all_to_all | solution.py:110
  (10 other events, 30.4 us)

commit v13 on v10

--- a/solution.py
+++ b/solution.py
@@ -68,38 +68,43 @@
     up_local = w_up[0, 0]
     down_local = w_down[0, 0]
 
-    if small_dp:
-        down_parts = []
-        for s in range(n_dp):
-            piece = lax.dynamic_slice_in_dim(down_local, dring.ahead(d_me, s) * columns, columns, 1)
-            down_parts.append(piece)
-        down_parts, tokens = lax.optimization_barrier((down_parts, tokens))
+    def resplit_down(p, anchor):
+        if not small_dp:
+            return lax.all_to_all(down_local, "dp", 1, 0, tiled=True), anchor
+        parts = [lax.dynamic_slice_in_dim(down_local, dring.ahead(d_me, s) * columns, columns, 1) for s in range(n_dp)]
+        parts, anchor = lax.optimization_barrier((parts, anchor))
         for s in range(1, n_dp):
-            down_parts[s] = lax.ppermute(down_parts[s], "dp", [(i, dring.ahead(i, s)) for i in range(n_dp)])
-        down_full = jnp.concatenate(down_parts, axis=0)
-    else:
-        down_full = lax.all_to_all(down_local, "dp", 1, 0, tiled=True)
+            parts[s] = lax.ppermute(parts[s], AXES, dp_pairs(p, s))
+        return jnp.concatenate(parts, axis=0), anchor
+
+    down_full = {}
+    down_full[0], tokens = resplit_down(0, tokens)
 
     route_ids = expert_ids[0]
     route_gates = gates[0]
     maps = [build_maps(route_ids[m], route_gates[m], ering, e_me, rows_all) for m in range(micro)]
     dispatch_map = jnp.stack([mp[0] for mp in maps])
     combine_map = jnp.stack([mp[1] for mp in maps])
+    absolute_dispatch = dispatch_map
     if ering.xor:
         maps = [build_maps(route_ids[m], route_gates[m], ering, 0, rows_all) for m in range(micro)]
-        dispatch_map = jnp.stack([mp[0] for mp in maps])
+        absolute_dispatch = jnp.stack([mp[0] for mp in maps])
         combine_map = jnp.stack([mp[1] for mp in maps])
 
     def layer(current, p):
-        outgoing = jnp.einsum("mrt,mtd->mrd", dispatch_map, current, preferred_element_type=jnp.float32)
-        outgoing = outgoing.astype(jnp.bfloat16).reshape(micro, n_exp, CAP, width)
-        if ering.xor:
+        if p == 0 and ering.xor:
+            outgoing = jnp.einsum("mrt,mtd->mrd", absolute_dispatch, current, preferred_element_type=jnp.float32)
+            outgoing = outgoing.astype(jnp.bfloat16).reshape(micro, n_exp, CAP, width)
             flat_rows = lax.all_to_all(outgoing, "expert", 1, 1, tiled=True).reshape(-1, width)
+            in_block_order = True
         else:
+            outgoing = jnp.einsum("mrt,mtd->mrd", dispatch_map, current, preferred_element_type=jnp.float32)
+            outgoing = outgoing.astype(jnp.bfloat16).reshape(micro, n_exp, CAP, width)
             arrived = [outgoing[:, 0]]
             for s in range(1, n_exp):
                 arrived.append(lax.ppermute(outgoing[:, s], AXES, expert_pairs(p, s, False)))
             flat_rows = jnp.stack(arrived, axis=1).reshape(-1, width)
+            in_block_order = False
         squares = jnp.mean(jnp.square(flat_rows.astype(jnp.float32)), axis=1, keepdims=True)
         inv_rms = lax.rsqrt(squares + 1e-05)
         gate_act = jnp.dot(flat_rows, gate_local, preferred_element_type=jnp.float32) * inv_rms
@@ -112,10 +117,15 @@
             hidden_full = jnp.concatenate(parts, axis=1)
         else:
             hidden_full = lax.all_gather(hidden, "dp", axis=1, tiled=True)
-        expert_out = jnp.dot(hidden_full, down_full, preferred_element_type=jnp.float32).astype(jnp.bfloat16)
+        expert_out = jnp.dot(hidden_full, down_full[p], preferred_element_type=jnp.float32).astype(jnp.bfloat16)
         expert_out = expert_out.reshape(micro, n_exp, CAP, columns)
         if ering.xor:
-            returned = lax.all_to_all(expert_out, "expert", 1, 1, tiled=True).reshape(micro, rows_all, columns)
+            if in_block_order:
+                by_block = expert_out
+            else:
+                order = jnp.stack([ering.place(j, e_me) for j in range(n_exp)])
+                by_block = jnp.take(expert_out, order, axis=1)
+            returned = lax.all_to_all(by_block, "expert", 1, 1, tiled=True).reshape(micro, rows_all, columns)
         else:
             returned = [expert_out[:, 0]]
             for s in range(1, n_exp):
@@ -135,6 +145,9 @@
     result = None
     for p in range(n_pipe):
         cols = layer(current, p)
+        if p + 1 < n_pipe:
+            down_full[p + 1], cols = resplit_down(p + 1, cols)
+            down_full[p + 1], cols = lax.optimization_barrier((down_full[p + 1], cols))
         result = cols if result is None else jnp.where(p_me == p, cols, result)
         if p + 1 < n_pipe:
             if small_dp:

time: 104 us -> 104 us (level)
  starting transfers between devices: 31.3 us -> 46.5 us
  waiting for transfers between devices: 44.4 us -> 33.7 us
  blocking collectives: 12.3 us -> 6.77 us
  other arithmetic: 1.56 us -> 4.49 us
  local copies, waits for them, and re-layouts: 8.92 us -> 6.23 us
  matrix products: 4.42 us -> 5.51 us
    ppermute x3 -> x9, starting transfers between devices: 3.74 us -> 21.9 us  [the longest x6 13.6 us: resplit_down(): parts[s] = lax.ppermute(parts[s], AXES, dp_pairs(p, s))]
    ppermute x4, waiting for transfers between devices: 21.7 us -> 8.3 us  [per_device(): parts.append(lax.ppermute(cols, AXES, pairs))]
    all_to_all x1, waiting for transfers between devices: 0.01 us -> 6.2 us  [layer(): lax.all_to_all(outgoing, 'expert', 1, 1, tiled=True).reshape(-1, width)]
    all_to_all x1, blocking collectives: 12.3 us -> 6.77 us  [layer(): lax.all_to_all(by_block, 'expert', 1, 1, tiled=True)]
    all_to_all x2 -> x1, waiting for transfers between devices: 7.93 us -> 4.05 us  [layer(): lax.all_to_all(by_block, 'expert', 1, 1, tiled=True)]
    all_to_all x2 -> x1, starting transfers between devices: 6.73 us -> 3.85 us  [layer(): lax.all_to_all(by_block, 'expert', 1, 1, tiled=True)]
    ppermute x6, waiting for transfers between devices: 1.42 us -> 3.56 us  [layer(): parts.append(lax.ppermute(hidden, AXES, dp_pairs(p, s)))]
    concatenate x0 -> x1, other arithmetic: none -> 2.01 us  [resplit_down(): return (jnp.concatenate(parts, axis=0), anchor)]
  transfers between devices with their start and end apart: 16 -> 21, of which waited for: 10 -> 9; matrix products, arithmetic and copies ran while one was open for 2% -> 2% of each run, Pallas kernels for 0% -> 0%
where the time goes in v13:
time: 104 us
  starting transfers between devices  46.5 us (45%)
  waiting for transfers between devices  33.7 us (32%)
  blocking collectives  6.77 us (7%)
  local copies, waits for them, and re-layouts  6.23 us (6%)
  matrix products  5.51 us (5%)
  other arithmetic  4.49 us (4%)
    ppermute x6, starting transfers between devices, resplit_down(): parts[s] = lax.ppermute(parts[s], AXES, dp_pairs(p, s))  13.6 us
    ppermute x6, starting transfers between devices, layer(): parts.append(lax.ppermute(hidden, AXES, dp_pairs(p, s)))  11.3 us
    ppermute x3, starting transfers between devices, layer(): lax.ppermute(outgoing[:, s], AXES, expert_pairs(p, s, False))  8.37 us
    ppermute x4, waiting for transfers between devices, per_device(): parts.append(lax.ppermute(cols, AXES, pairs))  8.3 us
    ppermute x6, waiting for transfers between devices, resplit_down(): parts[s] = lax.ppermute(parts[s], AXES, dp_pairs(p, s))  7.78 us
    all_to_all x1, blocking collectives, layer(): lax.all_to_all(by_block, 'expert', 1, 1, tiled=True)  6.77 us
    all_to_all x1, waiting for transfers between devices, layer(): lax.all_to_all(outgoing, 'expert', 1, 1, tiled=True).reshape(-1, width)  6.2 us
    ppermute x4, starting transfers between devices, per_device(): parts.append(lax.ppermute(cols, AXES, pairs))  5.16 us
  transfers between devices with their start and end apart: 21, of which 9 were waited for; matrix products, arithmetic and copies ran while one was open for 2% of the time, Pallas kernels for 0%

profile of v13, /device:TPU:1, one launch (start us, length us, event | category | flops | bytes accessed | tf_op | source)
XLA Modules:
  0.0 103.7 jit_solution(4715163799623882561)
XLA Ops:
  0.0 2.2 %dynamic-slice_bitcast_fusion = (bf16[176,768]{1,0:T(8,128)(2,1)}, bf16[176,768]{1,0:T(8,128)(2,1)}, bf16[176,768]{1,0:T(8,128)(2,1)S(1)}, bf16[176,768]{1,0:T(8,128)(2,1)}) fusion(bf16[1,1,176,3072]{3,2,1,0:T(8,128)(2,1)} %param.11, s32[]{:T(128)S(6)} %select_n.83, s32[]{:T(128)S(6)} %select_n.81, s32[]{:T(128)S(6)} %select_n.80, s32[]{:T(128)S(6)} %select_n.82), kind=kLoop, calls=%fused_computation.37 | loop fusion | bytes 2162704 | tf_op jit(solution)/shard_map/dynamic_slice | solution.py:74
  5.2 4.3 %all-to-all-start = ((bf16[2,4,16,3072]{3,2,0,1:T(8,128)(2,1)}), bf16[2,4,16,3072]{3,2,0,1:T(8,128)(2,1)S(1)}, u32[]{:S(2)}, u32[]{:S(2)}) async-start(bf16[2,4,16,3072]{3,2,0,1:T(8,128)(2,1)} %copy.141), calls=%async_computation | async-start | bytes 1572864 | tf_op jit(solution)/shard_map/all_to_all | solution.py:98
  10.8 1.4 %collective-permute-start.4 = (bf16[176,768]{1,0:T(8,128)(2,1)}, bf16[176,768]{1,0:T(8,128)(2,1)}, u32[]{:S(2)}, u32[]{:S(2)}) collective-permute-start(bf16[176,768]{1,0:T(8,128)(2,1)} %get-tuple-element.24), channel_id=1, source_target_pairs={{0,16},{1,17},{2,18},{3,19},{8,24},{9,25},{10,26},{11,27},{16,0},{... | collective-permute-start | bytes 811016 | tf_op jit(solution)/shard_map/ppermute | solution.py:77
  13.5 6.2 %all-to-all-done = bf16[2,4,16,3072]{3,2,0,1:T(8,128)(2,1)S(1)} async-done(((bf16[2,4,16,3072]{3,2,0,1:T(8,128)(2,1)}), bf16[2,4,16,3072]{3,2,0,1:T(8,128)(2,1)S(1)}, u32[]{:S(2)}, u32[]{:S(2)}) %all-to-all-start) | async-done | bytes 786464 | tf_op jit(solution)/shard_map/all_to_all | solution.py:98
  23.9 1.5 %convolution_convert_fusion.3 = bf16[128,768]{1,0:T(8,128)(2,1)S(1)} fusion(bf16[176,768]{1,0:T(8,128)(2,1)} %collective-permute-done.5, bf16[176,768]{1,0:T(8,128)(2,1)} %collective-permute-done.4, bf16[176,768]{1,0:T(8,128)(2,1)} %collective-permute-done.3, bf16[176,768]{1,0:T(8,128)(2,1)S(1)} %get-tuple-element.22, ...), kind=kOutput, calls=%fused_computation.7 | convolution fusion | flops 143556608 | bytes 1458176 | tf_op jit(solution)/shard_map/dot_general | solution.py:120
  25.4 6.8 %all_to_all.15 = bf16[2,4,16,768]{3,2,0,1:T(8,128)(2,1)S(1)} all-to-all(bf16[2,4,16,768]{3,2,0,1:T(8,128)(2,1)S(1)} %copy.144), channel_id=1, replica_groups=mesh['dp'=4,'pipe'=2,'expert'=4] {'expert'}, dimensions={1} | all-to-all | bytes 393216 | tf_op jit(solution)/shard_map/all_to_all | solution.py:128
  32.5 3.3 %collective-permute-start.6 = (bf16[176,768]{1,0:T(8,128)(2,1)}, bf16[176,768]{1,0:T(8,128)(2,1)S(1)}, u32[]{:S(2)}, u32[]{:S(2)}) collective-permute-start(bf16[176,768]{1,0:T(8,128)(2,1)} %get-tuple-element.23), channel_id=1, source_target_pairs={{4,12},{5,13},{6,14},{7,15},{12,4},{13,5},{14,6},{15,7},{20,28},{2... | collective-permute-start | bytes 811016 | tf_op jit(solution)/shard_map/ppermute | solution.py:77
  35.8 4.2 %collective-permute-start.7 = (bf16[176,768]{1,0:T(8,128)(2,1)}, bf16[176,768]{1,0:T(8,128)(2,1)S(1)}, u32[]{:S(2)}, u32[]{:S(2)}) collective-permute-start(bf16[176,768]{1,0:T(8,128)(2,1)} %get-tuple-element.24), channel_id=1, source_target_pairs={{4,20},{5,21},{6,22},{7,23},{12,28},{13,29},{14,30},{15,31},{20,4}... | collective-permute-start | bytes 811016 | tf_op jit(solution)/shard_map/ppermute | solution.py:77
  40.0 1.9 %collective-permute-start.8 = (bf16[176,768]{1,0:T(8,128)(2,1)}, bf16[176,768]{1,0:T(8,128)(2,1)}, u32[]{:S(2)}, u32[]{:S(2)}) collective-permute-start(bf16[176,768]{1,0:T(8,128)(2,1)} %get-tuple-element.25), channel_id=1, source_target_pairs={{4,28},{5,29},{6,30},{7,31},{12,20},{13,21},{14,22},{15,23},{20,12... | collective-permute-start | bytes 811016 | tf_op jit(solution)/shard_map/ppermute | solution.py:77
  42.1 7.8 %collective-permute-done.7 = bf16[176,768]{1,0:T(8,128)(2,1)S(1)} collective-permute-done((bf16[176,768]{1,0:T(8,128)(2,1)}, bf16[176,768]{1,0:T(8,128)(2,1)S(1)}, u32[]{:S(2)}, u32[]{:S(2)}) %collective-permute-start.7) | collective-permute-done | bytes 270368 | tf_op jit(solution)/shard_map/ppermute | solution.py:77
  49.9 2.0 %pad_maximum_fusion = bf16[704,768]{1,0:T(8,128)(2,1)} fusion(bf16[176,768]{1,0:T(8,128)(2,1)} %collective-permute-done.8, bf16[176,768]{1,0:T(8,128)(2,1)S(1)} %collective-permute-done.7, bf16[176,768]{1,0:T(8,128)(2,1)S(1)} %collective-permute-done.6, bf16[176,768]{1,0:T(8,128)(2,1)S(1)} %get-tuple-element.22), kind=kLoop, calls=%fused_computation.29 | loop fusion | flops 4325376 | bytes 2162688 | tf_op jit(solution)/shard_map/concatenate | solution.py:78
  57.2 3.6 %collective-permute-done.10 = bf16[2,24,768]{2,1,0:T(8,128)(2,1)S(1)} collective-permute-done((bf16[2,24,768]{2,1,0:T(8,128)(2,1)S(1)}, bf16[2,24,768]{2,1,0:T(8,128)(2,1)S(1)}, u32[]{:S(2)}, u32[]{:S(2)}) %collective-permute-start.10) | collective-permute-done | bytes 73760 | tf_op jit(solution)/shard_map/ppermute | solution.py:159
  60.8 2.2 %collective-permute-done.11 = bf16[2,24,768]{2,1,0:T(8,128)(2,1)S(1)} collective-permute-done((bf16[2,24,768]{2,1,0:T(8,128)(2,1)S(1)}, bf16[2,24,768]{2,1,0:T(8,128)(2,1)S(1)}, u32[]{:S(2)}, u32[]{:S(2)}) %collective-permute-start.11) | collective-permute-done | bytes 73760 | tf_op jit(solution)/shard_map/ppermute | solution.py:159
  63.0 2.5 %collective-permute-done.12 = bf16[2,24,768]{2,1,0:T(8,128)(2,1)S(1)} collective-permute-done((bf16[2,24,768]{2,1,0:T(8,128)(2,1)S(1)}, bf16[2,24,768]{2,1,0:T(8,128)(2,1)S(1)}, u32[]{:S(2)}, u32[]{:S(2)}) %collective-permute-start.12) | collective-permute-done | bytes 73760 | tf_op jit(solution)/shard_map/ppermute | solution.py:159
  66.7 2.6 %collective-permute-start.13 = (bf16[2,16,3072]{2,1,0:T(8,128)(2,1)S(1)}, bf16[2,16,3072]{2,1,0:T(8,128)(2,1)S(1)}, u32[]{:S(2)}, u32[]{:S(2)}) collective-permute-start(bf16[2,16,3072]{2,1,0:T(8,128)(2,1)S(1)} %get-tuple-element.41), channel_id=1, source_target_pairs={{4,5},{5,4},{6,7},{7,6},{12,13},{13,12},{14,15},{15,14},{20,21},{2... | collective-permute-start | bytes 589832 | tf_op jit(solution)/shard_map/ppermute | solution.py:105
  69.4 2.3 %collective-permute-start.14 = (bf16[2,16,3072]{2,1,0:T(8,128)(2,1)S(1)}, bf16[2,16,3072]{2,1,0:T(8,128)(2,1)S(1)}, u32[]{:S(2)}, u32[]{:S(2)}) collective-permute-start(bf16[2,16,3072]{2,1,0:T(8,128)(2,1)S(1)} %get-tuple-element.40), channel_id=1, source_target_pairs={{4,6},{5,7},{6,4},{7,5},{12,14},{13,15},{14,12},{15,13},{20,22},{2... | collective-permute-start | bytes 589832 | tf_op jit(solution)/shard_map/ppermute | solution.py:105
  71.7 3.4 %collective-permute-start.15 = (bf16[2,16,3072]{2,1,0:T(8,128)(2,1)S(1)}, bf16[2,16,3072]{2,1,0:T(8,128)(2,1)S(1)}, u32[]{:S(2)}, u32[]{:S(2)}) collective-permute-start(bf16[2,16,3072]{2,1,0:T(8,128)(2,1)S(1)} %get-tuple-element.42), channel_id=1, source_target_pairs={{4,7},{5,6},{6,5},{7,4},{12,15},{13,14},{14,13},{15,12},{20,23},{2... | collective-permute-start | bytes 589832 | tf_op jit(solution)/shard_map/ppermute | solution.py:105
  75.8 3.2 %collective-permute-done.15 = bf16[2,16,3072]{2,1,0:T(8,128)(2,1)S(1)} collective-permute-done((bf16[2,16,3072]{2,1,0:T(8,128)(2,1)S(1)}, bf16[2,16,3072]{2,1,0:T(8,128)(2,1)S(1)}, u32[]{:S(2)}, u32[]{:S(2)}) %collective-permute-start.15) | collective-permute-done | bytes 196640 | tf_op jit(solution)/shard_map/ppermute | solution.py:105
  80.3 2.4 %collective-permute-start.16 = (bf16[128,176]{0,1:T(8,128)(2,1)S(1)}, bf16[128,176]{0,1:T(8,128)(2,1)S(1)}, u32[]{:S(2)}, u32[]{:S(2)}) collective-permute-start(bf16[128,176]{0,1:T(8,128)(2,1)S(1)} %fusion.7), channel_id=1, source_target_pairs={{4,12},{5,13},{6,14},{7,15},{12,4},{13,5},{14,6},{15,7},{20,28},{2... | collective-permute-start | bytes 135176 | tf_op jit(solution)/shard_map/ppermute | solution.py:116
  82.6 3.9 %collective-permute-start.17 = (bf16[128,176]{0,1:T(8,128)(2,1)S(1)}, bf16[128,176]{0,1:T(8,128)(2,1)S(1)}, u32[]{:S(2)}, u32[]{:S(2)}) collective-permute-start(bf16[128,176]{0,1:T(8,128)(2,1)S(1)} %fusion.7), channel_id=1, source_target_pairs={{4,20},{5,21},{6,22},{7,23},{12,28},{13,29},{14,30},{15,31},{20,4}... | collective-permute-start | bytes 135176 | tf_op jit(solution)/shard_map/ppermute | solution.py:116
  86.6 3.0 %collective-permute-start.18 = (bf16[128,176]{0,1:T(8,128)(2,1)S(1)}, bf16[128,176]{0,1:T(8,128)(2,1)S(1)}, u32[]{:S(2)}, u32[]{:S(2)}) collective-permute-start(bf16[128,176]{0,1:T(8,128)(2,1)S(1)} %fusion.7), channel_id=1, source_target_pairs={{4,28},{5,29},{6,30},{7,31},{12,20},{13,21},{14,22},{15,23},{20,12... | collective-permute-start | bytes 135176 | tf_op jit(solution)/shard_map/ppermute | solution.py:116
  89.6 3.5 %collective-permute-done.18 = bf16[128,176]{0,1:T(8,128)(2,1)S(1)} collective-permute-done((bf16[128,176]{0,1:T(8,128)(2,1)S(1)}, bf16[128,176]{0,1:T(8,128)(2,1)S(1)}, u32[]{:S(2)}, u32[]{:S(2)}) %collective-permute-start.18) | collective-permute-done | bytes 45088 | tf_op jit(solution)/shard_map/ppermute | solution.py:116
  94.9 3.8 %all-to-all-start.2 = ((bf16[2,4,16,768]{3,2,0,1:T(8,128)(2,1)}), bf16[2,4,16,768]{3,2,0,1:T(8,128)(2,1)S(1)}, u32[]{:S(2)}, u32[]{:S(2)}) async-start(bf16[2,4,16,768]{3,2,0,1:T(8,128)(2,1)} %select_bitcast_fusion.1), calls=%async_computation.2 | async-start | bytes 393216 | tf_op jit(solution)/shard_map/all_to_all | solution.py:128
  98.7 4.0 %all-to-all-done.2 = bf16[2,4,16,768]{3,2,0,1:T(8,128)(2,1)S(1)} async-done(((bf16[2,4,16,768]{3,2,0,1:T(8,128)(2,1)}), bf16[2,4,16,768]{3,2,0,1:T(8,128)(2,1)S(1)}, u32[]{:S(2)}, u32[]{:S(2)}) %all-to-all-start.2) | async-done | bytes 196640 | tf_op jit(solution)/shard_map/all_to_all | solution.py:128
  (89 shorter events, 21.0 us)
Async XLA Ops:
  0.0 20.2 %copy-start = (bf16[1,1,3072,176]{2,3,1,0:T(8,128)(2,1)S(1)}, bf16[1,1,3072,176]{2,3,1,0:T(8,128)(2,1)}, u32[]{:S(2)}) copy-start(bf16[1,1,3072,176]{2,3,1,0:T(8,128)(2,1)} %param.9) | copy-start | bytes 3244036
  5.2 14.6 %all-to-all-start = ((bf16[2,4,16,3072]{3,2,0,1:T(8,128)(2,1)}), bf16[2,4,16,3072]{3,2,0,1:T(8,128)(2,1)S(1)}, u32[]{:S(2)}, u32[]{:S(2)}) async-start(bf16[2,4,16,3072]{3,2,0,1:T(8,128)(2,1)} %copy.141), calls=%async_computation | async-start | bytes 1572864 | tf_op jit(solution)/shard_map/all_to_all | solution.py:98
  9.5 13.7 %collective-permute-start.3 = (bf16[176,768]{1,0:T(8,128)(2,1)}, bf16[176,768]{1,0:T(8,128)(2,1)}, u32[]{:S(2)}, u32[]{:S(2)}) collective-permute-start(bf16[176,768]{1,0:T(8,128)(2,1)} %get-tuple-element.23), channel_id=1, source_target_pairs={{0,8},{1,9},{2,10},{3,11},{8,0},{9,1},{10,2},{11,3},{16,24},{17,25... | collective-permute-start | bytes 811016 | tf_op jit(solution)/shard_map/ppermute | solution.py:77
  10.8 13.1 %collective-permute-start.4 = (bf16[176,768]{1,0:T(8,128)(2,1)}, bf16[176,768]{1,0:T(8,128)(2,1)}, u32[]{:S(2)}, u32[]{:S(2)}) collective-permute-start(bf16[176,768]{1,0:T(8,128)(2,1)} %get-tuple-element.24), channel_id=1, source_target_pairs={{0,16},{1,17},{2,18},{3,19},{8,24},{9,25},{10,26},{11,27},{16,0},{... | collective-permute-start | bytes 811016 | tf_op jit(solution)/shard_map/ppermute | solution.py:77
  12.2 11.7 %collective-permute-start.5 = (bf16[176,768]{1,0:T(8,128)(2,1)}, bf16[176,768]{1,0:T(8,128)(2,1)}, u32[]{:S(2)}, u32[]{:S(2)}) collective-permute-start(bf16[176,768]{1,0:T(8,128)(2,1)} %get-tuple-element.25), channel_id=1, source_target_pairs={{0,24},{1,25},{2,26},{3,27},{8,16},{9,17},{10,18},{11,19},{16,8},{... | collective-permute-start | bytes 811016 | tf_op jit(solution)/shard_map/ppermute | solution.py:77
  21.9 2.0 %collective-permute-start = (bf16[128,176]{0,1:T(8,128)(2,1)S(1)}, bf16[128,176]{0,1:T(8,128)(2,1)S(1)}, u32[]{:S(2)}, u32[]{:S(2)}) collective-permute-start(bf16[128,176]{0,1:T(8,128)(2,1)S(1)} %fusion.6), channel_id=1, source_target_pairs={{0,8},{1,9},{2,10},{3,11},{8,0},{9,1},{10,2},{11,3},{16,24},{17,25... | collective-permute-start | bytes 135176 | tf_op jit(solution)/shard_map/ppermute | solution.py:116
  22.5 1.4 %collective-permute-start.1 = (bf16[128,176]{0,1:T(8,128)(2,1)S(1)}, bf16[128,176]{0,1:T(8,128)(2,1)S(1)}, u32[]{:S(2)}, u32[]{:S(2)}) collective-permute-start(bf16[128,176]{0,1:T(8,128)(2,1)S(1)} %fusion.6), channel_id=1, source_target_pairs={{0,16},{1,17},{2,18},{3,19},{8,24},{9,25},{10,26},{11,27},{16,0},{... | collective-permute-start | bytes 135176 | tf_op jit(solution)/shard_map/ppermute | solution.py:116
  23.2 0.7 collective-permute-start.2
  32.4 23.4 %copy-start.4 = (bf16[2,24,768]{2,1,0:T(8,128)(2,1)}, bf16[2,24,768]{2,1,0:T(8,128)(2,1)S(1)}, u32[]{:S(2)}) copy-start(bf16[2,24,768]{2,1,0:T(8,128)(2,1)S(1)} %fusion) | copy-start | bytes 221188
  32.5 9.7 %collective-permute-start.6 = (bf16[176,768]{1,0:T(8,128)(2,1)}, bf16[176,768]{1,0:T(8,128)(2,1)S(1)}, u32[]{:S(2)}, u32[]{:S(2)}) collective-permute-start(bf16[176,768]{1,0:T(8,128)(2,1)} %get-tuple-element.23), channel_id=1, source_target_pairs={{4,12},{5,13},{6,14},{7,15},{12,4},{13,5},{14,6},{15,7},{20,28},{2... | collective-permute-start | bytes 811016 | tf_op jit(solution)/shard_map/ppermute | solution.py:77
  35.8 14.1 %collective-permute-start.7 = (bf16[176,768]{1,0:T(8,128)(2,1)}, bf16[176,768]{1,0:T(8,128)(2,1)S(1)}, u32[]{:S(2)}, u32[]{:S(2)}) collective-permute-start(bf16[176,768]{1,0:T(8,128)(2,1)} %get-tuple-element.24), channel_id=1, source_target_pairs={{4,20},{5,21},{6,22},{7,23},{12,28},{13,29},{14,30},{15,31},{20,4}... | collective-permute-start | bytes 811016 | tf_op jit(solution)/shard_map/ppermute | solution.py:77
  40.0 9.9 %collective-permute-start.8 = (bf16[176,768]{1,0:T(8,128)(2,1)}, bf16[176,768]{1,0:T(8,128)(2,1)}, u32[]{:S(2)}, u32[]{:S(2)}) collective-permute-start(bf16[176,768]{1,0:T(8,128)(2,1)} %get-tuple-element.25), channel_id=1, source_target_pairs={{4,28},{5,29},{6,30},{7,31},{12,20},{13,21},{14,22},{15,23},{20,12... | collective-permute-start | bytes 811016 | tf_op jit(solution)/shard_map/ppermute | solution.py:77
  51.9 5.3 %collective-permute-start.9 = (bf16[2,24,768]{2,1,0:T(8,128)(2,1)S(1)}, bf16[2,24,768]{2,1,0:T(8,128)(2,1)S(1)}, u32[]{:S(2)}, u32[]{:S(2)}) collective-permute-start(bf16[2,24,768]{2,1,0:T(8,128)(2,1)S(1)} %fusion), channel_id=1, source_target_pairs={{0,4},{1,5},{2,6},{3,7},{8,12},{9,13},{10,14},{11,15},{16,20},{17,... | collective-permute-start | bytes 221192 | tf_op jit(solution)/shard_map/ppermute | solution.py:159
  53.2 7.6 %collective-permute-start.10 = (bf16[2,24,768]{2,1,0:T(8,128)(2,1)S(1)}, bf16[2,24,768]{2,1,0:T(8,128)(2,1)S(1)}, u32[]{:S(2)}, u32[]{:S(2)}) collective-permute-start(bf16[2,24,768]{2,1,0:T(8,128)(2,1)S(1)} %fusion), channel_id=1, source_target_pairs={{0,12},{1,13},{2,14},{3,15},{8,4},{9,5},{10,6},{11,7},{16,28},{17,... | collective-permute-start | bytes 221192 | tf_op jit(solution)/shard_map/ppermute | solution.py:159
  54.5 8.5 %collective-permute-start.11 = (bf16[2,24,768]{2,1,0:T(8,128)(2,1)S(1)}, bf16[2,24,768]{2,1,0:T(8,128)(2,1)S(1)}, u32[]{:S(2)}, u32[]{:S(2)}) collective-permute-start(bf16[2,24,768]{2,1,0:T(8,128)(2,1)S(1)} %fusion), channel_id=1, source_target_pairs={{0,20},{1,21},{2,22},{3,23},{8,28},{9,29},{10,30},{11,31},{16,4},{... | collective-permute-start | bytes 221192 | tf_op jit(solution)/shard_map/ppermute | solution.py:159
  55.8 9.7 %collective-permute-start.12 = (bf16[2,24,768]{2,1,0:T(8,128)(2,1)S(1)}, bf16[2,24,768]{2,1,0:T(8,128)(2,1)S(1)}, u32[]{:S(2)}, u32[]{:S(2)}) collective-permute-start(bf16[2,24,768]{2,1,0:T(8,128)(2,1)S(1)} %fusion), channel_id=1, source_target_pairs={{0,28},{1,29},{2,30},{3,31},{8,20},{9,21},{10,22},{11,23},{16,12},... | collective-permute-start | bytes 221192 | tf_op jit(solution)/shard_map/ppermute | solution.py:159
  66.7 8.5 %collective-permute-start.13 = (bf16[2,16,3072]{2,1,0:T(8,128)(2,1)S(1)}, bf16[2,16,3072]{2,1,0:T(8,128)(2,1)S(1)}, u32[]{:S(2)}, u32[]{:S(2)}) collective-permute-start(bf16[2,16,3072]{2,1,0:T(8,128)(2,1)S(1)} %get-tuple-element.41), channel_id=1, source_target_pairs={{4,5},{5,4},{6,7},{7,6},{12,13},{13,12},{14,15},{15,14},{20,21},{2... | collective-permute-start | bytes 589832 | tf_op jit(solution)/shard_map/ppermute | solution.py:105
  69.4 6.4 %collective-permute-start.14 = (bf16[2,16,3072]{2,1,0:T(8,128)(2,1)S(1)}, bf16[2,16,3072]{2,1,0:T(8,128)(2,1)S(1)}, u32[]{:S(2)}, u32[]{:S(2)}) collective-permute-start(bf16[2,16,3072]{2,1,0:T(8,128)(2,1)S(1)} %get-tuple-element.40), channel_id=1, source_target_pairs={{4,6},{5,7},{6,4},{7,5},{12,14},{13,15},{14,12},{15,13},{20,22},{2... | collective-permute-start | bytes 589832 | tf_op jit(solution)/shard_map/ppermute | solution.py:105
  71.7 7.3 %collective-permute-start.15 = (bf16[2,16,3072]{2,1,0:T(8,128)(2,1)S(1)}, bf16[2,16,3072]{2,1,0:T(8,128)(2,1)S(1)}, u32[]{:S(2)}, u32[]{:S(2)}) collective-permute-start(bf16[2,16,3072]{2,1,0:T(8,128)(2,1)S(1)} %get-tuple-element.42), channel_id=1, source_target_pairs={{4,7},{5,6},{6,5},{7,4},{12,15},{13,14},{14,13},{15,12},{20,23},{2... | collective-permute-start | bytes 589832 | tf_op jit(solution)/shard_map/ppermute | solution.py:105
  79.8 13.3 %copy-start.2 = (bf16[704,768]{1,0:T(8,128)(2,1)S(1)}, bf16[704,768]{1,0:T(8,128)(2,1)}, u32[]{:S(2)}) copy-start(bf16[704,768]{1,0:T(8,128)(2,1)} %pad_maximum_fusion) | copy-start | bytes 3244036
  80.3 9.3 %collective-permute-start.16 = (bf16[128,176]{0,1:T(8,128)(2,1)S(1)}, bf16[128,176]{0,1:T(8,128)(2,1)S(1)}, u32[]{:S(2)}, u32[]{:S(2)}) collective-permute-start(bf16[128,176]{0,1:T(8,128)(2,1)S(1)} %fusion.7), channel_id=1, source_target_pairs={{4,12},{5,13},{6,14},{7,15},{12,4},{13,5},{14,6},{15,7},{20,28},{2... | collective-permute-start | bytes 135176 | tf_op jit(solution)/shard_map/ppermute | solution.py:116
  82.6 7.0 %collective-permute-start.17 = (bf16[128,176]{0,1:T(8,128)(2,1)S(1)}, bf16[128,176]{0,1:T(8,128)(2,1)S(1)}, u32[]{:S(2)}, u32[]{:S(2)}) collective-permute-start(bf16[128,176]{0,1:T(8,128)(2,1)S(1)} %fusion.7), channel_id=1, source_target_pairs={{4,20},{5,21},{6,22},{7,23},{12,28},{13,29},{14,30},{15,31},{20,4}... | collective-permute-start | bytes 135176 | tf_op jit(solution)/shard_map/ppermute | solution.py:116
  86.6 6.6 %collective-permute-start.18 = (bf16[128,176]{0,1:T(8,128)(2,1)S(1)}, bf16[128,176]{0,1:T(8,128)(2,1)S(1)}, u32[]{:S(2)}, u32[]{:S(2)}) collective-permute-start(bf16[128,176]{0,1:T(8,128)(2,1)S(1)} %fusion.7), channel_id=1, source_target_pairs={{4,28},{5,29},{6,30},{7,31},{12,20},{13,21},{14,22},{15,23},{20,12... | collective-permute-start | bytes 135176 | tf_op jit(solution)/shard_map/ppermute | solution.py:116
  94.9 7.9 %all-to-all-start.2 = ((bf16[2,4,16,768]{3,2,0,1:T(8,128)(2,1)}), bf16[2,4,16,768]{3,2,0,1:T(8,128)(2,1)S(1)}, u32[]{:S(2)}, u32[]{:S(2)}) async-start(bf16[2,4,16,768]{3,2,0,1:T(8,128)(2,1)} %select_bitcast_fusion.1), calls=%async_computation.2 | async-start | bytes 393216 | tf_op jit(solution)/shard_map/all_to_all | solution.py:128
  (5 other events, 20.3 us)

commit v14 on v10

--- a/solution.py
+++ b/solution.py
@@ -85,21 +85,26 @@
     maps = [build_maps(route_ids[m], route_gates[m], ering, e_me, rows_all) for m in range(micro)]
     dispatch_map = jnp.stack([mp[0] for mp in maps])
     combine_map = jnp.stack([mp[1] for mp in maps])
+    absolute_dispatch = dispatch_map
     if ering.xor:
         maps = [build_maps(route_ids[m], route_gates[m], ering, 0, rows_all) for m in range(micro)]
-        dispatch_map = jnp.stack([mp[0] for mp in maps])
+        absolute_dispatch = jnp.stack([mp[0] for mp in maps])
         combine_map = jnp.stack([mp[1] for mp in maps])
 
     def layer(current, p):
-        outgoing = jnp.einsum("mrt,mtd->mrd", dispatch_map, current, preferred_element_type=jnp.float32)
-        outgoing = outgoing.astype(jnp.bfloat16).reshape(micro, n_exp, CAP, width)
-        if ering.xor:
+        if p == 0 and ering.xor:
+            outgoing = jnp.einsum("mrt,mtd->mrd", absolute_dispatch, current, preferred_element_type=jnp.float32)
+            outgoing = outgoing.astype(jnp.bfloat16).reshape(micro, n_exp, CAP, width)
             flat_rows = lax.all_to_all(outgoing, "expert", 1, 1, tiled=True).reshape(-1, width)
+            in_block_order = True
         else:
+            outgoing = jnp.einsum("mrt,mtd->mrd", dispatch_map, current, preferred_element_type=jnp.float32)
+            outgoing = outgoing.astype(jnp.bfloat16).reshape(micro, n_exp, CAP, width)
             arrived = [outgoing[:, 0]]
             for s in range(1, n_exp):
                 arrived.append(lax.ppermute(outgoing[:, s], AXES, expert_pairs(p, s, False)))
             flat_rows = jnp.stack(arrived, axis=1).reshape(-1, width)
+            in_block_order = False
         squares = jnp.mean(jnp.square(flat_rows.astype(jnp.float32)), axis=1, keepdims=True)
         inv_rms = lax.rsqrt(squares + 1e-05)
         gate_act = jnp.dot(flat_rows, gate_local, preferred_element_type=jnp.float32) * inv_rms
@@ -115,7 +120,12 @@
         expert_out = jnp.dot(hidden_full, down_full, preferred_element_type=jnp.float32).astype(jnp.bfloat16)
         expert_out = expert_out.reshape(micro, n_exp, CAP, columns)
         if ering.xor:
-            returned = lax.all_to_all(expert_out, "expert", 1, 1, tiled=True).reshape(micro, rows_all, columns)
+            if in_block_order:
+                by_block = expert_out
+            else:
+                order = jnp.stack([ering.place(j, e_me) for j in range(n_exp)])
+                by_block = jnp.take(expert_out, order, axis=1)
+            returned = lax.all_to_all(by_block, "expert", 1, 1, tiled=True).reshape(micro, rows_all, columns)
         else:
             returned = [expert_out[:, 0]]
             for s in range(1, n_exp):

time: 104 us -> 105 us (level)
  blocking collectives: 12.3 us -> 0 us
  starting transfers between devices: 31.3 us -> 39.5 us
  waiting for transfers between devices: 44.4 us -> 47.9 us
  other arithmetic: 1.56 us -> 3.15 us
    all_to_all x1 -> x0, blocking collectives: 12.3 us -> none  [layer(): lax.all_to_all(outgoing, 'expert', 1, 1, tiled=True).reshape(-1, width)]
    ppermute x0 -> x3, starting transfers between devices: none -> 8.37 us  [layer(): lax.ppermute(outgoing[:, s], AXES, expert_pairs(p, s, False))]
    ppermute x0 -> x3, waiting for transfers between devices: none -> 3.75 us  [layer(): lax.ppermute(outgoing[:, s], AXES, expert_pairs(p, s, False))]
  transfers between devices with their start and end apart: 16 -> 19, of which waited for: 10 -> 11; matrix products, arithmetic and copies ran while one was open for 2% -> 3% of each run, Pallas kernels for 0% -> 0%
where the time goes in v14:
time: 105 us; the launch traced here: 104 us
  waiting for transfers between devices  47.9 us (46%)
  starting transfers between devices  39.5 us (38%)
  local copies, waits for them, and re-layouts  8.72 us (8%)
  matrix products  4.46 us (4%)
  other arithmetic  3.15 us (3%)
    ppermute x4, waiting for transfers between devices, per_device(): parts.append(lax.ppermute(cols, AXES, pairs))  21.7 us
    ppermute x3, waiting for transfers between devices, per_device(): lax.ppermute(down_parts[s], 'dp', [(i, dring.ahead(i, s)) for i in range(...  13.2 us
    ppermute x6, starting transfers between devices, layer(): parts.append(lax.ppermute(hidden, AXES, dp_pairs(p, s)))  11.3 us
    ppermute x3, starting transfers between devices, layer(): lax.ppermute(outgoing[:, s], AXES, expert_pairs(p, s, False))  8.37 us
    all_to_all x2, waiting for transfers between devices, layer(): lax.all_to_all(by_block, 'expert', 1, 1, tiled=True)  7.9 us
    all_to_all x2, starting transfers between devices, layer(): lax.all_to_all(by_block, 'expert', 1, 1, tiled=True)  6.73 us
    ppermute x4, starting transfers between devices, per_device(): parts.append(lax.ppermute(cols, AXES, pairs))  5.17 us
    all_to_all x1, starting transfers between devices, layer(): lax.all_to_all(outgoing, 'expert', 1, 1, tiled=True).reshape(-1, width)  4.26 us
  transfers between devices with their start and end apart: 19, of which 11 were waited for; matrix products, arithmetic and copies ran while one was open for 3% of the time, Pallas kernels for 0%

profile of v14, /device:TPU:1, one launch (start us, length us, event | category | flops | bytes accessed | tf_op | source)
XLA Modules:
  0.0 104.3 jit_solution(15508617698177510085)
XLA Ops:
  0.0 2.2 %dynamic-slice_bitcast_fusion = (bf16[176,768]{1,0:T(8,128)(2,1)}, bf16[176,768]{1,0:T(8,128)(2,1)}, bf16[176,768]{1,0:T(8,128)(2,1)S(1)}, bf16[176,768]{1,0:T(8,128)(2,1)}) fusion(bf16[1,1,176,3072]{3,2,1,0:T(8,128)(2,1)} %param.11, s32[]{:T(128)S(6)} %select_n.79, s32[]{:T(128)S(6)} %select_n.77, s32[]{:T(128)S(6)} %select_n.76, s32[]{:T(128)S(6)} %select_n.78), kind=kLoop, calls=%fused_computation.29 | loop fusion | bytes 2162704 | tf_op jit(solution)/shard_map/dynamic_slice | solution.py:74
  5.8 4.3 %all-to-all-start = ((bf16[2,4,16,3072]{3,2,0,1:T(8,128)(2,1)}), bf16[2,4,16,3072]{3,2,0,1:T(8,128)(2,1)S(1)}, u32[]{:S(2)}, u32[]{:S(2)}) async-start(bf16[2,4,16,3072]{3,2,0,1:T(8,128)(2,1)} %copy.141), calls=%async_computation | async-start | bytes 1572864 | tf_op jit(solution)/shard_map/all_to_all | solution.py:98
  10.0 1.4 %collective-permute-start.3 = (bf16[176,768]{1,0:T(8,128)(2,1)}, bf16[176,768]{1,0:T(8,128)(2,1)S(1)}, u32[]{:S(2)}, u32[]{:S(2)}) collective-permute-start(bf16[176,768]{1,0:T(8,128)(2,1)} %get-tuple-element.12), channel_id=1, source_target_pairs={{0,8},{8,0},{16,24},{24,16},{1,9},{9,1},{17,25},{25,17},{2,10},{10... | collective-permute-start | bytes 811016 | tf_op jit(solution)/shard_map/ppermute | solution.py:78
  11.5 2.3 %collective-permute-start.4 = (bf16[176,768]{1,0:T(8,128)(2,1)}, bf16[176,768]{1,0:T(8,128)(2,1)S(1)}, u32[]{:S(2)}, u32[]{:S(2)}) collective-permute-start(bf16[176,768]{1,0:T(8,128)(2,1)} %get-tuple-element.13), channel_id=1, source_target_pairs={{0,16},{8,24},{16,0},{24,8},{1,17},{9,25},{17,1},{25,9},{2,18},{10... | collective-permute-start | bytes 811016 | tf_op jit(solution)/shard_map/ppermute | solution.py:78
  13.9 8.3 %collective-permute-done.3 = bf16[176,768]{1,0:T(8,128)(2,1)S(1)} collective-permute-done((bf16[176,768]{1,0:T(8,128)(2,1)}, bf16[176,768]{1,0:T(8,128)(2,1)S(1)}, u32[]{:S(2)}, u32[]{:S(2)}) %collective-permute-start.3) | collective-permute-done | bytes 270368 | tf_op jit(solution)/shard_map/ppermute | solution.py:78
  26.8 4.5 %collective-permute-done.5 = bf16[176,768]{1,0:T(8,128)(2,1)} collective-permute-done((bf16[176,768]{1,0:T(8,128)(2,1)}, bf16[176,768]{1,0:T(8,128)(2,1)}, u32[]{:S(2)}, u32[]{:S(2)}) %collective-permute-start.5) | collective-permute-done | bytes 270368 | tf_op jit(solution)/shard_map/ppermute | solution.py:78
  33.4 3.4 %all-to-all-start.1 = ((bf16[2,4,16,768]{3,2,0,1:T(8,128)(2,1)}), bf16[2,4,16,768]{3,2,0,1:T(8,128)(2,1)S(1)}, u32[]{:S(2)}, u32[]{:S(2)}) async-start(bf16[2,4,16,768]{3,2,0,1:T(8,128)(2,1)} %copy.144), calls=%async_computation.1 | async-start | bytes 393216 | tf_op jit(solution)/shard_map/all_to_all | solution.py:128
  36.9 3.9 %all-to-all-done.1 = bf16[2,4,16,768]{3,2,0,1:T(8,128)(2,1)S(1)} async-done(((bf16[2,4,16,768]{3,2,0,1:T(8,128)(2,1)}), bf16[2,4,16,768]{3,2,0,1:T(8,128)(2,1)S(1)}, u32[]{:S(2)}, u32[]{:S(2)}) %all-to-all-start.1) | async-done | bytes 196640 | tf_op jit(solution)/shard_map/all_to_all | solution.py:128
  41.0 1.3 %collective-permute-start.9 = (bf16[2,24,768]{2,1,0:T(8,128)(2,1)S(1)}, bf16[2,24,768]{2,1,0:T(8,128)(2,1)S(1)}, u32[]{:S(2)}, u32[]{:S(2)}) collective-permute-start(bf16[2,24,768]{2,1,0:T(8,128)(2,1)S(1)} %fusion), channel_id=1, source_target_pairs={{0,28},{1,29},{2,30},{3,31},{8,20},{9,21},{10,22},{11,23},{16,12},... | collective-permute-start | bytes 221192 | tf_op jit(solution)/shard_map/ppermute | solution.py:156
  42.3 1.3 %collective-permute-start.8 = (bf16[2,24,768]{2,1,0:T(8,128)(2,1)S(1)}, bf16[2,24,768]{2,1,0:T(8,128)(2,1)S(1)}, u32[]{:S(2)}, u32[]{:S(2)}) collective-permute-start(bf16[2,24,768]{2,1,0:T(8,128)(2,1)S(1)} %fusion), channel_id=1, source_target_pairs={{0,20},{1,21},{2,22},{3,23},{8,28},{9,29},{10,30},{11,31},{16,4},{... | collective-permute-start | bytes 221192 | tf_op jit(solution)/shard_map/ppermute | solution.py:156
  43.6 1.3 %collective-permute-start.7 = (bf16[2,24,768]{2,1,0:T(8,128)(2,1)S(1)}, bf16[2,24,768]{2,1,0:T(8,128)(2,1)S(1)}, u32[]{:S(2)}, u32[]{:S(2)}) collective-permute-start(bf16[2,24,768]{2,1,0:T(8,128)(2,1)S(1)} %fusion), channel_id=1, source_target_pairs={{0,12},{1,13},{2,14},{3,15},{8,4},{9,5},{10,6},{11,7},{16,28},{17,... | collective-permute-start | bytes 221192 | tf_op jit(solution)/shard_map/ppermute | solution.py:156
  44.9 1.3 %collective-permute-start.6 = (bf16[2,24,768]{2,1,0:T(8,128)(2,1)S(1)}, bf16[2,24,768]{2,1,0:T(8,128)(2,1)S(1)}, u32[]{:S(2)}, u32[]{:S(2)}) collective-permute-start(bf16[2,24,768]{2,1,0:T(8,128)(2,1)S(1)} %fusion), channel_id=1, source_target_pairs={{0,4},{1,5},{2,6},{3,7},{8,12},{9,13},{10,14},{11,15},{16,20},{17,... | collective-permute-start | bytes 221192 | tf_op jit(solution)/shard_map/ppermute | solution.py:156
  46.3 18.8 %collective-permute-done.9 = bf16[2,24,768]{2,1,0:T(8,128)(2,1)S(1)} collective-permute-done((bf16[2,24,768]{2,1,0:T(8,128)(2,1)S(1)}, bf16[2,24,768]{2,1,0:T(8,128)(2,1)S(1)}, u32[]{:S(2)}, u32[]{:S(2)}) %collective-permute-start.9) | collective-permute-done | bytes 73760 | tf_op jit(solution)/shard_map/ppermute | solution.py:156
  65.1 2.5 %collective-permute-done.8 = bf16[2,24,768]{2,1,0:T(8,128)(2,1)S(1)} collective-permute-done((bf16[2,24,768]{2,1,0:T(8,128)(2,1)S(1)}, bf16[2,24,768]{2,1,0:T(8,128)(2,1)S(1)}, u32[]{:S(2)}, u32[]{:S(2)}) %collective-permute-start.8) | collective-permute-done | bytes 73760 | tf_op jit(solution)/shard_map/ppermute | solution.py:156
  69.3 2.7 %collective-permute-start.12 = (bf16[2,16,3072]{2,1,0:T(8,128)(2,1)S(1)}, bf16[2,16,3072]{2,1,0:T(8,128)(2,1)S(1)}, u32[]{:S(2)}, u32[]{:S(2)}) collective-permute-start(bf16[2,16,3072]{2,1,0:T(8,128)(2,1)S(1)} %get-tuple-element.28), channel_id=1, source_target_pairs={{4,7},{5,6},{6,5},{7,4},{12,15},{13,14},{14,13},{15,12},{20,23},{2... | collective-permute-start | bytes 589832 | tf_op jit(solution)/shard_map/ppermute | solution.py:105
  72.0 3.1 %collective-permute-start.11 = (bf16[2,16,3072]{2,1,0:T(8,128)(2,1)S(1)}, bf16[2,16,3072]{2,1,0:T(8,128)(2,1)S(1)}, u32[]{:S(2)}, u32[]{:S(2)}) collective-permute-start(bf16[2,16,3072]{2,1,0:T(8,128)(2,1)S(1)} %get-tuple-element.26), channel_id=1, source_target_pairs={{4,6},{5,7},{6,4},{7,5},{12,14},{13,15},{14,12},{15,13},{20,22},{2... | collective-permute-start | bytes 589832 | tf_op jit(solution)/shard_map/ppermute | solution.py:105
  75.1 2.6 %collective-permute-start.10 = (bf16[2,16,3072]{2,1,0:T(8,128)(2,1)S(1)}, bf16[2,16,3072]{2,1,0:T(8,128)(2,1)S(1)}, u32[]{:S(2)}, u32[]{:S(2)}) collective-permute-start(bf16[2,16,3072]{2,1,0:T(8,128)(2,1)S(1)} %get-tuple-element.27), channel_id=1, source_target_pairs={{4,5},{5,4},{6,7},{7,6},{12,13},{13,12},{14,15},{15,14},{20,21},{2... | collective-permute-start | bytes 589832 | tf_op jit(solution)/shard_map/ppermute | solution.py:105
  78.7 2.8 %collective-permute-done.10 = bf16[2,16,3072]{2,1,0:T(8,128)(2,1)S(1)} collective-permute-done((bf16[2,16,3072]{2,1,0:T(8,128)(2,1)S(1)}, bf16[2,16,3072]{2,1,0:T(8,128)(2,1)S(1)}, u32[]{:S(2)}, u32[]{:S(2)}) %collective-permute-start.10) | collective-permute-done | bytes 196640 | tf_op jit(solution)/shard_map/ppermute | solution.py:105
  83.6 3.3 %collective-permute-start.15 = (bf16[128,176]{0,1:T(8,128)(2,1)S(1)}, bf16[128,176]{0,1:T(8,128)(2,1)S(1)}, u32[]{:S(2)}, u32[]{:S(2)}) collective-permute-start(bf16[128,176]{0,1:T(8,128)(2,1)S(1)} %fusion.7), channel_id=1, source_target_pairs={{4,28},{5,29},{6,30},{7,31},{12,20},{13,21},{14,22},{15,23},{20,12... | collective-permute-start | bytes 135176 | tf_op jit(solution)/shard_map/ppermute | solution.py:116
  86.9 1.9 %collective-permute-start.14 = (bf16[128,176]{0,1:T(8,128)(2,1)S(1)}, bf16[128,176]{0,1:T(8,128)(2,1)S(1)}, u32[]{:S(2)}, u32[]{:S(2)}) collective-permute-start(bf16[128,176]{0,1:T(8,128)(2,1)S(1)} %fusion.7), channel_id=1, source_target_pairs={{4,20},{5,21},{6,22},{7,23},{12,28},{13,29},{14,30},{15,31},{20,4}... | collective-permute-start | bytes 135176 | tf_op jit(solution)/shard_map/ppermute | solution.py:116
  88.8 4.0 %collective-permute-start.13 = (bf16[128,176]{0,1:T(8,128)(2,1)S(1)}, bf16[128,176]{0,1:T(8,128)(2,1)S(1)}, u32[]{:S(2)}, u32[]{:S(2)}) collective-permute-start(bf16[128,176]{0,1:T(8,128)(2,1)S(1)} %fusion.7), channel_id=1, source_target_pairs={{4,12},{5,13},{6,14},{7,15},{12,4},{13,5},{14,6},{15,7},{20,28},{2... | collective-permute-start | bytes 135176 | tf_op jit(solution)/shard_map/ppermute | solution.py:116
  93.0 1.3 %collective-permute-done.13 = bf16[128,176]{0,1:T(8,128)(2,1)S(1)} collective-permute-done((bf16[128,176]{0,1:T(8,128)(2,1)S(1)}, bf16[128,176]{0,1:T(8,128)(2,1)S(1)}, u32[]{:S(2)}, u32[]{:S(2)}) %collective-permute-start.13) | collective-permute-done | bytes 45088 | tf_op jit(solution)/shard_map/ppermute | solution.py:116
  96.0 3.4 %all-to-all-start.2 = ((bf16[2,4,16,768]{3,2,0,1:T(8,128)(2,1)}), bf16[2,4,16,768]{3,2,0,1:T(8,128)(2,1)S(1)}, u32[]{:S(2)}, u32[]{:S(2)}) async-start(bf16[2,4,16,768]{3,2,0,1:T(8,128)(2,1)} %select_bitcast_fusion.1), calls=%async_computation.2 | async-start | bytes 393216 | tf_op jit(solution)/shard_map/all_to_all | solution.py:128
  99.4 4.0 %all-to-all-done.2 = bf16[2,4,16,768]{3,2,0,1:T(8,128)(2,1)S(1)} async-done(((bf16[2,4,16,768]{3,2,0,1:T(8,128)(2,1)}), bf16[2,4,16,768]{3,2,0,1:T(8,128)(2,1)S(1)}, u32[]{:S(2)}, u32[]{:S(2)}) %all-to-all-start.2) | async-done | bytes 196640 | tf_op jit(solution)/shard_map/all_to_all | solution.py:128
  (92 shorter events, 17.9 us)
Async XLA Ops:
  0.0 23.1 %copy-start = (bf16[1,1,3072,176]{2,3,1,0:T(8,128)(2,1)S(1)}, bf16[1,1,3072,176]{2,3,1,0:T(8,128)(2,1)}, u32[]{:S(2)}) copy-start(bf16[1,1,3072,176]{2,3,1,0:T(8,128)(2,1)} %param.9) | copy-start | bytes 3244036
  5.8 16.8 %all-to-all-start = ((bf16[2,4,16,3072]{3,2,0,1:T(8,128)(2,1)}), bf16[2,4,16,3072]{3,2,0,1:T(8,128)(2,1)S(1)}, u32[]{:S(2)}, u32[]{:S(2)}) async-start(bf16[2,4,16,3072]{3,2,0,1:T(8,128)(2,1)} %copy.141), calls=%async_computation | async-start | bytes 1572864 | tf_op jit(solution)/shard_map/all_to_all | solution.py:98
  10.0 12.1 %collective-permute-start.3 = (bf16[176,768]{1,0:T(8,128)(2,1)}, bf16[176,768]{1,0:T(8,128)(2,1)S(1)}, u32[]{:S(2)}, u32[]{:S(2)}) collective-permute-start(bf16[176,768]{1,0:T(8,128)(2,1)} %get-tuple-element.12), channel_id=1, source_target_pairs={{0,8},{8,0},{16,24},{24,16},{1,9},{9,1},{17,25},{25,17},{2,10},{10... | collective-permute-start | bytes 811016 | tf_op jit(solution)/shard_map/ppermute | solution.py:78
  11.5 11.1 %collective-permute-start.4 = (bf16[176,768]{1,0:T(8,128)(2,1)}, bf16[176,768]{1,0:T(8,128)(2,1)S(1)}, u32[]{:S(2)}, u32[]{:S(2)}) collective-permute-start(bf16[176,768]{1,0:T(8,128)(2,1)} %get-tuple-element.13), channel_id=1, source_target_pairs={{0,16},{8,24},{16,0},{24,8},{1,17},{9,25},{17,1},{25,9},{2,18},{10... | collective-permute-start | bytes 811016 | tf_op jit(solution)/shard_map/ppermute | solution.py:78
  13.8 17.5 %collective-permute-start.5 = (bf16[176,768]{1,0:T(8,128)(2,1)}, bf16[176,768]{1,0:T(8,128)(2,1)}, u32[]{:S(2)}, u32[]{:S(2)}) collective-permute-start(bf16[176,768]{1,0:T(8,128)(2,1)} %get-tuple-element.14), channel_id=1, source_target_pairs={{0,24},{8,16},{16,8},{24,0},{1,25},{9,17},{17,9},{25,1},{2,26},{10... | collective-permute-start | bytes 811016 | tf_op jit(solution)/shard_map/ppermute | solution.py:78
  24.8 7.5 %collective-permute-start.2 = (bf16[128,176]{0,1:T(8,128)(2,1)S(1)}, bf16[128,176]{0,1:T(8,128)(2,1)S(1)}, u32[]{:S(2)}, u32[]{:S(2)}) collective-permute-start(bf16[128,176]{0,1:T(8,128)(2,1)S(1)} %fusion.6), channel_id=1, source_target_pairs={{0,24},{1,25},{2,26},{3,27},{8,16},{9,17},{10,18},{11,19},{16,8},{... | collective-permute-start | bytes 135176 | tf_op jit(solution)/shard_map/ppermute | solution.py:116
  25.4 6.9 %collective-permute-start.1 = (bf16[128,176]{0,1:T(8,128)(2,1)S(1)}, bf16[128,176]{0,1:T(8,128)(2,1)S(1)}, u32[]{:S(2)}, u32[]{:S(2)}) collective-permute-start(bf16[128,176]{0,1:T(8,128)(2,1)S(1)} %fusion.6), channel_id=1, source_target_pairs={{0,16},{1,17},{2,18},{3,19},{8,24},{9,25},{10,26},{11,27},{16,0},{... | collective-permute-start | bytes 135176 | tf_op jit(solution)/shard_map/ppermute | solution.py:116
  26.1 6.2 %collective-permute-start = (bf16[128,176]{0,1:T(8,128)(2,1)S(1)}, bf16[128,176]{0,1:T(8,128)(2,1)S(1)}, u32[]{:S(2)}, u32[]{:S(2)}) collective-permute-start(bf16[128,176]{0,1:T(8,128)(2,1)S(1)} %fusion.6), channel_id=1, source_target_pairs={{0,8},{1,9},{2,10},{3,11},{8,0},{9,1},{10,2},{11,3},{16,24},{17,25... | collective-permute-start | bytes 135176 | tf_op jit(solution)/shard_map/ppermute | solution.py:116
  32.3 4.5 %copy-start.7 = (s32[24,2]{0,1:T(2,128)S(1)}, s32[24,2]{0,1:T(2,128)}, u32[]{:S(2)}) copy-start(s32[24,2]{0,1:T(2,128)} %get-tuple-element.29) | copy-start | bytes 580
  32.3 4.5 %copy-start.8 = (s32[24,2]{0,1:T(2,128)S(1)}, s32[24,2]{0,1:T(2,128)}, u32[]{:S(2)}) copy-start(s32[24,2]{0,1:T(2,128)} %get-tuple-element.34) | copy-start | bytes 580
  33.4 7.4 %all-to-all-start.1 = ((bf16[2,4,16,768]{3,2,0,1:T(8,128)(2,1)}), bf16[2,4,16,768]{3,2,0,1:T(8,128)(2,1)S(1)}, u32[]{:S(2)}, u32[]{:S(2)}) async-start(bf16[2,4,16,768]{3,2,0,1:T(8,128)(2,1)} %copy.144), calls=%async_computation.1 | async-start | bytes 393216 | tf_op jit(solution)/shard_map/all_to_all | solution.py:128
  41.0 27.0 %copy-start.4 = (bf16[2,24,768]{2,1,0:T(8,128)(2,1)}, bf16[2,24,768]{2,1,0:T(8,128)(2,1)S(1)}, u32[]{:S(2)}) copy-start(bf16[2,24,768]{2,1,0:T(8,128)(2,1)S(1)} %fusion) | copy-start | bytes 221188
  41.0 24.1 %collective-permute-start.9 = (bf16[2,24,768]{2,1,0:T(8,128)(2,1)S(1)}, bf16[2,24,768]{2,1,0:T(8,128)(2,1)S(1)}, u32[]{:S(2)}, u32[]{:S(2)}) collective-permute-start(bf16[2,24,768]{2,1,0:T(8,128)(2,1)S(1)} %fusion), channel_id=1, source_target_pairs={{0,28},{1,29},{2,30},{3,31},{8,20},{9,21},{10,22},{11,23},{16,12},... | collective-permute-start | bytes 221192 | tf_op jit(solution)/shard_map/ppermute | solution.py:156
  42.3 25.2 %collective-permute-start.8 = (bf16[2,24,768]{2,1,0:T(8,128)(2,1)S(1)}, bf16[2,24,768]{2,1,0:T(8,128)(2,1)S(1)}, u32[]{:S(2)}, u32[]{:S(2)}) collective-permute-start(bf16[2,24,768]{2,1,0:T(8,128)(2,1)S(1)} %fusion), channel_id=1, source_target_pairs={{0,20},{1,21},{2,22},{3,23},{8,28},{9,29},{10,30},{11,31},{16,4},{... | collective-permute-start | bytes 221192 | tf_op jit(solution)/shard_map/ppermute | solution.py:156
  43.6 24.4 %collective-permute-start.7 = (bf16[2,24,768]{2,1,0:T(8,128)(2,1)S(1)}, bf16[2,24,768]{2,1,0:T(8,128)(2,1)S(1)}, u32[]{:S(2)}, u32[]{:S(2)}) collective-permute-start(bf16[2,24,768]{2,1,0:T(8,128)(2,1)S(1)} %fusion), channel_id=1, source_target_pairs={{0,12},{1,13},{2,14},{3,15},{8,4},{9,5},{10,6},{11,7},{16,28},{17,... | collective-permute-start | bytes 221192 | tf_op jit(solution)/shard_map/ppermute | solution.py:156
  44.9 23.1 %collective-permute-start.6 = (bf16[2,24,768]{2,1,0:T(8,128)(2,1)S(1)}, bf16[2,24,768]{2,1,0:T(8,128)(2,1)S(1)}, u32[]{:S(2)}, u32[]{:S(2)}) collective-permute-start(bf16[2,24,768]{2,1,0:T(8,128)(2,1)S(1)} %fusion), channel_id=1, source_target_pairs={{0,4},{1,5},{2,6},{3,7},{8,12},{9,13},{10,14},{11,15},{16,20},{17,... | collective-permute-start | bytes 221192 | tf_op jit(solution)/shard_map/ppermute | solution.py:156
  69.3 8.5 %collective-permute-start.12 = (bf16[2,16,3072]{2,1,0:T(8,128)(2,1)S(1)}, bf16[2,16,3072]{2,1,0:T(8,128)(2,1)S(1)}, u32[]{:S(2)}, u32[]{:S(2)}) collective-permute-start(bf16[2,16,3072]{2,1,0:T(8,128)(2,1)S(1)} %get-tuple-element.28), channel_id=1, source_target_pairs={{4,7},{5,6},{6,5},{7,4},{12,15},{13,14},{14,13},{15,12},{20,23},{2... | collective-permute-start | bytes 589832 | tf_op jit(solution)/shard_map/ppermute | solution.py:105
  72.0 6.7 %collective-permute-start.11 = (bf16[2,16,3072]{2,1,0:T(8,128)(2,1)S(1)}, bf16[2,16,3072]{2,1,0:T(8,128)(2,1)S(1)}, u32[]{:S(2)}, u32[]{:S(2)}) collective-permute-start(bf16[2,16,3072]{2,1,0:T(8,128)(2,1)S(1)} %get-tuple-element.26), channel_id=1, source_target_pairs={{4,6},{5,7},{6,4},{7,5},{12,14},{13,15},{14,12},{15,13},{20,22},{2... | collective-permute-start | bytes 589832 | tf_op jit(solution)/shard_map/ppermute | solution.py:105
  75.1 6.4 %collective-permute-start.10 = (bf16[2,16,3072]{2,1,0:T(8,128)(2,1)S(1)}, bf16[2,16,3072]{2,1,0:T(8,128)(2,1)S(1)}, u32[]{:S(2)}, u32[]{:S(2)}) collective-permute-start(bf16[2,16,3072]{2,1,0:T(8,128)(2,1)S(1)} %get-tuple-element.27), channel_id=1, source_target_pairs={{4,5},{5,4},{6,7},{7,6},{12,13},{13,12},{14,15},{15,14},{20,21},{2... | collective-permute-start | bytes 589832 | tf_op jit(solution)/shard_map/ppermute | solution.py:105
  83.6 9.4 %collective-permute-start.15 = (bf16[128,176]{0,1:T(8,128)(2,1)S(1)}, bf16[128,176]{0,1:T(8,128)(2,1)S(1)}, u32[]{:S(2)}, u32[]{:S(2)}) collective-permute-start(bf16[128,176]{0,1:T(8,128)(2,1)S(1)} %fusion.7), channel_id=1, source_target_pairs={{4,28},{5,29},{6,30},{7,31},{12,20},{13,21},{14,22},{15,23},{20,12... | collective-permute-start | bytes 135176 | tf_op jit(solution)/shard_map/ppermute | solution.py:116
  86.9 6.1 %collective-permute-start.14 = (bf16[128,176]{0,1:T(8,128)(2,1)S(1)}, bf16[128,176]{0,1:T(8,128)(2,1)S(1)}, u32[]{:S(2)}, u32[]{:S(2)}) collective-permute-start(bf16[128,176]{0,1:T(8,128)(2,1)S(1)} %fusion.7), channel_id=1, source_target_pairs={{4,20},{5,21},{6,22},{7,23},{12,28},{13,29},{14,30},{15,31},{20,4}... | collective-permute-start | bytes 135176 | tf_op jit(solution)/shard_map/ppermute | solution.py:116
  88.8 5.5 %collective-permute-start.13 = (bf16[128,176]{0,1:T(8,128)(2,1)S(1)}, bf16[128,176]{0,1:T(8,128)(2,1)S(1)}, u32[]{:S(2)}, u32[]{:S(2)}) collective-permute-start(bf16[128,176]{0,1:T(8,128)(2,1)S(1)} %fusion.7), channel_id=1, source_target_pairs={{4,12},{5,13},{6,14},{7,15},{12,4},{13,5},{14,6},{15,7},{20,28},{2... | collective-permute-start | bytes 135176 | tf_op jit(solution)/shard_map/ppermute | solution.py:116
  94.6 8.7 %copy-start.5 = (bf16[2,24,768]{2,1,0:T(8,128)(2,1)S(1)}, bf16[2,24,768]{2,1,0:T(8,128)(2,1)}, u32[]{:S(2)}) copy-start(bf16[2,24,768]{2,1,0:T(8,128)(2,1)} %copy-done.4) | copy-start | bytes 221188
  96.0 7.4 %all-to-all-start.2 = ((bf16[2,4,16,768]{3,2,0,1:T(8,128)(2,1)}), bf16[2,4,16,768]{3,2,0,1:T(8,128)(2,1)S(1)}, u32[]{:S(2)}, u32[]{:S(2)}) async-start(bf16[2,4,16,768]{3,2,0,1:T(8,128)(2,1)} %select_bitcast_fusion.1), calls=%async_computation.2 | async-start | bytes 393216 | tf_op jit(solution)/shard_map/all_to_all | solution.py:128
  (5 other events, 11.4 us)

commit v15 on v9

--- a/solution.py
+++ b/solution.py
@@ -103,10 +103,11 @@
         up_act = jnp.dot(flat_rows, up_local, preferred_element_type=jnp.float32) * inv_rms
         hidden = (jax.nn.silu(gate_act) * up_act).astype(jnp.bfloat16)
         if small_dp:
-            parts = [hidden]
-            for s in range(1, n_dp):
-                parts.append(lax.ppermute(hidden, AXES, dp_pairs(p, s)))
-            hidden_full = jnp.concatenate(parts, axis=1)
+            spread = jnp.broadcast_to(hidden[None], (n_dp,) + hidden.shape)
+            gathered = lax.all_to_all(spread, "dp", 0, 0, tiled=True)
+            order = jnp.stack([dring.behind(d_me, s) for s in range(n_dp)])
+            gathered = jnp.take(gathered, order, axis=0)
+            hidden_full = jnp.transpose(gathered, (1, 0, 2)).reshape(hidden.shape[0], n_dp * units)
         else:
             hidden_full = lax.all_gather(hidden, "dp", axis=1, tiled=True)
         expert_out = jnp.dot(hidden_full, down_full, preferred_element_type=jnp.float32).astype(jnp.bfloat16)

time: 95.6 us -> 95.2 us (level)
  blocking collectives: 0 us -> 8.35 us
  starting transfers between devices: 40.1 us -> 33.4 us
  waiting for transfers between devices: 35 us -> 30.7 us
  local copies, waits for them, and re-layouts: 10.4 us -> 12.3 us
    ppermute x6 -> x0, starting transfers between devices: 11.3 us -> none  [layer(): parts.append(lax.ppermute(hidden, AXES, dp_pairs(p, s)))]
    ppermute x4, waiting for transfers between devices: 20.3 us -> 11 us  [per_device(): parts.append(lax.ppermute(cols, AXES, pairs))]
    all_to_all x0 -> x1, blocking collectives: none -> 8.35 us  [layer(): gathered = lax.all_to_all(spread, 'dp', 0, 0, tiled=True)]
    all_to_all x0 -> x1, waiting for transfers between devices: none -> 7.92 us  [layer(): gathered = lax.all_to_all(spread, 'dp', 0, 0, tiled=True)]
    all_to_all x0 -> x1, starting transfers between devices: none -> 4.51 us  [layer(): gathered = lax.all_to_all(spread, 'dp', 0, 0, tiled=True)]
    ppermute x3, waiting for transfers between devices: 1.51 us -> 0.01 us  [per_device(): lax.ppermute(down_parts[s], 'dp', [(i, dring.ahead(i, s)) for i in range(...]
    ppermute x6 -> x0, waiting for transfers between devices: 1.42 us -> none  [layer(): parts.append(lax.ppermute(hidden, AXES, dp_pairs(p, s)))]
    gather x0 -> x2, local copies, waits for them, and re-layouts: none -> 1.28 us  [layer(): gathered = jnp.take(gathered, order, axis=0)]
  transfers between devices with their start and end apart: 21 -> 16, of which waited for: 10 -> 9; matrix products, arithmetic and copies ran while one was open for 9% -> 10% of each run, Pallas kernels for 0% -> 0%
where the time goes in v15:
time: 95.2 us; the launch traced here: 94.3 us
  starting transfers between devices  33.4 us (35%)
  waiting for transfers between devices  30.7 us (32%)
  local copies, waits for them, and re-layouts  12.3 us (13%)
  blocking collectives  8.35 us (9%)
  other arithmetic  4.58 us (5%)
  matrix products  4.44 us (5%)
    ppermute x6, starting transfers between devices, layer(): lax.ppermute(outgoing[:, s], AXES, expert_pairs(p, s, False))  12.4 us
    ppermute x4, waiting for transfers between devices, per_device(): parts.append(lax.ppermute(cols, AXES, pairs))  11 us
    all_to_all x1, blocking collectives, layer(): gathered = lax.all_to_all(spread, 'dp', 0, 0, tiled=True)  8.35 us
    all_to_all x1, waiting for transfers between devices, layer(): gathered = lax.all_to_all(spread, 'dp', 0, 0, tiled=True)  7.92 us
    all_to_all x2, waiting for transfers between devices, layer(): lax.all_to_all(by_block, 'expert', 1, 1, tiled=True)  7.88 us
    all_to_all x2, starting transfers between devices, layer(): lax.all_to_all(by_block, 'expert', 1, 1, tiled=True)  6.8 us
    ppermute x4, starting transfers between devices, per_device(): parts.append(lax.ppermute(cols, AXES, pairs))  5.17 us
    all_to_all x1, starting transfers between devices, layer(): gathered = lax.all_to_all(spread, 'dp', 0, 0, tiled=True)  4.51 us
  transfers between devices with their start and end apart: 16, of which 9 were waited for; matrix products, arithmetic and copies ran while one was open for 10% of the time, Pallas kernels for 0%

profile of v15, /device:TPU:1, one launch (start us, length us, event | category | flops | bytes accessed | tf_op | source)
XLA Modules:
  0.0 94.3 jit_solution(11994145500577898993)
XLA Ops:
  0.0 2.2 %dynamic-slice_bitcast_fusion = (bf16[176,768]{1,0:T(8,128)(2,1)}, bf16[176,768]{1,0:T(8,128)(2,1)}, bf16[176,768]{1,0:T(8,128)(2,1)S(1)}, bf16[176,768]{1,0:T(8,128)(2,1)}) fusion(bf16[1,1,176,3072]{3,2,1,0:T(8,128)(2,1)} %param.15, s32[]{:T(128)S(6)} %select_n.72, s32[]{:T(128)S(6)} %select_n.70, s32[]{:T(128)S(6)} %select_n.69, s32[]{:T(128)S(6)} %select_n.71), kind=kLoop, calls=%fused_computation.33 | loop fusion | bytes 2162704 | tf_op jit(solution)/shard_map/dynamic_slice | solution.py:74
  2.2 2.1 %collective-permute-start.3 = (bf16[176,768]{1,0:T(8,128)(2,1)}, bf16[176,768]{1,0:T(8,128)(2,1)}, u32[]{:S(2)}, u32[]{:S(2)}) collective-permute-start(bf16[176,768]{1,0:T(8,128)(2,1)} %get-tuple-element.14), channel_id=1, source_target_pairs={{0,8},{8,0},{16,24},{24,16},{1,9},{9,1},{17,25},{25,17},{2,10},{10... | collective-permute-start | bytes 811016 | tf_op jit(solution)/shard_map/ppermute | solution.py:78
  4.4 2.3 %collective-permute-start.4 = (bf16[176,768]{1,0:T(8,128)(2,1)}, bf16[176,768]{1,0:T(8,128)(2,1)}, u32[]{:S(2)}, u32[]{:S(2)}) collective-permute-start(bf16[176,768]{1,0:T(8,128)(2,1)} %get-tuple-element.15), channel_id=1, source_target_pairs={{0,16},{8,24},{16,0},{24,8},{1,17},{9,25},{17,1},{25,9},{2,18},{10... | collective-permute-start | bytes 811016 | tf_op jit(solution)/shard_map/ppermute | solution.py:78
  9.4 1.3 %collective-permute-start = (bf16[2,16,3072]{2,1,0:T(8,128)(2,1)}, bf16[2,16,3072]{2,1,0:T(8,128)(2,1)}, u32[]{:S(2)}, u32[]{:S(2)}) collective-permute-start(bf16[2,16,3072]{2,1,0:T(8,128)(2,1)} %get-tuple-element.35), channel_id=1, source_target_pairs={{0,1},{1,0},{2,3},{3,2},{8,9},{9,8},{10,11},{11,10},{16,17},{17,16... | collective-permute-start | bytes 589832 | tf_op jit(solution)/shard_map/ppermute | solution.py:98
  10.7 1.4 %collective-permute-start.1 = (bf16[2,16,3072]{2,1,0:T(8,128)(2,1)S(1)}, bf16[2,16,3072]{2,1,0:T(8,128)(2,1)}, u32[]{:S(2)}, u32[]{:S(2)}) collective-permute-start(bf16[2,16,3072]{2,1,0:T(8,128)(2,1)S(1)} %get-tuple-element.34), channel_id=1, source_target_pairs={{0,2},{1,3},{2,0},{3,1},{8,10},{9,11},{10,8},{11,9},{16,18},{17,19... | collective-permute-start | bytes 589832 | tf_op jit(solution)/shard_map/ppermute | solution.py:98
  12.1 1.3 %collective-permute-start.2 = (bf16[2,16,3072]{2,1,0:T(8,128)(2,1)S(1)}, bf16[2,16,3072]{2,1,0:T(8,128)(2,1)}, u32[]{:S(2)}, u32[]{:S(2)}) collective-permute-start(bf16[2,16,3072]{2,1,0:T(8,128)(2,1)S(1)} %get-tuple-element.36), channel_id=1, source_target_pairs={{0,3},{1,2},{2,1},{3,0},{8,11},{9,10},{10,9},{11,8},{16,19},{17,18... | collective-permute-start | bytes 589832 | tf_op jit(solution)/shard_map/ppermute | solution.py:98
  13.8 1.3 %multiply_reduce_fusion.1 = (f32[2,4,16]{2,1,0:T(4,128)S(1)}, bf16[2,4,16,3072]{3,2,1,0:T(8,128)(2,1)S(1)}) fusion(bf16[2,1,16,3072]{3,2,1,0:T(8,128)(2,1)} %bitcast.28, bf16[2,1,16,3072]{3,2,1,0:T(8,128)(2,1)} %bitcast.26, bf16[2,1,16,3072]{3,2,1,0:T(8,128)(2,1)} %bitcast.24, bf16[2,1,16,3072]{3,2,1,0:T(8,128)(2,1)S(1)} %get-tuple-element.33), kind=kLoop, calls=%fused_computation.8 | loop fusion | flops 2359168 | bytes 1573376 | tf_op jit(solution)/shard_map/reduce_sum | solution.py:100
  17.7 4.5 %all-to-all-start = ((bf16[4,128,176]{1,2,0:T(8,128)(2,1)}), bf16[4,128,176]{1,2,0:T(8,128)(2,1)S(1)}, u32[]{:S(2)}, u32[]{:S(2)}) async-start(bf16[4,128,176]{1,2,0:T(8,128)(2,1)} %broadcast_in_dim.85), calls=%async_computation | async-start | bytes 360448 | tf_op jit(solution)/shard_map/all_to_all | solution.py:107
  25.1 7.9 %all-to-all-done = bf16[4,128,176]{1,2,0:T(8,128)(2,1)S(1)} async-done(((bf16[4,128,176]{1,2,0:T(8,128)(2,1)}), bf16[4,128,176]{1,2,0:T(8,128)(2,1)S(1)}, u32[]{:S(2)}, u32[]{:S(2)}) %all-to-all-start) | async-done | bytes 180256 | tf_op jit(solution)/shard_map/all_to_all | solution.py:107
  35.5 3.4 %all-to-all-start.1 = ((bf16[2,4,16,768]{3,2,0,1:T(8,128)(2,1)}), bf16[2,4,16,768]{3,2,0,1:T(8,128)(2,1)S(1)}, u32[]{:S(2)}, u32[]{:S(2)}) async-start(bf16[2,4,16,768]{3,2,0,1:T(8,128)(2,1)} %select_bitcast_fusion.2), calls=%async_computation.1 | async-start | bytes 393216 | tf_op jit(solution)/shard_map/all_to_all | solution.py:118
  39.1 3.9 %all-to-all-done.1 = bf16[2,4,16,768]{3,2,0,1:T(8,128)(2,1)S(1)} async-done(((bf16[2,4,16,768]{3,2,0,1:T(8,128)(2,1)}), bf16[2,4,16,768]{3,2,0,1:T(8,128)(2,1)S(1)}, u32[]{:S(2)}, u32[]{:S(2)}) %all-to-all-start.1) | async-done | bytes 196640 | tf_op jit(solution)/shard_map/all_to_all | solution.py:118
  43.2 1.3 %collective-permute-start.6 = (bf16[2,24,768]{2,1,0:T(8,128)(2,1)S(1)}, bf16[2,24,768]{2,1,0:T(8,128)(2,1)S(1)}, u32[]{:S(2)}, u32[]{:S(2)}) collective-permute-start(bf16[2,24,768]{2,1,0:T(8,128)(2,1)S(1)} %fusion), channel_id=1, source_target_pairs={{0,4},{1,5},{2,6},{3,7},{8,12},{9,13},{10,14},{11,15},{16,20},{17,... | collective-permute-start | bytes 221192 | tf_op jit(solution)/shard_map/ppermute | solution.py:146
  44.5 1.3 %collective-permute-start.7 = (bf16[2,24,768]{2,1,0:T(8,128)(2,1)S(1)}, bf16[2,24,768]{2,1,0:T(8,128)(2,1)S(1)}, u32[]{:S(2)}, u32[]{:S(2)}) collective-permute-start(bf16[2,24,768]{2,1,0:T(8,128)(2,1)S(1)} %fusion), channel_id=1, source_target_pairs={{0,12},{1,13},{2,14},{3,15},{8,4},{9,5},{10,6},{11,7},{16,28},{17,... | collective-permute-start | bytes 221192 | tf_op jit(solution)/shard_map/ppermute | solution.py:146
  45.8 1.3 %collective-permute-start.8 = (bf16[2,24,768]{2,1,0:T(8,128)(2,1)S(1)}, bf16[2,24,768]{2,1,0:T(8,128)(2,1)S(1)}, u32[]{:S(2)}, u32[]{:S(2)}) collective-permute-start(bf16[2,24,768]{2,1,0:T(8,128)(2,1)S(1)} %fusion), channel_id=1, source_target_pairs={{0,20},{1,21},{2,22},{3,23},{8,28},{9,29},{10,30},{11,31},{16,4},{... | collective-permute-start | bytes 221192 | tf_op jit(solution)/shard_map/ppermute | solution.py:146
  48.4 4.2 %collective-permute-done.6 = bf16[2,24,768]{2,1,0:T(8,128)(2,1)S(1)} collective-permute-done((bf16[2,24,768]{2,1,0:T(8,128)(2,1)S(1)}, bf16[2,24,768]{2,1,0:T(8,128)(2,1)S(1)}, u32[]{:S(2)}, u32[]{:S(2)}) %collective-permute-start.6) | collective-permute-done | bytes 73760 | tf_op jit(solution)/shard_map/ppermute | solution.py:146
  52.6 3.6 %collective-permute-done.7 = bf16[2,24,768]{2,1,0:T(8,128)(2,1)S(1)} collective-permute-done((bf16[2,24,768]{2,1,0:T(8,128)(2,1)S(1)}, bf16[2,24,768]{2,1,0:T(8,128)(2,1)S(1)}, u32[]{:S(2)}, u32[]{:S(2)}) %collective-permute-start.7) | collective-permute-done | bytes 73760 | tf_op jit(solution)/shard_map/ppermute | solution.py:146
  57.0 2.3 %collective-permute-done.9 = bf16[2,24,768]{2,1,0:T(8,128)(2,1)S(1)} collective-permute-done((bf16[2,24,768]{2,1,0:T(8,128)(2,1)S(1)}, bf16[2,24,768]{2,1,0:T(8,128)(2,1)S(1)}, u32[]{:S(2)}, u32[]{:S(2)}) %collective-permute-start.9) | collective-permute-done | bytes 73760 | tf_op jit(solution)/shard_map/ppermute | solution.py:146
  60.6 2.7 %collective-permute-start.10 = (bf16[2,16,3072]{2,1,0:T(8,128)(2,1)S(1)}, bf16[2,16,3072]{2,1,0:T(8,128)(2,1)S(1)}, u32[]{:S(2)}, u32[]{:S(2)}) collective-permute-start(bf16[2,16,3072]{2,1,0:T(8,128)(2,1)S(1)} %get-tuple-element.31), channel_id=1, source_target_pairs={{4,5},{5,4},{6,7},{7,6},{12,13},{13,12},{14,15},{15,14},{20,21},{2... | collective-permute-start | bytes 589832 | tf_op jit(solution)/shard_map/ppermute | solution.py:98
  63.3 2.2 %collective-permute-start.11 = (bf16[2,16,3072]{2,1,0:T(8,128)(2,1)S(1)}, bf16[2,16,3072]{2,1,0:T(8,128)(2,1)S(1)}, u32[]{:S(2)}, u32[]{:S(2)}) collective-permute-start(bf16[2,16,3072]{2,1,0:T(8,128)(2,1)S(1)} %get-tuple-element.30), channel_id=1, source_target_pairs={{4,6},{5,7},{6,4},{7,5},{12,14},{13,15},{14,12},{15,13},{20,22},{2... | collective-permute-start | bytes 589832 | tf_op jit(solution)/shard_map/ppermute | solution.py:98
  65.5 3.5 %collective-permute-start.12 = (bf16[2,16,3072]{2,1,0:T(8,128)(2,1)S(1)}, bf16[2,16,3072]{2,1,0:T(8,128)(2,1)S(1)}, u32[]{:S(2)}, u32[]{:S(2)}) collective-permute-start(bf16[2,16,3072]{2,1,0:T(8,128)(2,1)S(1)} %get-tuple-element.32), channel_id=1, source_target_pairs={{4,7},{5,6},{6,5},{7,4},{12,15},{13,14},{14,13},{15,12},{20,23},{2... | collective-permute-start | bytes 589832 | tf_op jit(solution)/shard_map/ppermute | solution.py:98
  70.0 2.9 %collective-permute-done.12 = bf16[2,16,3072]{2,1,0:T(8,128)(2,1)S(1)} collective-permute-done((bf16[2,16,3072]{2,1,0:T(8,128)(2,1)S(1)}, bf16[2,16,3072]{2,1,0:T(8,128)(2,1)S(1)}, u32[]{:S(2)}, u32[]{:S(2)}) %collective-permute-start.12) | collective-permute-done | bytes 196640 | tf_op jit(solution)/shard_map/ppermute | solution.py:98
  75.1 8.3 %all_to_all.20 = bf16[4,128,176]{1,2,0:T(8,128)(2,1)S(1)} all-to-all(bf16[4,128,176]{1,2,0:T(8,128)(2,1)S(1)} %broadcast_in_dim.87), channel_id=1, replica_groups=mesh['dp'=4,'pipe'=2,'expert'=4] {'dp'}, dimensions={0} | all-to-all | bytes 360448 | tf_op jit(solution)/shard_map/all_to_all | solution.py:107
  86.1 3.4 %all-to-all-start.3 = ((bf16[2,4,16,768]{3,2,0,1:T(8,128)(2,1)}), bf16[2,4,16,768]{3,2,0,1:T(8,128)(2,1)S(1)}, u32[]{:S(2)}, u32[]{:S(2)}) async-start(bf16[2,4,16,768]{3,2,0,1:T(8,128)(2,1)} %select_bitcast_fusion.1), calls=%async_computation.3 | async-start | bytes 393216 | tf_op jit(solution)/shard_map/all_to_all | solution.py:118
  89.4 4.0 %all-to-all-done.3 = bf16[2,4,16,768]{3,2,0,1:T(8,128)(2,1)S(1)} async-done(((bf16[2,4,16,768]{3,2,0,1:T(8,128)(2,1)}), bf16[2,4,16,768]{3,2,0,1:T(8,128)(2,1)S(1)}, u32[]{:S(2)}, u32[]{:S(2)}) %all-to-all-start.3) | async-done | bytes 196640 | tf_op jit(solution)/shard_map/all_to_all | solution.py:118
  (99 shorter events, 21.0 us)
Async XLA Ops:
  0.0 15.3 %copy-start = (bf16[1,1,3072,176]{2,3,1,0:T(8,128)(2,1)S(1)}, bf16[1,1,3072,176]{2,3,1,0:T(8,128)(2,1)}, u32[]{:S(2)}) copy-start(bf16[1,1,3072,176]{2,3,1,0:T(8,128)(2,1)} %param.13) | copy-start | bytes 3244036
  0.0 8.2 %copy-start.3 = (bf16[2,24,3072]{2,1,0:T(8,128)(2,1)S(1)}, bf16[2,24,3072]{2,1,0:T(8,128)(2,1)}, u32[]{:S(2)}) copy-start(bf16[2,24,3072]{2,1,0:T(8,128)(2,1)} %param.10) | copy-start | bytes 884740
  2.2 19.9 %collective-permute-start.3 = (bf16[176,768]{1,0:T(8,128)(2,1)}, bf16[176,768]{1,0:T(8,128)(2,1)}, u32[]{:S(2)}, u32[]{:S(2)}) collective-permute-start(bf16[176,768]{1,0:T(8,128)(2,1)} %get-tuple-element.14), channel_id=1, source_target_pairs={{0,8},{8,0},{16,24},{24,16},{1,9},{9,1},{17,25},{25,17},{2,10},{10... | collective-permute-start | bytes 811016 | tf_op jit(solution)/shard_map/ppermute | solution.py:78
  4.4 18.8 %collective-permute-start.4 = (bf16[176,768]{1,0:T(8,128)(2,1)}, bf16[176,768]{1,0:T(8,128)(2,1)}, u32[]{:S(2)}, u32[]{:S(2)}) collective-permute-start(bf16[176,768]{1,0:T(8,128)(2,1)} %get-tuple-element.15), channel_id=1, source_target_pairs={{0,16},{8,24},{16,0},{24,8},{1,17},{9,25},{17,1},{25,9},{2,18},{10... | collective-permute-start | bytes 811016 | tf_op jit(solution)/shard_map/ppermute | solution.py:78
  9.4 4.3 %collective-permute-start = (bf16[2,16,3072]{2,1,0:T(8,128)(2,1)}, bf16[2,16,3072]{2,1,0:T(8,128)(2,1)}, u32[]{:S(2)}, u32[]{:S(2)}) collective-permute-start(bf16[2,16,3072]{2,1,0:T(8,128)(2,1)} %get-tuple-element.35), channel_id=1, source_target_pairs={{0,1},{1,0},{2,3},{3,2},{8,9},{9,8},{10,11},{11,10},{16,17},{17,16... | collective-permute-start | bytes 589832 | tf_op jit(solution)/shard_map/ppermute | solution.py:98
  10.7 3.0 %collective-permute-start.1 = (bf16[2,16,3072]{2,1,0:T(8,128)(2,1)S(1)}, bf16[2,16,3072]{2,1,0:T(8,128)(2,1)}, u32[]{:S(2)}, u32[]{:S(2)}) collective-permute-start(bf16[2,16,3072]{2,1,0:T(8,128)(2,1)S(1)} %get-tuple-element.34), channel_id=1, source_target_pairs={{0,2},{1,3},{2,0},{3,1},{8,10},{9,11},{10,8},{11,9},{16,18},{17,19... | collective-permute-start | bytes 589832 | tf_op jit(solution)/shard_map/ppermute | solution.py:98
  12.1 1.7 %collective-permute-start.2 = (bf16[2,16,3072]{2,1,0:T(8,128)(2,1)S(1)}, bf16[2,16,3072]{2,1,0:T(8,128)(2,1)}, u32[]{:S(2)}, u32[]{:S(2)}) collective-permute-start(bf16[2,16,3072]{2,1,0:T(8,128)(2,1)S(1)} %get-tuple-element.36), channel_id=1, source_target_pairs={{0,3},{1,2},{2,1},{3,0},{8,11},{9,10},{10,9},{11,8},{16,19},{17,18... | collective-permute-start | bytes 589832 | tf_op jit(solution)/shard_map/ppermute | solution.py:98
  13.5 20.1 %copy-start.5 = (pred[4]{0:T(512)(128)(4,1)}, pred[4]{0:T(512)(128)(4,1)S(1)}, u32[]{:S(2)}) copy-start(pred[4]{0:T(512)(128)(4,1)S(1)} %get-tuple-element.21) | copy-start | bytes 16
  13.5 19.5 %copy-start.8 = (s32[1024]{0:T(1024)}, s32[1024]{0:T(1024)S(1)}, u32[]{:S(2)}) copy-start(s32[1024]{0:T(1024)S(1)} %pad_clamp_fusion.2) | copy-start | bytes 12292
  13.6 21.0 %copy-start.10 = (pred[4]{0:T(512)(128)(4,1)}, pred[4]{0:T(512)(128)(4,1)S(1)}, u32[]{:S(2)}) copy-start(pred[4]{0:T(512)(128)(4,1)S(1)} %get-tuple-element.19) | copy-start | bytes 16
  13.7 20.4 %copy-start.9 = (s32[1024]{0:T(1024)}, s32[1024]{0:T(1024)S(1)}, u32[]{:S(2)}) copy-start(s32[1024]{0:T(1024)S(1)} %pad_clamp_fusion.1) | copy-start | bytes 12292
  13.7 10.5 %collective-permute-start.5 = (bf16[176,768]{1,0:T(8,128)(2,1)}, bf16[176,768]{1,0:T(8,128)(2,1)}, u32[]{:S(2)}, u32[]{:S(2)}) collective-permute-start(bf16[176,768]{1,0:T(8,128)(2,1)} %get-tuple-element.16), channel_id=1, source_target_pairs={{0,24},{8,16},{16,8},{24,0},{1,25},{9,17},{17,9},{25,1},{2,26},{10... | collective-permute-start | bytes 811016 | tf_op jit(solution)/shard_map/ppermute | solution.py:78
  17.7 15.4 %all-to-all-start = ((bf16[4,128,176]{1,2,0:T(8,128)(2,1)}), bf16[4,128,176]{1,2,0:T(8,128)(2,1)S(1)}, u32[]{:S(2)}, u32[]{:S(2)}) async-start(bf16[4,128,176]{1,2,0:T(8,128)(2,1)} %broadcast_in_dim.85), calls=%async_computation | async-start | bytes 360448 | tf_op jit(solution)/shard_map/all_to_all | solution.py:107
  35.5 7.5 %all-to-all-start.1 = ((bf16[2,4,16,768]{3,2,0,1:T(8,128)(2,1)}), bf16[2,4,16,768]{3,2,0,1:T(8,128)(2,1)S(1)}, u32[]{:S(2)}, u32[]{:S(2)}) async-start(bf16[2,4,16,768]{3,2,0,1:T(8,128)(2,1)} %select_bitcast_fusion.2), calls=%async_computation.1 | async-start | bytes 393216 | tf_op jit(solution)/shard_map/all_to_all | solution.py:118
  38.9 21.1 %copy-start.6 = (pred[4]{0:T(512)(128)(4,1)S(1)}, pred[4]{0:T(512)(128)(4,1)}, u32[]{:S(2)}) copy-start(pred[4]{0:T(512)(128)(4,1)} %copy-done.5) | copy-start | bytes 16
  43.2 9.4 %collective-permute-start.6 = (bf16[2,24,768]{2,1,0:T(8,128)(2,1)S(1)}, bf16[2,24,768]{2,1,0:T(8,128)(2,1)S(1)}, u32[]{:S(2)}, u32[]{:S(2)}) collective-permute-start(bf16[2,24,768]{2,1,0:T(8,128)(2,1)S(1)} %fusion), channel_id=1, source_target_pairs={{0,4},{1,5},{2,6},{3,7},{8,12},{9,13},{10,14},{11,15},{16,20},{17,... | collective-permute-start | bytes 221192 | tf_op jit(solution)/shard_map/ppermute | solution.py:146
  44.5 11.7 %collective-permute-start.7 = (bf16[2,24,768]{2,1,0:T(8,128)(2,1)S(1)}, bf16[2,24,768]{2,1,0:T(8,128)(2,1)S(1)}, u32[]{:S(2)}, u32[]{:S(2)}) collective-permute-start(bf16[2,24,768]{2,1,0:T(8,128)(2,1)S(1)} %fusion), channel_id=1, source_target_pairs={{0,12},{1,13},{2,14},{3,15},{8,4},{9,5},{10,6},{11,7},{16,28},{17,... | collective-permute-start | bytes 221192 | tf_op jit(solution)/shard_map/ppermute | solution.py:146
  45.8 11.3 %collective-permute-start.8 = (bf16[2,24,768]{2,1,0:T(8,128)(2,1)S(1)}, bf16[2,24,768]{2,1,0:T(8,128)(2,1)S(1)}, u32[]{:S(2)}, u32[]{:S(2)}) collective-permute-start(bf16[2,24,768]{2,1,0:T(8,128)(2,1)S(1)} %fusion), channel_id=1, source_target_pairs={{0,20},{1,21},{2,22},{3,23},{8,28},{9,29},{10,30},{11,31},{16,4},{... | collective-permute-start | bytes 221192 | tf_op jit(solution)/shard_map/ppermute | solution.py:146
  47.1 12.3 %collective-permute-start.9 = (bf16[2,24,768]{2,1,0:T(8,128)(2,1)S(1)}, bf16[2,24,768]{2,1,0:T(8,128)(2,1)S(1)}, u32[]{:S(2)}, u32[]{:S(2)}) collective-permute-start(bf16[2,24,768]{2,1,0:T(8,128)(2,1)S(1)} %fusion), channel_id=1, source_target_pairs={{0,28},{1,29},{2,30},{3,31},{8,20},{9,21},{10,22},{11,23},{16,12},... | collective-permute-start | bytes 221192 | tf_op jit(solution)/shard_map/ppermute | solution.py:146
  60.6 8.4 %collective-permute-start.10 = (bf16[2,16,3072]{2,1,0:T(8,128)(2,1)S(1)}, bf16[2,16,3072]{2,1,0:T(8,128)(2,1)S(1)}, u32[]{:S(2)}, u32[]{:S(2)}) collective-permute-start(bf16[2,16,3072]{2,1,0:T(8,128)(2,1)S(1)} %get-tuple-element.31), channel_id=1, source_target_pairs={{4,5},{5,4},{6,7},{7,6},{12,13},{13,12},{14,15},{15,14},{20,21},{2... | collective-permute-start | bytes 589832 | tf_op jit(solution)/shard_map/ppermute | solution.py:98
  63.3 6.7 %collective-permute-start.11 = (bf16[2,16,3072]{2,1,0:T(8,128)(2,1)S(1)}, bf16[2,16,3072]{2,1,0:T(8,128)(2,1)S(1)}, u32[]{:S(2)}, u32[]{:S(2)}) collective-permute-start(bf16[2,16,3072]{2,1,0:T(8,128)(2,1)S(1)} %get-tuple-element.30), channel_id=1, source_target_pairs={{4,6},{5,7},{6,4},{7,5},{12,14},{13,15},{14,12},{15,13},{20,22},{2... | collective-permute-start | bytes 589832 | tf_op jit(solution)/shard_map/ppermute | solution.py:98
  65.5 7.5 %collective-permute-start.12 = (bf16[2,16,3072]{2,1,0:T(8,128)(2,1)S(1)}, bf16[2,16,3072]{2,1,0:T(8,128)(2,1)S(1)}, u32[]{:S(2)}, u32[]{:S(2)}) collective-permute-start(bf16[2,16,3072]{2,1,0:T(8,128)(2,1)S(1)} %get-tuple-element.32), channel_id=1, source_target_pairs={{4,7},{5,6},{6,5},{7,4},{12,15},{13,14},{14,13},{15,12},{20,23},{2... | collective-permute-start | bytes 589832 | tf_op jit(solution)/shard_map/ppermute | solution.py:98
  74.6 9.6 %copy-start.7 = (pred[4]{0:T(512)(128)(4,1)S(1)}, pred[4]{0:T(512)(128)(4,1)}, u32[]{:S(2)}) copy-start(pred[4]{0:T(512)(128)(4,1)} %copy-done.5) | copy-start | bytes 16
  86.1 7.4 %all-to-all-start.3 = ((bf16[2,4,16,768]{3,2,0,1:T(8,128)(2,1)}), bf16[2,4,16,768]{3,2,0,1:T(8,128)(2,1)S(1)}, u32[]{:S(2)}, u32[]{:S(2)}) async-start(bf16[2,4,16,768]{3,2,0,1:T(8,128)(2,1)} %select_bitcast_fusion.1), calls=%async_computation.3 | async-start | bytes 393216 | tf_op jit(solution)/shard_map/all_to_all | solution.py:118
  (5 other events, 15.3 us)

commit v16 on v9

--- a/solution.py
+++ b/solution.py
@@ -75,7 +75,7 @@
             down_parts.append(piece)
         down_parts, tokens = lax.optimization_barrier((down_parts, tokens))
         for s in range(1, n_dp):
-            down_parts[s] = lax.ppermute(down_parts[s], "dp", [(i, dring.ahead(i, s)) for i in range(n_dp)])
+            down_parts[s] = lax.ppermute(down_parts[s], AXES, dp_pairs(0, s))
         down_full = jnp.concatenate(down_parts, axis=0)
     else:
         down_full = lax.all_to_all(down_local, "dp", 1, 0, tiled=True)
@@ -102,14 +102,22 @@
         gate_act = jnp.dot(flat_rows, gate_local, preferred_element_type=jnp.float32) * inv_rms
         up_act = jnp.dot(flat_rows, up_local, preferred_element_type=jnp.float32) * inv_rms
         hidden = (jax.nn.silu(gate_act) * up_act).astype(jnp.bfloat16)
-        if small_dp:
-            parts = [hidden]
+        if small_dp and p > 0:
+            partial = jnp.dot(hidden, down_local, preferred_element_type=jnp.float32)
+            total = lax.dynamic_slice_in_dim(partial, d_me * columns, columns, 1)
             for s in range(1, n_dp):
-                parts.append(lax.ppermute(hidden, AXES, dp_pairs(p, s)))
-            hidden_full = jnp.concatenate(parts, axis=1)
+                chunk = lax.dynamic_slice_in_dim(partial, dring.ahead(d_me, s) * columns, columns, 1)
+                total = total + lax.ppermute(chunk.astype(jnp.bfloat16), AXES, dp_pairs(p, s)).astype(jnp.float32)
+            expert_out = total.astype(jnp.bfloat16)
         else:
-            hidden_full = lax.all_gather(hidden, "dp", axis=1, tiled=True)
-        expert_out = jnp.dot(hidden_full, down_full, preferred_element_type=jnp.float32).astype(jnp.bfloat16)
+            if small_dp:
+                parts = [hidden]
+                for s in range(1, n_dp):
+                    parts.append(lax.ppermute(hidden, AXES, dp_pairs(p, s)))
+                hidden_full = jnp.concatenate(parts, axis=1)
+            else:
+                hidden_full = lax.all_gather(hidden, "dp", axis=1, tiled=True)
+            expert_out = jnp.dot(hidden_full, down_full, preferred_element_type=jnp.float32).astype(jnp.bfloat16)
         expert_out = expert_out.reshape(micro, n_exp, CAP, columns)
         if ering.xor:
             order = jnp.stack([ering.place(j, e_me) for j in range(n_exp)])

time: 95.6 us -> 112 us (1.17)
  waiting for transfers between devices: 35 us -> 50.1 us
  matrix products: 4.43 us -> 8.42 us
  local copies, waits for them, and re-layouts: 10.4 us -> 7.72 us
  starting transfers between devices: 40.1 us -> 38.5 us
    ppermute x6 -> x3, starting transfers between devices: 11.3 us -> 1.99 us  [layer(): parts.append(lax.ppermute(hidden, AXES, dp_pairs(p, s)))]
    ppermute x4, waiting for transfers between devices: 20.3 us -> 29.3 us  [per_device(): parts.append(lax.ppermute(cols, AXES, pairs))]
    ppermute x3 -> x6, starting transfers between devices: 4.51 us -> 12.5 us  [the longest x3 8.37 us: layer(): lax.ppermute(chunk.astype(jnp.bfloat16), AXES, dp_pairs(p, s))]
    ppermute x3 -> x6, waiting for transfers between devices: 1.51 us -> 7.44 us  [the longest x3 7.43 us: layer(): lax.ppermute(chunk.astype(jnp.bfloat16), AXES, dp_pairs(p, s))]
    unnamed x21 -> x18, local copies, waits for them, and re-layouts: 3.57 us -> 0.69 us
    dot_general x0 -> x1, matrix products: none -> 2.38 us  [layer(): partial = jnp.dot(hidden, down_local, preferred_element_type=jnp.float32)]
    all_to_all x2, waiting for transfers between devices: 7.95 us -> 9.53 us  [layer(): lax.all_to_all(by_block, 'expert', 1, 1, tiled=True)]
    ppermute x6 -> x3, waiting for transfers between devices: 1.42 us -> 0.01 us  [layer(): parts.append(lax.ppermute(hidden, AXES, dp_pairs(p, s)))]
  transfers between devices with their start and end apart: 21 -> 21, of which waited for: 10 -> 9; matrix products, arithmetic and copies ran while one was open for 9% -> 5% of each run, Pallas kernels for 0% -> 0%
where the time goes in v16:
time: 112 us; the launch traced here: 111 us
  waiting for transfers between devices  50.1 us (45%)
  starting transfers between devices  38.5 us (34%)
  matrix products  8.42 us (8%)
  local copies, waits for them, and re-layouts  7.72 us (7%)
  other arithmetic  5.49 us (5%)
    ppermute x4, waiting for transfers between devices, per_device(): parts.append(lax.ppermute(cols, AXES, pairs))  29.3 us
    ppermute x6, starting transfers between devices, layer(): lax.ppermute(outgoing[:, s], AXES, expert_pairs(p, s, False))  11.2 us
    all_to_all x2, waiting for transfers between devices, layer(): lax.all_to_all(by_block, 'expert', 1, 1, tiled=True)  9.53 us
    ppermute x3, starting transfers between devices, layer(): lax.ppermute(chunk.astype(jnp.bfloat16), AXES, dp_pairs(p, s))  8.37 us
    all_to_all x2, starting transfers between devices, layer(): lax.all_to_all(by_block, 'expert', 1, 1, tiled=True)  7.63 us
    ppermute x3, waiting for transfers between devices, layer(): lax.ppermute(chunk.astype(jnp.bfloat16), AXES, dp_pairs(p, s))  7.43 us
    ppermute x4, starting transfers between devices, per_device(): parts.append(lax.ppermute(cols, AXES, pairs))  5.17 us
    ppermute x3, starting transfers between devices, per_device(): down_parts[s] = lax.ppermute(down_parts[s], AXES, dp_pairs(0, s))  4.1 us
  transfers between devices with their start and end apart: 21, of which 9 were waited for; matrix products, arithmetic and copies ran while one was open for 5% of the time, Pallas kernels for 0%

profile of v16, /device:TPU:1, one launch (start us, length us, event | category | flops | bytes accessed | tf_op | source)
XLA Modules:
  0.0 110.7 jit_solution(7874054294099268243)
XLA Ops:
  0.0 2.3 %dynamic-slice_bitcast_fusion = (bf16[176,768]{1,0:T(8,128)(2,1)}, bf16[176,768]{1,0:T(8,128)(2,1)}, bf16[176,768]{1,0:T(8,128)(2,1)}, bf16[176,768]{1,0:T(8,128)(2,1)}) fusion(bf16[1,1,176,3072]{3,2,1,0:T(8,128)(2,1)} %param.13, s32[]{:T(128)S(6)} %select_n.70, s32[]{:T(128)S(6)} %select_n.69, s32[]{:T(128)S(6)} %select_n.68, s32[]{:T(128)S(6)} %select_n.67), kind=kLoop, calls=%fused_computation.43 | loop fusion | bytes 2162704 | tf_op jit(solution)/shard_map/dynamic_slice | solution.py:74
  2.3 1.4 %collective-permute-start.6 = (bf16[176,768]{1,0:T(8,128)(2,1)}, bf16[176,768]{1,0:T(8,128)(2,1)}, u32[]{:S(2)}, u32[]{:S(2)}) collective-permute-start(bf16[176,768]{1,0:T(8,128)(2,1)} %get-tuple-element.13), channel_id=1, source_target_pairs={{0,8},{1,9},{2,10},{3,11},{8,0},{9,1},{10,2},{11,3},{16,24},{17,25... | collective-permute-start | bytes 811016 | tf_op jit(solution)/shard_map/ppermute | solution.py:78
  3.7 1.4 %collective-permute-start.7 = (bf16[176,768]{1,0:T(8,128)(2,1)}, bf16[176,768]{1,0:T(8,128)(2,1)}, u32[]{:S(2)}, u32[]{:S(2)}) collective-permute-start(bf16[176,768]{1,0:T(8,128)(2,1)} %get-tuple-element.14), channel_id=1, source_target_pairs={{0,16},{1,17},{2,18},{3,19},{8,24},{9,25},{10,26},{11,27},{16,0},{... | collective-permute-start | bytes 811016 | tf_op jit(solution)/shard_map/ppermute | solution.py:78
  9.3 1.4 %collective-permute-start.2 = (bf16[2,16,3072]{2,1,0:T(8,128)(2,1)S(1)}, bf16[2,16,3072]{2,1,0:T(8,128)(2,1)}, u32[]{:S(2)}, u32[]{:S(2)}) collective-permute-start(bf16[2,16,3072]{2,1,0:T(8,128)(2,1)S(1)} %get-tuple-element.36), channel_id=1, source_target_pairs={{0,3},{1,2},{2,1},{3,0},{8,11},{9,10},{10,9},{11,8},{16,19},{17,18... | collective-permute-start | bytes 589832 | tf_op jit(solution)/shard_map/ppermute | solution.py:98
  10.7 1.4 %collective-permute-start.8 = (bf16[176,768]{1,0:T(8,128)(2,1)}, bf16[176,768]{1,0:T(8,128)(2,1)}, u32[]{:S(2)}, u32[]{:S(2)}) collective-permute-start(bf16[176,768]{1,0:T(8,128)(2,1)} %get-tuple-element.15), channel_id=1, source_target_pairs={{0,24},{1,25},{2,26},{3,27},{8,16},{9,17},{10,18},{11,19},{16,8},{... | collective-permute-start | bytes 811016 | tf_op jit(solution)/shard_map/ppermute | solution.py:78
  17.3 1.5 %convolution_convert_fusion.2 = bf16[128,768]{1,0:T(8,128)(2,1)S(1)} fusion(bf16[176,768]{1,0:T(8,128)(2,1)} %collective-permute-done.8, bf16[176,768]{1,0:T(8,128)(2,1)} %collective-permute-done.7, bf16[176,768]{1,0:T(8,128)(2,1)} %collective-permute-done.6, bf16[176,768]{1,0:T(8,128)(2,1)S(1)} %copy-done.4, ...), kind=kOutput, calls=%fused_computation.7 | convolution fusion | flops 143556608 | bytes 1458176 | tf_op jit(solution)/shard_map/dot_general | solution.py:120
  20.1 4.3 %all-to-all-start = ((bf16[2,4,16,768]{3,2,0,1:T(8,128)(2,1)}), bf16[2,4,16,768]{3,2,0,1:T(8,128)(2,1)S(1)}, u32[]{:S(2)}, u32[]{:S(2)}) async-start(bf16[2,4,16,768]{3,2,0,1:T(8,128)(2,1)} %select_bitcast_fusion.2), calls=%async_computation | async-start | bytes 393216 | tf_op jit(solution)/shard_map/all_to_all | solution.py:125
  24.5 5.5 %all-to-all-done = bf16[2,4,16,768]{3,2,0,1:T(8,128)(2,1)S(1)} async-done(((bf16[2,4,16,768]{3,2,0,1:T(8,128)(2,1)}), bf16[2,4,16,768]{3,2,0,1:T(8,128)(2,1)S(1)}, u32[]{:S(2)}, u32[]{:S(2)}) %all-to-all-start) | async-done | bytes 196640 | tf_op jit(solution)/shard_map/all_to_all | solution.py:125
  35.6 26.3 %collective-permute-done.12 = bf16[2,24,768]{2,1,0:T(8,128)(2,1)S(1)} collective-permute-done((bf16[2,24,768]{2,1,0:T(8,128)(2,1)S(1)}, bf16[2,24,768]{2,1,0:T(8,128)(2,1)S(1)}, u32[]{:S(2)}, u32[]{:S(2)}) %collective-permute-start.12) | collective-permute-done | bytes 73760 | tf_op jit(solution)/shard_map/ppermute | solution.py:153
  61.8 1.5 %collective-permute-done.11 = bf16[2,24,768]{2,1,0:T(8,128)(2,1)S(1)} collective-permute-done((bf16[2,24,768]{2,1,0:T(8,128)(2,1)S(1)}, bf16[2,24,768]{2,1,0:T(8,128)(2,1)S(1)}, u32[]{:S(2)}, u32[]{:S(2)}) %collective-permute-start.11) | collective-permute-done | bytes 73760 | tf_op jit(solution)/shard_map/ppermute | solution.py:153
  63.4 1.5 %collective-permute-done.10 = bf16[2,24,768]{2,1,0:T(8,128)(2,1)S(1)} collective-permute-done((bf16[2,24,768]{2,1,0:T(8,128)(2,1)S(1)}, bf16[2,24,768]{2,1,0:T(8,128)(2,1)S(1)}, u32[]{:S(2)}, u32[]{:S(2)}) %collective-permute-start.10) | collective-permute-done | bytes 73760 | tf_op jit(solution)/shard_map/ppermute | solution.py:153
  66.1 2.7 %collective-permute-start.14 = (bf16[2,16,3072]{2,1,0:T(8,128)(2,1)S(1)}, bf16[2,16,3072]{2,1,0:T(8,128)(2,1)S(1)}, u32[]{:S(2)}, u32[]{:S(2)}) collective-permute-start(bf16[2,16,3072]{2,1,0:T(8,128)(2,1)S(1)} %get-tuple-element.30), channel_id=1, source_target_pairs={{4,6},{5,7},{6,4},{7,5},{12,14},{13,15},{14,12},{15,13},{20,22},{2... | collective-permute-start | bytes 589832 | tf_op jit(solution)/shard_map/ppermute | solution.py:98
  68.9 2.2 %collective-permute-start.13 = (bf16[2,16,3072]{2,1,0:T(8,128)(2,1)S(1)}, bf16[2,16,3072]{2,1,0:T(8,128)(2,1)S(1)}, u32[]{:S(2)}, u32[]{:S(2)}) collective-permute-start(bf16[2,16,3072]{2,1,0:T(8,128)(2,1)S(1)} %get-tuple-element.31), channel_id=1, source_target_pairs={{4,5},{5,4},{6,7},{7,6},{12,13},{13,12},{14,15},{15,14},{20,21},{2... | collective-permute-start | bytes 589832 | tf_op jit(solution)/shard_map/ppermute | solution.py:98
  71.0 3.5 %collective-permute-start.15 = (bf16[2,16,3072]{2,1,0:T(8,128)(2,1)S(1)}, bf16[2,16,3072]{2,1,0:T(8,128)(2,1)S(1)}, u32[]{:S(2)}, u32[]{:S(2)}) collective-permute-start(bf16[2,16,3072]{2,1,0:T(8,128)(2,1)S(1)} %get-tuple-element.32), channel_id=1, source_target_pairs={{4,7},{5,6},{6,5},{7,4},{12,15},{13,14},{14,13},{15,12},{20,23},{2... | collective-permute-start | bytes 589832 | tf_op jit(solution)/shard_map/ppermute | solution.py:98
  75.3 3.1 %collective-permute-done.15 = bf16[2,16,3072]{2,1,0:T(8,128)(2,1)S(1)} collective-permute-done((bf16[2,16,3072]{2,1,0:T(8,128)(2,1)S(1)}, bf16[2,16,3072]{2,1,0:T(8,128)(2,1)S(1)}, u32[]{:S(2)}, u32[]{:S(2)}) %collective-permute-start.15) | collective-permute-done | bytes 196640 | tf_op jit(solution)/shard_map/ppermute | solution.py:98
  78.7 1.8 %convolution_multiply_fusion.1 = f32[128,176]{0,1:T(8,128)S(1)} fusion(bf16[128,3072]{1,0:T(8,128)(2,1)S(1)} %bitcast.122, bf16[1,1,3072,176]{2,3,1,0:T(8,128)(2,1)} %param.11, f32[128]{0:T(128)S(1)} %rsqrt.25), kind=kOutput, calls=%fused_computation.14 | convolution fusion | flops 138434560 | bytes 1958400 | tf_op jit(solution)/shard_map/dot_general | solution.py:102
  80.5 2.4 %fusion.8 = f32[128,3072]{1,0:T(8,128)} fusion(bf16[128,3072]{1,0:T(8,128)(2,1)S(1)} %bitcast.123, bf16[1,1,176,3072]{3,2,1,0:T(8,128)(2,1)S(1)} %copy-done.1, bf16[1,1,3072,176]{2,3,1,0:T(8,128)(2,1)S(1)} %copy-done, f32[128,176]{0,1:T(8,128)S(1)} %convolution_multiply_fusion.1, f32[128]{0:T(128)S(1)} %rsqrt.25), kind=kOutput, calls=%fused_computation.22 | convolution fusion | flops 276981760 | bytes 4612608 | tf_op jit(solution)/shard_map/dot_general | solution.py:106
  84.2 3.1 %collective-permute-start.16 = (bf16[128,768]{1,0:T(8,128)(2,1)S(1)}, bf16[128,768]{1,0:T(8,128)(2,1)S(1)}, u32[]{:S(2)}, u32[]{:S(2)}) collective-permute-start(bf16[128,768]{1,0:T(8,128)(2,1)S(1)} %get-tuple-element.22), channel_id=1, source_target_pairs={{4,12},{5,13},{6,14},{7,15},{12,4},{13,5},{14,6},{15,7},{20,28},{2... | collective-permute-start | bytes 589832 | tf_op jit(solution)/shard_map/ppermute | solution.py:110
  87.3 2.8 %collective-permute-start.18 = (bf16[128,768]{1,0:T(8,128)(2,1)S(1)}, bf16[128,768]{1,0:T(8,128)(2,1)S(1)}, u32[]{:S(2)}, u32[]{:S(2)}) collective-permute-start(bf16[128,768]{1,0:T(8,128)(2,1)S(1)} %get-tuple-element.23), channel_id=1, source_target_pairs={{4,28},{5,29},{6,30},{7,31},{12,20},{13,21},{14,22},{15,23},{20,12... | collective-permute-start | bytes 589832 | tf_op jit(solution)/shard_map/ppermute | solution.py:110
  90.1 2.4 %collective-permute-start.17 = (bf16[128,768]{1,0:T(8,128)(2,1)S(1)}, bf16[128,768]{1,0:T(8,128)(2,1)S(1)}, u32[]{:S(2)}, u32[]{:S(2)}) collective-permute-start(bf16[128,768]{1,0:T(8,128)(2,1)S(1)} %get-tuple-element.24), channel_id=1, source_target_pairs={{4,20},{5,21},{6,22},{7,23},{12,28},{13,29},{14,30},{15,31},{20,4}... | collective-permute-start | bytes 589832 | tf_op jit(solution)/shard_map/ppermute | solution.py:110
  92.6 3.1 %collective-permute-done.18 = bf16[128,768]{1,0:T(8,128)(2,1)S(1)} collective-permute-done((bf16[128,768]{1,0:T(8,128)(2,1)S(1)}, bf16[128,768]{1,0:T(8,128)(2,1)S(1)}, u32[]{:S(2)}, u32[]{:S(2)}) %collective-permute-start.18) | collective-permute-done | bytes 196640 | tf_op jit(solution)/shard_map/ppermute | solution.py:110
  95.6 4.4 %collective-permute-done.17 = bf16[128,768]{1,0:T(8,128)(2,1)S(1)} collective-permute-done((bf16[128,768]{1,0:T(8,128)(2,1)S(1)}, bf16[128,768]{1,0:T(8,128)(2,1)S(1)}, u32[]{:S(2)}, u32[]{:S(2)}) %collective-permute-start.17) | collective-permute-done | bytes 196640 | tf_op jit(solution)/shard_map/ppermute | solution.py:110
  102.4 3.4 %all-to-all-start.1 = ((bf16[2,4,16,768]{3,2,0,1:T(8,128)(2,1)}), bf16[2,4,16,768]{3,2,0,1:T(8,128)(2,1)S(1)}, u32[]{:S(2)}, u32[]{:S(2)}) async-start(bf16[2,4,16,768]{3,2,0,1:T(8,128)(2,1)} %select_bitcast_fusion.1), calls=%async_computation.1 | async-start | bytes 393216 | tf_op jit(solution)/shard_map/all_to_all | solution.py:125
  105.8 4.0 %all-to-all-done.1 = bf16[2,4,16,768]{3,2,0,1:T(8,128)(2,1)S(1)} async-done(((bf16[2,4,16,768]{3,2,0,1:T(8,128)(2,1)}), bf16[2,4,16,768]{3,2,0,1:T(8,128)(2,1)S(1)}, u32[]{:S(2)}, u32[]{:S(2)}) %all-to-all-start.1) | async-done | bytes 196640 | tf_op jit(solution)/shard_map/all_to_all | solution.py:125
  (90 shorter events, 23.1 us)
Async XLA Ops:
  0.0 14.7 %copy-start = (bf16[1,1,3072,176]{2,3,1,0:T(8,128)(2,1)S(1)}, bf16[1,1,3072,176]{2,3,1,0:T(8,128)(2,1)}, u32[]{:S(2)}) copy-start(bf16[1,1,3072,176]{2,3,1,0:T(8,128)(2,1)} %param.12) | copy-start | bytes 3244036
  0.0 6.6 %copy-start.3 = (bf16[2,24,3072]{2,1,0:T(8,128)(2,1)S(1)}, bf16[2,24,3072]{2,1,0:T(8,128)(2,1)}, u32[]{:S(2)}) copy-start(bf16[2,24,3072]{2,1,0:T(8,128)(2,1)} %param.8) | copy-start | bytes 884740
  2.3 15.0 %collective-permute-start.6 = (bf16[176,768]{1,0:T(8,128)(2,1)}, bf16[176,768]{1,0:T(8,128)(2,1)}, u32[]{:S(2)}, u32[]{:S(2)}) collective-permute-start(bf16[176,768]{1,0:T(8,128)(2,1)} %get-tuple-element.13), channel_id=1, source_target_pairs={{0,8},{1,9},{2,10},{3,11},{8,0},{9,1},{10,2},{11,3},{16,24},{17,25... | collective-permute-start | bytes 811016 | tf_op jit(solution)/shard_map/ppermute | solution.py:78
  3.7 13.6 %collective-permute-start.7 = (bf16[176,768]{1,0:T(8,128)(2,1)}, bf16[176,768]{1,0:T(8,128)(2,1)}, u32[]{:S(2)}, u32[]{:S(2)}) collective-permute-start(bf16[176,768]{1,0:T(8,128)(2,1)} %get-tuple-element.14), channel_id=1, source_target_pairs={{0,16},{1,17},{2,18},{3,19},{8,24},{9,25},{10,26},{11,27},{16,0},{... | collective-permute-start | bytes 811016 | tf_op jit(solution)/shard_map/ppermute | solution.py:78
  7.8 6.4 %copy-start.2 = (bf16[1,1,3072,176]{2,3,1,0:T(8,128)(2,1)S(1)}, bf16[1,1,3072,176]{2,3,1,0:T(8,128)(2,1)}, u32[]{:S(2)}) copy-start(bf16[1,1,3072,176]{2,3,1,0:T(8,128)(2,1)} %param.11) | copy-start | bytes 3244036
  7.8 2.9 %collective-permute-start.1 = (bf16[2,16,3072]{2,1,0:T(8,128)(2,1)}, bf16[2,16,3072]{2,1,0:T(8,128)(2,1)S(1)}, u32[]{:S(2)}, u32[]{:S(2)}) collective-permute-start(bf16[2,16,3072]{2,1,0:T(8,128)(2,1)} %get-tuple-element.34), channel_id=1, source_target_pairs={{0,2},{1,3},{2,0},{3,1},{8,10},{9,11},{10,8},{11,9},{16,18},{17,19... | collective-permute-start | bytes 589832 | tf_op jit(solution)/shard_map/ppermute | solution.py:98
  8.6 3.5 %collective-permute-start = (bf16[2,16,3072]{2,1,0:T(8,128)(2,1)S(1)}, bf16[2,16,3072]{2,1,0:T(8,128)(2,1)S(1)}, u32[]{:S(2)}, u32[]{:S(2)}) collective-permute-start(bf16[2,16,3072]{2,1,0:T(8,128)(2,1)S(1)} %get-tuple-element.35), channel_id=1, source_target_pairs={{0,1},{1,0},{2,3},{3,2},{8,9},{9,8},{10,11},{11,10},{16,17},{17,16... | collective-permute-start | bytes 589832 | tf_op jit(solution)/shard_map/ppermute | solution.py:98
  9.3 2.8 %collective-permute-start.2 = (bf16[2,16,3072]{2,1,0:T(8,128)(2,1)S(1)}, bf16[2,16,3072]{2,1,0:T(8,128)(2,1)}, u32[]{:S(2)}, u32[]{:S(2)}) collective-permute-start(bf16[2,16,3072]{2,1,0:T(8,128)(2,1)S(1)} %get-tuple-element.36), channel_id=1, source_target_pairs={{0,3},{1,2},{2,1},{3,0},{8,11},{9,10},{10,9},{11,8},{16,19},{17,18... | collective-permute-start | bytes 589832 | tf_op jit(solution)/shard_map/ppermute | solution.py:98
  10.7 6.6 %collective-permute-start.8 = (bf16[176,768]{1,0:T(8,128)(2,1)}, bf16[176,768]{1,0:T(8,128)(2,1)}, u32[]{:S(2)}, u32[]{:S(2)}) collective-permute-start(bf16[176,768]{1,0:T(8,128)(2,1)} %get-tuple-element.15), channel_id=1, source_target_pairs={{0,24},{1,25},{2,26},{3,27},{8,16},{9,17},{10,18},{11,19},{16,8},{... | collective-permute-start | bytes 811016 | tf_op jit(solution)/shard_map/ppermute | solution.py:78
  15.2 1.4 %collective-permute-start.5 = (bf16[128,176]{0,1:T(8,128)(2,1)S(1)}, bf16[128,176]{0,1:T(8,128)(2,1)S(1)}, u32[]{:S(2)}, u32[]{:S(2)}) collective-permute-start(bf16[128,176]{0,1:T(8,128)(2,1)S(1)} %fusion.6), channel_id=1, source_target_pairs={{0,24},{1,25},{2,26},{3,27},{8,16},{9,17},{10,18},{11,19},{16,8},{... | collective-permute-start | bytes 135176 | tf_op jit(solution)/shard_map/ppermute | solution.py:116
  15.8 1.4 %collective-permute-start.4 = (bf16[128,176]{0,1:T(8,128)(2,1)S(1)}, bf16[128,176]{0,1:T(8,128)(2,1)S(1)}, u32[]{:S(2)}, u32[]{:S(2)}) collective-permute-start(bf16[128,176]{0,1:T(8,128)(2,1)S(1)} %fusion.6), channel_id=1, source_target_pairs={{0,16},{1,17},{2,18},{3,19},{8,24},{9,25},{10,26},{11,27},{16,0},{... | collective-permute-start | bytes 135176 | tf_op jit(solution)/shard_map/ppermute | solution.py:116
  16.5 0.8 collective-permute-start.3
  20.1 9.9 %all-to-all-start = ((bf16[2,4,16,768]{3,2,0,1:T(8,128)(2,1)}), bf16[2,4,16,768]{3,2,0,1:T(8,128)(2,1)S(1)}, u32[]{:S(2)}, u32[]{:S(2)}) async-start(bf16[2,4,16,768]{3,2,0,1:T(8,128)(2,1)} %select_bitcast_fusion.2), calls=%async_computation | async-start | bytes 393216 | tf_op jit(solution)/shard_map/all_to_all | solution.py:125
  30.3 31.6 %collective-permute-start.12 = (bf16[2,24,768]{2,1,0:T(8,128)(2,1)S(1)}, bf16[2,24,768]{2,1,0:T(8,128)(2,1)S(1)}, u32[]{:S(2)}, u32[]{:S(2)}) collective-permute-start(bf16[2,24,768]{2,1,0:T(8,128)(2,1)S(1)} %fusion), channel_id=1, source_target_pairs={{0,28},{1,29},{2,30},{3,31},{8,20},{9,21},{10,22},{11,23},{16,12},... | collective-permute-start | bytes 221192 | tf_op jit(solution)/shard_map/ppermute | solution.py:153
  31.6 31.8 %collective-permute-start.11 = (bf16[2,24,768]{2,1,0:T(8,128)(2,1)S(1)}, bf16[2,24,768]{2,1,0:T(8,128)(2,1)S(1)}, u32[]{:S(2)}, u32[]{:S(2)}) collective-permute-start(bf16[2,24,768]{2,1,0:T(8,128)(2,1)S(1)} %fusion), channel_id=1, source_target_pairs={{0,20},{1,21},{2,22},{3,23},{8,28},{9,29},{10,30},{11,31},{16,4},{... | collective-permute-start | bytes 221192 | tf_op jit(solution)/shard_map/ppermute | solution.py:153
  32.9 32.0 %collective-permute-start.10 = (bf16[2,24,768]{2,1,0:T(8,128)(2,1)S(1)}, bf16[2,24,768]{2,1,0:T(8,128)(2,1)S(1)}, u32[]{:S(2)}, u32[]{:S(2)}) collective-permute-start(bf16[2,24,768]{2,1,0:T(8,128)(2,1)S(1)} %fusion), channel_id=1, source_target_pairs={{0,12},{1,13},{2,14},{3,15},{8,4},{9,5},{10,6},{11,7},{16,28},{17,... | collective-permute-start | bytes 221192 | tf_op jit(solution)/shard_map/ppermute | solution.py:153
  34.2 30.7 %collective-permute-start.9 = (bf16[2,24,768]{2,1,0:T(8,128)(2,1)S(1)}, bf16[2,24,768]{2,1,0:T(8,128)(2,1)S(1)}, u32[]{:S(2)}, u32[]{:S(2)}) collective-permute-start(bf16[2,24,768]{2,1,0:T(8,128)(2,1)S(1)} %fusion), channel_id=1, source_target_pairs={{0,4},{1,5},{2,6},{3,7},{8,12},{9,13},{10,14},{11,15},{16,20},{17,... | collective-permute-start | bytes 221192 | tf_op jit(solution)/shard_map/ppermute | solution.py:153
  66.1 8.4 %collective-permute-start.14 = (bf16[2,16,3072]{2,1,0:T(8,128)(2,1)S(1)}, bf16[2,16,3072]{2,1,0:T(8,128)(2,1)S(1)}, u32[]{:S(2)}, u32[]{:S(2)}) collective-permute-start(bf16[2,16,3072]{2,1,0:T(8,128)(2,1)S(1)} %get-tuple-element.30), channel_id=1, source_target_pairs={{4,6},{5,7},{6,4},{7,5},{12,14},{13,15},{14,12},{15,13},{20,22},{2... | collective-permute-start | bytes 589832 | tf_op jit(solution)/shard_map/ppermute | solution.py:98
  68.9 6.4 %collective-permute-start.13 = (bf16[2,16,3072]{2,1,0:T(8,128)(2,1)S(1)}, bf16[2,16,3072]{2,1,0:T(8,128)(2,1)S(1)}, u32[]{:S(2)}, u32[]{:S(2)}) collective-permute-start(bf16[2,16,3072]{2,1,0:T(8,128)(2,1)S(1)} %get-tuple-element.31), channel_id=1, source_target_pairs={{4,5},{5,4},{6,7},{7,6},{12,13},{13,12},{14,15},{15,14},{20,21},{2... | collective-permute-start | bytes 589832 | tf_op jit(solution)/shard_map/ppermute | solution.py:98
  71.0 7.3 %collective-permute-start.15 = (bf16[2,16,3072]{2,1,0:T(8,128)(2,1)S(1)}, bf16[2,16,3072]{2,1,0:T(8,128)(2,1)S(1)}, u32[]{:S(2)}, u32[]{:S(2)}) collective-permute-start(bf16[2,16,3072]{2,1,0:T(8,128)(2,1)S(1)} %get-tuple-element.32), channel_id=1, source_target_pairs={{4,7},{5,6},{6,5},{7,4},{12,15},{13,14},{14,13},{15,12},{20,23},{2... | collective-permute-start | bytes 589832 | tf_op jit(solution)/shard_map/ppermute | solution.py:98
  84.2 8.4 %collective-permute-start.16 = (bf16[128,768]{1,0:T(8,128)(2,1)S(1)}, bf16[128,768]{1,0:T(8,128)(2,1)S(1)}, u32[]{:S(2)}, u32[]{:S(2)}) collective-permute-start(bf16[128,768]{1,0:T(8,128)(2,1)S(1)} %get-tuple-element.22), channel_id=1, source_target_pairs={{4,12},{5,13},{6,14},{7,15},{12,4},{13,5},{14,6},{15,7},{20,28},{2... | collective-permute-start | bytes 589832 | tf_op jit(solution)/shard_map/ppermute | solution.py:110
  87.3 8.3 %collective-permute-start.18 = (bf16[128,768]{1,0:T(8,128)(2,1)S(1)}, bf16[128,768]{1,0:T(8,128)(2,1)S(1)}, u32[]{:S(2)}, u32[]{:S(2)}) collective-permute-start(bf16[128,768]{1,0:T(8,128)(2,1)S(1)} %get-tuple-element.23), channel_id=1, source_target_pairs={{4,28},{5,29},{6,30},{7,31},{12,20},{13,21},{14,22},{15,23},{20,12... | collective-permute-start | bytes 589832 | tf_op jit(solution)/shard_map/ppermute | solution.py:110
  90.1 9.9 %collective-permute-start.17 = (bf16[128,768]{1,0:T(8,128)(2,1)S(1)}, bf16[128,768]{1,0:T(8,128)(2,1)S(1)}, u32[]{:S(2)}, u32[]{:S(2)}) collective-permute-start(bf16[128,768]{1,0:T(8,128)(2,1)S(1)} %get-tuple-element.24), channel_id=1, source_target_pairs={{4,20},{5,21},{6,22},{7,23},{12,28},{13,29},{14,30},{15,31},{20,4}... | collective-permute-start | bytes 589832 | tf_op jit(solution)/shard_map/ppermute | solution.py:110
  102.4 7.4 %all-to-all-start.1 = ((bf16[2,4,16,768]{3,2,0,1:T(8,128)(2,1)}), bf16[2,4,16,768]{3,2,0,1:T(8,128)(2,1)S(1)}, u32[]{:S(2)}, u32[]{:S(2)}) async-start(bf16[2,4,16,768]{3,2,0,1:T(8,128)(2,1)} %select_bitcast_fusion.1), calls=%async_computation.1 | async-start | bytes 393216 | tf_op jit(solution)/shard_map/all_to_all | solution.py:125
  (6 other events, 15.7 us)

commit v17 on v15

--- a/solution.py
+++ b/solution.py
@@ -102,12 +102,17 @@
         gate_act = jnp.dot(flat_rows, gate_local, preferred_element_type=jnp.float32) * inv_rms
         up_act = jnp.dot(flat_rows, up_local, preferred_element_type=jnp.float32) * inv_rms
         hidden = (jax.nn.silu(gate_act) * up_act).astype(jnp.bfloat16)
-        if small_dp:
+        if small_dp and p == 0:
             spread = jnp.broadcast_to(hidden[None], (n_dp,) + hidden.shape)
             gathered = lax.all_to_all(spread, "dp", 0, 0, tiled=True)
             order = jnp.stack([dring.behind(d_me, s) for s in range(n_dp)])
             gathered = jnp.take(gathered, order, axis=0)
             hidden_full = jnp.transpose(gathered, (1, 0, 2)).reshape(hidden.shape[0], n_dp * units)
+        elif small_dp:
+            parts = [hidden]
+            for s in range(1, n_dp):
+                parts.append(lax.ppermute(hidden, AXES, dp_pairs(p, s)))
+            hidden_full = jnp.concatenate(parts, axis=1)
         else:
             hidden_full = lax.all_gather(hidden, "dp", axis=1, tiled=True)
         expert_out = jnp.dot(hidden_full, down_full, preferred_element_type=jnp.float32).astype(jnp.bfloat16)

time: 95.2 us -> 99 us (1.040)
  starting transfers between devices: 33.4 us -> 43.1 us
  blocking collectives: 8.35 us -> 0 us
  waiting for transfers between devices: 30.7 us -> 33.9 us
    ppermute x0 -> x3, starting transfers between devices: none -> 9.27 us  [layer(): parts.append(lax.ppermute(hidden, AXES, dp_pairs(p, s)))]
    all_to_all x1 -> x0, blocking collectives: 8.35 us -> none  [layer(): gathered = lax.all_to_all(spread, 'dp', 0, 0, tiled=True)]
    ppermute x0 -> x3, waiting for transfers between devices: none -> 3.22 us  [layer(): parts.append(lax.ppermute(hidden, AXES, dp_pairs(p, s)))]
    unnamed x29 -> x27, local copies, waits for them, and re-layouts: 3.59 us -> 3.59 us
  transfers between devices with their start and end apart: 16 -> 19, of which waited for: 9 -> 10; matrix products, arithmetic and copies ran while one was open for 10% -> 9% of each run, Pallas kernels for 0% -> 0%
where the time goes in v17:
time: 99 us; the launch traced here: 98.1 us
  starting transfers between devices  43.1 us (44%)
  waiting for transfers between devices  33.9 us (34%)
  local copies, waits for them, and re-layouts  11.7 us (12%)
  other arithmetic  4.49 us (5%)
  matrix products  4.45 us (4%)
    ppermute x6, starting transfers between devices, layer(): lax.ppermute(outgoing[:, s], AXES, expert_pairs(p, s, False))  12.4 us
    ppermute x4, waiting for transfers between devices, per_device(): parts.append(lax.ppermute(cols, AXES, pairs))  11 us
    ppermute x3, starting transfers between devices, layer(): parts.append(lax.ppermute(hidden, AXES, dp_pairs(p, s)))  9.27 us
    all_to_all x2, waiting for transfers between devices, layer(): lax.all_to_all(by_block, 'expert', 1, 1, tiled=True)  7.99 us
    all_to_all x1, waiting for transfers between devices, layer(): gathered = lax.all_to_all(spread, 'dp', 0, 0, tiled=True)  7.89 us
    all_to_all x2, starting transfers between devices, layer(): lax.all_to_all(by_block, 'expert', 1, 1, tiled=True)  7.29 us
    ppermute x4, starting transfers between devices, per_device(): parts.append(lax.ppermute(cols, AXES, pairs))  5.17 us
    ppermute x3, starting transfers between devices, per_device(): lax.ppermute(down_parts[s], 'dp', [(i, dring.ahead(i, s)) for i in range(...  4.51 us
  transfers between devices with their start and end apart: 19, of which 10 were waited for; matrix products, arithmetic and copies ran while one was open for 9% of the time, Pallas kernels for 0%

profile of v17, /device:TPU:1, one launch (start us, length us, event | category | flops | bytes accessed | tf_op | source)
XLA Modules:
  0.0 98.1 jit_solution(3116919600814601419)
XLA Ops:
  0.0 2.2 %dynamic-slice_bitcast_fusion = (bf16[176,768]{1,0:T(8,128)(2,1)}, bf16[176,768]{1,0:T(8,128)(2,1)}, bf16[176,768]{1,0:T(8,128)(2,1)S(1)}, bf16[176,768]{1,0:T(8,128)(2,1)}) fusion(bf16[1,1,176,3072]{3,2,1,0:T(8,128)(2,1)} %param.13, s32[]{:T(128)S(6)} %select_n.76, s32[]{:T(128)S(6)} %select_n.74, s32[]{:T(128)S(6)} %select_n.73, s32[]{:T(128)S(6)} %select_n.75), kind=kLoop, calls=%fused_computation.32 | loop fusion | bytes 2162704 | tf_op jit(solution)/shard_map/dynamic_slice | solution.py:74
  2.2 2.1 %collective-permute-start.3 = (bf16[176,768]{1,0:T(8,128)(2,1)}, bf16[176,768]{1,0:T(8,128)(2,1)}, u32[]{:S(2)}, u32[]{:S(2)}) collective-permute-start(bf16[176,768]{1,0:T(8,128)(2,1)} %get-tuple-element.13), channel_id=1, source_target_pairs={{0,8},{8,0},{16,24},{24,16},{1,9},{9,1},{17,25},{25,17},{2,10},{10... | collective-permute-start | bytes 811016 | tf_op jit(solution)/shard_map/ppermute | solution.py:78
  4.4 2.3 %collective-permute-start.4 = (bf16[176,768]{1,0:T(8,128)(2,1)}, bf16[176,768]{1,0:T(8,128)(2,1)}, u32[]{:S(2)}, u32[]{:S(2)}) collective-permute-start(bf16[176,768]{1,0:T(8,128)(2,1)} %get-tuple-element.14), channel_id=1, source_target_pairs={{0,16},{8,24},{16,0},{24,8},{1,17},{9,25},{17,1},{25,9},{2,18},{10... | collective-permute-start | bytes 811016 | tf_op jit(solution)/shard_map/ppermute | solution.py:78
  9.4 1.3 %collective-permute-start = (bf16[2,16,3072]{2,1,0:T(8,128)(2,1)}, bf16[2,16,3072]{2,1,0:T(8,128)(2,1)}, u32[]{:S(2)}, u32[]{:S(2)}) collective-permute-start(bf16[2,16,3072]{2,1,0:T(8,128)(2,1)} %get-tuple-element.32), channel_id=1, source_target_pairs={{0,1},{1,0},{2,3},{3,2},{8,9},{9,8},{10,11},{11,10},{16,17},{17,16... | collective-permute-start | bytes 589832 | tf_op jit(solution)/shard_map/ppermute | solution.py:98
  10.7 1.4 %collective-permute-start.1 = (bf16[2,16,3072]{2,1,0:T(8,128)(2,1)S(1)}, bf16[2,16,3072]{2,1,0:T(8,128)(2,1)}, u32[]{:S(2)}, u32[]{:S(2)}) collective-permute-start(bf16[2,16,3072]{2,1,0:T(8,128)(2,1)S(1)} %get-tuple-element.31), channel_id=1, source_target_pairs={{0,2},{1,3},{2,0},{3,1},{8,10},{9,11},{10,8},{11,9},{16,18},{17,19... | collective-permute-start | bytes 589832 | tf_op jit(solution)/shard_map/ppermute | solution.py:98
  12.1 1.3 %collective-permute-start.2 = (bf16[2,16,3072]{2,1,0:T(8,128)(2,1)S(1)}, bf16[2,16,3072]{2,1,0:T(8,128)(2,1)}, u32[]{:S(2)}, u32[]{:S(2)}) collective-permute-start(bf16[2,16,3072]{2,1,0:T(8,128)(2,1)S(1)} %get-tuple-element.33), channel_id=1, source_target_pairs={{0,3},{1,2},{2,1},{3,0},{8,11},{9,10},{10,9},{11,8},{16,19},{17,18... | collective-permute-start | bytes 589832 | tf_op jit(solution)/shard_map/ppermute | solution.py:98
  13.8 1.3 %multiply_reduce_fusion.1 = (f32[2,4,16]{2,1,0:T(4,128)S(1)}, bf16[2,4,16,3072]{3,2,1,0:T(8,128)(2,1)S(1)}) fusion(bf16[2,1,16,3072]{3,2,1,0:T(8,128)(2,1)} %bitcast.28, bf16[2,1,16,3072]{3,2,1,0:T(8,128)(2,1)} %bitcast.26, bf16[2,1,16,3072]{3,2,1,0:T(8,128)(2,1)} %bitcast.24, bf16[2,1,16,3072]{3,2,1,0:T(8,128)(2,1)S(1)} %get-tuple-element.30), kind=kLoop, calls=%fused_computation.7 | loop fusion | flops 2359168 | bytes 1573376 | tf_op jit(solution)/shard_map/reduce_sum | solution.py:100
  17.7 4.5 %all-to-all-start = ((bf16[4,128,176]{1,2,0:T(8,128)(2,1)}), bf16[4,128,176]{1,2,0:T(8,128)(2,1)S(1)}, u32[]{:S(2)}, u32[]{:S(2)}) async-start(bf16[4,128,176]{1,2,0:T(8,128)(2,1)} %broadcast_in_dim.81), calls=%async_computation | async-start | bytes 360448 | tf_op jit(solution)/shard_map/all_to_all | solution.py:107
  25.1 7.9 %all-to-all-done = bf16[4,128,176]{1,2,0:T(8,128)(2,1)S(1)} async-done(((bf16[4,128,176]{1,2,0:T(8,128)(2,1)}), bf16[4,128,176]{1,2,0:T(8,128)(2,1)S(1)}, u32[]{:S(2)}, u32[]{:S(2)}) %all-to-all-start) | async-done | bytes 180256 | tf_op jit(solution)/shard_map/all_to_all | solution.py:107
  35.4 3.4 %all-to-all-start.1 = ((bf16[2,4,16,768]{3,2,0,1:T(8,128)(2,1)}), bf16[2,4,16,768]{3,2,0,1:T(8,128)(2,1)S(1)}, u32[]{:S(2)}, u32[]{:S(2)}) async-start(bf16[2,4,16,768]{3,2,0,1:T(8,128)(2,1)} %select_bitcast_fusion.2), calls=%async_computation.1 | async-start | bytes 393216 | tf_op jit(solution)/shard_map/all_to_all | solution.py:123
  39.0 3.9 %all-to-all-done.1 = bf16[2,4,16,768]{3,2,0,1:T(8,128)(2,1)S(1)} async-done(((bf16[2,4,16,768]{3,2,0,1:T(8,128)(2,1)}), bf16[2,4,16,768]{3,2,0,1:T(8,128)(2,1)S(1)}, u32[]{:S(2)}, u32[]{:S(2)}) %all-to-all-start.1) | async-done | bytes 196640 | tf_op jit(solution)/shard_map/all_to_all | solution.py:123
  48.4 4.2 %collective-permute-done.6 = bf16[2,24,768]{2,1,0:T(8,128)(2,1)S(1)} collective-permute-done((bf16[2,24,768]{2,1,0:T(8,128)(2,1)S(1)}, bf16[2,24,768]{2,1,0:T(8,128)(2,1)S(1)}, u32[]{:S(2)}, u32[]{:S(2)}) %collective-permute-start.6) | collective-permute-done | bytes 73760 | tf_op jit(solution)/shard_map/ppermute | solution.py:151
  52.6 3.6 %collective-permute-done.7 = bf16[2,24,768]{2,1,0:T(8,128)(2,1)S(1)} collective-permute-done((bf16[2,24,768]{2,1,0:T(8,128)(2,1)S(1)}, bf16[2,24,768]{2,1,0:T(8,128)(2,1)S(1)}, u32[]{:S(2)}, u32[]{:S(2)}) %collective-permute-start.7) | collective-permute-done | bytes 73760 | tf_op jit(solution)/shard_map/ppermute | solution.py:151
  57.0 2.3 %collective-permute-done.9 = bf16[2,24,768]{2,1,0:T(8,128)(2,1)S(1)} collective-permute-done((bf16[2,24,768]{2,1,0:T(8,128)(2,1)S(1)}, bf16[2,24,768]{2,1,0:T(8,128)(2,1)S(1)}, u32[]{:S(2)}, u32[]{:S(2)}) %collective-permute-start.9) | collective-permute-done | bytes 73760 | tf_op jit(solution)/shard_map/ppermute | solution.py:151
  60.7 2.7 %collective-permute-start.10 = (bf16[2,16,3072]{2,1,0:T(8,128)(2,1)S(1)}, bf16[2,16,3072]{2,1,0:T(8,128)(2,1)S(1)}, u32[]{:S(2)}, u32[]{:S(2)}) collective-permute-start(bf16[2,16,3072]{2,1,0:T(8,128)(2,1)S(1)} %get-tuple-element.28), channel_id=1, source_target_pairs={{4,5},{5,4},{6,7},{7,6},{12,13},{13,12},{14,15},{15,14},{20,21},{2... | collective-permute-start | bytes 589832 | tf_op jit(solution)/shard_map/ppermute | solution.py:98
  63.4 2.2 %collective-permute-start.11 = (bf16[2,16,3072]{2,1,0:T(8,128)(2,1)S(1)}, bf16[2,16,3072]{2,1,0:T(8,128)(2,1)S(1)}, u32[]{:S(2)}, u32[]{:S(2)}) collective-permute-start(bf16[2,16,3072]{2,1,0:T(8,128)(2,1)S(1)} %get-tuple-element.27), channel_id=1, source_target_pairs={{4,6},{5,7},{6,4},{7,5},{12,14},{13,15},{14,12},{15,13},{20,22},{2... | collective-permute-start | bytes 589832 | tf_op jit(solution)/shard_map/ppermute | solution.py:98
  65.6 3.5 %collective-permute-start.12 = (bf16[2,16,3072]{2,1,0:T(8,128)(2,1)S(1)}, bf16[2,16,3072]{2,1,0:T(8,128)(2,1)S(1)}, u32[]{:S(2)}, u32[]{:S(2)}) collective-permute-start(bf16[2,16,3072]{2,1,0:T(8,128)(2,1)S(1)} %get-tuple-element.29), channel_id=1, source_target_pairs={{4,7},{5,6},{6,5},{7,4},{12,15},{13,14},{14,13},{15,12},{20,23},{2... | collective-permute-start | bytes 589832 | tf_op jit(solution)/shard_map/ppermute | solution.py:98
  69.8 3.1 %collective-permute-done.12 = bf16[2,16,3072]{2,1,0:T(8,128)(2,1)S(1)} collective-permute-done((bf16[2,16,3072]{2,1,0:T(8,128)(2,1)S(1)}, bf16[2,16,3072]{2,1,0:T(8,128)(2,1)S(1)}, u32[]{:S(2)}, u32[]{:S(2)}) %collective-permute-start.12) | collective-permute-done | bytes 196640 | tf_op jit(solution)/shard_map/ppermute | solution.py:98
  75.0 2.4 %collective-permute-start.13 = (bf16[128,176]{0,1:T(8,128)(2,1)S(1)}, bf16[128,176]{0,1:T(8,128)(2,1)S(1)}, u32[]{:S(2)}, u32[]{:S(2)}) collective-permute-start(bf16[128,176]{0,1:T(8,128)(2,1)S(1)} %fusion.7), channel_id=1, source_target_pairs={{4,12},{5,13},{6,14},{7,15},{12,4},{13,5},{14,6},{15,7},{20,28},{2... | collective-permute-start | bytes 135176 | tf_op jit(solution)/shard_map/ppermute | solution.py:114
  77.4 3.6 %collective-permute-start.14 = (bf16[128,176]{0,1:T(8,128)(2,1)S(1)}, bf16[128,176]{0,1:T(8,128)(2,1)S(1)}, u32[]{:S(2)}, u32[]{:S(2)}) collective-permute-start(bf16[128,176]{0,1:T(8,128)(2,1)S(1)} %fusion.7), channel_id=1, source_target_pairs={{4,20},{5,21},{6,22},{7,23},{12,28},{13,29},{14,30},{15,31},{20,4}... | collective-permute-start | bytes 135176 | tf_op jit(solution)/shard_map/ppermute | solution.py:114
  80.9 3.3 %collective-permute-start.15 = (bf16[128,176]{0,1:T(8,128)(2,1)S(1)}, bf16[128,176]{0,1:T(8,128)(2,1)S(1)}, u32[]{:S(2)}, u32[]{:S(2)}) collective-permute-start(bf16[128,176]{0,1:T(8,128)(2,1)S(1)} %fusion.7), channel_id=1, source_target_pairs={{4,28},{5,29},{6,30},{7,31},{12,20},{13,21},{14,22},{15,23},{20,12... | collective-permute-start | bytes 135176 | tf_op jit(solution)/shard_map/ppermute | solution.py:114
  84.3 3.2 %collective-permute-done.15 = bf16[128,176]{0,1:T(8,128)(2,1)S(1)} collective-permute-done((bf16[128,176]{0,1:T(8,128)(2,1)S(1)}, bf16[128,176]{0,1:T(8,128)(2,1)S(1)}, u32[]{:S(2)}, u32[]{:S(2)}) %collective-permute-start.15) | collective-permute-done | bytes 45088 | tf_op jit(solution)/shard_map/ppermute | solution.py:114
  89.4 3.9 %all-to-all-start.2 = ((bf16[2,4,16,768]{3,2,0,1:T(8,128)(2,1)}), bf16[2,4,16,768]{3,2,0,1:T(8,128)(2,1)S(1)}, u32[]{:S(2)}, u32[]{:S(2)}) async-start(bf16[2,4,16,768]{3,2,0,1:T(8,128)(2,1)} %select_bitcast_fusion.1), calls=%async_computation.2 | async-start | bytes 393216 | tf_op jit(solution)/shard_map/all_to_all | solution.py:123
  93.2 4.0 %all-to-all-done.2 = bf16[2,4,16,768]{3,2,0,1:T(8,128)(2,1)S(1)} async-done(((bf16[2,4,16,768]{3,2,0,1:T(8,128)(2,1)}), bf16[2,4,16,768]{3,2,0,1:T(8,128)(2,1)S(1)}, u32[]{:S(2)}, u32[]{:S(2)}) %all-to-all-start.2) | async-done | bytes 196640 | tf_op jit(solution)/shard_map/all_to_all | solution.py:123
  (98 shorter events, 23.9 us)
Async XLA Ops:
  2.2 20.0 %collective-permute-start.3 = (bf16[176,768]{1,0:T(8,128)(2,1)}, bf16[176,768]{1,0:T(8,128)(2,1)}, u32[]{:S(2)}, u32[]{:S(2)}) collective-permute-start(bf16[176,768]{1,0:T(8,128)(2,1)} %get-tuple-element.13), channel_id=1, source_target_pairs={{0,8},{8,0},{16,24},{24,16},{1,9},{9,1},{17,25},{25,17},{2,10},{10... | collective-permute-start | bytes 811016 | tf_op jit(solution)/shard_map/ppermute | solution.py:78
  4.4 18.8 %collective-permute-start.4 = (bf16[176,768]{1,0:T(8,128)(2,1)}, bf16[176,768]{1,0:T(8,128)(2,1)}, u32[]{:S(2)}, u32[]{:S(2)}) collective-permute-start(bf16[176,768]{1,0:T(8,128)(2,1)} %get-tuple-element.14), channel_id=1, source_target_pairs={{0,16},{8,24},{16,0},{24,8},{1,17},{9,25},{17,1},{25,9},{2,18},{10... | collective-permute-start | bytes 811016 | tf_op jit(solution)/shard_map/ppermute | solution.py:78
  9.4 4.3 %collective-permute-start = (bf16[2,16,3072]{2,1,0:T(8,128)(2,1)}, bf16[2,16,3072]{2,1,0:T(8,128)(2,1)}, u32[]{:S(2)}, u32[]{:S(2)}) collective-permute-start(bf16[2,16,3072]{2,1,0:T(8,128)(2,1)} %get-tuple-element.32), channel_id=1, source_target_pairs={{0,1},{1,0},{2,3},{3,2},{8,9},{9,8},{10,11},{11,10},{16,17},{17,16... | collective-permute-start | bytes 589832 | tf_op jit(solution)/shard_map/ppermute | solution.py:98
  10.7 3.1 %collective-permute-start.1 = (bf16[2,16,3072]{2,1,0:T(8,128)(2,1)S(1)}, bf16[2,16,3072]{2,1,0:T(8,128)(2,1)}, u32[]{:S(2)}, u32[]{:S(2)}) collective-permute-start(bf16[2,16,3072]{2,1,0:T(8,128)(2,1)S(1)} %get-tuple-element.31), channel_id=1, source_target_pairs={{0,2},{1,3},{2,0},{3,1},{8,10},{9,11},{10,8},{11,9},{16,18},{17,19... | collective-permute-start | bytes 589832 | tf_op jit(solution)/shard_map/ppermute | solution.py:98
  12.1 1.7 %collective-permute-start.2 = (bf16[2,16,3072]{2,1,0:T(8,128)(2,1)S(1)}, bf16[2,16,3072]{2,1,0:T(8,128)(2,1)}, u32[]{:S(2)}, u32[]{:S(2)}) collective-permute-start(bf16[2,16,3072]{2,1,0:T(8,128)(2,1)S(1)} %get-tuple-element.33), channel_id=1, source_target_pairs={{0,3},{1,2},{2,1},{3,0},{8,11},{9,10},{10,9},{11,8},{16,19},{17,18... | collective-permute-start | bytes 589832 | tf_op jit(solution)/shard_map/ppermute | solution.py:98
  13.5 19.6 %copy-start.6 = (s32[1024]{0:T(1024)}, s32[1024]{0:T(1024)S(1)}, u32[]{:S(2)}) copy-start(s32[1024]{0:T(1024)S(1)} %pad_clamp_fusion.1) | copy-start | bytes 12292
  13.6 21.1 %copy-start.7 = (pred[4]{0:T(512)(128)(4,1)}, pred[4]{0:T(512)(128)(4,1)S(1)}, u32[]{:S(2)}) copy-start(pred[4]{0:T(512)(128)(4,1)S(1)} %get-tuple-element.18) | copy-start | bytes 16
  13.6 20.5 %copy-start.5 = (s32[1024]{0:T(1024)}, s32[1024]{0:T(1024)S(1)}, u32[]{:S(2)}) copy-start(s32[1024]{0:T(1024)S(1)} %pad_clamp_fusion) | copy-start | bytes 12292
  13.7 19.9 %copy-start.9 = (pred[4]{0:T(512)(128)(4,1)}, pred[4]{0:T(512)(128)(4,1)S(1)}, u32[]{:S(2)}) copy-start(pred[4]{0:T(512)(128)(4,1)S(1)} %compare_and_fusion.1) | copy-start | bytes 16
  13.7 10.4 %collective-permute-start.5 = (bf16[176,768]{1,0:T(8,128)(2,1)}, bf16[176,768]{1,0:T(8,128)(2,1)}, u32[]{:S(2)}, u32[]{:S(2)}) collective-permute-start(bf16[176,768]{1,0:T(8,128)(2,1)} %get-tuple-element.15), channel_id=1, source_target_pairs={{0,24},{8,16},{16,8},{24,0},{1,25},{9,17},{17,9},{25,1},{2,26},{10... | collective-permute-start | bytes 811016 | tf_op jit(solution)/shard_map/ppermute | solution.py:78
  17.7 15.3 %all-to-all-start = ((bf16[4,128,176]{1,2,0:T(8,128)(2,1)}), bf16[4,128,176]{1,2,0:T(8,128)(2,1)S(1)}, u32[]{:S(2)}, u32[]{:S(2)}) async-start(bf16[4,128,176]{1,2,0:T(8,128)(2,1)} %broadcast_in_dim.81), calls=%async_computation | async-start | bytes 360448 | tf_op jit(solution)/shard_map/all_to_all | solution.py:107
  35.4 7.5 %all-to-all-start.1 = ((bf16[2,4,16,768]{3,2,0,1:T(8,128)(2,1)}), bf16[2,4,16,768]{3,2,0,1:T(8,128)(2,1)S(1)}, u32[]{:S(2)}, u32[]{:S(2)}) async-start(bf16[2,4,16,768]{3,2,0,1:T(8,128)(2,1)} %select_bitcast_fusion.2), calls=%async_computation.1 | async-start | bytes 393216 | tf_op jit(solution)/shard_map/all_to_all | solution.py:123
  38.9 21.2 %copy-start.10 = (pred[4]{0:T(512)(128)(4,1)S(1)}, pred[4]{0:T(512)(128)(4,1)}, u32[]{:S(2)}) copy-start(pred[4]{0:T(512)(128)(4,1)} %copy-done.9) | copy-start | bytes 16
  43.2 9.4 %collective-permute-start.6 = (bf16[2,24,768]{2,1,0:T(8,128)(2,1)S(1)}, bf16[2,24,768]{2,1,0:T(8,128)(2,1)S(1)}, u32[]{:S(2)}, u32[]{:S(2)}) collective-permute-start(bf16[2,24,768]{2,1,0:T(8,128)(2,1)S(1)} %fusion), channel_id=1, source_target_pairs={{0,4},{1,5},{2,6},{3,7},{8,12},{9,13},{10,14},{11,15},{16,20},{17,... | collective-permute-start | bytes 221192 | tf_op jit(solution)/shard_map/ppermute | solution.py:151
  44.5 11.7 %collective-permute-start.7 = (bf16[2,24,768]{2,1,0:T(8,128)(2,1)S(1)}, bf16[2,24,768]{2,1,0:T(8,128)(2,1)S(1)}, u32[]{:S(2)}, u32[]{:S(2)}) collective-permute-start(bf16[2,24,768]{2,1,0:T(8,128)(2,1)S(1)} %fusion), channel_id=1, source_target_pairs={{0,12},{1,13},{2,14},{3,15},{8,4},{9,5},{10,6},{11,7},{16,28},{17,... | collective-permute-start | bytes 221192 | tf_op jit(solution)/shard_map/ppermute | solution.py:151
  45.8 11.3 %collective-permute-start.8 = (bf16[2,24,768]{2,1,0:T(8,128)(2,1)S(1)}, bf16[2,24,768]{2,1,0:T(8,128)(2,1)S(1)}, u32[]{:S(2)}, u32[]{:S(2)}) collective-permute-start(bf16[2,24,768]{2,1,0:T(8,128)(2,1)S(1)} %fusion), channel_id=1, source_target_pairs={{0,20},{1,21},{2,22},{3,23},{8,28},{9,29},{10,30},{11,31},{16,4},{... | collective-permute-start | bytes 221192 | tf_op jit(solution)/shard_map/ppermute | solution.py:151
  47.1 12.3 %collective-permute-start.9 = (bf16[2,24,768]{2,1,0:T(8,128)(2,1)S(1)}, bf16[2,24,768]{2,1,0:T(8,128)(2,1)S(1)}, u32[]{:S(2)}, u32[]{:S(2)}) collective-permute-start(bf16[2,24,768]{2,1,0:T(8,128)(2,1)S(1)} %fusion), channel_id=1, source_target_pairs={{0,28},{1,29},{2,30},{3,31},{8,20},{9,21},{10,22},{11,23},{16,12},... | collective-permute-start | bytes 221192 | tf_op jit(solution)/shard_map/ppermute | solution.py:151
  60.7 8.4 %collective-permute-start.10 = (bf16[2,16,3072]{2,1,0:T(8,128)(2,1)S(1)}, bf16[2,16,3072]{2,1,0:T(8,128)(2,1)S(1)}, u32[]{:S(2)}, u32[]{:S(2)}) collective-permute-start(bf16[2,16,3072]{2,1,0:T(8,128)(2,1)S(1)} %get-tuple-element.28), channel_id=1, source_target_pairs={{4,5},{5,4},{6,7},{7,6},{12,13},{13,12},{14,15},{15,14},{20,21},{2... | collective-permute-start | bytes 589832 | tf_op jit(solution)/shard_map/ppermute | solution.py:98
  63.4 6.4 %collective-permute-start.11 = (bf16[2,16,3072]{2,1,0:T(8,128)(2,1)S(1)}, bf16[2,16,3072]{2,1,0:T(8,128)(2,1)S(1)}, u32[]{:S(2)}, u32[]{:S(2)}) collective-permute-start(bf16[2,16,3072]{2,1,0:T(8,128)(2,1)S(1)} %get-tuple-element.27), channel_id=1, source_target_pairs={{4,6},{5,7},{6,4},{7,5},{12,14},{13,15},{14,12},{15,13},{20,22},{2... | collective-permute-start | bytes 589832 | tf_op jit(solution)/shard_map/ppermute | solution.py:98
  65.6 7.3 %collective-permute-start.12 = (bf16[2,16,3072]{2,1,0:T(8,128)(2,1)S(1)}, bf16[2,16,3072]{2,1,0:T(8,128)(2,1)S(1)}, u32[]{:S(2)}, u32[]{:S(2)}) collective-permute-start(bf16[2,16,3072]{2,1,0:T(8,128)(2,1)S(1)} %get-tuple-element.29), channel_id=1, source_target_pairs={{4,7},{5,6},{6,5},{7,4},{12,15},{13,14},{14,13},{15,12},{20,23},{2... | collective-permute-start | bytes 589832 | tf_op jit(solution)/shard_map/ppermute | solution.py:98
  75.0 9.3 %collective-permute-start.13 = (bf16[128,176]{0,1:T(8,128)(2,1)S(1)}, bf16[128,176]{0,1:T(8,128)(2,1)S(1)}, u32[]{:S(2)}, u32[]{:S(2)}) collective-permute-start(bf16[128,176]{0,1:T(8,128)(2,1)S(1)} %fusion.7), channel_id=1, source_target_pairs={{4,12},{5,13},{6,14},{7,15},{12,4},{13,5},{14,6},{15,7},{20,28},{2... | collective-permute-start | bytes 135176 | tf_op jit(solution)/shard_map/ppermute | solution.py:114
  77.4 6.9 %collective-permute-start.14 = (bf16[128,176]{0,1:T(8,128)(2,1)S(1)}, bf16[128,176]{0,1:T(8,128)(2,1)S(1)}, u32[]{:S(2)}, u32[]{:S(2)}) collective-permute-start(bf16[128,176]{0,1:T(8,128)(2,1)S(1)} %fusion.7), channel_id=1, source_target_pairs={{4,20},{5,21},{6,22},{7,23},{12,28},{13,29},{14,30},{15,31},{20,4}... | collective-permute-start | bytes 135176 | tf_op jit(solution)/shard_map/ppermute | solution.py:114
  80.9 6.6 %collective-permute-start.15 = (bf16[128,176]{0,1:T(8,128)(2,1)S(1)}, bf16[128,176]{0,1:T(8,128)(2,1)S(1)}, u32[]{:S(2)}, u32[]{:S(2)}) collective-permute-start(bf16[128,176]{0,1:T(8,128)(2,1)S(1)} %fusion.7), channel_id=1, source_target_pairs={{4,28},{5,29},{6,30},{7,31},{12,20},{13,21},{14,22},{15,23},{20,12... | collective-permute-start | bytes 135176 | tf_op jit(solution)/shard_map/ppermute | solution.py:114
  89.4 7.9 %all-to-all-start.2 = ((bf16[2,4,16,768]{3,2,0,1:T(8,128)(2,1)}), bf16[2,4,16,768]{3,2,0,1:T(8,128)(2,1)S(1)}, u32[]{:S(2)}, u32[]{:S(2)}) async-start(bf16[2,4,16,768]{3,2,0,1:T(8,128)(2,1)} %select_bitcast_fusion.1), calls=%async_computation.2 | async-start | bytes 393216 | tf_op jit(solution)/shard_map/all_to_all | solution.py:123
  (7 other events, 51.4 us)

commit v18 on v9

--- a/solution.py
+++ b/solution.py
@@ -86,9 +86,10 @@
     dispatch_map = jnp.stack([mp[0] for mp in maps])
     combine_map = jnp.stack([mp[1] for mp in maps])
     if ering.xor:
-        combine_map = jnp.stack(
-            [build_maps(route_ids[m], route_gates[m], ering, 0, rows_all)[1] for m in range(micro)]
-        )
+        flat_ids = route_ids.reshape(micro, -1)
+        onehot = (flat_ids[:, :, None] == jnp.arange(n_exp, dtype=jnp.int32)).astype(jnp.int32)
+        before = jnp.cumsum(onehot, axis=1) - onehot
+        pair_rows = flat_ids * CAP + jnp.sum(before * onehot, axis=2)
 
     def layer(current, p):
         outgoing = jnp.einsum("mrt,mtd->mrd", dispatch_map, current, preferred_element_type=jnp.float32)
@@ -120,13 +121,18 @@
             for s in range(1, n_exp):
                 returned.append(lax.ppermute(expert_out[:, s], AXES, expert_pairs(p, s, True)))
             returned = jnp.stack(returned, axis=1).reshape(micro, rows_all, columns)
-        mixed = jnp.einsum(
-            "mrt,mrc->mtc",
-            combine_map,
-            returned.astype(jnp.float32),
-            precision=lax.Precision.HIGHEST,
-            preferred_element_type=jnp.float32,
-        )
+        if ering.xor:
+            picked = jnp.take_along_axis(returned, pair_rows[:, :, None], axis=1).astype(jnp.float32)
+            picked = picked.reshape(micro, tok_rows, TOP, columns)
+            mixed = jnp.sum(route_gates[:, :, :, None] * picked, axis=2)
+        else:
+            mixed = jnp.einsum(
+                "mrt,mrc->mtc",
+                combine_map,
+                returned.astype(jnp.float32),
+                precision=lax.Precision.HIGHEST,
+                preferred_element_type=jnp.float32,
+            )
         current_cols = lax.dynamic_slice_in_dim(current, d_me * columns, columns, 2)
         return (current_cols.astype(jnp.float32) + mixed).astype(jnp.bfloat16)
 

time: 95.6 us -> 100 us (1.046)
  local copies, waits for them, and re-layouts: 10.4 us -> 14.6 us
  other arithmetic: 4.39 us -> 6.34 us
  matrix products: 4.43 us -> 3.37 us
    gather x0 -> x3, local copies, waits for them, and re-layouts: none -> 3.62 us  [layer(): jnp.take_along_axis(returned, pair_rows[:, :, None], axis=1)]
    dot_general x2 -> x0, matrix products: 1.07 us -> none  [layer(): jnp.einsum('mrt,mrc->mtc', combine_map, returned.astype(jnp.float32), pre...]
    unnamed x21 -> x28, local copies, waits for them, and re-layouts: 3.57 us -> 3.65 us
where the time goes in v18:
time: 100 us; the launch traced here: 99.3 us
  starting transfers between devices  40.2 us (40%)
  waiting for transfers between devices  34.2 us (34%)
  local copies, waits for them, and re-layouts  14.6 us (15%)
  other arithmetic  6.34 us (6%)
  matrix products  3.37 us (3%)
    ppermute x4, waiting for transfers between devices, per_device(): parts.append(lax.ppermute(cols, AXES, pairs))  20.3 us
    ppermute x6, starting transfers between devices, layer(): lax.ppermute(outgoing[:, s], AXES, expert_pairs(p, s, False))  12.4 us
    ppermute x6, starting transfers between devices, layer(): parts.append(lax.ppermute(hidden, AXES, dp_pairs(p, s)))  11.3 us
    all_to_all x2, waiting for transfers between devices, layer(): lax.all_to_all(by_block, 'expert', 1, 1, tiled=True)  7.79 us
    all_to_all x2, starting transfers between devices, layer(): lax.all_to_all(by_block, 'expert', 1, 1, tiled=True)  6.93 us
    ppermute x4, starting transfers between devices, per_device(): parts.append(lax.ppermute(cols, AXES, pairs))  5.17 us
    ppermute x3, starting transfers between devices, per_device(): lax.ppermute(down_parts[s], 'dp', [(i, dring.ahead(i, s)) for i in range(...  4.51 us
    ppermute x6, waiting for transfers between devices, layer(): lax.ppermute(outgoing[:, s], AXES, expert_pairs(p, s, False))  3.84 us
  transfers between devices with their start and end apart: 21, of which 10 were waited for; matrix products, arithmetic and copies ran while one was open for 9% of the time, Pallas kernels for 0%

profile of v18, /device:TPU:1, one launch (start us, length us, event | category | flops | bytes accessed | tf_op | source)
XLA Modules:
  0.0 99.3 jit_solution(4185881336737714199)
XLA Ops:
  0.0 2.2 %dynamic-slice_bitcast_fusion = (bf16[176,768]{1,0:T(8,128)(2,1)}, bf16[176,768]{1,0:T(8,128)(2,1)}, bf16[176,768]{1,0:T(8,128)(2,1)S(1)}, bf16[176,768]{1,0:T(8,128)(2,1)}) fusion(bf16[1,1,176,3072]{3,2,1,0:T(8,128)(2,1)} %param.15, s32[]{:T(128)S(6)} %select_n.63, s32[]{:T(128)S(6)} %select_n.61, s32[]{:T(128)S(6)} %select_n.60, s32[]{:T(128)S(6)} %select_n.62), kind=kLoop, calls=%fused_computation.29 | loop fusion | bytes 2162704 | tf_op jit(solution)/shard_map/dynamic_slice | solution.py:74
  2.2 2.1 %collective-permute-start.6 = (bf16[176,768]{1,0:T(8,128)(2,1)}, bf16[176,768]{1,0:T(8,128)(2,1)}, u32[]{:S(2)}, u32[]{:S(2)}) collective-permute-start(bf16[176,768]{1,0:T(8,128)(2,1)} %get-tuple-element.14), channel_id=1, source_target_pairs={{0,8},{8,0},{16,24},{24,16},{1,9},{9,1},{17,25},{25,17},{2,10},{10... | collective-permute-start | bytes 811016 | tf_op jit(solution)/shard_map/ppermute | solution.py:78
  4.4 2.3 %collective-permute-start.7 = (bf16[176,768]{1,0:T(8,128)(2,1)}, bf16[176,768]{1,0:T(8,128)(2,1)}, u32[]{:S(2)}, u32[]{:S(2)}) collective-permute-start(bf16[176,768]{1,0:T(8,128)(2,1)} %get-tuple-element.15), channel_id=1, source_target_pairs={{0,16},{8,24},{16,0},{24,8},{1,17},{9,25},{17,1},{25,9},{2,18},{10... | collective-permute-start | bytes 811016 | tf_op jit(solution)/shard_map/ppermute | solution.py:78
  9.4 1.3 %collective-permute-start.2 = (bf16[2,16,3072]{2,1,0:T(8,128)(2,1)}, bf16[2,16,3072]{2,1,0:T(8,128)(2,1)}, u32[]{:S(2)}, u32[]{:S(2)}) collective-permute-start(bf16[2,16,3072]{2,1,0:T(8,128)(2,1)} %get-tuple-element.34), channel_id=1, source_target_pairs={{0,3},{1,2},{2,1},{3,0},{8,11},{9,10},{10,9},{11,8},{16,19},{17,18... | collective-permute-start | bytes 589832 | tf_op jit(solution)/shard_map/ppermute | solution.py:99
  10.7 1.3 %collective-permute-start.1 = (bf16[2,16,3072]{2,1,0:T(8,128)(2,1)S(1)}, bf16[2,16,3072]{2,1,0:T(8,128)(2,1)}, u32[]{:S(2)}, u32[]{:S(2)}) collective-permute-start(bf16[2,16,3072]{2,1,0:T(8,128)(2,1)S(1)} %get-tuple-element.32), channel_id=1, source_target_pairs={{0,2},{1,3},{2,0},{3,1},{8,10},{9,11},{10,8},{11,9},{16,18},{17,19... | collective-permute-start | bytes 589832 | tf_op jit(solution)/shard_map/ppermute | solution.py:99
  12.1 1.3 %collective-permute-start = (bf16[2,16,3072]{2,1,0:T(8,128)(2,1)S(1)}, bf16[2,16,3072]{2,1,0:T(8,128)(2,1)}, u32[]{:S(2)}, u32[]{:S(2)}) collective-permute-start(bf16[2,16,3072]{2,1,0:T(8,128)(2,1)S(1)} %get-tuple-element.33), channel_id=1, source_target_pairs={{0,1},{1,0},{2,3},{3,2},{8,9},{9,8},{10,11},{11,10},{16,17},{17,16... | collective-permute-start | bytes 589832 | tf_op jit(solution)/shard_map/ppermute | solution.py:99
  14.4 1.3 %multiply_reduce_fusion.1 = (f32[2,4,16]{2,1,0:T(4,128)S(1)}, bf16[2,4,16,3072]{3,2,1,0:T(8,128)(2,1)S(1)}) fusion(bf16[2,1,16,3072]{3,2,1,0:T(8,128)(2,1)} %bitcast.25, bf16[2,1,16,3072]{3,2,1,0:T(8,128)(2,1)} %bitcast.23, bf16[2,1,16,3072]{3,2,1,0:T(8,128)(2,1)} %bitcast.21, bf16[2,1,16,3072]{3,2,1,0:T(8,128)(2,1)S(1)} %get-tuple-element.31), kind=kLoop, calls=%fused_computation.8 | loop fusion | flops 2359168 | bytes 1573376 | tf_op jit(solution)/shard_map/reduce_sum | solution.py:101
  25.1 3.4 %all-to-all-start = ((bf16[2,4,16,768]{3,2,0,1:T(8,128)(2,1)}), bf16[2,4,16,768]{3,2,0,1:T(8,128)(2,1)S(1)}, u32[]{:S(2)}, u32[]{:S(2)}) async-start(bf16[2,4,16,768]{3,2,0,1:T(8,128)(2,1)} %select_bitcast_fusion.2), calls=%async_computation | async-start | bytes 393216 | tf_op jit(solution)/shard_map/all_to_all | solution.py:118
  28.8 3.8 %all-to-all-done = bf16[2,4,16,768]{3,2,0,1:T(8,128)(2,1)S(1)} async-done(((bf16[2,4,16,768]{3,2,0,1:T(8,128)(2,1)}), bf16[2,4,16,768]{3,2,0,1:T(8,128)(2,1)S(1)}, u32[]{:S(2)}, u32[]{:S(2)}) %all-to-all-start) | async-done | bytes 196640 | tf_op jit(solution)/shard_map/all_to_all | solution.py:118
  32.6 1.8 %gather_fusion.2 = bf16[96,768]{1,0:T(8,128)(2,1)S(1)} fusion(bf16[2,64,768]{2,1,0:T(8,128)(2,1)S(1)} %bitcast.127, s32[96]{0:T(128)S(1)} %reshape.412), kind=kCustom, calls=%fused_computation.1.clone | custom fusion | bytes 295680 | tf_op jit(solution)/shard_map/jit(take_along_axis)/gather | solution.py:125
  35.1 1.3 %collective-permute-start.12 = (bf16[2,24,768]{2,1,0:T(8,128)(2,1)S(1)}, bf16[2,24,768]{2,1,0:T(8,128)(2,1)S(1)}, u32[]{:S(2)}, u32[]{:S(2)}) collective-permute-start(bf16[2,24,768]{2,1,0:T(8,128)(2,1)S(1)} %add_convert_fusion.1), channel_id=1, source_target_pairs={{0,28},{1,29},{2,30},{3,31},{8,20},{9,21},{10,22},{11,23},{16,12},... | collective-permute-start | bytes 221192 | tf_op jit(solution)/shard_map/ppermute | solution.py:151
  36.4 1.3 %collective-permute-start.11 = (bf16[2,24,768]{2,1,0:T(8,128)(2,1)S(1)}, bf16[2,24,768]{2,1,0:T(8,128)(2,1)S(1)}, u32[]{:S(2)}, u32[]{:S(2)}) collective-permute-start(bf16[2,24,768]{2,1,0:T(8,128)(2,1)S(1)} %add_convert_fusion.1), channel_id=1, source_target_pairs={{0,20},{1,21},{2,22},{3,23},{8,28},{9,29},{10,30},{11,31},{16,4},{... | collective-permute-start | bytes 221192 | tf_op jit(solution)/shard_map/ppermute | solution.py:151
  40.4 17.2 %collective-permute-done.12 = bf16[2,24,768]{2,1,0:T(8,128)(2,1)S(1)} collective-permute-done((bf16[2,24,768]{2,1,0:T(8,128)(2,1)S(1)}, bf16[2,24,768]{2,1,0:T(8,128)(2,1)S(1)}, u32[]{:S(2)}, u32[]{:S(2)}) %collective-permute-start.12) | collective-permute-done | bytes 73760 | tf_op jit(solution)/shard_map/ppermute | solution.py:151
  57.6 1.8 %collective-permute-done.11 = bf16[2,24,768]{2,1,0:T(8,128)(2,1)S(1)} collective-permute-done((bf16[2,24,768]{2,1,0:T(8,128)(2,1)S(1)}, bf16[2,24,768]{2,1,0:T(8,128)(2,1)S(1)}, u32[]{:S(2)}, u32[]{:S(2)}) %collective-permute-start.11) | collective-permute-done | bytes 73760 | tf_op jit(solution)/shard_map/ppermute | solution.py:151
  61.9 2.7 %collective-permute-start.15 = (bf16[2,16,3072]{2,1,0:T(8,128)(2,1)S(1)}, bf16[2,16,3072]{2,1,0:T(8,128)(2,1)S(1)}, u32[]{:S(2)}, u32[]{:S(2)}) collective-permute-start(bf16[2,16,3072]{2,1,0:T(8,128)(2,1)S(1)} %get-tuple-element.30), channel_id=1, source_target_pairs={{4,7},{5,6},{6,5},{7,4},{12,15},{13,14},{14,13},{15,12},{20,23},{2... | collective-permute-start | bytes 589832 | tf_op jit(solution)/shard_map/ppermute | solution.py:99
  64.6 3.1 %collective-permute-start.14 = (bf16[2,16,3072]{2,1,0:T(8,128)(2,1)S(1)}, bf16[2,16,3072]{2,1,0:T(8,128)(2,1)S(1)}, u32[]{:S(2)}, u32[]{:S(2)}) collective-permute-start(bf16[2,16,3072]{2,1,0:T(8,128)(2,1)S(1)} %get-tuple-element.28), channel_id=1, source_target_pairs={{4,6},{5,7},{6,4},{7,5},{12,14},{13,15},{14,12},{15,13},{20,22},{2... | collective-permute-start | bytes 589832 | tf_op jit(solution)/shard_map/ppermute | solution.py:99
  67.8 2.6 %collective-permute-start.13 = (bf16[2,16,3072]{2,1,0:T(8,128)(2,1)S(1)}, bf16[2,16,3072]{2,1,0:T(8,128)(2,1)S(1)}, u32[]{:S(2)}, u32[]{:S(2)}) collective-permute-start(bf16[2,16,3072]{2,1,0:T(8,128)(2,1)S(1)} %get-tuple-element.29), channel_id=1, source_target_pairs={{4,5},{5,4},{6,7},{7,6},{12,13},{13,12},{14,15},{15,14},{20,21},{2... | collective-permute-start | bytes 589832 | tf_op jit(solution)/shard_map/ppermute | solution.py:99
  71.4 2.8 %collective-permute-done.13 = bf16[2,16,3072]{2,1,0:T(8,128)(2,1)S(1)} collective-permute-done((bf16[2,16,3072]{2,1,0:T(8,128)(2,1)S(1)}, bf16[2,16,3072]{2,1,0:T(8,128)(2,1)S(1)}, u32[]{:S(2)}, u32[]{:S(2)}) %collective-permute-start.13) | collective-permute-done | bytes 196640 | tf_op jit(solution)/shard_map/ppermute | solution.py:99
  76.2 3.8 %collective-permute-start.18 = (bf16[128,176]{0,1:T(8,128)(2,1)S(1)}, bf16[128,176]{0,1:T(8,128)(2,1)S(1)}, u32[]{:S(2)}, u32[]{:S(2)}) collective-permute-start(bf16[128,176]{0,1:T(8,128)(2,1)S(1)} %fusion.3), channel_id=1, source_target_pairs={{4,28},{5,29},{6,30},{7,31},{12,20},{13,21},{14,22},{15,23},{20,12... | collective-permute-start | bytes 135176 | tf_op jit(solution)/shard_map/ppermute | solution.py:109
  80.0 1.9 %collective-permute-start.17 = (bf16[128,176]{0,1:T(8,128)(2,1)S(1)}, bf16[128,176]{0,1:T(8,128)(2,1)S(1)}, u32[]{:S(2)}, u32[]{:S(2)}) collective-permute-start(bf16[128,176]{0,1:T(8,128)(2,1)S(1)} %fusion.3), channel_id=1, source_target_pairs={{4,20},{5,21},{6,22},{7,23},{12,28},{13,29},{14,30},{15,31},{20,4}... | collective-permute-start | bytes 135176 | tf_op jit(solution)/shard_map/ppermute | solution.py:109
  82.0 3.6 %collective-permute-start.16 = (bf16[128,176]{0,1:T(8,128)(2,1)S(1)}, bf16[128,176]{0,1:T(8,128)(2,1)S(1)}, u32[]{:S(2)}, u32[]{:S(2)}) collective-permute-start(bf16[128,176]{0,1:T(8,128)(2,1)S(1)} %fusion.3), channel_id=1, source_target_pairs={{4,12},{5,13},{6,14},{7,15},{12,4},{13,5},{14,6},{15,7},{20,28},{2... | collective-permute-start | bytes 135176 | tf_op jit(solution)/shard_map/ppermute | solution.py:109
  88.6 3.5 %all-to-all-start.1 = ((bf16[2,4,16,768]{3,2,0,1:T(8,128)(2,1)}), bf16[2,4,16,768]{3,2,0,1:T(8,128)(2,1)S(1)}, u32[]{:S(2)}, u32[]{:S(2)}) async-start(bf16[2,4,16,768]{3,2,0,1:T(8,128)(2,1)} %select_bitcast_fusion.1), calls=%async_computation.1 | async-start | bytes 393216 | tf_op jit(solution)/shard_map/all_to_all | solution.py:118
  92.1 4.0 %all-to-all-done.1 = bf16[2,4,16,768]{3,2,0,1:T(8,128)(2,1)S(1)} async-done(((bf16[2,4,16,768]{3,2,0,1:T(8,128)(2,1)}), bf16[2,4,16,768]{3,2,0,1:T(8,128)(2,1)S(1)}, u32[]{:S(2)}, u32[]{:S(2)}) %all-to-all-start.1) | async-done | bytes 196640 | tf_op jit(solution)/shard_map/all_to_all | solution.py:118
  96.2 1.8 %gather_fusion.4 = bf16[96,768]{1,0:T(8,128)(2,1)S(1)} fusion(bf16[2,64,768]{2,1,0:T(8,128)(2,1)S(1)} %bitcast.126, s32[96]{0:T(128)S(1)} %reshape.412), kind=kCustom, calls=%fused_computation.3.clone | custom fusion | bytes 295680 | tf_op jit(solution)/shard_map/jit(take_along_axis)/gather | solution.py:125
  (117 shorter events, 26.4 us)
Async XLA Ops:
  0.0 15.9 %copy-start = (bf16[1,1,3072,176]{2,3,1,0:T(8,128)(2,1)S(1)}, bf16[1,1,3072,176]{2,3,1,0:T(8,128)(2,1)}, u32[]{:S(2)}) copy-start(bf16[1,1,3072,176]{2,3,1,0:T(8,128)(2,1)} %param.13) | copy-start | bytes 3244036
  2.2 16.7 %collective-permute-start.6 = (bf16[176,768]{1,0:T(8,128)(2,1)}, bf16[176,768]{1,0:T(8,128)(2,1)}, u32[]{:S(2)}, u32[]{:S(2)}) collective-permute-start(bf16[176,768]{1,0:T(8,128)(2,1)} %get-tuple-element.14), channel_id=1, source_target_pairs={{0,8},{8,0},{16,24},{24,16},{1,9},{9,1},{17,25},{25,17},{2,10},{10... | collective-permute-start | bytes 811016 | tf_op jit(solution)/shard_map/ppermute | solution.py:78
  4.4 16.2 %collective-permute-start.7 = (bf16[176,768]{1,0:T(8,128)(2,1)}, bf16[176,768]{1,0:T(8,128)(2,1)}, u32[]{:S(2)}, u32[]{:S(2)}) collective-permute-start(bf16[176,768]{1,0:T(8,128)(2,1)} %get-tuple-element.15), channel_id=1, source_target_pairs={{0,16},{8,24},{16,0},{24,8},{1,17},{9,25},{17,1},{25,9},{2,18},{10... | collective-permute-start | bytes 811016 | tf_op jit(solution)/shard_map/ppermute | solution.py:78
  9.4 4.9 %collective-permute-start.2 = (bf16[2,16,3072]{2,1,0:T(8,128)(2,1)}, bf16[2,16,3072]{2,1,0:T(8,128)(2,1)}, u32[]{:S(2)}, u32[]{:S(2)}) collective-permute-start(bf16[2,16,3072]{2,1,0:T(8,128)(2,1)} %get-tuple-element.34), channel_id=1, source_target_pairs={{0,3},{1,2},{2,1},{3,0},{8,11},{9,10},{10,9},{11,8},{16,19},{17,18... | collective-permute-start | bytes 589832 | tf_op jit(solution)/shard_map/ppermute | solution.py:99
  10.7 3.7 %collective-permute-start.1 = (bf16[2,16,3072]{2,1,0:T(8,128)(2,1)S(1)}, bf16[2,16,3072]{2,1,0:T(8,128)(2,1)}, u32[]{:S(2)}, u32[]{:S(2)}) collective-permute-start(bf16[2,16,3072]{2,1,0:T(8,128)(2,1)S(1)} %get-tuple-element.32), channel_id=1, source_target_pairs={{0,2},{1,3},{2,0},{3,1},{8,10},{9,11},{10,8},{11,9},{16,18},{17,19... | collective-permute-start | bytes 589832 | tf_op jit(solution)/shard_map/ppermute | solution.py:99
  12.1 2.3 %collective-permute-start = (bf16[2,16,3072]{2,1,0:T(8,128)(2,1)S(1)}, bf16[2,16,3072]{2,1,0:T(8,128)(2,1)}, u32[]{:S(2)}, u32[]{:S(2)}) collective-permute-start(bf16[2,16,3072]{2,1,0:T(8,128)(2,1)S(1)} %get-tuple-element.33), channel_id=1, source_target_pairs={{0,1},{1,0},{2,3},{3,2},{8,9},{9,8},{10,11},{11,10},{16,17},{17,16... | collective-permute-start | bytes 589832 | tf_op jit(solution)/shard_map/ppermute | solution.py:99
  14.3 20.1 %copy-start.9 = (pred[2,48]{1,0:T(4,128)(4,1)}, pred[2,48]{1,0:T(4,128)(4,1)S(1)}, u32[]{:S(2)}) copy-start(pred[2,48]{1,0:T(4,128)(4,1)S(1)} %and_bitcast_fusion) | copy-start | bytes 292
  14.3 8.1 %collective-permute-start.8 = (bf16[176,768]{1,0:T(8,128)(2,1)}, bf16[176,768]{1,0:T(8,128)(2,1)}, u32[]{:S(2)}, u32[]{:S(2)}) collective-permute-start(bf16[176,768]{1,0:T(8,128)(2,1)} %get-tuple-element.16), channel_id=1, source_target_pairs={{0,24},{8,16},{16,8},{24,0},{1,25},{9,17},{17,9},{25,1},{2,26},{10... | collective-permute-start | bytes 811016 | tf_op jit(solution)/shard_map/ppermute | solution.py:78
  17.6 5.8 %collective-permute-start.5 = (bf16[128,176]{0,1:T(8,128)(2,1)S(1)}, bf16[128,176]{0,1:T(8,128)(2,1)S(1)}, u32[]{:S(2)}, u32[]{:S(2)}) collective-permute-start(bf16[128,176]{0,1:T(8,128)(2,1)S(1)} %fusion.2), channel_id=1, source_target_pairs={{0,24},{1,25},{2,26},{3,27},{8,16},{9,17},{10,18},{11,19},{16,8},{... | collective-permute-start | bytes 135176 | tf_op jit(solution)/shard_map/ppermute | solution.py:109
  18.3 5.2 %collective-permute-start.4 = (bf16[128,176]{0,1:T(8,128)(2,1)S(1)}, bf16[128,176]{0,1:T(8,128)(2,1)S(1)}, u32[]{:S(2)}, u32[]{:S(2)}) collective-permute-start(bf16[128,176]{0,1:T(8,128)(2,1)S(1)} %fusion.2), channel_id=1, source_target_pairs={{0,16},{1,17},{2,18},{3,19},{8,24},{9,25},{10,26},{11,27},{16,0},{... | collective-permute-start | bytes 135176 | tf_op jit(solution)/shard_map/ppermute | solution.py:109
  18.9 4.5 %collective-permute-start.3 = (bf16[128,176]{0,1:T(8,128)(2,1)S(1)}, bf16[128,176]{0,1:T(8,128)(2,1)S(1)}, u32[]{:S(2)}, u32[]{:S(2)}) collective-permute-start(bf16[128,176]{0,1:T(8,128)(2,1)S(1)} %fusion.2), channel_id=1, source_target_pairs={{0,8},{1,9},{2,10},{3,11},{8,0},{9,1},{10,2},{11,3},{16,24},{17,25... | collective-permute-start | bytes 135176 | tf_op jit(solution)/shard_map/ppermute | solution.py:109
  25.1 7.5 %all-to-all-start = ((bf16[2,4,16,768]{3,2,0,1:T(8,128)(2,1)}), bf16[2,4,16,768]{3,2,0,1:T(8,128)(2,1)S(1)}, u32[]{:S(2)}, u32[]{:S(2)}) async-start(bf16[2,4,16,768]{3,2,0,1:T(8,128)(2,1)} %select_bitcast_fusion.2), calls=%async_computation | async-start | bytes 393216 | tf_op jit(solution)/shard_map/all_to_all | solution.py:118
  35.1 22.5 %collective-permute-start.12 = (bf16[2,24,768]{2,1,0:T(8,128)(2,1)S(1)}, bf16[2,24,768]{2,1,0:T(8,128)(2,1)S(1)}, u32[]{:S(2)}, u32[]{:S(2)}) collective-permute-start(bf16[2,24,768]{2,1,0:T(8,128)(2,1)S(1)} %add_convert_fusion.1), channel_id=1, source_target_pairs={{0,28},{1,29},{2,30},{3,31},{8,20},{9,21},{10,22},{11,23},{16,12},... | collective-permute-start | bytes 221192 | tf_op jit(solution)/shard_map/ppermute | solution.py:151
  36.4 23.0 %collective-permute-start.11 = (bf16[2,24,768]{2,1,0:T(8,128)(2,1)S(1)}, bf16[2,24,768]{2,1,0:T(8,128)(2,1)S(1)}, u32[]{:S(2)}, u32[]{:S(2)}) collective-permute-start(bf16[2,24,768]{2,1,0:T(8,128)(2,1)S(1)} %add_convert_fusion.1), channel_id=1, source_target_pairs={{0,20},{1,21},{2,22},{3,23},{8,28},{9,29},{10,30},{11,31},{16,4},{... | collective-permute-start | bytes 221192 | tf_op jit(solution)/shard_map/ppermute | solution.py:151
  37.7 23.0 %collective-permute-start.10 = (bf16[2,24,768]{2,1,0:T(8,128)(2,1)S(1)}, bf16[2,24,768]{2,1,0:T(8,128)(2,1)S(1)}, u32[]{:S(2)}, u32[]{:S(2)}) collective-permute-start(bf16[2,24,768]{2,1,0:T(8,128)(2,1)S(1)} %add_convert_fusion.1), channel_id=1, source_target_pairs={{0,12},{1,13},{2,14},{3,15},{8,4},{9,5},{10,6},{11,7},{16,28},{17,... | collective-permute-start | bytes 221192 | tf_op jit(solution)/shard_map/ppermute | solution.py:151
  39.0 21.7 %collective-permute-start.9 = (bf16[2,24,768]{2,1,0:T(8,128)(2,1)S(1)}, bf16[2,24,768]{2,1,0:T(8,128)(2,1)S(1)}, u32[]{:S(2)}, u32[]{:S(2)}) collective-permute-start(bf16[2,24,768]{2,1,0:T(8,128)(2,1)S(1)} %add_convert_fusion.1), channel_id=1, source_target_pairs={{0,4},{1,5},{2,6},{3,7},{8,12},{9,13},{10,14},{11,15},{16,20},{17,... | collective-permute-start | bytes 221192 | tf_op jit(solution)/shard_map/ppermute | solution.py:151
  61.9 8.4 %collective-permute-start.15 = (bf16[2,16,3072]{2,1,0:T(8,128)(2,1)S(1)}, bf16[2,16,3072]{2,1,0:T(8,128)(2,1)S(1)}, u32[]{:S(2)}, u32[]{:S(2)}) collective-permute-start(bf16[2,16,3072]{2,1,0:T(8,128)(2,1)S(1)} %get-tuple-element.30), channel_id=1, source_target_pairs={{4,7},{5,6},{6,5},{7,4},{12,15},{13,14},{14,13},{15,12},{20,23},{2... | collective-permute-start | bytes 589832 | tf_op jit(solution)/shard_map/ppermute | solution.py:99
  64.6 6.7 %collective-permute-start.14 = (bf16[2,16,3072]{2,1,0:T(8,128)(2,1)S(1)}, bf16[2,16,3072]{2,1,0:T(8,128)(2,1)S(1)}, u32[]{:S(2)}, u32[]{:S(2)}) collective-permute-start(bf16[2,16,3072]{2,1,0:T(8,128)(2,1)S(1)} %get-tuple-element.28), channel_id=1, source_target_pairs={{4,6},{5,7},{6,4},{7,5},{12,14},{13,15},{14,12},{15,13},{20,22},{2... | collective-permute-start | bytes 589832 | tf_op jit(solution)/shard_map/ppermute | solution.py:99
  67.8 6.4 %collective-permute-start.13 = (bf16[2,16,3072]{2,1,0:T(8,128)(2,1)S(1)}, bf16[2,16,3072]{2,1,0:T(8,128)(2,1)S(1)}, u32[]{:S(2)}, u32[]{:S(2)}) collective-permute-start(bf16[2,16,3072]{2,1,0:T(8,128)(2,1)S(1)} %get-tuple-element.29), channel_id=1, source_target_pairs={{4,5},{5,4},{6,7},{7,6},{12,13},{13,12},{14,15},{15,14},{20,21},{2... | collective-permute-start | bytes 589832 | tf_op jit(solution)/shard_map/ppermute | solution.py:99
  76.2 11.7 %copy-start.8 = (pred[4]{0:T(512)(128)(4,1)S(1)}, pred[4]{0:T(512)(128)(4,1)}, u32[]{:S(2)}) copy-start(pred[4]{0:T(512)(128)(4,1)} %copy-done.7) | copy-start | bytes 16
  76.2 9.3 %collective-permute-start.18 = (bf16[128,176]{0,1:T(8,128)(2,1)S(1)}, bf16[128,176]{0,1:T(8,128)(2,1)S(1)}, u32[]{:S(2)}, u32[]{:S(2)}) collective-permute-start(bf16[128,176]{0,1:T(8,128)(2,1)S(1)} %fusion.3), channel_id=1, source_target_pairs={{4,28},{5,29},{6,30},{7,31},{12,20},{13,21},{14,22},{15,23},{20,12... | collective-permute-start | bytes 135176 | tf_op jit(solution)/shard_map/ppermute | solution.py:109
  80.0 5.7 %collective-permute-start.17 = (bf16[128,176]{0,1:T(8,128)(2,1)S(1)}, bf16[128,176]{0,1:T(8,128)(2,1)S(1)}, u32[]{:S(2)}, u32[]{:S(2)}) collective-permute-start(bf16[128,176]{0,1:T(8,128)(2,1)S(1)} %fusion.3), channel_id=1, source_target_pairs={{4,20},{5,21},{6,22},{7,23},{12,28},{13,29},{14,30},{15,31},{20,4}... | collective-permute-start | bytes 135176 | tf_op jit(solution)/shard_map/ppermute | solution.py:109
  82.0 5.0 %collective-permute-start.16 = (bf16[128,176]{0,1:T(8,128)(2,1)S(1)}, bf16[128,176]{0,1:T(8,128)(2,1)S(1)}, u32[]{:S(2)}, u32[]{:S(2)}) collective-permute-start(bf16[128,176]{0,1:T(8,128)(2,1)S(1)} %fusion.3), channel_id=1, source_target_pairs={{4,12},{5,13},{6,14},{7,15},{12,4},{13,5},{14,6},{15,7},{20,28},{2... | collective-permute-start | bytes 135176 | tf_op jit(solution)/shard_map/ppermute | solution.py:109
  88.6 7.5 %all-to-all-start.1 = ((bf16[2,4,16,768]{3,2,0,1:T(8,128)(2,1)}), bf16[2,4,16,768]{3,2,0,1:T(8,128)(2,1)S(1)}, u32[]{:S(2)}, u32[]{:S(2)}) async-start(bf16[2,4,16,768]{3,2,0,1:T(8,128)(2,1)} %select_bitcast_fusion.1), calls=%async_computation.1 | async-start | bytes 393216 | tf_op jit(solution)/shard_map/all_to_all | solution.py:118
  (9 other events, 44.8 us)

commit v19 on v9

--- a/solution.py
+++ b/solution.py
@@ -90,6 +90,9 @@
             [build_maps(route_ids[m], route_gates[m], ering, 0, rows_all)[1] for m in range(micro)]
         )
 
+    gates_high = combine_map.astype(jnp.bfloat16)
+    gates_low = (combine_map - gates_high.astype(jnp.float32)).astype(jnp.bfloat16)
+
     def layer(current, p):
         outgoing = jnp.einsum("mrt,mtd->mrd", dispatch_map, current, preferred_element_type=jnp.float32)
         outgoing = outgoing.astype(jnp.bfloat16).reshape(micro, n_exp, CAP, width)
@@ -120,13 +123,8 @@
             for s in range(1, n_exp):
                 returned.append(lax.ppermute(expert_out[:, s], AXES, expert_pairs(p, s, True)))
             returned = jnp.stack(returned, axis=1).reshape(micro, rows_all, columns)
-        mixed = jnp.einsum(
-            "mrt,mrc->mtc",
-            combine_map,
-            returned.astype(jnp.float32),
-            precision=lax.Precision.HIGHEST,
-            preferred_element_type=jnp.float32,
-        )
+        mixed = jnp.einsum("mrt,mrc->mtc", gates_high, returned, preferred_element_type=jnp.float32)
+        mixed = mixed + jnp.einsum("mrt,mrc->mtc", gates_low, returned, preferred_element_type=jnp.float32)
         current_cols = lax.dynamic_slice_in_dim(current, d_me * columns, columns, 2)
         return (current_cols.astype(jnp.float32) + mixed).astype(jnp.bfloat16)
 

time: 95.6 us -> 95.8 us (level)
  no operation moved by 1% of the time
where the time goes in v19:
time: 95.8 us; the launch traced here: 95 us
  starting transfers between devices  40.1 us (42%)
  waiting for transfers between devices  35 us (37%)
  local copies, waits for them, and re-layouts  10.4 us (11%)
  matrix products  4.62 us (5%)
  other arithmetic  4.39 us (5%)
    ppermute x4, waiting for transfers between devices, per_device(): parts.append(lax.ppermute(cols, AXES, pairs))  20.3 us
    ppermute x6, starting transfers between devices, layer(): lax.ppermute(outgoing[:, s], AXES, expert_pairs(p, s, False))  12.4 us
    ppermute x6, starting transfers between devices, layer(): parts.append(lax.ppermute(hidden, AXES, dp_pairs(p, s)))  11.3 us
    all_to_all x2, waiting for transfers between devices, layer(): lax.all_to_all(by_block, 'expert', 1, 1, tiled=True)  7.95 us
    all_to_all x2, starting transfers between devices, layer(): lax.all_to_all(by_block, 'expert', 1, 1, tiled=True)  6.8 us
    ppermute x4, starting transfers between devices, per_device(): parts.append(lax.ppermute(cols, AXES, pairs))  5.17 us
    ppermute x3, starting transfers between devices, per_device(): lax.ppermute(down_parts[s], 'dp', [(i, dring.ahead(i, s)) for i in range(...  4.51 us
    ppermute x6, waiting for transfers between devices, layer(): lax.ppermute(outgoing[:, s], AXES, expert_pairs(p, s, False))  3.84 us
  transfers between devices with their start and end apart: 21, of which 10 were waited for; matrix products, arithmetic and copies ran while one was open for 9% of the time, Pallas kernels for 0%

profile of v19, /device:TPU:1, one launch (start us, length us, event | category | flops | bytes accessed | tf_op | source)
XLA Modules:
  0.0 95.0 jit_solution(16628437439838487450)
XLA Ops:
  0.0 2.2 %dynamic-slice_bitcast_fusion = (bf16[176,768]{1,0:T(8,128)(2,1)}, bf16[176,768]{1,0:T(8,128)(2,1)}, bf16[176,768]{1,0:T(8,128)(2,1)S(1)}, bf16[176,768]{1,0:T(8,128)(2,1)}) fusion(bf16[1,1,176,3072]{3,2,1,0:T(8,128)(2,1)} %param.13, s32[]{:T(128)S(6)} %select_n.66, s32[]{:T(128)S(6)} %select_n.64, s32[]{:T(128)S(6)} %select_n.63, s32[]{:T(128)S(6)} %select_n.65), kind=kLoop, calls=%fused_computation.33 | loop fusion | bytes 2162704 | tf_op jit(solution)/shard_map/dynamic_slice | solution.py:74
  2.3 2.1 %collective-permute-start.6 = (bf16[176,768]{1,0:T(8,128)(2,1)}, bf16[176,768]{1,0:T(8,128)(2,1)}, u32[]{:S(2)}, u32[]{:S(2)}) collective-permute-start(bf16[176,768]{1,0:T(8,128)(2,1)} %get-tuple-element.13), channel_id=1, source_target_pairs={{0,8},{8,0},{16,24},{24,16},{1,9},{9,1},{17,25},{25,17},{2,10},{10... | collective-permute-start | bytes 811016 | tf_op jit(solution)/shard_map/ppermute | solution.py:78
  4.4 2.3 %collective-permute-start.7 = (bf16[176,768]{1,0:T(8,128)(2,1)}, bf16[176,768]{1,0:T(8,128)(2,1)}, u32[]{:S(2)}, u32[]{:S(2)}) collective-permute-start(bf16[176,768]{1,0:T(8,128)(2,1)} %get-tuple-element.14), channel_id=1, source_target_pairs={{0,16},{8,24},{16,0},{24,8},{1,17},{9,25},{17,1},{25,9},{2,18},{10... | collective-permute-start | bytes 811016 | tf_op jit(solution)/shard_map/ppermute | solution.py:78
  9.4 1.3 %collective-permute-start.2 = (bf16[2,16,3072]{2,1,0:T(8,128)(2,1)}, bf16[2,16,3072]{2,1,0:T(8,128)(2,1)}, u32[]{:S(2)}, u32[]{:S(2)}) collective-permute-start(bf16[2,16,3072]{2,1,0:T(8,128)(2,1)} %get-tuple-element.33), channel_id=1, source_target_pairs={{0,3},{1,2},{2,1},{3,0},{8,11},{9,10},{10,9},{11,8},{16,19},{17,18... | collective-permute-start | bytes 589832 | tf_op jit(solution)/shard_map/ppermute | solution.py:101
  10.8 1.3 %collective-permute-start.1 = (bf16[2,16,3072]{2,1,0:T(8,128)(2,1)S(1)}, bf16[2,16,3072]{2,1,0:T(8,128)(2,1)}, u32[]{:S(2)}, u32[]{:S(2)}) collective-permute-start(bf16[2,16,3072]{2,1,0:T(8,128)(2,1)S(1)} %get-tuple-element.31), channel_id=1, source_target_pairs={{0,2},{1,3},{2,0},{3,1},{8,10},{9,11},{10,8},{11,9},{16,18},{17,19... | collective-permute-start | bytes 589832 | tf_op jit(solution)/shard_map/ppermute | solution.py:101
  12.1 1.3 %collective-permute-start = (bf16[2,16,3072]{2,1,0:T(8,128)(2,1)S(1)}, bf16[2,16,3072]{2,1,0:T(8,128)(2,1)}, u32[]{:S(2)}, u32[]{:S(2)}) collective-permute-start(bf16[2,16,3072]{2,1,0:T(8,128)(2,1)S(1)} %get-tuple-element.32), channel_id=1, source_target_pairs={{0,1},{1,0},{2,3},{3,2},{8,9},{9,8},{10,11},{11,10},{16,17},{17,16... | collective-permute-start | bytes 589832 | tf_op jit(solution)/shard_map/ppermute | solution.py:101
  13.8 1.3 %multiply_reduce_fusion.1 = (f32[2,4,16]{2,1,0:T(4,128)S(1)}, bf16[2,4,16,3072]{3,2,1,0:T(8,128)(2,1)S(1)}) fusion(bf16[2,1,16,3072]{3,2,1,0:T(8,128)(2,1)} %bitcast.28, bf16[2,1,16,3072]{3,2,1,0:T(8,128)(2,1)} %bitcast.26, bf16[2,1,16,3072]{3,2,1,0:T(8,128)(2,1)} %bitcast.24, bf16[2,1,16,3072]{3,2,1,0:T(8,128)(2,1)S(1)} %get-tuple-element.30), kind=kLoop, calls=%fused_computation.6 | loop fusion | flops 2359168 | bytes 1573376 | tf_op jit(solution)/shard_map/reduce_sum | solution.py:103
  20.9 1.5 %collective-permute-done.8 = bf16[176,768]{1,0:T(8,128)(2,1)} collective-permute-done((bf16[176,768]{1,0:T(8,128)(2,1)}, bf16[176,768]{1,0:T(8,128)(2,1)}, u32[]{:S(2)}, u32[]{:S(2)}) %collective-permute-start.8) | collective-permute-done | bytes 270368 | tf_op jit(solution)/shard_map/ppermute | solution.py:78
  25.1 3.4 %all-to-all-start = ((bf16[2,4,16,768]{3,2,0,1:T(8,128)(2,1)}), bf16[2,4,16,768]{3,2,0,1:T(8,128)(2,1)S(1)}, u32[]{:S(2)}, u32[]{:S(2)}) async-start(bf16[2,4,16,768]{3,2,0,1:T(8,128)(2,1)} %select_bitcast_fusion.2), calls=%async_computation | async-start | bytes 393216 | tf_op jit(solution)/shard_map/all_to_all | solution.py:120
  28.7 3.9 %all-to-all-done = bf16[2,4,16,768]{3,2,0,1:T(8,128)(2,1)S(1)} async-done(((bf16[2,4,16,768]{3,2,0,1:T(8,128)(2,1)}), bf16[2,4,16,768]{3,2,0,1:T(8,128)(2,1)S(1)}, u32[]{:S(2)}, u32[]{:S(2)}) %all-to-all-start) | async-done | bytes 196640 | tf_op jit(solution)/shard_map/all_to_all | solution.py:120
  33.0 1.3 %collective-permute-start.12 = (bf16[2,24,768]{2,1,0:T(8,128)(2,1)S(1)}, bf16[2,24,768]{2,1,0:T(8,128)(2,1)S(1)}, u32[]{:S(2)}, u32[]{:S(2)}) collective-permute-start(bf16[2,24,768]{2,1,0:T(8,128)(2,1)S(1)} %fusion.3), channel_id=1, source_target_pairs={{0,28},{1,29},{2,30},{3,31},{8,20},{9,21},{10,22},{11,23},{16,12},... | collective-permute-start | bytes 221192 | tf_op jit(solution)/shard_map/ppermute | solution.py:143
  34.3 1.3 %collective-permute-start.11 = (bf16[2,24,768]{2,1,0:T(8,128)(2,1)S(1)}, bf16[2,24,768]{2,1,0:T(8,128)(2,1)S(1)}, u32[]{:S(2)}, u32[]{:S(2)}) collective-permute-start(bf16[2,24,768]{2,1,0:T(8,128)(2,1)S(1)} %fusion.3), channel_id=1, source_target_pairs={{0,20},{1,21},{2,22},{3,23},{8,28},{9,29},{10,30},{11,31},{16,4},{... | collective-permute-start | bytes 221192 | tf_op jit(solution)/shard_map/ppermute | solution.py:143
  35.6 1.3 %collective-permute-start.10 = (bf16[2,24,768]{2,1,0:T(8,128)(2,1)S(1)}, bf16[2,24,768]{2,1,0:T(8,128)(2,1)S(1)}, u32[]{:S(2)}, u32[]{:S(2)}) collective-permute-start(bf16[2,24,768]{2,1,0:T(8,128)(2,1)S(1)} %fusion.3), channel_id=1, source_target_pairs={{0,12},{1,13},{2,14},{3,15},{8,4},{9,5},{10,6},{11,7},{16,28},{17,... | collective-permute-start | bytes 221192 | tf_op jit(solution)/shard_map/ppermute | solution.py:143
  38.2 17.2 %collective-permute-done.12 = bf16[2,24,768]{2,1,0:T(8,128)(2,1)S(1)} collective-permute-done((bf16[2,24,768]{2,1,0:T(8,128)(2,1)S(1)}, bf16[2,24,768]{2,1,0:T(8,128)(2,1)S(1)}, u32[]{:S(2)}, u32[]{:S(2)}) %collective-permute-start.12) | collective-permute-done | bytes 73760 | tf_op jit(solution)/shard_map/ppermute | solution.py:143
  55.5 1.8 %collective-permute-done.11 = bf16[2,24,768]{2,1,0:T(8,128)(2,1)S(1)} collective-permute-done((bf16[2,24,768]{2,1,0:T(8,128)(2,1)S(1)}, bf16[2,24,768]{2,1,0:T(8,128)(2,1)S(1)}, u32[]{:S(2)}, u32[]{:S(2)}) %collective-permute-start.11) | collective-permute-done | bytes 73760 | tf_op jit(solution)/shard_map/ppermute | solution.py:143
  59.8 2.7 %collective-permute-start.15 = (bf16[2,16,3072]{2,1,0:T(8,128)(2,1)S(1)}, bf16[2,16,3072]{2,1,0:T(8,128)(2,1)S(1)}, u32[]{:S(2)}, u32[]{:S(2)}) collective-permute-start(bf16[2,16,3072]{2,1,0:T(8,128)(2,1)S(1)} %get-tuple-element.29), channel_id=1, source_target_pairs={{4,7},{5,6},{6,5},{7,4},{12,15},{13,14},{14,13},{15,12},{20,23},{2... | collective-permute-start | bytes 589832 | tf_op jit(solution)/shard_map/ppermute | solution.py:101
  62.5 3.1 %collective-permute-start.14 = (bf16[2,16,3072]{2,1,0:T(8,128)(2,1)S(1)}, bf16[2,16,3072]{2,1,0:T(8,128)(2,1)S(1)}, u32[]{:S(2)}, u32[]{:S(2)}) collective-permute-start(bf16[2,16,3072]{2,1,0:T(8,128)(2,1)S(1)} %get-tuple-element.27), channel_id=1, source_target_pairs={{4,6},{5,7},{6,4},{7,5},{12,14},{13,15},{14,12},{15,13},{20,22},{2... | collective-permute-start | bytes 589832 | tf_op jit(solution)/shard_map/ppermute | solution.py:101
  65.6 2.6 %collective-permute-start.13 = (bf16[2,16,3072]{2,1,0:T(8,128)(2,1)S(1)}, bf16[2,16,3072]{2,1,0:T(8,128)(2,1)S(1)}, u32[]{:S(2)}, u32[]{:S(2)}) collective-permute-start(bf16[2,16,3072]{2,1,0:T(8,128)(2,1)S(1)} %get-tuple-element.28), channel_id=1, source_target_pairs={{4,5},{5,4},{6,7},{7,6},{12,13},{13,12},{14,15},{15,14},{20,21},{2... | collective-permute-start | bytes 589832 | tf_op jit(solution)/shard_map/ppermute | solution.py:101
  69.2 2.8 %collective-permute-done.13 = bf16[2,16,3072]{2,1,0:T(8,128)(2,1)S(1)} collective-permute-done((bf16[2,16,3072]{2,1,0:T(8,128)(2,1)S(1)}, bf16[2,16,3072]{2,1,0:T(8,128)(2,1)S(1)}, u32[]{:S(2)}, u32[]{:S(2)}) %collective-permute-start.13) | collective-permute-done | bytes 196640 | tf_op jit(solution)/shard_map/ppermute | solution.py:101
  74.1 3.8 %collective-permute-start.18 = (bf16[128,176]{0,1:T(8,128)(2,1)S(1)}, bf16[128,176]{0,1:T(8,128)(2,1)S(1)}, u32[]{:S(2)}, u32[]{:S(2)}) collective-permute-start(bf16[128,176]{0,1:T(8,128)(2,1)S(1)} %fusion.9), channel_id=1, source_target_pairs={{4,28},{5,29},{6,30},{7,31},{12,20},{13,21},{14,22},{15,23},{20,12... | collective-permute-start | bytes 135176 | tf_op jit(solution)/shard_map/ppermute | solution.py:111
  77.9 1.9 %collective-permute-start.17 = (bf16[128,176]{0,1:T(8,128)(2,1)S(1)}, bf16[128,176]{0,1:T(8,128)(2,1)S(1)}, u32[]{:S(2)}, u32[]{:S(2)}) collective-permute-start(bf16[128,176]{0,1:T(8,128)(2,1)S(1)} %fusion.9), channel_id=1, source_target_pairs={{4,20},{5,21},{6,22},{7,23},{12,28},{13,29},{14,30},{15,31},{20,4}... | collective-permute-start | bytes 135176 | tf_op jit(solution)/shard_map/ppermute | solution.py:111
  79.8 3.6 %collective-permute-start.16 = (bf16[128,176]{0,1:T(8,128)(2,1)S(1)}, bf16[128,176]{0,1:T(8,128)(2,1)S(1)}, u32[]{:S(2)}, u32[]{:S(2)}) collective-permute-start(bf16[128,176]{0,1:T(8,128)(2,1)S(1)} %fusion.9), channel_id=1, source_target_pairs={{4,12},{5,13},{6,14},{7,15},{12,4},{13,5},{14,6},{15,7},{20,28},{2... | collective-permute-start | bytes 135176 | tf_op jit(solution)/shard_map/ppermute | solution.py:111
  86.6 3.4 %all-to-all-start.1 = ((bf16[2,4,16,768]{3,2,0,1:T(8,128)(2,1)}), bf16[2,4,16,768]{3,2,0,1:T(8,128)(2,1)S(1)}, u32[]{:S(2)}, u32[]{:S(2)}) async-start(bf16[2,4,16,768]{3,2,0,1:T(8,128)(2,1)} %select_bitcast_fusion.1), calls=%async_computation.1 | async-start | bytes 393216 | tf_op jit(solution)/shard_map/all_to_all | solution.py:120
  90.0 4.0 %all-to-all-done.1 = bf16[2,4,16,768]{3,2,0,1:T(8,128)(2,1)S(1)} async-done(((bf16[2,4,16,768]{3,2,0,1:T(8,128)(2,1)}), bf16[2,4,16,768]{3,2,0,1:T(8,128)(2,1)S(1)}, u32[]{:S(2)}, u32[]{:S(2)}) %all-to-all-start.1) | async-done | bytes 196640 | tf_op jit(solution)/shard_map/all_to_all | solution.py:120
  (95 shorter events, 22.8 us)
Async XLA Ops:
  0.0 15.2 %copy-start = (bf16[1,1,3072,176]{2,3,1,0:T(8,128)(2,1)S(1)}, bf16[1,1,3072,176]{2,3,1,0:T(8,128)(2,1)}, u32[]{:S(2)}) copy-start(bf16[1,1,3072,176]{2,3,1,0:T(8,128)(2,1)} %param.11) | copy-start | bytes 3244036
  2.3 16.0 %collective-permute-start.6 = (bf16[176,768]{1,0:T(8,128)(2,1)}, bf16[176,768]{1,0:T(8,128)(2,1)}, u32[]{:S(2)}, u32[]{:S(2)}) collective-permute-start(bf16[176,768]{1,0:T(8,128)(2,1)} %get-tuple-element.13), channel_id=1, source_target_pairs={{0,8},{8,0},{16,24},{24,16},{1,9},{9,1},{17,25},{25,17},{2,10},{10... | collective-permute-start | bytes 811016 | tf_op jit(solution)/shard_map/ppermute | solution.py:78
  4.4 15.6 %collective-permute-start.7 = (bf16[176,768]{1,0:T(8,128)(2,1)}, bf16[176,768]{1,0:T(8,128)(2,1)}, u32[]{:S(2)}, u32[]{:S(2)}) collective-permute-start(bf16[176,768]{1,0:T(8,128)(2,1)} %get-tuple-element.14), channel_id=1, source_target_pairs={{0,16},{8,24},{16,0},{24,8},{1,17},{9,25},{17,1},{25,9},{2,18},{10... | collective-permute-start | bytes 811016 | tf_op jit(solution)/shard_map/ppermute | solution.py:78
  9.4 4.2 %collective-permute-start.2 = (bf16[2,16,3072]{2,1,0:T(8,128)(2,1)}, bf16[2,16,3072]{2,1,0:T(8,128)(2,1)}, u32[]{:S(2)}, u32[]{:S(2)}) collective-permute-start(bf16[2,16,3072]{2,1,0:T(8,128)(2,1)} %get-tuple-element.33), channel_id=1, source_target_pairs={{0,3},{1,2},{2,1},{3,0},{8,11},{9,10},{10,9},{11,8},{16,19},{17,18... | collective-permute-start | bytes 589832 | tf_op jit(solution)/shard_map/ppermute | solution.py:101
  10.8 3.0 %collective-permute-start.1 = (bf16[2,16,3072]{2,1,0:T(8,128)(2,1)S(1)}, bf16[2,16,3072]{2,1,0:T(8,128)(2,1)}, u32[]{:S(2)}, u32[]{:S(2)}) collective-permute-start(bf16[2,16,3072]{2,1,0:T(8,128)(2,1)S(1)} %get-tuple-element.31), channel_id=1, source_target_pairs={{0,2},{1,3},{2,0},{3,1},{8,10},{9,11},{10,8},{11,9},{16,18},{17,19... | collective-permute-start | bytes 589832 | tf_op jit(solution)/shard_map/ppermute | solution.py:101
  12.1 1.6 %collective-permute-start = (bf16[2,16,3072]{2,1,0:T(8,128)(2,1)S(1)}, bf16[2,16,3072]{2,1,0:T(8,128)(2,1)}, u32[]{:S(2)}, u32[]{:S(2)}) collective-permute-start(bf16[2,16,3072]{2,1,0:T(8,128)(2,1)S(1)} %get-tuple-element.32), channel_id=1, source_target_pairs={{0,1},{1,0},{2,3},{3,2},{8,9},{9,8},{10,11},{11,10},{16,17},{17,16... | collective-permute-start | bytes 589832 | tf_op jit(solution)/shard_map/ppermute | solution.py:101
  13.5 10.8 %copy-start.6 = (pred[4]{0:T(512)(128)(4,1)}, pred[4]{0:T(512)(128)(4,1)S(1)}, u32[]{:S(2)}) copy-start(pred[4]{0:T(512)(128)(4,1)S(1)} %get-tuple-element.18) | copy-start | bytes 16
  13.7 8.8 %collective-permute-start.8 = (bf16[176,768]{1,0:T(8,128)(2,1)}, bf16[176,768]{1,0:T(8,128)(2,1)}, u32[]{:S(2)}, u32[]{:S(2)}) collective-permute-start(bf16[176,768]{1,0:T(8,128)(2,1)} %get-tuple-element.15), channel_id=1, source_target_pairs={{0,24},{8,16},{16,8},{24,0},{1,25},{9,17},{17,9},{25,1},{2,26},{10... | collective-permute-start | bytes 811016 | tf_op jit(solution)/shard_map/ppermute | solution.py:78
  16.9 6.5 %collective-permute-start.5 = (bf16[128,176]{0,1:T(8,128)(2,1)S(1)}, bf16[128,176]{0,1:T(8,128)(2,1)S(1)}, u32[]{:S(2)}, u32[]{:S(2)}) collective-permute-start(bf16[128,176]{0,1:T(8,128)(2,1)S(1)} %fusion.8), channel_id=1, source_target_pairs={{0,24},{1,25},{2,26},{3,27},{8,16},{9,17},{10,18},{11,19},{16,8},{... | collective-permute-start | bytes 135176 | tf_op jit(solution)/shard_map/ppermute | solution.py:111
  17.6 5.8 %collective-permute-start.4 = (bf16[128,176]{0,1:T(8,128)(2,1)S(1)}, bf16[128,176]{0,1:T(8,128)(2,1)S(1)}, u32[]{:S(2)}, u32[]{:S(2)}) collective-permute-start(bf16[128,176]{0,1:T(8,128)(2,1)S(1)} %fusion.8), channel_id=1, source_target_pairs={{0,16},{1,17},{2,18},{3,19},{8,24},{9,25},{10,26},{11,27},{16,0},{... | collective-permute-start | bytes 135176 | tf_op jit(solution)/shard_map/ppermute | solution.py:111
  18.3 5.1 %collective-permute-start.3 = (bf16[128,176]{0,1:T(8,128)(2,1)S(1)}, bf16[128,176]{0,1:T(8,128)(2,1)S(1)}, u32[]{:S(2)}, u32[]{:S(2)}) collective-permute-start(bf16[128,176]{0,1:T(8,128)(2,1)S(1)} %fusion.8), channel_id=1, source_target_pairs={{0,8},{1,9},{2,10},{3,11},{8,0},{9,1},{10,2},{11,3},{16,24},{17,25... | collective-permute-start | bytes 135176 | tf_op jit(solution)/shard_map/ppermute | solution.py:111
  25.1 7.5 %all-to-all-start = ((bf16[2,4,16,768]{3,2,0,1:T(8,128)(2,1)}), bf16[2,4,16,768]{3,2,0,1:T(8,128)(2,1)S(1)}, u32[]{:S(2)}, u32[]{:S(2)}) async-start(bf16[2,4,16,768]{3,2,0,1:T(8,128)(2,1)} %select_bitcast_fusion.2), calls=%async_computation | async-start | bytes 393216 | tf_op jit(solution)/shard_map/all_to_all | solution.py:120
  33.0 22.5 %collective-permute-start.12 = (bf16[2,24,768]{2,1,0:T(8,128)(2,1)S(1)}, bf16[2,24,768]{2,1,0:T(8,128)(2,1)S(1)}, u32[]{:S(2)}, u32[]{:S(2)}) collective-permute-start(bf16[2,24,768]{2,1,0:T(8,128)(2,1)S(1)} %fusion.3), channel_id=1, source_target_pairs={{0,28},{1,29},{2,30},{3,31},{8,20},{9,21},{10,22},{11,23},{16,12},... | collective-permute-start | bytes 221192 | tf_op jit(solution)/shard_map/ppermute | solution.py:143
  34.3 23.0 %collective-permute-start.11 = (bf16[2,24,768]{2,1,0:T(8,128)(2,1)S(1)}, bf16[2,24,768]{2,1,0:T(8,128)(2,1)S(1)}, u32[]{:S(2)}, u32[]{:S(2)}) collective-permute-start(bf16[2,24,768]{2,1,0:T(8,128)(2,1)S(1)} %fusion.3), channel_id=1, source_target_pairs={{0,20},{1,21},{2,22},{3,23},{8,28},{9,29},{10,30},{11,31},{16,4},{... | collective-permute-start | bytes 221192 | tf_op jit(solution)/shard_map/ppermute | solution.py:143
  35.6 23.0 %collective-permute-start.10 = (bf16[2,24,768]{2,1,0:T(8,128)(2,1)S(1)}, bf16[2,24,768]{2,1,0:T(8,128)(2,1)S(1)}, u32[]{:S(2)}, u32[]{:S(2)}) collective-permute-start(bf16[2,24,768]{2,1,0:T(8,128)(2,1)S(1)} %fusion.3), channel_id=1, source_target_pairs={{0,12},{1,13},{2,14},{3,15},{8,4},{9,5},{10,6},{11,7},{16,28},{17,... | collective-permute-start | bytes 221192 | tf_op jit(solution)/shard_map/ppermute | solution.py:143
  36.9 21.7 %collective-permute-start.9 = (bf16[2,24,768]{2,1,0:T(8,128)(2,1)S(1)}, bf16[2,24,768]{2,1,0:T(8,128)(2,1)S(1)}, u32[]{:S(2)}, u32[]{:S(2)}) collective-permute-start(bf16[2,24,768]{2,1,0:T(8,128)(2,1)S(1)} %fusion.3), channel_id=1, source_target_pairs={{0,4},{1,5},{2,6},{3,7},{8,12},{9,13},{10,14},{11,15},{16,20},{17,... | collective-permute-start | bytes 221192 | tf_op jit(solution)/shard_map/ppermute | solution.py:143
  59.8 8.4 %collective-permute-start.15 = (bf16[2,16,3072]{2,1,0:T(8,128)(2,1)S(1)}, bf16[2,16,3072]{2,1,0:T(8,128)(2,1)S(1)}, u32[]{:S(2)}, u32[]{:S(2)}) collective-permute-start(bf16[2,16,3072]{2,1,0:T(8,128)(2,1)S(1)} %get-tuple-element.29), channel_id=1, source_target_pairs={{4,7},{5,6},{6,5},{7,4},{12,15},{13,14},{14,13},{15,12},{20,23},{2... | collective-permute-start | bytes 589832 | tf_op jit(solution)/shard_map/ppermute | solution.py:101
  62.5 6.7 %collective-permute-start.14 = (bf16[2,16,3072]{2,1,0:T(8,128)(2,1)S(1)}, bf16[2,16,3072]{2,1,0:T(8,128)(2,1)S(1)}, u32[]{:S(2)}, u32[]{:S(2)}) collective-permute-start(bf16[2,16,3072]{2,1,0:T(8,128)(2,1)S(1)} %get-tuple-element.27), channel_id=1, source_target_pairs={{4,6},{5,7},{6,4},{7,5},{12,14},{13,15},{14,12},{15,13},{20,22},{2... | collective-permute-start | bytes 589832 | tf_op jit(solution)/shard_map/ppermute | solution.py:101
  65.6 6.4 %collective-permute-start.13 = (bf16[2,16,3072]{2,1,0:T(8,128)(2,1)S(1)}, bf16[2,16,3072]{2,1,0:T(8,128)(2,1)S(1)}, u32[]{:S(2)}, u32[]{:S(2)}) collective-permute-start(bf16[2,16,3072]{2,1,0:T(8,128)(2,1)S(1)} %get-tuple-element.28), channel_id=1, source_target_pairs={{4,5},{5,4},{6,7},{7,6},{12,13},{13,12},{14,15},{15,14},{20,21},{2... | collective-permute-start | bytes 589832 | tf_op jit(solution)/shard_map/ppermute | solution.py:101
  74.1 11.8 %copy-start.7 = (pred[4]{0:T(512)(128)(4,1)S(1)}, pred[4]{0:T(512)(128)(4,1)}, u32[]{:S(2)}) copy-start(pred[4]{0:T(512)(128)(4,1)} %copy-done.6) | copy-start | bytes 16
  74.1 9.3 %collective-permute-start.18 = (bf16[128,176]{0,1:T(8,128)(2,1)S(1)}, bf16[128,176]{0,1:T(8,128)(2,1)S(1)}, u32[]{:S(2)}, u32[]{:S(2)}) collective-permute-start(bf16[128,176]{0,1:T(8,128)(2,1)S(1)} %fusion.9), channel_id=1, source_target_pairs={{4,28},{5,29},{6,30},{7,31},{12,20},{13,21},{14,22},{15,23},{20,12... | collective-permute-start | bytes 135176 | tf_op jit(solution)/shard_map/ppermute | solution.py:111
  77.9 5.7 %collective-permute-start.17 = (bf16[128,176]{0,1:T(8,128)(2,1)S(1)}, bf16[128,176]{0,1:T(8,128)(2,1)S(1)}, u32[]{:S(2)}, u32[]{:S(2)}) collective-permute-start(bf16[128,176]{0,1:T(8,128)(2,1)S(1)} %fusion.9), channel_id=1, source_target_pairs={{4,20},{5,21},{6,22},{7,23},{12,28},{13,29},{14,30},{15,31},{20,4}... | collective-permute-start | bytes 135176 | tf_op jit(solution)/shard_map/ppermute | solution.py:111
  79.8 5.0 %collective-permute-start.16 = (bf16[128,176]{0,1:T(8,128)(2,1)S(1)}, bf16[128,176]{0,1:T(8,128)(2,1)S(1)}, u32[]{:S(2)}, u32[]{:S(2)}) collective-permute-start(bf16[128,176]{0,1:T(8,128)(2,1)S(1)} %fusion.9), channel_id=1, source_target_pairs={{4,12},{5,13},{6,14},{7,15},{12,4},{13,5},{14,6},{15,7},{20,28},{2... | collective-permute-start | bytes 135176 | tf_op jit(solution)/shard_map/ppermute | solution.py:111
  86.6 7.4 %all-to-all-start.1 = ((bf16[2,4,16,768]{3,2,0,1:T(8,128)(2,1)}), bf16[2,4,16,768]{3,2,0,1:T(8,128)(2,1)S(1)}, u32[]{:S(2)}, u32[]{:S(2)}) async-start(bf16[2,4,16,768]{3,2,0,1:T(8,128)(2,1)} %select_bitcast_fusion.1), calls=%async_computation.1 | async-start | bytes 393216 | tf_op jit(solution)/shard_map/all_to_all | solution.py:120
  (6 other events, 32.7 us)
